TPU v7x, 32 devices: a whole 2x2x4 slice. The times are simulated.
32 devices in a mesh: dp: 4 (over y, x), expert: 8 (over z, core).
Axes of the slice: x: 2, y: 2, z: 4, core: 2. Of those that a mesh axis runs over, the one named last changes fastest.
Arguments:
- tokens: bfloat16 [4096, 3584], P(('dp', 'expert')), may hold values from -6 to 6
- gate_probs: float32 [4096, 8], P(('dp', 'expert')), may hold values from 0.1 to 1
- expert_ids: int32 [4096, 8], P(('dp', 'expert')), may hold values from 0 to 63, all different within a row; in each aligned block of 128 rows (0 to 127, 128 to 255, ...) at most 24 rows name the same one
- cotangent: bfloat16 [4096, 3584], P(('dp', 'expert')), may hold values from -6 to 6
- w_gate: bfloat16 [8, 3584, 2048], P('expert', None, 'dp'), may hold values from -0.09375 to 0.09375
- w_up: bfloat16 [8, 3584, 2048], P('expert', None, 'dp'), may hold values from -0.09375 to 0.09375
- w_down: bfloat16 [8, 2048, 3584], P('expert', 'dp'), may hold values from -0.125 to 0.125
Outputs:
- layer_out: bfloat16 [4096, 3584], P(('dp', 'expert'))
- grad_tokens: bfloat16 [4096, 3584], P(('dp', 'expert'))
- grad_probs: float32 [4096, 8], P(('dp', 'expert'))
- grad_gate: bfloat16 [8, 3584, 2048], P('expert', None, 'dp')
- grad_up: bfloat16 [8, 3584, 2048], P('expert', None, 'dp')
- grad_down: bfloat16 [8, 2048, 3584], P('expert', 'dp')
Inputs may be any that keep to these rules, and one draw needn't show every extreme that they name: `expert_ids`: each token names 8 distinct ids. Among the 128 tokens of one device no id is named by more than 24 of them, a bound that some block reaches. Only ids below 8 belong to the window.
All inputs are finite; a program needn't handle non-finite values.
Results may differ from a plain program's by a relative error of at most 0.012.
Values may be sent and summed in bfloat16 or wider, within the bound.
No kernel may reach another device: no remote copies, remote signals or barrier semaphores. Data moves between devices by JAX's collectives and lax.ppermute only.
A program may use at most 192 MiB of HBM per device.

v0:
```python
import jax
import jax.numpy as jnp
from jax import lax
from jax.sharding import PartitionSpec as P


def slot_table(flat_ids, experts, capacity, sentinel):
    matches = (flat_ids[:, None] == jnp.arange(experts, dtype=jnp.int32)[None, :]).astype(jnp.int32)
    earlier = jnp.cumsum(matches, axis=0) - matches
    slot_pos = jnp.sum(earlier * matches, axis=1)
    target = jnp.where(flat_ids < experts, flat_ids * capacity + slot_pos, experts * capacity)
    flat_index = jnp.arange(flat_ids.shape[0], dtype=jnp.int32)
    blank_table = jnp.full((experts * capacity,), sentinel, jnp.int32)
    return blank_table.at[target].set(flat_index, mode="drop")


def contract_last(left, right):
    return lax.dot_general(
        left, right, (((1,), (1,)), ((), ())), preferred_element_type=jnp.float32
    )


def contract_first(left, right):
    return lax.dot_general(
        left, right, (((0,), (0,)), ((), ())), preferred_element_type=jnp.float32
    )


def on_device(tokens, gate_probs, expert_ids, cotangent, w_gate, w_up, w_down):
    tok_count, model_width = tokens.shape
    top_k = expert_ids.shape[1]
    experts = lax.axis_size("expert")
    groups = lax.axis_size("dp")
    capacity = 3 * tok_count * top_k // (16 * experts)
    flat_count = tok_count * top_k
    slots = slot_table(expert_ids.reshape(-1), experts, capacity, flat_count)
    token_of = slots // top_k
    zero_row = jnp.zeros((1, model_width), jnp.bfloat16)
    send_x = jnp.concatenate([tokens, zero_row], 0)[token_of]
    rows_dy = jnp.concatenate([cotangent, zero_row], 0)[token_of]
    prob_rows = jnp.concatenate([gate_probs.reshape(-1), jnp.zeros((1,), jnp.float32)], 0)[slots]
    send_c = (prob_rows[:, None] * rows_dy.astype(jnp.float32)).astype(jnp.bfloat16)
    fanned_x = jnp.tile(send_x, (groups, 1))
    fanned_c = jnp.tile(send_c, (groups, 1))
    rows_x, rows_c = (
        lax.all_to_all(fanned_x, ("dp", "expert"), split_axis=0, concat_axis=0, tiled=True),
        lax.all_to_all(fanned_c, ("dp", "expert"), split_axis=0, concat_axis=0, tiled=True),
    )
    gate_w = w_gate[0]
    up_w = w_up[0]
    down_w = w_down[0]
    gate_pre = jnp.dot(rows_x, gate_w, preferred_element_type=jnp.float32)
    up_pre = jnp.dot(rows_x, up_w, preferred_element_type=jnp.float32)
    sigmoid_g = jax.nn.sigmoid(gate_pre)
    activated = gate_pre * sigmoid_g
    hidden = (activated * up_pre).astype(jnp.bfloat16)
    part_out = jnp.dot(hidden, down_w, preferred_element_type=jnp.float32).astype(jnp.bfloat16)
    returned = lax.all_to_all(part_out, ("dp", "expert"), split_axis=0, concat_axis=0, tiled=True)
    out_rows = jnp.sum(
        returned.astype(jnp.float32).reshape(groups, experts * capacity, model_width), axis=0
    )
    grad_hidden = contract_last(rows_c, down_w)
    grad_upin = (grad_hidden * activated).astype(jnp.bfloat16)
    grad_gatein = (grad_hidden * up_pre * sigmoid_g * (1.0 + gate_pre * (1.0 - sigmoid_g))).astype(
        jnp.bfloat16
    )
    part_dx = (contract_last(grad_gatein, gate_w) + contract_last(grad_upin, up_w)).astype(
        jnp.bfloat16
    )
    returned_dx = lax.all_to_all(part_dx, ("dp", "expert"), split_axis=0, concat_axis=0, tiled=True)
    dx_rows = jnp.sum(
        returned_dx.astype(jnp.float32).reshape(groups, experts * capacity, model_width), axis=0
    )
    new_gate = contract_first(rows_x, grad_gatein).astype(jnp.bfloat16)[None]
    new_up = contract_first(rows_x, grad_upin).astype(jnp.bfloat16)[None]
    new_down = contract_first(hidden, rows_c).astype(jnp.bfloat16)[None]
    owner = (token_of[None, :] == jnp.arange(tok_count, dtype=jnp.int32)[:, None]).astype(
        jnp.float32
    )
    layer_out = jnp.dot(
        owner * prob_rows[None, :],
        out_rows,
        precision=lax.Precision.HIGHEST,
        preferred_element_type=jnp.float32,
    ).astype(jnp.bfloat16)
    grad_tokens = jnp.dot(
        owner, dx_rows, precision=lax.Precision.HIGHEST, preferred_element_type=jnp.float32
    ).astype(jnp.bfloat16)
    score_rows = jnp.sum(rows_dy.astype(jnp.float32) * out_rows, axis=1)
    grad_probs = (
        jnp.zeros((flat_count + 1,), jnp.float32)
        .at[slots]
        .set(score_rows)[:flat_count]
        .reshape(tok_count, top_k)
    )
    return (layer_out, grad_tokens, grad_probs, new_gate, new_up, new_down)


def solution(mesh):
    return jax.shard_map(
        on_device,
        mesh=mesh,
        in_specs=(
            P(("dp", "expert"), None),
            P(("dp", "expert"), None),
            P(("dp", "expert"), None),
            P(("dp", "expert"), None),
            P("expert", None, "dp"),
            P("expert", None, "dp"),
            P("expert", "dp", None),
        ),
        out_specs=(
            P(("dp", "expert"), None),
            P(("dp", "expert"), None),
            P(("dp", "expert"), None),
            P("expert", None, "dp"),
            P("expert", None, "dp"),
            P("expert", "dp", None),
        ),
        check_vma=False,
    )
```

profile of v0, /device:TPU:0, one launch (start us, length us, event | category | flops | bytes accessed | tf_op | source)
XLA Modules:
  0.0 548.8 jit_solution(694235847284773781)
XLA Ops:
  0.6 0.7 broadcast_compare_fusion
  2.0 0.8 copy.15
  3.4 2.3 reduce-window.6
  6.3 4.3 scatter_custom_fusion
  10.6 1.2 concatenate.10
  11.9 1.4 gather_fusion.1
  13.3 2.9 tile.4
  16.2 7.4 %all-to-all-start = ((bf16[32,24,3584]{2,1,0:T(8,128)(2,1)}), bf16[32,24,3584]{2,1,0:T(8,128)(2,1)}, u32[]{:S(2)}, u32[]{:S(2)}) async-start(bf16[32,24,3584]{2,1,0:T(8,128)(2,1)} %bitcast.74), calls=%async_computation | async-start | bytes 11010048 | tf_op jit(solution)/shard_map/all_to_all | solution.py:46
  23.9 1.4 gather_fusion.2
  25.3 1.4 gather_fusion
  27.1 119.6 %all-to-all-done = bf16[32,24,3584]{2,1,0:T(8,128)(2,1)} async-done(((bf16[32,24,3584]{2,1,0:T(8,128)(2,1)}), bf16[32,24,3584]{2,1,0:T(8,128)(2,1)}, u32[]{:S(2)}, u32[]{:S(2)}) %all-to-all-start) | async-done | bytes 5505056 | tf_op jit(solution)/shard_map/all_to_all | solution.py:46
  146.7 2.8 tile.5
  149.5 3.6 all-to-all-start.2
  153.2 7.9 %fusion.7 = f32[768,512]{1,0:T(8,128)} fusion(bf16[768,3584]{1,0:T(8,128)(2,1)} %bitcast.4, bf16[1,3584,512]{2,1,0:T(8,128)(2,1)} %param.12), kind=kOutput, calls=%fused_computation.21 | convolution fusion | flops 2818572288 | bytes 10747904 | tf_op jit(solution)/shard_map/dot_general | solution.py:53
  161.1 6.7 %fusion.11 = f32[768,512]{1,0:T(8,128)} fusion(bf16[768,3584]{1,0:T(8,128)(2,1)} %bitcast.4, bf16[1,3584,512]{2,1,0:T(8,128)(2,1)S(1)} %copy-done.5), kind=kOutput, calls=%fused_computation.25 | convolution fusion | flops 2818572288 | bytes 10747904 | tf_op jit(solution)/shard_map/dot_general | solution.py:52
  167.8 108.5 %all-to-all-done.2 = bf16[32,24,3584]{2,1,0:T(8,128)(2,1)} async-done(((bf16[32,24,3584]{2,1,0:T(8,128)(2,1)}), bf16[32,24,3584]{2,1,0:T(8,128)(2,1)}, u32[]{:S(2)}, u32[]{:S(2)}) %all-to-all-start.2) | async-done | bytes 5505056 | tf_op jit(solution)/shard_map/all_to_all | solution.py:47
  276.3 8.3 %multiply_convert_fusion = (bf16[768,512]{1,0:T(8,128)(2,1)S(1)}, bf16[768,512]{1,0:T(8,128)(2,1)S(1)}, bf16[768,512]{1,0:T(8,128)(2,1)S(1)}) fusion(f32[768,512]{1,0:T(8,128)} %fusion.11, f32[768,512]{1,0:T(8,128)} %fusion.7, bf16[768,3584]{1,0:T(8,128)(2,1)} %bitcast.11, bf16[1,512,3584]{2,1,0:T(8,128)(2,1)} %param.13), kind=kOutput, calls=%fused_computation.31 | convolution fusion | flops 2824470528 | bytes 14680064 | tf_op jit(solution)/shard_map/dot_general | solution.py:18
  284.6 4.8 convolution_convert_fusion
  289.4 3.8 all-to-all-start.1
  293.2 5.2 fusion.9
  298.5 4.8 add_convert_fusion
  303.3 112.8 %all-to-all-done.1 = bf16[32,24,3584]{2,1,0:T(8,128)(2,1)} async-done(((bf16[32,24,3584]{2,1,0:T(8,128)(2,1)}), bf16[32,24,3584]{2,1,0:T(8,128)(2,1)}, u32[]{:S(2)}, u32[]{:S(2)}) %all-to-all-start.1) | async-done | bytes 5505056 | tf_op jit(solution)/shard_map/all_to_all | solution.py:58
  416.1 3.6 all-to-all-start.3
  419.7 7.1 %fusion.2 = bf16[1,512,3584]{2,1,0:T(8,128)(2,1)} fusion(bf16[768,512]{1,0:T(8,128)(2,1)S(1)} %get-tuple-element.16, bf16[768,3584]{1,0:T(8,128)(2,1)} %bitcast.11), kind=kOutput, calls=%fused_computation.14 | convolution fusion | flops 2820407296 | bytes 9961472 | tf_op jit(solution)/shard_map/dot_general | solution.py:24
  426.8 7.1 %fusion.1 = bf16[1,3584,512]{2,1,0:T(8,128)(2,1)} fusion(bf16[768,3584]{1,0:T(8,128)(2,1)} %bitcast.4, bf16[768,512]{1,0:T(8,128)(2,1)S(1)} %get-tuple-element.14), kind=kOutput, calls=%fused_computation.13 | convolution fusion | flops 2820407296 | bytes 9961472 | tf_op jit(solution)/shard_map/dot_general | solution.py:24
  433.9 7.1 %fusion = bf16[1,3584,512]{2,1,0:T(8,128)(2,1)} fusion(bf16[768,3584]{1,0:T(8,128)(2,1)} %bitcast.4, bf16[768,512]{1,0:T(8,128)(2,1)S(1)} %get-tuple-element.15), kind=kOutput, calls=%fused_computation.12 | convolution fusion | flops 2820407296 | bytes 9961472 | tf_op jit(solution)/shard_map/dot_general | solution.py:24
  441.0 3.7 convert_reduce_fusion.1
  445.2 1.4 scatter_custom_fusion.1
  447.4 2.7 convolution_convert_fusion.5
  450.0 92.8 %all-to-all-done.3 = bf16[32,24,3584]{2,1,0:T(8,128)(2,1)} async-done(((bf16[32,24,3584]{2,1,0:T(8,128)(2,1)}), bf16[32,24,3584]{2,1,0:T(8,128)(2,1)}, u32[]{:S(2)}, u32[]{:S(2)}) %all-to-all-start.3) | async-done | bytes 5505056 | tf_op jit(solution)/shard_map/all_to_all | solution.py:70
  542.9 3.7 convert_reduce_fusion
  546.6 2.2 convolution_convert_fusion.4
  (39 shorter events, 3.7 us)
Async XLA Ops:
  16.2 7.4 %copy-start.3 = (f32[128,8]{0,1:T(8,128)S(1)}, f32[128,8]{0,1:T(8,128)}, u32[]{:S(2)}) copy-start(f32[128,8]{0,1:T(8,128)} %param.8) | copy-start | bytes 12292
  16.2 7.6 %copy-start.2 = (bf16[128,3584]{1,0:T(8,128)(2,1)S(1)}, bf16[128,3584]{1,0:T(8,128)(2,1)}, u32[]{:S(2)}) copy-start(bf16[128,3584]{1,0:T(8,128)(2,1)} %param.10) | copy-start | bytes 2752516
  16.2 130.5 %all-to-all-start = ((bf16[32,24,3584]{2,1,0:T(8,128)(2,1)}), bf16[32,24,3584]{2,1,0:T(8,128)(2,1)}, u32[]{:S(2)}, u32[]{:S(2)}) async-start(bf16[32,24,3584]{2,1,0:T(8,128)(2,1)} %bitcast.74), calls=%async_computation | async-start | bytes 11010048 | tf_op jit(solution)/shard_map/all_to_all | solution.py:46
  25.3 124.2 %copy-start = (bf16[192,3584]{1,0:T(8,128)(2,1)}, bf16[192,3584]{1,0:T(8,128)(2,1)S(1)}, u32[]{:S(2)}) copy-start(bf16[192,3584]{1,0:T(8,128)(2,1)S(1)} %gather_fusion.2) | copy-start | bytes 4128772
  149.5 126.8 %all-to-all-start.2 = ((bf16[32,24,3584]{2,1,0:T(8,128)(2,1)}), bf16[32,24,3584]{2,1,0:T(8,128)(2,1)}, u32[]{:S(2)}, u32[]{:S(2)}) async-start(bf16[32,24,3584]{2,1,0:T(8,128)(2,1)} %bitcast.75), calls=%async_computation.2 | async-start | bytes 11010048 | tf_op jit(solution)/shard_map/all_to_all | solution.py:47
  153.1 8.0 %copy-start.5 = (bf16[1,3584,512]{2,1,0:T(8,128)(2,1)S(1)}, bf16[1,3584,512]{2,1,0:T(8,128)(2,1)}, u32[]{:S(2)}) copy-start(bf16[1,3584,512]{2,1,0:T(8,128)(2,1)} %param.11) | copy-start | bytes 11010052
  276.3 8.3 %copy-start.4 = (bf16[1,512,3584]{2,1,0:T(8,128)(2,1)S(1)}, bf16[1,512,3584]{2,1,0:T(8,128)(2,1)}, u32[]{:S(2)}) copy-start(bf16[1,512,3584]{2,1,0:T(8,128)(2,1)} %param.13) | copy-start | bytes 11010052
  289.4 126.7 %all-to-all-start.1 = ((bf16[32,24,3584]{2,1,0:T(8,128)(2,1)}), bf16[32,24,3584]{2,1,0:T(8,128)(2,1)}, u32[]{:S(2)}, u32[]{:S(2)}) async-start(bf16[32,24,3584]{2,1,0:T(8,128)(2,1)} %bitcast.77), calls=%async_computation.1 | async-start | bytes 11010048 | tf_op jit(solution)/shard_map/all_to_all | solution.py:58
  293.2 5.3 copy-start.6
  416.1 126.7 %all-to-all-start.3 = ((bf16[32,24,3584]{2,1,0:T(8,128)(2,1)}), bf16[32,24,3584]{2,1,0:T(8,128)(2,1)}, u32[]{:S(2)}, u32[]{:S(2)}) async-start(bf16[32,24,3584]{2,1,0:T(8,128)(2,1)} %bitcast.76), calls=%async_computation.3 | async-start | bytes 11010048 | tf_op jit(solution)/shard_map/all_to_all | solution.py:70
  441.0 3.7 copy-start.1
where the time goes:
time: 549 us
  waiting for transfers between devices  434 us (79%)
  matrix products  64 us (12%)
  local copies, waits for them, and re-layouts  19.6 us (4%)
  starting transfers between devices  18.4 us (3%)
  other arithmetic  12.1 us (2%)
    all_to_all x1, waiting for transfers between devices, on_device(): lax.all_to_all(fanned_x, ('dp', 'expert'), split_axis=0, concat_axis=0, t...  120 us
    all_to_all x1, waiting for transfers between devices, on_device(): lax.all_to_all(part_out, ('dp', 'expert'), split_axis=0, concat_axis=0, t...  113 us
    all_to_all x1, waiting for transfers between devices, on_device(): lax.all_to_all(fanned_c, ('dp', 'expert'), split_axis=0, concat_axis=0, t...  108 us
    all_to_all x1, waiting for transfers between devices, on_device(): lax.all_to_all(part_dx, ('dp', 'expert'), split_axis=0, concat_axis=0, ti...  92.8 us
    dot_general x3, matrix products, contract_first(): lax.dot_general(left, right, (((0,), (0,)), ((), ())), preferred_element_...  21.3 us
    dot_general x3, matrix products, contract_last(): lax.dot_general(left, right, (((1,), (1,)), ((), ())), preferred_element_...  18.4 us
  transfers between devices with their start and end apart: 4, of which 4 were waited for; matrix products, arithmetic and copies ran while one was open for 11% of the time, Pallas kernels for 0%

commit v1 on v0

--- a/solution.py
+++ b/solution.py
@@ -26,6 +26,20 @@
     )
 
 
+def dispatch(send_rows):
+    along_expert = lax.all_to_all(send_rows, "expert", split_axis=0, concat_axis=0, tiled=True)
+    return lax.all_gather(along_expert, "dp", axis=0, tiled=True)
+
+
+def gather_back(partial_rows, groups):
+    by_group = lax.all_to_all(partial_rows, "dp", split_axis=0, concat_axis=0, tiled=True)
+    rows = by_group.shape[0] // groups
+    summed = jnp.sum(by_group.astype(jnp.float32).reshape(groups, rows, -1), axis=0)
+    return lax.all_to_all(
+        summed.astype(jnp.bfloat16), "expert", split_axis=0, concat_axis=0, tiled=True
+    )
+
+
 def on_device(tokens, gate_probs, expert_ids, cotangent, w_gate, w_up, w_down):
     tok_count, model_width = tokens.shape
     top_k = expert_ids.shape[1]
@@ -40,12 +54,8 @@
     rows_dy = jnp.concatenate([cotangent, zero_row], 0)[token_of]
     prob_rows = jnp.concatenate([gate_probs.reshape(-1), jnp.zeros((1,), jnp.float32)], 0)[slots]
     send_c = (prob_rows[:, None] * rows_dy.astype(jnp.float32)).astype(jnp.bfloat16)
-    fanned_x = jnp.tile(send_x, (groups, 1))
-    fanned_c = jnp.tile(send_c, (groups, 1))
-    rows_x, rows_c = (
-        lax.all_to_all(fanned_x, ("dp", "expert"), split_axis=0, concat_axis=0, tiled=True),
-        lax.all_to_all(fanned_c, ("dp", "expert"), split_axis=0, concat_axis=0, tiled=True),
-    )
+    rows_x = dispatch(send_x)
+    rows_c = dispatch(send_c)
     gate_w = w_gate[0]
     up_w = w_up[0]
     down_w = w_down[0]
@@ -55,10 +65,7 @@
     activated = gate_pre * sigmoid_g
     hidden = (activated * up_pre).astype(jnp.bfloat16)
     part_out = jnp.dot(hidden, down_w, preferred_element_type=jnp.float32).astype(jnp.bfloat16)
-    returned = lax.all_to_all(part_out, ("dp", "expert"), split_axis=0, concat_axis=0, tiled=True)
-    out_rows = jnp.sum(
-        returned.astype(jnp.float32).reshape(groups, experts * capacity, model_width), axis=0
-    )
+    out_rows = gather_back(part_out, groups).astype(jnp.float32)
     grad_hidden = contract_last(rows_c, down_w)
     grad_upin = (grad_hidden * activated).astype(jnp.bfloat16)
     grad_gatein = (grad_hidden * up_pre * sigmoid_g * (1.0 + gate_pre * (1.0 - sigmoid_g))).astype(
@@ -67,10 +74,7 @@
     part_dx = (contract_last(grad_gatein, gate_w) + contract_last(grad_upin, up_w)).astype(
         jnp.bfloat16
     )
-    returned_dx = lax.all_to_all(part_dx, ("dp", "expert"), split_axis=0, concat_axis=0, tiled=True)
-    dx_rows = jnp.sum(
-        returned_dx.astype(jnp.float32).reshape(groups, experts * capacity, model_width), axis=0
-    )
+    dx_rows = gather_back(part_dx, groups).astype(jnp.float32)
     new_gate = contract_first(rows_x, grad_gatein).astype(jnp.bfloat16)[None]
     new_up = contract_first(rows_x, grad_upin).astype(jnp.bfloat16)[None]
     new_down = contract_first(hidden, rows_c).astype(jnp.bfloat16)[None]

time: 549 us -> 419 us (0.76)
  waiting for transfers between devices: 434 us -> 213 us
  blocking collectives: 0 us -> 76.7 us
  between operations: 0.89 us -> 14.3 us
  local copies, waits for them, and re-layouts: 19.6 us -> 14 us
    all_to_all x4, waiting for transfers between devices: 434 us -> 138 us  [the longest x2 102 us: gather_back(): lax.all_to_all(partial_rows, 'dp', split_axis=0, concat_axis=0, tiled=True)]
    all_to_all x0 -> x2, blocking collectives: none -> 76.7 us  [dispatch(): lax.all_to_all(send_rows, 'expert', split_axis=0, concat_axis=0, tiled=True)]
    all_gather x0 -> x2, waiting for transfers between devices: none -> 75.7 us  [dispatch(): return lax.all_gather(along_expert, 'dp', axis=0, tiled=True)]
    dot_general x3, matrix products: 18.4 us -> 24.8 us  [contract_last(): lax.dot_general(left, right, (((1,), (1,)), ((), ())), preferred_element_...]
    another operation x2 -> x0, local copies, waits for them, and re-layouts: 5.66 us -> none  [the longest x1 2.87 us: on_device(): fanned_x = jnp.tile(send_x, (groups, 1))]
  transfers between devices with their start and end apart: 4 -> 6, of which waited for: 4 -> 6; matrix products, arithmetic and copies ran while one was open for 11% -> 16% of each run, Pallas kernels for 0% -> 0%
where the time goes in v1:
time: 419 us
  waiting for transfers between devices  213 us (51%)
  blocking collectives  76.7 us (18%)
  matrix products  65.7 us (16%)
  starting transfers between devices  18.7 us (4%)
  other arithmetic  15.8 us (4%)
  between operations  14.3 us (3%)
  local copies, waits for them, and re-layouts  14 us (3%)
    all_to_all x2, waiting for transfers between devices, gather_back(): lax.all_to_all(partial_rows, 'dp', split_axis=0, concat_axis=0, tiled=True)  102 us
    all_to_all x2, blocking collectives, dispatch(): lax.all_to_all(send_rows, 'expert', split_axis=0, concat_axis=0, tiled=True)  76.7 us
    all_gather x2, waiting for transfers between devices, dispatch(): return lax.all_gather(along_expert, 'dp', axis=0, tiled=True)  75.7 us
    all_to_all x2, waiting for transfers between devices, gather_back(): lax.all_to_all(summed.astype(jnp.bfloat16), 'expert', split_axis=0, conca...  35.8 us
    dot_general x3, matrix products, contract_last(): lax.dot_general(left, right, (((1,), (1,)), ((), ())), preferred_element_...  24.8 us
    dot_general x3, matrix products, contract_first(): lax.dot_general(left, right, (((0,), (0,)), ((), ())), preferred_element_...  19.6 us
    all_to_all x2, starting transfers between devices, gather_back(): lax.all_to_all(partial_rows, 'dp', split_axis=0, concat_axis=0, tiled=True)  10.4 us
    reduce_sum x2, other arithmetic, gather_back(): jnp.sum(by_group.astype(jnp.float32).reshape(groups, rows, -1), axis=0)  9.71 us
  transfers between devices with their start and end apart: 6, of which 6 were waited for; matrix products, arithmetic and copies ran while one was open for 16% of the time, Pallas kernels for 0%

profile of v1, /device:TPU:0, one launch (start us, length us, event | category | flops | bytes accessed | tf_op | source)
XLA Modules:
  0.0 418.6 jit_solution(15458522235983196097)
XLA Ops:
  10.0 2.3 reduce-window.6
  12.9 4.3 %scatter_custom_fusion = s32[192]{0:T(256)S(1)} fusion(s32[1024]{0:T(1024)S(1)} %bitcast.81, s32[1024]{0:T(1024)S(1)} %iota.15, s32[]{:T(128)} %constant.15.clone.1), kind=kCustom, calls=%fused_computation.63 | custom fusion | bytes 772 | tf_op jit(solution)/shard_map/scatter | solution.py:14
  17.2 1.2 concatenate.10
  18.5 1.4 gather_fusion.1
  19.9 40.0 %all_to_all.57 = bf16[8,24,3584]{2,1,0:T(8,128)(2,1)} all-to-all(bf16[8,24,3584]{2,1,0:T(8,128)(2,1)S(1)} %bitcast.73), channel_id=1, replica_groups=mesh['dp'=4,'expert'=8] {'expert'}, dimensions={0} | all-to-all | bytes 2752512 | tf_op jit(solution)/shard_map/all_to_all | solution.py:30
  60.2 1.4 gather_fusion
  61.8 1.4 gather_fusion.2
  63.5 36.7 %all_to_all.58 = bf16[8,24,3584]{2,1,0:T(8,128)(2,1)} all-to-all(bf16[8,24,3584]{2,1,0:T(8,128)(2,1)S(1)} %fusion.13), channel_id=1, replica_groups=mesh['dp'=4,'expert'=8] {'expert'}, dimensions={0} | all-to-all | bytes 2752512 | tf_op jit(solution)/shard_map/all_to_all | solution.py:30
  100.3 22.3 %all-gather.3.cloned.1.call-done = bf16[768,3584]{1,0:T(8,128)(2,1)} async-done(((bf16[192,3584]{1,0:T(8,128)(2,1)}), bf16[768,3584]{1,0:T(8,128)(2,1)}) %all-gather.3.cloned.1.call-update) | async-done | bytes 5505040 | tf_op jit(solution)/shard_map/all_gather | solution.py:31
  122.6 7.9 %fusion.7 = f32[768,512]{1,0:T(8,128)} fusion(bf16[768,3584]{1,0:T(8,128)(2,1)} %all-gather.3.cloned.1.call-done, bf16[1,3584,512]{2,1,0:T(8,128)(2,1)} %param.12), kind=kOutput, calls=%fused_computation.19 | convolution fusion | flops 2818572288 | bytes 10747904 | tf_op jit(solution)/shard_map/dot_general | solution.py:63
  130.5 4.1 fusion.11
  134.7 53.4 %all-gather.5.cloned.1.call-done = bf16[768,3584]{1,0:T(8,128)(2,1)} async-done(((bf16[192,3584]{1,0:T(8,128)(2,1)}), bf16[768,3584]{1,0:T(8,128)(2,1)}) %all-gather.5.cloned.1.call-update) | async-done | bytes 5505040 | tf_op jit(solution)/shard_map/all_gather | solution.py:31
  188.1 9.2 %multiply_convert_fusion = (bf16[768,512]{1,0:T(8,128)(2,1)}, bf16[768,512]{1,0:T(8,128)(2,1)S(1)}, bf16[768,512]{1,0:T(8,128)(2,1)S(1)}) fusion(f32[768,512]{1,0:T(8,128)} %fusion.11, f32[768,512]{1,0:T(8,128)} %fusion.7, bf16[768,3584]{1,0:T(8,128)(2,1)} %all-gather.5.cloned.1.call-done, bf16[1,512,3584]{2,1,0:T(8,128)(2,1)} %param.13), kind=kOutput, calls=%fused_computation.29 | convolution fusion | flops 2824470528 | bytes 14680064 | tf_op jit(solution)/shard_map/dot_general | solution.py:18
  197.2 4.8 %convolution_convert_fusion = bf16[768,3584]{1,0:T(8,128)(2,1)} fusion(bf16[768,512]{1,0:T(8,128)(2,1)S(1)} %get-tuple-element.16, bf16[1,512,3584]{2,1,0:T(8,128)(2,1)S(1)} %copy-done.3), kind=kOutput, calls=%fused_computation.6 | convolution fusion | flops 2821324800 | bytes 9961472 | tf_op jit(solution)/shard_map/dot_general | solution.py:67
  202.0 5.3 %all-to-all-start.1 = ((bf16[4,192,3584]{2,1,0:T(8,128)(2,1)}), bf16[4,192,3584]{2,1,0:T(8,128)(2,1)}, u32[]{:S(2)}, u32[]{:S(2)}) async-start(bf16[4,192,3584]{2,1,0:T(8,128)(2,1)} %bitcast.75), calls=%async_computation.1 | async-start | bytes 11010048 | tf_op jit(solution)/shard_map/all_to_all | solution.py:35
  207.4 8.1 %fusion.9 = f32[768,3584]{1,0:T(8,128)} fusion(bf16[768,512]{1,0:T(8,128)(2,1)S(1)} %get-tuple-element.15, bf16[1,3584,512]{2,1,0:T(8,128)(2,1)} %param.11), kind=kOutput, calls=%fused_computation.21 | convolution fusion | flops 2818572288 | bytes 15466496 | tf_op jit(solution)/shard_map/dot_general | solution.py:18
  215.4 7.6 %add_convert_fusion = bf16[768,3584]{1,0:T(8,128)(2,1)} fusion(f32[768,3584]{1,0:T(8,128)} %fusion.9, bf16[768,512]{1,0:T(8,128)(2,1)S(1)} %copy-done.7, bf16[1,3584,512]{2,1,0:T(8,128)(2,1)S(1)} %copy-done.5), kind=kOutput, calls=%fused_computation.5 | convolution fusion | flops 2824077312 | bytes 20971520 | tf_op jit(solution)/shard_map/dot_general | solution.py:18
  223.0 45.9 %all-to-all-done.1 = bf16[4,192,3584]{2,1,0:T(8,128)(2,1)} async-done(((bf16[4,192,3584]{2,1,0:T(8,128)(2,1)}), bf16[4,192,3584]{2,1,0:T(8,128)(2,1)}, u32[]{:S(2)}, u32[]{:S(2)}) %all-to-all-start.1) | async-done | bytes 5505056 | tf_op jit(solution)/shard_map/all_to_all | solution.py:35
  268.9 5.1 %all-to-all-start.4 = ((bf16[4,192,3584]{2,1,0:T(8,128)(2,1)}), bf16[4,192,3584]{2,1,0:T(8,128)(2,1)}, u32[]{:S(2)}, u32[]{:S(2)}) async-start(bf16[4,192,3584]{2,1,0:T(8,128)(2,1)} %bitcast.74), calls=%async_computation.4 | async-start | bytes 11010048 | tf_op jit(solution)/shard_map/all_to_all | solution.py:35
  274.0 4.8 %reduce_sum.48 = bf16[192,3584]{1,0:T(8,128)(2,1)} reduce(bf16[4,192,3584]{2,1,0:T(8,128)(2,1)} %all-to-all-done.1, bf16[]{:T(256)} %constant.45.clone.1), dimensions={0}, to_apply=%region_4.5 | reduce | flops 2064384 | bytes 6881282 | tf_op jit(solution)/shard_map/reduce_sum | solution.py:37
  278.9 56.1 %all-to-all-done.4 = bf16[4,192,3584]{2,1,0:T(8,128)(2,1)} async-done(((bf16[4,192,3584]{2,1,0:T(8,128)(2,1)}), bf16[4,192,3584]{2,1,0:T(8,128)(2,1)}, u32[]{:S(2)}, u32[]{:S(2)}) %all-to-all-start.4) | async-done | bytes 5505056 | tf_op jit(solution)/shard_map/all_to_all | solution.py:35
  334.9 4.6 %all-to-all-start.2 = ((bf16[8,24,3584]{2,1,0:T(8,128)(2,1)}), bf16[8,24,3584]{2,1,0:T(8,128)(2,1)}, u32[]{:S(2)}, u32[]{:S(2)}) async-start(bf16[8,24,3584]{2,1,0:T(8,128)(2,1)} %bitcast.9), calls=%async_computation.2 | async-start | bytes 2752512 | tf_op jit(solution)/shard_map/all_to_all | solution.py:38
  339.6 4.9 %reduce_sum.49 = bf16[192,3584]{1,0:T(8,128)(2,1)} reduce(bf16[4,192,3584]{2,1,0:T(8,128)(2,1)} %all-to-all-done.4, bf16[]{:T(256)} %constant.45.clone.1), dimensions={0}, to_apply=%region_5.6 | reduce | flops 2064384 | bytes 6881282 | tf_op jit(solution)/shard_map/reduce_sum | solution.py:37
  344.4 28.9 %all-to-all-done.2 = bf16[8,24,3584]{2,1,0:T(8,128)(2,1)} async-done(((bf16[8,24,3584]{2,1,0:T(8,128)(2,1)}), bf16[8,24,3584]{2,1,0:T(8,128)(2,1)}, u32[]{:S(2)}, u32[]{:S(2)}) %all-to-all-start.2) | async-done | bytes 1376288 | tf_op jit(solution)/shard_map/all_to_all | solution.py:38
  373.3 3.6 all-to-all-start.5
  376.9 7.8 %fusion.2 = bf16[1,512,3584]{2,1,0:T(8,128)(2,1)} fusion(bf16[768,512]{1,0:T(8,128)(2,1)} %copy-done.6, bf16[768,3584]{1,0:T(8,128)(2,1)} %all-gather.5.cloned.1.call-done), kind=kOutput, calls=%fused_computation.12 | convolution fusion | flops 2820407296 | bytes 9961472 | tf_op jit(solution)/shard_map/dot_general | solution.py:24
  384.7 7.2 %fusion.1 = bf16[1,3584,512]{2,1,0:T(8,128)(2,1)} fusion(bf16[768,3584]{1,0:T(8,128)(2,1)} %all-gather.3.cloned.1.call-done, bf16[768,512]{1,0:T(8,128)(2,1)S(1)} %copy-done.8), kind=kOutput, calls=%fused_computation.11 | convolution fusion | flops 2820407296 | bytes 9961472 | tf_op jit(solution)/shard_map/dot_general | solution.py:24
  391.9 4.6 %fusion = bf16[1,3584,512]{2,1,0:T(8,128)(2,1)} fusion(bf16[768,3584]{1,0:T(8,128)(2,1)S(1)} %bitcast.83, bf16[768,512]{1,0:T(8,128)(2,1)S(1)} %get-tuple-element.15), kind=kOutput, calls=%fused_computation.10 | convolution fusion | flops 2820407296 | bytes 9961472 | tf_op jit(solution)/shard_map/dot_general | solution.py:24
  396.5 1.8 fusion.14
  400.4 3.1 convolution_convert_fusion.5
  403.5 6.9 %all-to-all-done.5 = bf16[8,24,3584]{2,1,0:T(8,128)(2,1)S(1)} async-done(((bf16[8,24,3584]{2,1,0:T(8,128)(2,1)}), bf16[8,24,3584]{2,1,0:T(8,128)(2,1)S(1)}, u32[]{:S(2)}, u32[]{:S(2)}) %all-to-all-start.5) | async-done | bytes 1376288 | tf_op jit(solution)/shard_map/all_to_all | solution.py:38
  410.4 1.3 convolution_convert_fusion.4
  (56 shorter events, 6.2 us)
Async XLA Ops:
  7.2 115.4 %all-gather.3.cloned.1.call-start = ((), (), s32[]{:S(2)}) async-start(), calls=%async_computation.6 | async-start | bytes 6881280 | tf_op jit(solution)/shard_map/all_gather | solution.py:31
  19.9 40.1 %copy-start.1 = (f32[128,8]{0,1:T(8,128)S(1)}, f32[128,8]{0,1:T(8,128)}, u32[]{:S(2)}) copy-start(f32[128,8]{0,1:T(8,128)} %param.8) | copy-start | bytes 12292
  19.9 41.8 %copy-start = (bf16[128,3584]{1,0:T(8,128)(2,1)S(1)}, bf16[128,3584]{1,0:T(8,128)(2,1)}, u32[]{:S(2)}) copy-start(bf16[128,3584]{1,0:T(8,128)(2,1)} %param.10) | copy-start | bytes 2752516
  59.9 128.2 %all-gather.5.cloned.1.call-start = ((), (), s32[]{:S(2)}) async-start(), calls=%async_computation.7 | async-start | bytes 6881280 | tf_op jit(solution)/shard_map/all_gather | solution.py:31
  122.6 8.0 %copy-start.2 = (bf16[768,3584]{1,0:T(8,128)(2,1)S(1)}, bf16[768,3584]{1,0:T(8,128)(2,1)}, u32[]{:S(2)}) copy-start(bf16[768,3584]{1,0:T(8,128)(2,1)} %all-gather.3.cloned.1.call-done) | copy-start | bytes 16515076
  122.6 8.0 %copy-start.4 = (bf16[1,3584,512]{2,1,0:T(8,128)(2,1)S(1)}, bf16[1,3584,512]{2,1,0:T(8,128)(2,1)}, u32[]{:S(2)}) copy-start(bf16[1,3584,512]{2,1,0:T(8,128)(2,1)} %param.11) | copy-start | bytes 11010052
  188.1 9.2 %copy-start.3 = (bf16[1,512,3584]{2,1,0:T(8,128)(2,1)S(1)}, bf16[1,512,3584]{2,1,0:T(8,128)(2,1)}, u32[]{:S(2)}) copy-start(bf16[1,512,3584]{2,1,0:T(8,128)(2,1)} %param.13) | copy-start | bytes 11010052
  197.2 4.8 %copy-start.6 = (bf16[768,512]{1,0:T(8,128)(2,1)}, bf16[768,512]{1,0:T(8,128)(2,1)S(1)}, u32[]{:S(2)}) copy-start(bf16[768,512]{1,0:T(8,128)(2,1)S(1)} %get-tuple-element.16) | copy-start | bytes 2359300
  202.0 66.9 %all-to-all-start.1 = ((bf16[4,192,3584]{2,1,0:T(8,128)(2,1)}), bf16[4,192,3584]{2,1,0:T(8,128)(2,1)}, u32[]{:S(2)}, u32[]{:S(2)}) async-start(bf16[4,192,3584]{2,1,0:T(8,128)(2,1)} %bitcast.75), calls=%async_computation.1 | async-start | bytes 11010048 | tf_op jit(solution)/shard_map/all_to_all | solution.py:35
  207.3 8.1 %copy-start.5 = (bf16[1,3584,512]{2,1,0:T(8,128)(2,1)S(1)}, bf16[1,3584,512]{2,1,0:T(8,128)(2,1)}, u32[]{:S(2)}) copy-start(bf16[1,3584,512]{2,1,0:T(8,128)(2,1)} %param.12) | copy-start | bytes 11010052
  207.4 8.1 %copy-start.7 = (bf16[768,512]{1,0:T(8,128)(2,1)S(1)}, bf16[768,512]{1,0:T(8,128)(2,1)}, u32[]{:S(2)}) copy-start(bf16[768,512]{1,0:T(8,128)(2,1)} %get-tuple-element.14) | copy-start | bytes 2359300
  268.9 66.1 %all-to-all-start.4 = ((bf16[4,192,3584]{2,1,0:T(8,128)(2,1)}), bf16[4,192,3584]{2,1,0:T(8,128)(2,1)}, u32[]{:S(2)}, u32[]{:S(2)}) async-start(bf16[4,192,3584]{2,1,0:T(8,128)(2,1)} %bitcast.74), calls=%async_computation.4 | async-start | bytes 11010048 | tf_op jit(solution)/shard_map/all_to_all | solution.py:35
  334.9 38.3 %all-to-all-start.2 = ((bf16[8,24,3584]{2,1,0:T(8,128)(2,1)}), bf16[8,24,3584]{2,1,0:T(8,128)(2,1)}, u32[]{:S(2)}, u32[]{:S(2)}) async-start(bf16[8,24,3584]{2,1,0:T(8,128)(2,1)} %bitcast.9), calls=%async_computation.2 | async-start | bytes 2752512 | tf_op jit(solution)/shard_map/all_to_all | solution.py:38
  373.3 37.1 %all-to-all-start.5 = ((bf16[8,24,3584]{2,1,0:T(8,128)(2,1)}), bf16[8,24,3584]{2,1,0:T(8,128)(2,1)S(1)}, u32[]{:S(2)}, u32[]{:S(2)}) async-start(bf16[8,24,3584]{2,1,0:T(8,128)(2,1)} %bitcast.14), calls=%async_computation.5 | async-start | bytes 2752512 | tf_op jit(solution)/shard_map/all_to_all | solution.py:38
  376.9 7.9 %copy-start.8 = (bf16[768,512]{1,0:T(8,128)(2,1)S(1)}, bf16[768,512]{1,0:T(8,128)(2,1)}, u32[]{:S(2)}) copy-start(bf16[768,512]{1,0:T(8,128)(2,1)} %get-tuple-element.14) | copy-start | bytes 2359300
  376.9 15.1 %slice-start = ((s8[5505024]{0:T(1024)(128)(4,1)}), s8[4194304]{0:T(1024)(128)(4,1)S(1)}, s32[]{:S(2)}) async-start(s8[5505024]{0:T(1024)(128)(4,1)} %bitcast.82), calls=%async_computation.8 | async-start | bytes 8388608
  384.7 7.2 %slice-start.1 = ((s8[5505024]{0:T(1024)(128)(4,1)}), s8[1310720]{0:T(1024)(128)(4,1)S(1)}, s32[]{:S(2)}) async-start(s8[5505024]{0:T(1024)(128)(4,1)} %bitcast.82), calls=%async_computation.9 | async-start | bytes 2621440
Sparse Core Ops, SparseCore 0:
  60.0 62.5 all-gather.2
  124.4 63.6 all-gather.4

commit v2 on v1

--- a/solution.py
+++ b/solution.py
@@ -32,12 +32,8 @@
 
 
 def gather_back(partial_rows, groups):
-    by_group = lax.all_to_all(partial_rows, "dp", split_axis=0, concat_axis=0, tiled=True)
-    rows = by_group.shape[0] // groups
-    summed = jnp.sum(by_group.astype(jnp.float32).reshape(groups, rows, -1), axis=0)
-    return lax.all_to_all(
-        summed.astype(jnp.bfloat16), "expert", split_axis=0, concat_axis=0, tiled=True
-    )
+    summed = lax.psum_scatter(partial_rows, "dp", scatter_dimension=0, tiled=True)
+    return lax.all_to_all(summed, "expert", split_axis=0, concat_axis=0, tiled=True)
 
 
 def on_device(tokens, gate_probs, expert_ids, cotangent, w_gate, w_up, w_down):

time: 419 us -> 381 us (0.909)
  waiting for transfers between devices: 213 us -> 193 us
  other arithmetic: 15.8 us -> 6.11 us
  starting transfers between devices: 18.7 us -> 9.56 us
    all_to_all x4 -> x2, waiting for transfers between devices: 138 us -> 7.68 us  [gather_back(): lax.all_to_all(summed, 'expert', split_axis=0, concat_axis=0, tiled=True)]
    reduce_scatter x0 -> x2, waiting for transfers between devices: none -> 110 us  [gather_back(): lax.psum_scatter(partial_rows, 'dp', scatter_dimension=0, tiled=True)]
    reduce_sum x2 -> x0, other arithmetic: 9.71 us -> none  [gather_back(): jnp.sum(by_group.astype(jnp.float32).reshape(groups, rows, -1), axis=0)]
    all_to_all x4 -> x2, starting transfers between devices: 18.6 us -> 9.22 us  [gather_back(): lax.all_to_all(summed, 'expert', split_axis=0, concat_axis=0, tiled=True)]
  transfers between devices with their start and end apart: 6 -> 6, of which waited for: 6 -> 5; matrix products, arithmetic and copies ran while one was open for 16% -> 15% of each run, Pallas kernels for 0% -> 0%
where the time goes in v2:
time: 381 us; the launch traced here: 380 us
  waiting for transfers between devices  193 us (51%)
  blocking collectives  76.7 us (20%)
  matrix products  66.6 us (17%)
  between operations  14 us (4%)
  local copies, waits for them, and re-layouts  13.9 us (4%)
  starting transfers between devices  9.56 us (3%)
  other arithmetic  6.11 us (2%)
    reduce_scatter x2, waiting for transfers between devices, gather_back(): lax.psum_scatter(partial_rows, 'dp', scatter_dimension=0, tiled=True)  110 us
    all_to_all x2, blocking collectives, dispatch(): lax.all_to_all(send_rows, 'expert', split_axis=0, concat_axis=0, tiled=True)  76.7 us
    all_gather x2, waiting for transfers between devices, dispatch(): return lax.all_gather(along_expert, 'dp', axis=0, tiled=True)  75.7 us
    dot_general x3, matrix products, contract_last(): lax.dot_general(left, right, (((1,), (1,)), ((), ())), preferred_element_...  24.9 us
    dot_general x3, matrix products, contract_first(): lax.dot_general(left, right, (((0,), (0,)), ((), ())), preferred_element_...  19 us
    all_to_all x2, starting transfers between devices, gather_back(): lax.all_to_all(summed, 'expert', split_axis=0, concat_axis=0, tiled=True)  9.22 us
    dot_general x1, matrix products, on_device(): up_pre = jnp.dot(rows_x, up_w, preferred_element_type=jnp.float32)  7.94 us
    all_to_all x2, waiting for transfers between devices, gather_back(): lax.all_to_all(summed, 'expert', split_axis=0, concat_axis=0, tiled=True)  7.68 us
  transfers between devices with their start and end apart: 6, of which 5 were waited for; matrix products, arithmetic and copies ran while one was open for 15% of the time, Pallas kernels for 0%

profile of v2, /device:TPU:0, one launch (start us, length us, event | category | flops | bytes accessed | tf_op | source)
XLA Modules:
  0.0 380.0 jit_solution(13085643132126633044)
XLA Ops:
  7.2 0.7 broadcast_compare_fusion
  7.9 0.7 broadcast_multiply_fusion
  8.6 0.8 copy.15
  10.0 2.3 reduce-window.6
  12.9 4.3 %scatter_custom_fusion = s32[192]{0:T(256)S(1)} fusion(s32[1024]{0:T(1024)S(1)} %bitcast.78, s32[1024]{0:T(1024)S(1)} %iota.15, s32[]{:T(128)} %constant.15.clone.1), kind=kCustom, calls=%fused_computation.63 | custom fusion | bytes 772 | tf_op jit(solution)/shard_map/scatter | solution.py:14
  17.2 1.2 concatenate.10
  18.5 1.4 gather_fusion.1
  19.9 40.0 %all_to_all.45 = bf16[8,24,3584]{2,1,0:T(8,128)(2,1)} all-to-all(bf16[8,24,3584]{2,1,0:T(8,128)(2,1)S(1)} %bitcast.71), channel_id=1, replica_groups=mesh['dp'=4,'expert'=8] {'expert'}, dimensions={0} | all-to-all | bytes 2752512 | tf_op jit(solution)/shard_map/all_to_all | solution.py:30
  60.2 1.4 gather_fusion
  61.8 1.4 gather_fusion.2
  63.5 36.7 %all_to_all.46 = bf16[8,24,3584]{2,1,0:T(8,128)(2,1)} all-to-all(bf16[8,24,3584]{2,1,0:T(8,128)(2,1)S(1)} %fusion.13), channel_id=1, replica_groups=mesh['dp'=4,'expert'=8] {'expert'}, dimensions={0} | all-to-all | bytes 2752512 | tf_op jit(solution)/shard_map/all_to_all | solution.py:30
  100.3 22.3 %all-gather.3.cloned.1.call-done = bf16[768,3584]{1,0:T(8,128)(2,1)} async-done(((bf16[192,3584]{1,0:T(8,128)(2,1)}), bf16[768,3584]{1,0:T(8,128)(2,1)}) %all-gather.3.cloned.1.call-update) | async-done | bytes 5505040 | tf_op jit(solution)/shard_map/all_gather | solution.py:31
  122.6 7.9 %fusion.7 = f32[768,512]{1,0:T(8,128)} fusion(bf16[768,3584]{1,0:T(8,128)(2,1)} %all-gather.3.cloned.1.call-done, bf16[1,3584,512]{2,1,0:T(8,128)(2,1)} %param.12), kind=kOutput, calls=%fused_computation.19 | convolution fusion | flops 2818572288 | bytes 10747904 | tf_op jit(solution)/shard_map/dot_general | solution.py:59
  130.6 4.1 %fusion.11 = f32[768,512]{1,0:T(8,128)} fusion(bf16[768,3584]{1,0:T(8,128)(2,1)S(1)} %copy-done.2, bf16[1,3584,512]{2,1,0:T(8,128)(2,1)S(1)} %copy-done.4), kind=kOutput, calls=%fused_computation.23 | convolution fusion | flops 2818572288 | bytes 10747904 | tf_op jit(solution)/shard_map/dot_general | solution.py:58
  134.7 53.4 %all-gather.5.cloned.1.call-done = bf16[768,3584]{1,0:T(8,128)(2,1)} async-done(((bf16[192,3584]{1,0:T(8,128)(2,1)}), bf16[768,3584]{1,0:T(8,128)(2,1)}) %all-gather.5.cloned.1.call-update) | async-done | bytes 5505040 | tf_op jit(solution)/shard_map/all_gather | solution.py:31
  188.1 9.2 %multiply_convert_fusion = (bf16[768,512]{1,0:T(8,128)(2,1)}, bf16[768,512]{1,0:T(8,128)(2,1)S(1)}, bf16[768,512]{1,0:T(8,128)(2,1)S(1)}) fusion(f32[768,512]{1,0:T(8,128)} %fusion.11, f32[768,512]{1,0:T(8,128)} %fusion.7, bf16[768,3584]{1,0:T(8,128)(2,1)} %all-gather.5.cloned.1.call-done, bf16[1,512,3584]{2,1,0:T(8,128)(2,1)} %param.13), kind=kOutput, calls=%fused_computation.29 | convolution fusion | flops 2824470528 | bytes 14680064 | tf_op jit(solution)/shard_map/dot_general | solution.py:18
  197.2 4.8 %convolution_convert_fusion = bf16[768,3584]{1,0:T(8,128)(2,1)} fusion(bf16[768,512]{1,0:T(8,128)(2,1)S(1)} %get-tuple-element.16, bf16[1,512,3584]{2,1,0:T(8,128)(2,1)S(1)} %copy-done.3), kind=kOutput, calls=%fused_computation.6 | convolution fusion | flops 2821324800 | bytes 9961472 | tf_op jit(solution)/shard_map/dot_general | solution.py:63
  202.3 8.2 %fusion.9 = f32[768,3584]{1,0:T(8,128)} fusion(bf16[768,512]{1,0:T(8,128)(2,1)S(1)} %get-tuple-element.15, bf16[1,3584,512]{2,1,0:T(8,128)(2,1)} %param.11), kind=kOutput, calls=%fused_computation.21 | convolution fusion | flops 2818572288 | bytes 15466496 | tf_op jit(solution)/shard_map/dot_general | solution.py:18
  210.6 7.5 %add_convert_fusion = bf16[768,3584]{1,0:T(8,128)(2,1)} fusion(f32[768,3584]{1,0:T(8,128)} %fusion.9, bf16[768,512]{1,0:T(8,128)(2,1)S(1)} %copy-done.6, bf16[1,3584,512]{2,1,0:T(8,128)(2,1)S(1)} %copy-done.5), kind=kOutput, calls=%fused_computation.5 | convolution fusion | flops 2824077312 | bytes 20971520 | tf_op jit(solution)/shard_map/dot_general | solution.py:18
  218.1 47.8 %reduce-scatter.3.cloned.1.call-done = bf16[192,3584]{1,0:T(8,128)(2,1)} async-done(((bf16[768,3584]{1,0:T(8,128)(2,1)}), bf16[192,3584]{1,0:T(8,128)(2,1)}) %reduce-scatter.3.cloned.1.call-update) | async-done | bytes 1376272 | tf_op jit(solution)/shard_map/reduce_scatter | solution.py:35
  265.9 4.6 %all-to-all-start.1 = ((bf16[8,24,3584]{2,1,0:T(8,128)(2,1)}), bf16[8,24,3584]{2,1,0:T(8,128)(2,1)}, u32[]{:S(2)}, u32[]{:S(2)}) async-start(bf16[8,24,3584]{2,1,0:T(8,128)(2,1)} %bitcast.75), calls=%async_computation.2 | async-start | bytes 2752512 | tf_op jit(solution)/shard_map/all_to_all | solution.py:36
  270.5 61.9 %reduce-scatter.5.cloned.1.call-done = bf16[192,3584]{1,0:T(8,128)(2,1)} async-done(((bf16[768,3584]{1,0:T(8,128)(2,1)}), bf16[192,3584]{1,0:T(8,128)(2,1)}) %reduce-scatter.5.cloned.1.call-update) | async-done | bytes 1376272 | tf_op jit(solution)/shard_map/reduce_scatter | solution.py:35
  332.4 4.6 %all-to-all-start.3 = ((bf16[8,24,3584]{2,1,0:T(8,128)(2,1)}), bf16[8,24,3584]{2,1,0:T(8,128)(2,1)}, u32[]{:S(2)}, u32[]{:S(2)}) async-start(bf16[8,24,3584]{2,1,0:T(8,128)(2,1)} %bitcast.74), calls=%async_computation.5 | async-start | bytes 2752512 | tf_op jit(solution)/shard_map/all_to_all | solution.py:36
  337.1 7.2 %fusion.2 = bf16[1,512,3584]{2,1,0:T(8,128)(2,1)} fusion(bf16[768,512]{1,0:T(8,128)(2,1)S(1)} %get-tuple-element.16, bf16[768,3584]{1,0:T(8,128)(2,1)} %all-gather.5.cloned.1.call-done), kind=kOutput, calls=%fused_computation.12 | convolution fusion | flops 2820407296 | bytes 9961472 | tf_op jit(solution)/shard_map/dot_general | solution.py:24
  344.3 7.2 %fusion.1 = bf16[1,3584,512]{2,1,0:T(8,128)(2,1)} fusion(bf16[768,3584]{1,0:T(8,128)(2,1)} %all-gather.3.cloned.1.call-done, bf16[768,512]{1,0:T(8,128)(2,1)S(1)} %copy-done.7), kind=kOutput, calls=%fused_computation.11 | convolution fusion | flops 2820407296 | bytes 9961472 | tf_op jit(solution)/shard_map/dot_general | solution.py:24
  351.5 4.6 %fusion = bf16[1,3584,512]{2,1,0:T(8,128)(2,1)} fusion(bf16[768,3584]{1,0:T(8,128)(2,1)S(1)} %bitcast.80, bf16[768,512]{1,0:T(8,128)(2,1)S(1)} %get-tuple-element.15), kind=kOutput, calls=%fused_computation.10 | convolution fusion | flops 2820407296 | bytes 9961472 | tf_op jit(solution)/shard_map/dot_general | solution.py:24
  356.1 1.8 fusion.14
  358.0 1.2 scatter_custom_fusion.1
  359.3 0.7 copy.18
  360.0 3.1 convolution_convert_fusion.5
  363.1 7.7 %all-to-all-done.3 = bf16[8,24,3584]{2,1,0:T(8,128)(2,1)} async-done(((bf16[8,24,3584]{2,1,0:T(8,128)(2,1)}), bf16[8,24,3584]{2,1,0:T(8,128)(2,1)}, u32[]{:S(2)}, u32[]{:S(2)}) %all-to-all-start.3) | async-done | bytes 1376288 | tf_op jit(solution)/shard_map/all_to_all | solution.py:36
  370.8 2.7 convolution_convert_fusion.4
  (54 shorter events, 2.5 us)
Async XLA Ops:
  7.2 115.4 %all-gather.3.cloned.1.call-start = ((), (), s32[]{:S(2)}) async-start(), calls=%async_computation.6 | async-start | bytes 6881280 | tf_op jit(solution)/shard_map/all_gather | solution.py:31
  19.9 40.1 %copy-start.1 = (f32[128,8]{0,1:T(8,128)S(1)}, f32[128,8]{0,1:T(8,128)}, u32[]{:S(2)}) copy-start(f32[128,8]{0,1:T(8,128)} %param.8) | copy-start | bytes 12292
  19.9 41.8 %copy-start = (bf16[128,3584]{1,0:T(8,128)(2,1)S(1)}, bf16[128,3584]{1,0:T(8,128)(2,1)}, u32[]{:S(2)}) copy-start(bf16[128,3584]{1,0:T(8,128)(2,1)} %param.10) | copy-start | bytes 2752516
  59.9 128.2 %all-gather.5.cloned.1.call-start = ((), (), s32[]{:S(2)}) async-start(), calls=%async_computation.8 | async-start | bytes 6881280 | tf_op jit(solution)/shard_map/all_gather | solution.py:31
  100.3 165.6 %reduce-scatter.3.cloned.1.call-start = ((), (), s32[]{:S(2)}) async-start(), calls=%async_computation.7 | async-start | bytes 6881280 | tf_op jit(solution)/shard_map/reduce_scatter | solution.py:35
  122.6 8.0 %copy-start.2 = (bf16[768,3584]{1,0:T(8,128)(2,1)S(1)}, bf16[768,3584]{1,0:T(8,128)(2,1)}, u32[]{:S(2)}) copy-start(bf16[768,3584]{1,0:T(8,128)(2,1)} %all-gather.3.cloned.1.call-done) | copy-start | bytes 16515076
  122.6 8.0 %copy-start.4 = (bf16[1,3584,512]{2,1,0:T(8,128)(2,1)S(1)}, bf16[1,3584,512]{2,1,0:T(8,128)(2,1)}, u32[]{:S(2)}) copy-start(bf16[1,3584,512]{2,1,0:T(8,128)(2,1)} %param.11) | copy-start | bytes 11010052
  188.1 9.2 %copy-start.3 = (bf16[1,512,3584]{2,1,0:T(8,128)(2,1)S(1)}, bf16[1,512,3584]{2,1,0:T(8,128)(2,1)}, u32[]{:S(2)}) copy-start(bf16[1,512,3584]{2,1,0:T(8,128)(2,1)} %param.13) | copy-start | bytes 11010052
  202.1 130.4 %reduce-scatter.5.cloned.1.call-start = ((), (), s32[]{:S(2)}) async-start(), calls=%async_computation.9 | async-start | bytes 6881280 | tf_op jit(solution)/shard_map/reduce_scatter | solution.py:35
  202.3 8.3 %copy-start.5 = (bf16[1,3584,512]{2,1,0:T(8,128)(2,1)S(1)}, bf16[1,3584,512]{2,1,0:T(8,128)(2,1)}, u32[]{:S(2)}) copy-start(bf16[1,3584,512]{2,1,0:T(8,128)(2,1)} %param.12) | copy-start | bytes 11010052
  202.3 8.3 %copy-start.6 = (bf16[768,512]{1,0:T(8,128)(2,1)S(1)}, bf16[768,512]{1,0:T(8,128)(2,1)}, u32[]{:S(2)}) copy-start(bf16[768,512]{1,0:T(8,128)(2,1)} %get-tuple-element.14) | copy-start | bytes 2359300
  265.9 66.6 %all-to-all-start.1 = ((bf16[8,24,3584]{2,1,0:T(8,128)(2,1)}), bf16[8,24,3584]{2,1,0:T(8,128)(2,1)}, u32[]{:S(2)}, u32[]{:S(2)}) async-start(bf16[8,24,3584]{2,1,0:T(8,128)(2,1)} %bitcast.75), calls=%async_computation.2 | async-start | bytes 2752512 | tf_op jit(solution)/shard_map/all_to_all | solution.py:36
  332.4 38.3 %all-to-all-start.3 = ((bf16[8,24,3584]{2,1,0:T(8,128)(2,1)}), bf16[8,24,3584]{2,1,0:T(8,128)(2,1)}, u32[]{:S(2)}, u32[]{:S(2)}) async-start(bf16[8,24,3584]{2,1,0:T(8,128)(2,1)} %bitcast.74), calls=%async_computation.5 | async-start | bytes 2752512 | tf_op jit(solution)/shard_map/all_to_all | solution.py:36
  337.1 7.2 %copy-start.7 = (bf16[768,512]{1,0:T(8,128)(2,1)S(1)}, bf16[768,512]{1,0:T(8,128)(2,1)}, u32[]{:S(2)}) copy-start(bf16[768,512]{1,0:T(8,128)(2,1)} %get-tuple-element.14) | copy-start | bytes 2359300
  337.1 14.5 %slice-start = ((s8[5505024]{0:T(1024)(128)(4,1)}), s8[4194304]{0:T(1024)(128)(4,1)S(1)}, s32[]{:S(2)}) async-start(s8[5505024]{0:T(1024)(128)(4,1)} %bitcast.79), calls=%async_computation.10 | async-start | bytes 8388608
  344.3 7.2 %slice-start.1 = ((s8[5505024]{0:T(1024)(128)(4,1)}), s8[1310720]{0:T(1024)(128)(4,1)S(1)}, s32[]{:S(2)}) async-start(s8[5505024]{0:T(1024)(128)(4,1)} %bitcast.79), calls=%async_computation.11 | async-start | bytes 2621440
Sparse Core Ops, SparseCore 0:
  60.0 62.5 all-gather.2
  124.4 63.6 all-gather.4
  202.2 63.6 reduce-scatter.2
  268.8 63.6 reduce-scatter.4

commit v3 on v2

--- a/solution.py
+++ b/solution.py
@@ -36,6 +36,33 @@
     return lax.all_to_all(summed, "expert", split_axis=0, concat_axis=0, tiled=True)
 
 
+def expert_forward(rows_x, gate_w, up_w, down_w):
+    gate_pre = jnp.dot(rows_x, gate_w, preferred_element_type=jnp.float32)
+    up_pre = jnp.dot(rows_x, up_w, preferred_element_type=jnp.float32)
+    hidden = (gate_pre * jax.nn.sigmoid(gate_pre) * up_pre).astype(jnp.bfloat16)
+    part_out = jnp.dot(hidden, down_w, preferred_element_type=jnp.float32).astype(jnp.bfloat16)
+    return lax.optimization_barrier((part_out, hidden, gate_pre, up_pre))
+
+
+def expert_backward(rows_c, gate_pre, up_pre, gate_w, up_w, down_w):
+    sigmoid_g = jax.nn.sigmoid(gate_pre)
+    activated = gate_pre * sigmoid_g
+    grad_hidden = contract_last(rows_c, down_w)
+    grad_upin = (grad_hidden * activated).astype(jnp.bfloat16)
+    grad_gatein = (grad_hidden * up_pre * sigmoid_g * (1.0 + gate_pre * (1.0 - sigmoid_g))).astype(
+        jnp.bfloat16
+    )
+    part_dx = (contract_last(grad_gatein, gate_w) + contract_last(grad_upin, up_w)).astype(
+        jnp.bfloat16
+    )
+    return part_dx, grad_gatein, grad_upin
+
+
+def join_slots(chunks, experts, model_width):
+    parts = [chunk.reshape(experts, -1, model_width) for chunk in chunks]
+    return jnp.concatenate(parts, axis=1).reshape(-1, model_width)
+
+
 def on_device(tokens, gate_probs, expert_ids, cotangent, w_gate, w_up, w_down):
     tok_count, model_width = tokens.shape
     top_k = expert_ids.shape[1]
@@ -50,30 +77,30 @@
     rows_dy = jnp.concatenate([cotangent, zero_row], 0)[token_of]
     prob_rows = jnp.concatenate([gate_probs.reshape(-1), jnp.zeros((1,), jnp.float32)], 0)[slots]
     send_c = (prob_rows[:, None] * rows_dy.astype(jnp.float32)).astype(jnp.bfloat16)
-    rows_x = dispatch(send_x)
-    rows_c = dispatch(send_c)
+    half = max(capacity // 2, 1)
+    bounds = [(lo, hi) for lo, hi in ((0, half), (half, capacity)) if hi > lo]
+    x_by_slot = send_x.reshape(experts, capacity, model_width)
+    c_by_slot = send_c.reshape(experts, capacity, model_width)
+    xs = [dispatch(x_by_slot[:, lo:hi].reshape(-1, model_width)) for lo, hi in bounds]
+    cs = [dispatch(c_by_slot[:, lo:hi].reshape(-1, model_width)) for lo, hi in bounds]
     gate_w = w_gate[0]
     up_w = w_up[0]
     down_w = w_down[0]
-    gate_pre = jnp.dot(rows_x, gate_w, preferred_element_type=jnp.float32)
-    up_pre = jnp.dot(rows_x, up_w, preferred_element_type=jnp.float32)
-    sigmoid_g = jax.nn.sigmoid(gate_pre)
-    activated = gate_pre * sigmoid_g
-    hidden = (activated * up_pre).astype(jnp.bfloat16)
-    part_out = jnp.dot(hidden, down_w, preferred_element_type=jnp.float32).astype(jnp.bfloat16)
-    out_rows = gather_back(part_out, groups).astype(jnp.float32)
-    grad_hidden = contract_last(rows_c, down_w)
-    grad_upin = (grad_hidden * activated).astype(jnp.bfloat16)
-    grad_gatein = (grad_hidden * up_pre * sigmoid_g * (1.0 + gate_pre * (1.0 - sigmoid_g))).astype(
-        jnp.bfloat16
-    )
-    part_dx = (contract_last(grad_gatein, gate_w) + contract_last(grad_upin, up_w)).astype(
-        jnp.bfloat16
-    )
-    dx_rows = gather_back(part_dx, groups).astype(jnp.float32)
-    new_gate = contract_first(rows_x, grad_gatein).astype(jnp.bfloat16)[None]
-    new_up = contract_first(rows_x, grad_upin).astype(jnp.bfloat16)[None]
-    new_down = contract_first(hidden, rows_c).astype(jnp.bfloat16)[None]
+    forwards = [expert_forward(rows_x, gate_w, up_w, down_w) for rows_x in xs]
+    outs = [gather_back(fw[0], groups) for fw in forwards]
+    backwards = [
+        expert_backward(rows_c, fw[2], fw[3], gate_w, up_w, down_w)
+        for rows_c, fw in zip(cs, forwards)
+    ]
+    dxs = [gather_back(bw[0], groups) for bw in backwards]
+    new_gate = sum(contract_first(rx, bw[1]) for rx, bw in zip(xs, backwards))
+    new_up = sum(contract_first(rx, bw[2]) for rx, bw in zip(xs, backwards))
+    new_down = sum(contract_first(fw[1], rc) for fw, rc in zip(forwards, cs))
+    new_gate = new_gate.astype(jnp.bfloat16)[None]
+    new_up = new_up.astype(jnp.bfloat16)[None]
+    new_down = new_down.astype(jnp.bfloat16)[None]
+    out_rows = join_slots(outs, experts, model_width).astype(jnp.float32)
+    dx_rows = join_slots(dxs, experts, model_width).astype(jnp.float32)
     owner = (token_of[None, :] == jnp.arange(tok_count, dtype=jnp.int32)[:, None]).astype(
         jnp.float32
     )

time: 381 us -> 436 us (1.14)
  blocking collectives: 76.7 us -> 109 us
  local copies, waits for them, and re-layouts: 13.9 us -> 30.1 us
  waiting for transfers between devices: 193 us -> 183 us
  starting transfers between devices: 9.56 us -> 18.9 us
  matrix products: 66.6 us -> 72.5 us
    all_to_all x2 -> x4, blocking collectives: 76.7 us -> 109 us  [dispatch(): lax.all_to_all(send_rows, 'expert', split_axis=0, concat_axis=0, tiled=True)]
    all_gather x2 -> x4, waiting for transfers between devices: 75.7 us -> 48.6 us  [dispatch(): return lax.all_gather(along_expert, 'dp', axis=0, tiled=True)]
    reduce_scatter x2 -> x4, waiting for transfers between devices: 110 us -> 124 us  [gather_back(): lax.psum_scatter(partial_rows, 'dp', scatter_dimension=0, tiled=True)]
    all_to_all x0 -> x8, local copies, waits for them, and re-layouts: none -> 12.3 us  [the longest x4 8.31 us: gather_back(): lax.all_to_all(summed, 'expert', split_axis=0, concat_axis=0, tiled=True)]
    dot_general x3 -> x6, matrix products: 19 us -> 29 us  [contract_first(): lax.dot_general(left, right, (((0,), (0,)), ((), ())), preferred_element_...]
    all_to_all x2 -> x4, starting transfers between devices: 9.22 us -> 18.4 us  [gather_back(): lax.all_to_all(summed, 'expert', split_axis=0, concat_axis=0, tiled=True)]
    dot_general x3 -> x6, matrix products: 24.9 us -> 20 us  [contract_last(): lax.dot_general(left, right, (((1,), (1,)), ((), ())), preferred_element_...]
    dot_general x3 -> x6, matrix products: 16.9 us -> 20.4 us  [the longest x2 9.19 us: expert_forward(): gate_pre = jnp.dot(rows_x, gate_w, preferred_element_type=jnp.float32)]
  transfers between devices with their start and end apart: 6 -> 12, of which waited for: 5 -> 7; matrix products, arithmetic and copies ran while one was open for 15% -> 18% of each run, Pallas kernels for 0% -> 0%
where the time goes in v3:
time: 436 us
  waiting for transfers between devices  183 us (42%)
  blocking collectives  109 us (25%)
  matrix products  72.5 us (17%)
  local copies, waits for them, and re-layouts  30.1 us (7%)
  starting transfers between devices  18.9 us (4%)
  between operations  14.6 us (3%)
  other arithmetic  8.13 us (2%)
    reduce_scatter x4, waiting for transfers between devices, gather_back(): lax.psum_scatter(partial_rows, 'dp', scatter_dimension=0, tiled=True)  124 us
    all_to_all x4, blocking collectives, dispatch(): lax.all_to_all(send_rows, 'expert', split_axis=0, concat_axis=0, tiled=True)  109 us
    all_gather x4, waiting for transfers between devices, dispatch(): return lax.all_gather(along_expert, 'dp', axis=0, tiled=True)  48.6 us
    dot_general x6, matrix products, contract_first(): lax.dot_general(left, right, (((0,), (0,)), ((), ())), preferred_element_...  29 us
    dot_general x6, matrix products, contract_last(): lax.dot_general(left, right, (((1,), (1,)), ((), ())), preferred_element_...  20 us
    all_to_all x4, starting transfers between devices, gather_back(): lax.all_to_all(summed, 'expert', split_axis=0, concat_axis=0, tiled=True)  18.4 us
    all_to_all x4, waiting for transfers between devices, gather_back(): lax.all_to_all(summed, 'expert', split_axis=0, concat_axis=0, tiled=True)  9.8 us
    dot_general x2, matrix products, expert_forward(): gate_pre = jnp.dot(rows_x, gate_w, preferred_element_type=jnp.float32)  9.19 us
  transfers between devices with their start and end apart: 12, of which 7 were waited for; matrix products, arithmetic and copies ran while one was open for 18% of the time, Pallas kernels for 0%

profile of v3, /device:TPU:0, one launch (start us, length us, event | category | flops | bytes accessed | tf_op | source)
XLA Modules:
  0.0 435.6 jit_solution(945280252774466416)
XLA Ops:
  12.9 4.3 scatter_custom_fusion
  20.1 29.9 %all_to_all.72 = bf16[8,12,3584]{2,1,0:T(8,128)(2,1)S(1)} all-to-all(bf16[8,12,3584]{2,1,0:T(8,128)(2,1)S(1)} %get-tuple-element.37), channel_id=1, replica_groups=mesh['dp'=4,'expert'=8] {'expert'}, dimensions={0} | all-to-all | bytes 1376256 | tf_op jit(solution)/shard_map/all_to_all | solution.py:30
  51.1 26.3 %all_to_all.73 = bf16[8,12,3584]{2,1,0:T(8,128)(2,1)S(1)} all-to-all(bf16[8,12,3584]{2,1,0:T(8,128)(2,1)S(1)} %get-tuple-element.36), channel_id=1, replica_groups=mesh['dp'=4,'expert'=8] {'expert'}, dimensions={0} | all-to-all | bytes 1376256 | tf_op jit(solution)/shard_map/all_to_all | solution.py:30
  82.9 26.2 %all_to_all.74 = bf16[8,12,3584]{2,1,0:T(8,128)(2,1)S(1)} all-to-all(bf16[8,12,3584]{2,1,0:T(8,128)(2,1)S(1)} %get-tuple-element.34), channel_id=1, replica_groups=mesh['dp'=4,'expert'=8] {'expert'}, dimensions={0} | all-to-all | bytes 1376256 | tf_op jit(solution)/shard_map/all_to_all | solution.py:30
  110.1 26.2 %all_to_all.75 = bf16[8,12,3584]{2,1,0:T(8,128)(2,1)S(1)} all-to-all(bf16[8,12,3584]{2,1,0:T(8,128)(2,1)S(1)} %get-tuple-element.35), channel_id=1, replica_groups=mesh['dp'=4,'expert'=8] {'expert'}, dimensions={0} | all-to-all | bytes 1376256 | tf_op jit(solution)/shard_map/all_to_all | solution.py:30
  137.4 4.6 %fusion.21 = f32[384,512]{1,0:T(8,128)S(1)} fusion(bf16[384,3584]{1,0:T(8,128)(2,1)} %all-gather.7.cloned.1.call-done, bf16[1,3584,512]{2,1,0:T(8,128)(2,1)} %param.11), kind=kOutput, calls=%fused_computation.35 | convolution fusion | flops 1409286144 | bytes 7208960 | tf_op jit(solution)/shard_map/dot_general | solution.py:40
  142.2 2.5 multiply_convert_fusion.5
  145.4 3.1 convolution_convert_fusion
  148.9 4.6 %fusion.23 = f32[384,512]{1,0:T(8,128)S(1)} fusion(bf16[384,3584]{1,0:T(8,128)(2,1)} %all-gather.5.cloned.1.call-done, bf16[1,3584,512]{2,1,0:T(8,128)(2,1)} %param.11), kind=kOutput, calls=%fused_computation.37 | convolution fusion | flops 1409286144 | bytes 7208960 | tf_op jit(solution)/shard_map/dot_general | solution.py:40
  153.6 2.5 multiply_convert_fusion.6
  156.8 3.1 convolution_convert_fusion.1
  160.0 16.6 %all-gather.9.cloned.1.call-done = bf16[384,3584]{1,0:T(8,128)(2,1)} async-done(((bf16[96,3584]{1,0:T(8,128)(2,1)}), bf16[384,3584]{1,0:T(8,128)(2,1)}) %all-gather.9.cloned.1.call-update) | async-done | bytes 2752528 | tf_op jit(solution)/shard_map/all_gather | solution.py:31
  176.7 5.2 %multiply_convert_fusion.3 = (bf16[384,512]{1,0:T(8,128)(2,1)S(1)}, bf16[384,512]{1,0:T(8,128)(2,1)S(1)}) fusion(f32[384,512]{1,0:T(8,128)} %copy-done.24, f32[384,512]{1,0:T(8,128)} %get-tuple-element.16, bf16[384,3584]{1,0:T(8,128)(2,1)} %all-gather.9.cloned.1.call-done, bf16[1,512,3584]{2,1,0:T(8,128)(2,1)} %param.13), kind=kOutput, calls=%fused_computation.46 | convolution fusion | flops 1411842048 | bytes 8781824 | tf_op jit(solution)/shard_map/dot_general | solution.py:18
  183.9 3.2 fusion
  187.2 32.0 %all-gather.11.cloned.1.call-done = bf16[384,3584]{1,0:T(8,128)(2,1)} async-done(((bf16[96,3584]{1,0:T(8,128)(2,1)}), bf16[384,3584]{1,0:T(8,128)(2,1)}) %all-gather.11.cloned.1.call-update) | async-done | bytes 2752528 | tf_op jit(solution)/shard_map/all_gather | solution.py:31
  219.1 5.2 %multiply_convert_fusion.1 = (bf16[384,512]{1,0:T(8,128)(2,1)S(1)}, bf16[384,512]{1,0:T(8,128)(2,1)S(1)}) fusion(f32[384,512]{1,0:T(8,128)} %copy-done.23, f32[384,512]{1,0:T(8,128)} %get-tuple-element.18, bf16[384,3584]{1,0:T(8,128)(2,1)} %all-gather.11.cloned.1.call-done, bf16[1,512,3584]{2,1,0:T(8,128)(2,1)} %param.13), kind=kOutput, calls=%fused_computation.43 | convolution fusion | flops 1411842048 | bytes 8781824 | tf_op jit(solution)/shard_map/dot_general | solution.py:18
  226.7 3.2 fusion.1
  229.9 33.3 %reduce-scatter.7.cloned.1.call-done = bf16[96,3584]{1,0:T(8,128)(2,1)} async-done(((bf16[384,3584]{1,0:T(8,128)(2,1)}), bf16[96,3584]{1,0:T(8,128)(2,1)}) %reduce-scatter.7.cloned.1.call-update) | async-done | bytes 688144 | tf_op jit(solution)/shard_map/reduce_scatter | solution.py:35
  265.4 4.6 %all-to-all-start.3 = ((bf16[8,12,3584]{2,1,0:T(8,128)(2,1)}), bf16[8,12,3584]{2,1,0:T(8,128)(2,1)}, u32[]{:S(2)}, u32[]{:S(2)}) async-start(bf16[8,12,3584]{2,1,0:T(8,128)(2,1)} %all_to_all.54), calls=%async_computation.5 | async-start | bytes 1835008 | tf_op jit(solution)/shard_map/all_to_all | solution.py:36
  270.0 37.5 %reduce-scatter.5.cloned.1.call-done = bf16[96,3584]{1,0:T(8,128)(2,1)} async-done(((bf16[384,3584]{1,0:T(8,128)(2,1)}), bf16[96,3584]{1,0:T(8,128)(2,1)}) %reduce-scatter.5.cloned.1.call-update) | async-done | bytes 688144 | tf_op jit(solution)/shard_map/reduce_scatter | solution.py:35
  309.5 4.6 %all-to-all-start.1 = ((bf16[8,12,3584]{2,1,0:T(8,128)(2,1)}), bf16[8,12,3584]{2,1,0:T(8,128)(2,1)}, u32[]{:S(2)}, u32[]{:S(2)}) async-start(bf16[8,12,3584]{2,1,0:T(8,128)(2,1)} %all_to_all.50), calls=%async_computation.2 | async-start | bytes 1835008 | tf_op jit(solution)/shard_map/all_to_all | solution.py:36
  314.1 3.9 fusion.42
  318.1 4.1 fusion.3
  322.1 29.6 %reduce-scatter.9.cloned.1.call-done = bf16[96,3584]{1,0:T(8,128)(2,1)} async-done(((bf16[384,3584]{1,0:T(8,128)(2,1)}), bf16[96,3584]{1,0:T(8,128)(2,1)}) %reduce-scatter.9.cloned.1.call-update) | async-done | bytes 688144 | tf_op jit(solution)/shard_map/reduce_scatter | solution.py:35
  353.8 4.6 %all-to-all-start.5 = ((bf16[8,12,3584]{2,1,0:T(8,128)(2,1)}), bf16[8,12,3584]{2,1,0:T(8,128)(2,1)}, u32[]{:S(2)}, u32[]{:S(2)}) async-start(bf16[8,12,3584]{2,1,0:T(8,128)(2,1)} %all_to_all.58), calls=%async_computation.8 | async-start | bytes 1835008 | tf_op jit(solution)/shard_map/all_to_all | solution.py:36
  358.4 4.0 fusion.41
  362.5 5.0 %fusion.43 = f32[512,3584]{1,0:T(8,128)} fusion(bf16[384,512]{1,0:T(8,128)(2,1)S(1)} %copy-done.19, bf16[384,3584]{1,0:T(8,128)(2,1)S(1)} %copy-done.10), kind=kOutput, calls=%fused_computation.87 | convolution fusion | flops 1409286144 | bytes 10485760 | tf_op jit(solution)/shard_map/dot_general | solution.py:24
  367.5 4.1 fusion.2
  371.5 23.9 %reduce-scatter.11.cloned.1.call-done = bf16[96,3584]{1,0:T(8,128)(2,1)} async-done(((bf16[384,3584]{1,0:T(8,128)(2,1)}), bf16[96,3584]{1,0:T(8,128)(2,1)}) %reduce-scatter.11.cloned.1.call-update) | async-done | bytes 688144 | tf_op jit(solution)/shard_map/reduce_scatter | solution.py:35
  397.5 4.6 %all-to-all-start.7 = ((bf16[8,12,3584]{2,1,0:T(8,128)(2,1)}), bf16[8,12,3584]{2,1,0:T(8,128)(2,1)S(1)}, u32[]{:S(2)}, u32[]{:S(2)}) async-start(bf16[8,12,3584]{2,1,0:T(8,128)(2,1)} %all_to_all.62), calls=%async_computation.11 | async-start | bytes 1835008 | tf_op jit(solution)/shard_map/all_to_all | solution.py:36
  402.1 7.9 %fusion.4 = bf16[1,512,3584]{2,1,0:T(8,128)(2,1)} fusion(f32[512,3584]{1,0:T(8,128)} %fusion.43, bf16[384,512]{1,0:T(8,128)(2,1)S(1)} %copy-done.17, bf16[384,3584]{1,0:T(8,128)(2,1)} %all-gather.11.cloned.1.call-done), kind=kOutput, calls=%fused_computation.16 | convolution fusion | flops 1412956160 | bytes 14155776 | tf_op jit(solution)/shard_map/dot_general | solution.py:24
  416.1 9.8 %all-to-all-done.7 = bf16[8,12,3584]{2,1,0:T(8,128)(2,1)S(1)} async-done(((bf16[8,12,3584]{2,1,0:T(8,128)(2,1)}), bf16[8,12,3584]{2,1,0:T(8,128)(2,1)S(1)}, u32[]{:S(2)}, u32[]{:S(2)}) %all-to-all-start.7) | async-done | bytes 688160 | tf_op jit(solution)/shard_map/all_to_all | solution.py:36
  (122 shorter events, 40.9 us)
Async XLA Ops:
  7.2 130.3 %all-gather.7.cloned.1.call-start = ((), (), s32[]{:S(2)}) async-start(), calls=%async_computation.14 | async-start | bytes 3440640 | tf_op jit(solution)/shard_map/all_gather | solution.py:31
  51.0 27.5 %copy-start.20 = (f32[128,8]{0,1:T(8,128)S(1)}, f32[128,8]{0,1:T(8,128)}, u32[]{:S(2)}) copy-start(f32[128,8]{0,1:T(8,128)} %param.8) | copy-start | bytes 12292
  51.1 29.2 %copy-start.15 = (bf16[128,3584]{1,0:T(8,128)(2,1)S(1)}, bf16[128,3584]{1,0:T(8,128)(2,1)}, u32[]{:S(2)}) copy-start(bf16[128,3584]{1,0:T(8,128)(2,1)} %param.10) | copy-start | bytes 2752516
  51.1 97.8 %all-gather.5.cloned.1.call-start = ((), (), s32[]{:S(2)}) async-start(), calls=%async_computation.12 | async-start | bytes 3440640 | tf_op jit(solution)/shard_map/all_gather | solution.py:31
  78.5 98.2 %all-gather.9.cloned.1.call-start = ((), (), s32[]{:S(2)}) async-start(), calls=%async_computation.16 | async-start | bytes 3440640 | tf_op jit(solution)/shard_map/all_gather | solution.py:31
  110.1 109.0 %all-gather.11.cloned.1.call-start = ((), (), s32[]{:S(2)}) async-start(), calls=%async_computation.18 | async-start | bytes 3440640 | tf_op jit(solution)/shard_map/all_gather | solution.py:31
  137.3 125.9 %reduce-scatter.7.cloned.1.call-start = ((), (), s32[]{:S(2)}) async-start(), calls=%async_computation.15 | async-start | bytes 3440640 | tf_op jit(solution)/shard_map/reduce_scatter | solution.py:35
  137.4 4.6 %copy-start = (bf16[384,3584]{1,0:T(8,128)(2,1)S(1)}, bf16[384,3584]{1,0:T(8,128)(2,1)}, u32[]{:S(2)}) copy-start(bf16[384,3584]{1,0:T(8,128)(2,1)} %all-gather.7.cloned.1.call-done) | copy-start | bytes 8257540
  137.4 4.8 %copy-start.3 = (bf16[1,3584,512]{2,1,0:T(8,128)(2,1)S(1)}, bf16[1,3584,512]{2,1,0:T(8,128)(2,1)}, u32[]{:S(2)}) copy-start(bf16[1,3584,512]{2,1,0:T(8,128)(2,1)} %param.12) | copy-start | bytes 11010052
  142.2 2.5 copy-start.23
  142.2 3.2 copy-start.21
  148.6 158.8 %reduce-scatter.5.cloned.1.call-start = ((), (), s32[]{:S(2)}) async-start(), calls=%async_computation.13 | async-start | bytes 3440640 | tf_op jit(solution)/shard_map/reduce_scatter | solution.py:35
  148.8 4.6 %copy-start.4 = (bf16[1,3584,512]{2,1,0:T(8,128)(2,1)S(1)}, bf16[1,3584,512]{2,1,0:T(8,128)(2,1)}, u32[]{:S(2)}) copy-start(bf16[1,3584,512]{2,1,0:T(8,128)(2,1)} %param.12) | copy-start | bytes 11010052
  148.9 4.8 %copy-start.7 = (bf16[384,3584]{1,0:T(8,128)(2,1)S(1)}, bf16[384,3584]{1,0:T(8,128)(2,1)}, u32[]{:S(2)}) copy-start(bf16[384,3584]{1,0:T(8,128)(2,1)} %all-gather.5.cloned.1.call-done) | copy-start | bytes 8257540
  153.6 2.5 copy-start.24
  153.6 3.2 copy-start.22
  160.0 191.7 %reduce-scatter.9.cloned.1.call-start = ((), (), s32[]{:S(2)}) async-start(), calls=%async_computation.17 | async-start | bytes 3440640 | tf_op jit(solution)/shard_map/reduce_scatter | solution.py:35
  176.7 5.2 %copy-start.1 = (bf16[1,3584,512]{2,1,0:T(8,128)(2,1)S(1)}, bf16[1,3584,512]{2,1,0:T(8,128)(2,1)}, u32[]{:S(2)}) copy-start(bf16[1,3584,512]{2,1,0:T(8,128)(2,1)} %param.11) | copy-start | bytes 11010052
  181.9 2.0 copy-start.5
  187.1 208.3 %reduce-scatter.11.cloned.1.call-start = ((), (), s32[]{:S(2)}) async-start(), calls=%async_computation.19 | async-start | bytes 3440640 | tf_op jit(solution)/shard_map/reduce_scatter | solution.py:35
  219.1 5.2 %copy-start.2 = (bf16[1,3584,512]{2,1,0:T(8,128)(2,1)S(1)}, bf16[1,3584,512]{2,1,0:T(8,128)(2,1)}, u32[]{:S(2)}) copy-start(bf16[1,3584,512]{2,1,0:T(8,128)(2,1)} %param.11) | copy-start | bytes 11010052
  224.4 2.3 copy-start.6
  265.4 44.1 %all-to-all-start.3 = ((bf16[8,12,3584]{2,1,0:T(8,128)(2,1)}), bf16[8,12,3584]{2,1,0:T(8,128)(2,1)}, u32[]{:S(2)}, u32[]{:S(2)}) async-start(bf16[8,12,3584]{2,1,0:T(8,128)(2,1)} %all_to_all.54), calls=%async_computation.5 | async-start | bytes 1835008 | tf_op jit(solution)/shard_map/all_to_all | solution.py:36
  309.5 44.3 %all-to-all-start.1 = ((bf16[8,12,3584]{2,1,0:T(8,128)(2,1)}), bf16[8,12,3584]{2,1,0:T(8,128)(2,1)}, u32[]{:S(2)}, u32[]{:S(2)}) async-start(bf16[8,12,3584]{2,1,0:T(8,128)(2,1)} %all_to_all.50), calls=%async_computation.2 | async-start | bytes 1835008 | tf_op jit(solution)/shard_map/all_to_all | solution.py:36
  314.1 3.9 copy-start.14
  353.8 43.7 %all-to-all-start.5 = ((bf16[8,12,3584]{2,1,0:T(8,128)(2,1)}), bf16[8,12,3584]{2,1,0:T(8,128)(2,1)}, u32[]{:S(2)}, u32[]{:S(2)}) async-start(bf16[8,12,3584]{2,1,0:T(8,128)(2,1)} %all_to_all.58), calls=%async_computation.8 | async-start | bytes 1835008 | tf_op jit(solution)/shard_map/all_to_all | solution.py:36
  358.4 4.0 copy-start.10
  358.4 4.1 copy-start.19
  362.4 5.0 %copy-start.12 = (bf16[384,512]{1,0:T(8,128)(2,1)S(1)}, bf16[384,512]{1,0:T(8,128)(2,1)}, u32[]{:S(2)}) copy-start(bf16[384,512]{1,0:T(8,128)(2,1)} %copy-done.11) | copy-start | bytes 1179652
  371.5 30.5 %copy-start.17 = (bf16[384,512]{1,0:T(8,128)(2,1)S(1)}, bf16[384,512]{1,0:T(8,128)(2,1)}, u32[]{:S(2)}) copy-start(bf16[384,512]{1,0:T(8,128)(2,1)} %copy-done.16) | copy-start | bytes 1179652
  397.5 28.4 %all-to-all-start.7 = ((bf16[8,12,3584]{2,1,0:T(8,128)(2,1)}), bf16[8,12,3584]{2,1,0:T(8,128)(2,1)S(1)}, u32[]{:S(2)}, u32[]{:S(2)}) async-start(bf16[8,12,3584]{2,1,0:T(8,128)(2,1)} %all_to_all.62), calls=%async_computation.11 | async-start | bytes 1835008 | tf_op jit(solution)/shard_map/all_to_all | solution.py:36
  410.0 1.9 copy-start.9
  (5 other events, 5.9 us)
Sparse Core Ops, SparseCore 0:
  51.2 39.6 all-gather.6
  93.3 40.7 all-gather.4
  135.9 40.7 all-gather.8
  178.4 40.7 all-gather.10
  222.6 40.6 reduce-scatter.6
  266.7 40.6 reduce-scatter.4
  311.0 40.6 reduce-scatter.8
  354.7 40.6 reduce-scatter.10

commit v4 on v2

--- a/solution.py
+++ b/solution.py
@@ -26,9 +26,8 @@
     )
 
 
-def dispatch(send_rows):
-    along_expert = lax.all_to_all(send_rows, "expert", split_axis=0, concat_axis=0, tiled=True)
-    return lax.all_gather(along_expert, "dp", axis=0, tiled=True)
+def along_expert(send_rows):
+    return lax.all_to_all(send_rows, "expert", split_axis=0, concat_axis=0, tiled=True)
 
 
 def gather_back(partial_rows, groups):
@@ -50,8 +49,9 @@
     rows_dy = jnp.concatenate([cotangent, zero_row], 0)[token_of]
     prob_rows = jnp.concatenate([gate_probs.reshape(-1), jnp.zeros((1,), jnp.float32)], 0)[slots]
     send_c = (prob_rows[:, None] * rows_dy.astype(jnp.float32)).astype(jnp.bfloat16)
-    rows_x = dispatch(send_x)
-    rows_c = dispatch(send_c)
+    rows_x = lax.all_gather(along_expert(send_x), "dp", axis=0, tiled=True)
+    rows_x, c_along = lax.optimization_barrier((rows_x, along_expert(send_c)))
+    rows_c = lax.all_gather(c_along, "dp", axis=0, tiled=True)
     gate_w = w_gate[0]
     up_w = w_up[0]
     down_w = w_down[0]
@@ -61,6 +61,9 @@
     activated = gate_pre * sigmoid_g
     hidden = (activated * up_pre).astype(jnp.bfloat16)
     part_out = jnp.dot(hidden, down_w, preferred_element_type=jnp.float32).astype(jnp.bfloat16)
+    part_out, hidden, gate_pre, up_pre = lax.optimization_barrier((part_out, hidden, gate_pre, up_pre))
+    sigmoid_g = jax.nn.sigmoid(gate_pre)
+    activated = gate_pre * sigmoid_g
     out_rows = gather_back(part_out, groups).astype(jnp.float32)
     grad_hidden = contract_last(rows_c, down_w)
     grad_upin = (grad_hidden * activated).astype(jnp.bfloat16)

time: 381 us -> 369 us (0.969)
  waiting for transfers between devices: 193 us -> 154 us
  blocking collectives: 76.7 us -> 115 us
  matrix products: 66.6 us -> 61 us
  starting transfers between devices: 9.56 us -> 4.95 us
    all_to_all x2 -> x3, blocking collectives: 76.7 us -> 115 us  [the longest x2 76.7 us: along_expert(): lax.all_to_all(send_rows, 'expert', split_axis=0, concat_axis=0, tiled=True)]
    reduce_scatter x2, waiting for transfers between devices: 110 us -> 73.2 us  [gather_back(): lax.psum_scatter(partial_rows, 'dp', scatter_dimension=0, tiled=True)]
    all_to_all x2 -> x1, starting transfers between devices: 9.22 us -> 4.61 us  [gather_back(): lax.all_to_all(summed, 'expert', split_axis=0, concat_axis=0, tiled=True)]
    all_gather x2, waiting for transfers between devices: 75.7 us -> 71.2 us  [the longest x1 48.9 us: on_device(): rows_c = lax.all_gather(c_along, 'dp', axis=0, tiled=True)]
    all_to_all x2 -> x1, waiting for transfers between devices: 7.68 us -> 9.77 us  [gather_back(): lax.all_to_all(summed, 'expert', split_axis=0, concat_axis=0, tiled=True)]
  transfers between devices with their start and end apart: 6 -> 5, of which waited for: 5 -> 5; matrix products, arithmetic and copies ran while one was open for 15% -> 17% of each run, Pallas kernels for 0% -> 0%
where the time goes in v4:
time: 369 us
  waiting for transfers between devices  154 us (42%)
  blocking collectives  115 us (31%)
  matrix products  61 us (17%)
  local copies, waits for them, and re-layouts  14.9 us (4%)
  between operations  14 us (4%)
  starting transfers between devices  4.95 us (1%)
  other arithmetic  4.72 us (1%)
    all_to_all x2, blocking collectives, along_expert(): lax.all_to_all(send_rows, 'expert', split_axis=0, concat_axis=0, tiled=True)  76.7 us
    reduce_scatter x2, waiting for transfers between devices, gather_back(): lax.psum_scatter(partial_rows, 'dp', scatter_dimension=0, tiled=True)  73.2 us
    all_gather x1, waiting for transfers between devices, on_device(): rows_c = lax.all_gather(c_along, 'dp', axis=0, tiled=True)  48.9 us
    all_to_all x1, blocking collectives, gather_back(): lax.all_to_all(summed, 'expert', split_axis=0, concat_axis=0, tiled=True)  38.2 us
    all_gather x1, waiting for transfers between devices, on_device(): rows_x = lax.all_gather(along_expert(send_x), 'dp', axis=0, tiled=True)  22.3 us
    dot_general x3, matrix products, contract_last(): lax.dot_general(left, right, (((1,), (1,)), ((), ())), preferred_element_...  21.8 us
    dot_general x3, matrix products, contract_first(): lax.dot_general(left, right, (((0,), (0,)), ((), ())), preferred_element_...  19.6 us
    all_to_all x1, waiting for transfers between devices, gather_back(): lax.all_to_all(summed, 'expert', split_axis=0, concat_axis=0, tiled=True)  9.77 us
  transfers between devices with their start and end apart: 5, of which 5 were waited for; matrix products, arithmetic and copies ran while one was open for 17% of the time, Pallas kernels for 0%

profile of v4, /device:TPU:0, one launch (start us, length us, event | category | flops | bytes accessed | tf_op | source)
XLA Modules:
  0.0 368.9 jit_solution(4227576593701537726)
XLA Ops:
  7.2 0.7 broadcast_compare_fusion
  7.9 0.7 broadcast_multiply_fusion
  8.6 0.8 copy.15
  10.0 2.3 reduce-window.6
  12.9 4.3 %scatter_custom_fusion = s32[192]{0:T(256)S(1)} fusion(s32[1024]{0:T(1024)S(1)} %bitcast.81, s32[1024]{0:T(1024)S(1)} %iota.15, s32[]{:T(128)} %constant.15.clone.1), kind=kCustom, calls=%fused_computation.62 | custom fusion | bytes 772 | tf_op jit(solution)/shard_map/scatter | solution.py:14
  17.2 1.2 concatenate.10
  18.5 1.4 gather_fusion.1
  19.9 40.0 %all_to_all.45 = bf16[8,24,3584]{2,1,0:T(8,128)(2,1)} all-to-all(bf16[8,24,3584]{2,1,0:T(8,128)(2,1)S(1)} %bitcast.74), channel_id=1, replica_groups=mesh['dp'=4,'expert'=8] {'expert'}, dimensions={0} | all-to-all | bytes 2752512 | tf_op jit(solution)/shard_map/all_to_all | solution.py:30
  60.2 1.4 gather_fusion
  61.8 1.4 gather_fusion.2
  63.5 36.7 %all_to_all.46 = bf16[8,24,3584]{2,1,0:T(8,128)(2,1)} all-to-all(bf16[8,24,3584]{2,1,0:T(8,128)(2,1)S(1)} %fusion.13), channel_id=1, replica_groups=mesh['dp'=4,'expert'=8] {'expert'}, dimensions={0} | all-to-all | bytes 2752512 | tf_op jit(solution)/shard_map/all_to_all | solution.py:30
  100.3 22.3 %all-gather.3.cloned.1.call-done = bf16[768,3584]{1,0:T(8,128)(2,1)} async-done(((bf16[192,3584]{1,0:T(8,128)(2,1)}), bf16[768,3584]{1,0:T(8,128)(2,1)}) %all-gather.3.cloned.1.call-update) | async-done | bytes 5505040 | tf_op jit(solution)/shard_map/all_gather | solution.py:52
  122.7 6.2 %fusion.11 = f32[768,512]{1,0:T(8,128)S(1)} fusion(bf16[768,3584]{1,0:T(8,128)(2,1)} %all-gather.3.cloned.1.call-done, bf16[1,3584,512]{2,1,0:T(8,128)(2,1)} %param.11), kind=kOutput, calls=%fused_computation.23 | convolution fusion | flops 2818572288 | bytes 10747904 | tf_op jit(solution)/shard_map/dot_general | solution.py:58
  129.0 4.2 %multiply_convert_fusion.2 = (bf16[768,512]{1,0:T(8,128)(2,1)S(1)}, f32[768,512]{1,0:T(8,128)}) fusion(f32[768,512]{1,0:T(8,128)S(1)} %fusion.11, bf16[768,3584]{1,0:T(8,128)(2,1)S(1)} %copy-done.2, bf16[1,3584,512]{2,1,0:T(8,128)(2,1)S(1)} %copy-done.5), kind=kOutput, calls=%fused_computation.32 | convolution fusion | flops 2820931584 | bytes 13107200 | tf_op jit(solution)/shard_map/dot_general | solution.py:59
  133.2 0.9 copy-done.7
  134.1 4.8 %convolution_convert_fusion = bf16[768,3584]{1,0:T(8,128)(2,1)} fusion(bf16[768,512]{1,0:T(8,128)(2,1)S(1)} %get-tuple-element.17, bf16[1,512,3584]{2,1,0:T(8,128)(2,1)S(1)} %copy-done.3), kind=kOutput, calls=%fused_computation.6 | convolution fusion | flops 2821324800 | bytes 9961472 | tf_op jit(solution)/shard_map/dot_general | solution.py:63
  139.2 48.9 %all-gather.5.cloned.1.call-done = bf16[768,3584]{1,0:T(8,128)(2,1)} async-done(((bf16[192,3584]{1,0:T(8,128)(2,1)}), bf16[768,3584]{1,0:T(8,128)(2,1)}) %all-gather.5.cloned.1.call-update) | async-done | bytes 5505040 | tf_op jit(solution)/shard_map/all_gather | solution.py:54
  188.1 8.1 %multiply_convert_fusion = (bf16[768,512]{1,0:T(8,128)(2,1)S(1)}, bf16[768,512]{1,0:T(8,128)(2,1)S(1)}) fusion(f32[768,512]{1,0:T(8,128)} %copy-done.10, f32[768,512]{1,0:T(8,128)} %get-tuple-element.15, bf16[768,3584]{1,0:T(8,128)(2,1)} %all-gather.5.cloned.1.call-done, bf16[1,512,3584]{2,1,0:T(8,128)(2,1)} %param.13), kind=kOutput, calls=%fused_computation.29 | convolution fusion | flops 2823684096 | bytes 13893632 | tf_op jit(solution)/shard_map/dot_general | solution.py:18
  196.3 5.8 %fusion.9 = f32[768,3584]{1,0:T(8,128)} fusion(bf16[768,512]{1,0:T(8,128)(2,1)S(1)} %get-tuple-element.27, bf16[1,3584,512]{2,1,0:T(8,128)(2,1)S(1)} %copy-done.4), kind=kOutput, calls=%fused_computation.21 | convolution fusion | flops 2818572288 | bytes 15466496 | tf_op jit(solution)/shard_map/dot_general | solution.py:18
  202.0 7.8 %add_convert_fusion = bf16[768,3584]{1,0:T(8,128)(2,1)} fusion(f32[768,3584]{1,0:T(8,128)} %fusion.9, bf16[768,512]{1,0:T(8,128)(2,1)S(1)} %get-tuple-element.26, bf16[1,3584,512]{2,1,0:T(8,128)(2,1)S(1)} %copy-done.6), kind=kOutput, calls=%fused_computation.5 | convolution fusion | flops 2824077312 | bytes 20971520 | tf_op jit(solution)/shard_map/dot_general | solution.py:18
  209.9 44.9 %reduce-scatter.3.cloned.1.call-done = bf16[192,3584]{1,0:T(8,128)(2,1)} async-done(((bf16[768,3584]{1,0:T(8,128)(2,1)}), bf16[192,3584]{1,0:T(8,128)(2,1)}) %reduce-scatter.3.cloned.1.call-update) | async-done | bytes 1376272 | tf_op jit(solution)/shard_map/reduce_scatter | solution.py:34
  254.8 38.2 %all_to_all.47 = bf16[8,24,3584]{2,1,0:T(8,128)(2,1)S(1)} all-to-all(bf16[8,24,3584]{2,1,0:T(8,128)(2,1)} %bitcast.78), channel_id=1, replica_groups=mesh['dp'=4,'expert'=8] {'expert'}, dimensions={0} | all-to-all | bytes 2752512 | tf_op jit(solution)/shard_map/all_to_all | solution.py:35
  293.0 28.3 %reduce-scatter.5.cloned.1.call-done = bf16[192,3584]{1,0:T(8,128)(2,1)} async-done(((bf16[768,3584]{1,0:T(8,128)(2,1)}), bf16[192,3584]{1,0:T(8,128)(2,1)}) %reduce-scatter.5.cloned.1.call-update) | async-done | bytes 1376272 | tf_op jit(solution)/shard_map/reduce_scatter | solution.py:34
  321.4 4.6 %all-to-all-start.3 = ((bf16[8,24,3584]{2,1,0:T(8,128)(2,1)}), bf16[8,24,3584]{2,1,0:T(8,128)(2,1)}, u32[]{:S(2)}, u32[]{:S(2)}) async-start(bf16[8,24,3584]{2,1,0:T(8,128)(2,1)} %bitcast.77), calls=%async_computation.5 | async-start | bytes 2752512 | tf_op jit(solution)/shard_map/all_to_all | solution.py:35
  326.0 7.8 %fusion.1 = bf16[1,3584,512]{2,1,0:T(8,128)(2,1)} fusion(bf16[768,3584]{1,0:T(8,128)(2,1)} %all-gather.3.cloned.1.call-done, bf16[768,512]{1,0:T(8,128)(2,1)} %copy-done.9), kind=kOutput, calls=%fused_computation.11 | convolution fusion | flops 2820407296 | bytes 9961472 | tf_op jit(solution)/shard_map/dot_general | solution.py:24
  333.8 7.3 %fusion = bf16[1,3584,512]{2,1,0:T(8,128)(2,1)} fusion(bf16[768,3584]{1,0:T(8,128)(2,1)} %all-gather.3.cloned.1.call-done, bf16[768,512]{1,0:T(8,128)(2,1)S(1)} %get-tuple-element.27), kind=kOutput, calls=%fused_computation.10 | convolution fusion | flops 2820407296 | bytes 9961472 | tf_op jit(solution)/shard_map/dot_general | solution.py:24
  341.1 4.5 %fusion.2 = bf16[1,512,3584]{2,1,0:T(8,128)(2,1)} fusion(bf16[768,512]{1,0:T(8,128)(2,1)S(1)} %copy-done.8, bf16[768,3584]{1,0:T(8,128)(2,1)S(1)} %bitcast.83), kind=kOutput, calls=%fused_computation.12 | convolution fusion | flops 2820407296 | bytes 9961472 | tf_op jit(solution)/shard_map/dot_general | solution.py:24
  346.1 1.2 scatter_custom_fusion.1
  347.4 0.7 copy.18
  348.1 1.8 convolution_convert_fusion.5
  349.9 9.8 %all-to-all-done.3 = bf16[8,24,3584]{2,1,0:T(8,128)(2,1)} async-done(((bf16[8,24,3584]{2,1,0:T(8,128)(2,1)}), bf16[8,24,3584]{2,1,0:T(8,128)(2,1)}, u32[]{:S(2)}, u32[]{:S(2)}) %all-to-all-start.3) | async-done | bytes 1376288 | tf_op jit(solution)/shard_map/all_to_all | solution.py:35
  359.7 2.7 convolution_convert_fusion.4
  (59 shorter events, 3.0 us)
Async XLA Ops:
  7.2 115.4 %all-gather.3.cloned.1.call-start = ((), (), s32[]{:S(2)}) async-start(), calls=%async_computation.6 | async-start | bytes 6881280 | tf_op jit(solution)/shard_map/all_gather | solution.py:52
  19.9 40.1 %copy-start.1 = (f32[128,8]{0,1:T(8,128)S(1)}, f32[128,8]{0,1:T(8,128)}, u32[]{:S(2)}) copy-start(f32[128,8]{0,1:T(8,128)} %param.8) | copy-start | bytes 12292
  19.9 41.8 %copy-start = (bf16[128,3584]{1,0:T(8,128)(2,1)S(1)}, bf16[128,3584]{1,0:T(8,128)(2,1)}, u32[]{:S(2)}) copy-start(bf16[128,3584]{1,0:T(8,128)(2,1)} %param.10) | copy-start | bytes 2752516
  59.9 128.2 %all-gather.5.cloned.1.call-start = ((), (), s32[]{:S(2)}) async-start(), calls=%async_computation.8 | async-start | bytes 6881280 | tf_op jit(solution)/shard_map/all_gather | solution.py:54
  122.6 132.2 %reduce-scatter.3.cloned.1.call-start = ((), (), s32[]{:S(2)}) async-start(), calls=%async_computation.7 | async-start | bytes 6881280 | tf_op jit(solution)/shard_map/reduce_scatter | solution.py:34
  122.7 6.2 %copy-start.2 = (bf16[768,3584]{1,0:T(8,128)(2,1)S(1)}, bf16[768,3584]{1,0:T(8,128)(2,1)}, u32[]{:S(2)}) copy-start(bf16[768,3584]{1,0:T(8,128)(2,1)} %all-gather.3.cloned.1.call-done) | copy-start | bytes 16515076
  122.7 6.3 %copy-start.5 = (bf16[1,3584,512]{2,1,0:T(8,128)(2,1)S(1)}, bf16[1,3584,512]{2,1,0:T(8,128)(2,1)}, u32[]{:S(2)}) copy-start(bf16[1,3584,512]{2,1,0:T(8,128)(2,1)} %param.12) | copy-start | bytes 11010052
  129.0 4.2 %copy-start.10 = (f32[768,512]{1,0:T(8,128)}, f32[768,512]{1,0:T(8,128)S(1)}, u32[]{:S(2)}) copy-start(f32[768,512]{1,0:T(8,128)S(1)} %fusion.11) | copy-start | bytes 4718596
  129.0 5.1 %copy-start.3 = (bf16[1,512,3584]{2,1,0:T(8,128)(2,1)S(1)}, bf16[1,512,3584]{2,1,0:T(8,128)(2,1)}, u32[]{:S(2)}) copy-start(bf16[1,512,3584]{2,1,0:T(8,128)(2,1)} %param.13) | copy-start | bytes 11010052
  133.2 0.9 copy-start.7
  138.9 182.5 %reduce-scatter.5.cloned.1.call-start = ((), (), s32[]{:S(2)}) async-start(), calls=%async_computation.9 | async-start | bytes 6881280 | tf_op jit(solution)/shard_map/reduce_scatter | solution.py:34
  188.1 8.2 %copy-start.4 = (bf16[1,3584,512]{2,1,0:T(8,128)(2,1)S(1)}, bf16[1,3584,512]{2,1,0:T(8,128)(2,1)}, u32[]{:S(2)}) copy-start(bf16[1,3584,512]{2,1,0:T(8,128)(2,1)} %param.11) | copy-start | bytes 11010052
  196.2 5.8 %copy-start.9 = (bf16[768,512]{1,0:T(8,128)(2,1)}, bf16[768,512]{1,0:T(8,128)(2,1)S(1)}, u32[]{:S(2)}) copy-start(bf16[768,512]{1,0:T(8,128)(2,1)S(1)} %get-tuple-element.26) | copy-start | bytes 2359300
  196.3 5.8 %copy-start.6 = (bf16[1,3584,512]{2,1,0:T(8,128)(2,1)S(1)}, bf16[1,3584,512]{2,1,0:T(8,128)(2,1)}, u32[]{:S(2)}) copy-start(bf16[1,3584,512]{2,1,0:T(8,128)(2,1)} %param.12) | copy-start | bytes 11010052
  321.4 38.3 %all-to-all-start.3 = ((bf16[8,24,3584]{2,1,0:T(8,128)(2,1)}), bf16[8,24,3584]{2,1,0:T(8,128)(2,1)}, u32[]{:S(2)}, u32[]{:S(2)}) async-start(bf16[8,24,3584]{2,1,0:T(8,128)(2,1)} %bitcast.77), calls=%async_computation.5 | async-start | bytes 2752512 | tf_op jit(solution)/shard_map/all_to_all | solution.py:35
  326.0 15.1 %slice-start = ((s8[5505024]{0:T(1024)(128)(4,1)}), s8[4194304]{0:T(1024)(128)(4,1)S(1)}, s32[]{:S(2)}) async-start(s8[5505024]{0:T(1024)(128)(4,1)} %bitcast.82), calls=%async_computation.10 | async-start | bytes 8388608
  333.8 7.3 %slice-start.1 = ((s8[5505024]{0:T(1024)(128)(4,1)}), s8[1310720]{0:T(1024)(128)(4,1)S(1)}, s32[]{:S(2)}) async-start(s8[5505024]{0:T(1024)(128)(4,1)} %bitcast.82), calls=%async_computation.11 | async-start | bytes 2621440
  333.8 7.3 %copy-start.8 = (bf16[768,512]{1,0:T(8,128)(2,1)S(1)}, bf16[768,512]{1,0:T(8,128)(2,1)}, u32[]{:S(2)}) copy-start(bf16[768,512]{1,0:T(8,128)(2,1)} %copy-done.7) | copy-start | bytes 2359300
Sparse Core Ops, SparseCore 0:
  60.0 62.5 all-gather.2
  124.4 63.6 all-gather.4
  191.1 63.6 reduce-scatter.2
  257.7 63.6 reduce-scatter.4

commit v5 on v4

--- a/solution.py
+++ b/solution.py
@@ -30,8 +30,15 @@
     return lax.all_to_all(send_rows, "expert", split_axis=0, concat_axis=0, tiled=True)
 
 
+def replicate_dp(rows, groups):
+    return lax.all_to_all(jnp.tile(rows, (groups, 1)), "dp", split_axis=0, concat_axis=0, tiled=True)
+
+
 def gather_back(partial_rows, groups):
-    summed = lax.psum_scatter(partial_rows, "dp", scatter_dimension=0, tiled=True)
+    by_group = lax.all_to_all(partial_rows, "dp", split_axis=0, concat_axis=0, tiled=True)
+    rows = by_group.shape[0] // groups
+    summed = jnp.sum(by_group.astype(jnp.float32).reshape(groups, rows, -1), axis=0)
+    summed = summed.astype(jnp.bfloat16)
     return lax.all_to_all(summed, "expert", split_axis=0, concat_axis=0, tiled=True)
 
 
@@ -49,9 +56,9 @@
     rows_dy = jnp.concatenate([cotangent, zero_row], 0)[token_of]
     prob_rows = jnp.concatenate([gate_probs.reshape(-1), jnp.zeros((1,), jnp.float32)], 0)[slots]
     send_c = (prob_rows[:, None] * rows_dy.astype(jnp.float32)).astype(jnp.bfloat16)
-    rows_x = lax.all_gather(along_expert(send_x), "dp", axis=0, tiled=True)
+    rows_x = replicate_dp(along_expert(send_x), groups)
     rows_x, c_along = lax.optimization_barrier((rows_x, along_expert(send_c)))
-    rows_c = lax.all_gather(c_along, "dp", axis=0, tiled=True)
+    rows_c = replicate_dp(c_along, groups)
     gate_w = w_gate[0]
     up_w = w_up[0]
     down_w = w_down[0]

time: 369 us -> 435 us (1.18)
  waiting for transfers between devices: 154 us -> 200 us
  starting transfers between devices: 4.95 us -> 30 us
  between operations: 14 us -> 0.91 us
  blocking collectives: 115 us -> 102 us
  other arithmetic: 4.72 us -> 15.8 us
  matrix products: 61 us -> 66.1 us
  local copies, waits for them, and re-layouts: 14.9 us -> 19.6 us
    all_to_all x0 -> x4, waiting for transfers between devices: none -> 167 us  [the longest x2 95.3 us: gather_back(): lax.all_to_all(partial_rows, 'dp', split_axis=0, concat_axis=0, tiled=True)]
    reduce_scatter x2 -> x0, waiting for transfers between devices: 73.2 us -> none  [gather_back(): lax.psum_scatter(partial_rows, 'dp', scatter_dimension=0, tiled=True)]
    all_gather x2 -> x0, waiting for transfers between devices: 71.2 us -> none  [the longest x1 48.9 us: on_device(): rows_c = lax.all_gather(c_along, 'dp', axis=0, tiled=True)]
    all_to_all x2 -> x1, blocking collectives: 76.7 us -> 36 us  [along_expert(): lax.all_to_all(send_rows, 'expert', split_axis=0, concat_axis=0, tiled=True)]
    all_to_all x1, blocking collectives: 38.2 us -> 65.6 us  [replicate_dp(): lax.all_to_all(jnp.tile(rows, (groups, 1)), 'dp', split_axis=0, concat_ax...]
    all_to_all x1 -> x2, waiting for transfers between devices: 9.77 us -> 33.2 us  [gather_back(): lax.all_to_all(summed, 'expert', split_axis=0, concat_axis=0, tiled=True)]
    all_to_all x0 -> x4, starting transfers between devices: none -> 21.9 us  [the longest x2 10.4 us: gather_back(): lax.all_to_all(partial_rows, 'dp', split_axis=0, concat_axis=0, tiled=True)]
    reduce_sum x0 -> x2, other arithmetic: none -> 9.7 us  [gather_back(): jnp.sum(by_group.astype(jnp.float32).reshape(groups, rows, -1), axis=0)]
  transfers between devices with their start and end apart: 5 -> 6, of which waited for: 5 -> 6; matrix products, arithmetic and copies ran while one was open for 17% -> 19% of each run, Pallas kernels for 0% -> 0%
where the time goes in v5:
time: 435 us; the launch traced here: 434 us
  waiting for transfers between devices  200 us (46%)
  blocking collectives  102 us (23%)
  matrix products  66.1 us (15%)
  starting transfers between devices  30 us (7%)
  local copies, waits for them, and re-layouts  19.6 us (5%)
  other arithmetic  15.8 us (4%)
    all_to_all x2, waiting for transfers between devices, gather_back(): lax.all_to_all(partial_rows, 'dp', split_axis=0, concat_axis=0, tiled=True)  95.3 us
    all_to_all x1, blocking collectives, replicate_dp(): lax.all_to_all(jnp.tile(rows, (groups, 1)), 'dp', split_axis=0, concat_ax...  65.6 us
    all_to_all x1, waiting for transfers between devices, replicate_dp(): lax.all_to_all(jnp.tile(rows, (groups, 1)), 'dp', split_axis=0, concat_ax...  41.7 us
    all_to_all x1, blocking collectives, along_expert(): lax.all_to_all(send_rows, 'expert', split_axis=0, concat_axis=0, tiled=True)  36 us
    all_to_all x2, waiting for transfers between devices, gather_back(): lax.all_to_all(summed, 'expert', split_axis=0, concat_axis=0, tiled=True)  33.2 us
    all_to_all x1, waiting for transfers between devices, along_expert(): lax.all_to_all(send_rows, 'expert', split_axis=0, concat_axis=0, tiled=True)  30.2 us
    dot_general x3, matrix products, contract_first(): lax.dot_general(left, right, (((0,), (0,)), ((), ())), preferred_element_...  21.9 us
    dot_general x3, matrix products, contract_last(): lax.dot_general(left, right, (((1,), (1,)), ((), ())), preferred_element_...  21.4 us
  transfers between devices with their start and end apart: 6, of which 6 were waited for; matrix products, arithmetic and copies ran while one was open for 19% of the time, Pallas kernels for 0%

profile of v5, /device:TPU:0, one launch (start us, length us, event | category | flops | bytes accessed | tf_op | source)
XLA Modules:
  0.0 434.5 jit_solution(4122549609458967111)
XLA Ops:
  3.4 2.3 reduce-window.6
  6.3 4.3 scatter_custom_fusion
  11.9 2.5 gather_fusion.1
  14.4 6.5 %all-to-all-start = ((bf16[8,24,3584]{2,1,0:T(8,128)(2,1)}), bf16[8,24,3584]{2,1,0:T(8,128)(2,1)}, u32[]{:S(2)}, u32[]{:S(2)}) async-start(bf16[8,24,3584]{2,1,0:T(8,128)(2,1)} %bitcast.3), calls=%async_computation | async-start | bytes 2752512 | tf_op jit(solution)/shard_map/all_to_all | solution.py:30
  24.4 30.2 %all-to-all-done = bf16[8,24,3584]{2,1,0:T(8,128)(2,1)} async-done(((bf16[8,24,3584]{2,1,0:T(8,128)(2,1)}), bf16[8,24,3584]{2,1,0:T(8,128)(2,1)}, u32[]{:S(2)}, u32[]{:S(2)}) %all-to-all-start) | async-done | bytes 1376288 | tf_op jit(solution)/shard_map/all_to_all | solution.py:30
  54.6 36.0 %all_to_all.72 = bf16[8,24,3584]{2,1,0:T(8,128)(2,1)S(1)} all-to-all(bf16[8,24,3584]{2,1,0:T(8,128)(2,1)S(1)} %fusion.13), channel_id=1, replica_groups=mesh['dp'=4,'expert'=8] {'expert'}, dimensions={0} | all-to-all | bytes 2752512 | tf_op jit(solution)/shard_map/all_to_all | solution.py:30
  90.6 1.8 tile.7
  92.4 65.6 %all_to_all.73 = bf16[4,192,3584]{2,1,0:T(8,128)(2,1)} all-to-all(bf16[4,192,3584]{2,1,0:T(8,128)(2,1)S(1)} %tile.7), channel_id=1, replica_groups=mesh['dp'=4,'expert'=8] {'dp'}, dimensions={0} | all-to-all | bytes 11010048 | tf_op jit(solution)/shard_map/all_to_all | solution.py:34
  158.0 2.8 tile.8
  160.8 5.1 %all-to-all-start.5 = ((bf16[4,192,3584]{2,1,0:T(8,128)(2,1)}), bf16[4,192,3584]{2,1,0:T(8,128)(2,1)}, u32[]{:S(2)}, u32[]{:S(2)}) async-start(bf16[4,192,3584]{2,1,0:T(8,128)(2,1)} %tile.8), calls=%async_computation.5 | async-start | bytes 11010048 | tf_op jit(solution)/shard_map/all_to_all | solution.py:34
  165.9 6.2 %fusion.11 = f32[768,512]{1,0:T(8,128)S(1)} fusion(bf16[768,3584]{1,0:T(8,128)(2,1)} %bitcast.77, bf16[1,3584,512]{2,1,0:T(8,128)(2,1)} %param.11), kind=kOutput, calls=%fused_computation.23 | convolution fusion | flops 2818572288 | bytes 10747904 | tf_op jit(solution)/shard_map/dot_general | solution.py:65
  172.2 7.4 %multiply_convert_fusion.2 = (bf16[768,512]{1,0:T(8,128)(2,1)S(1)}, f32[768,512]{1,0:T(8,128)}) fusion(f32[768,512]{1,0:T(8,128)S(1)} %fusion.11, bf16[768,3584]{1,0:T(8,128)(2,1)} %bitcast.78, bf16[1,3584,512]{2,1,0:T(8,128)(2,1)S(1)} %copy-done.4), kind=kOutput, calls=%fused_computation.32 | convolution fusion | flops 2820931584 | bytes 13107200 | tf_op jit(solution)/shard_map/dot_general | solution.py:66
  179.6 4.8 %convolution_convert_fusion = bf16[768,3584]{1,0:T(8,128)(2,1)} fusion(bf16[768,512]{1,0:T(8,128)(2,1)S(1)} %get-tuple-element.17, bf16[1,512,3584]{2,1,0:T(8,128)(2,1)S(1)} %copy-done.2), kind=kOutput, calls=%fused_computation.6 | convolution fusion | flops 2821324800 | bytes 9961472 | tf_op jit(solution)/shard_map/dot_general | solution.py:70
  184.4 41.7 %all-to-all-done.5 = bf16[4,192,3584]{2,1,0:T(8,128)(2,1)} async-done(((bf16[4,192,3584]{2,1,0:T(8,128)(2,1)}), bf16[4,192,3584]{2,1,0:T(8,128)(2,1)}, u32[]{:S(2)}, u32[]{:S(2)}) %all-to-all-start.5) | async-done | bytes 5505056 | tf_op jit(solution)/shard_map/all_to_all | solution.py:34
  226.1 5.3 %all-to-all-start.3 = ((bf16[4,192,3584]{2,1,0:T(8,128)(2,1)}), bf16[4,192,3584]{2,1,0:T(8,128)(2,1)}, u32[]{:S(2)}, u32[]{:S(2)}) async-start(bf16[4,192,3584]{2,1,0:T(8,128)(2,1)} %bitcast.81), calls=%async_computation.3 | async-start | bytes 11010048 | tf_op jit(solution)/shard_map/all_to_all | solution.py:38
  231.4 8.1 %multiply_convert_fusion = (bf16[768,512]{1,0:T(8,128)(2,1)S(1)}, bf16[768,512]{1,0:T(8,128)(2,1)S(1)}) fusion(f32[768,512]{1,0:T(8,128)} %copy-done.9, f32[768,512]{1,0:T(8,128)} %get-tuple-element.15, bf16[768,3584]{1,0:T(8,128)(2,1)} %bitcast.14, bf16[1,512,3584]{2,1,0:T(8,128)(2,1)} %param.13), kind=kOutput, calls=%fused_computation.29 | convolution fusion | flops 2823684096 | bytes 13893632 | tf_op jit(solution)/shard_map/dot_general | solution.py:18
  239.6 5.7 %fusion.9 = f32[768,3584]{1,0:T(8,128)} fusion(bf16[768,512]{1,0:T(8,128)(2,1)S(1)} %get-tuple-element.27, bf16[1,3584,512]{2,1,0:T(8,128)(2,1)S(1)} %copy-done.3), kind=kOutput, calls=%fused_computation.21 | convolution fusion | flops 2818572288 | bytes 15466496 | tf_op jit(solution)/shard_map/dot_general | solution.py:18
  245.4 7.5 %add_convert_fusion = bf16[768,3584]{1,0:T(8,128)(2,1)} fusion(f32[768,3584]{1,0:T(8,128)} %fusion.9, bf16[768,512]{1,0:T(8,128)(2,1)S(1)} %get-tuple-element.26, bf16[1,3584,512]{2,1,0:T(8,128)(2,1)S(1)} %copy-done.5), kind=kOutput, calls=%fused_computation.5 | convolution fusion | flops 2824077312 | bytes 20971520 | tf_op jit(solution)/shard_map/dot_general | solution.py:18
  252.9 39.3 %all-to-all-done.3 = bf16[4,192,3584]{2,1,0:T(8,128)(2,1)} async-done(((bf16[4,192,3584]{2,1,0:T(8,128)(2,1)}), bf16[4,192,3584]{2,1,0:T(8,128)(2,1)}, u32[]{:S(2)}, u32[]{:S(2)}) %all-to-all-start.3) | async-done | bytes 5505056 | tf_op jit(solution)/shard_map/all_to_all | solution.py:38
  292.1 5.1 %all-to-all-start.6 = ((bf16[4,192,3584]{2,1,0:T(8,128)(2,1)}), bf16[4,192,3584]{2,1,0:T(8,128)(2,1)}, u32[]{:S(2)}, u32[]{:S(2)}) async-start(bf16[4,192,3584]{2,1,0:T(8,128)(2,1)} %bitcast.82), calls=%async_computation.6 | async-start | bytes 11010048 | tf_op jit(solution)/shard_map/all_to_all | solution.py:38
  297.2 4.8 %reduce_sum.48 = bf16[192,3584]{1,0:T(8,128)(2,1)} reduce(bf16[4,192,3584]{2,1,0:T(8,128)(2,1)} %all-to-all-done.3, bf16[]{:T(256)} %constant.45.clone.1), dimensions={0}, to_apply=%region_4.5 | reduce | flops 2064384 | bytes 6881282 | tf_op jit(solution)/shard_map/reduce_sum | solution.py:40
  302.1 56.0 %all-to-all-done.6 = bf16[4,192,3584]{2,1,0:T(8,128)(2,1)} async-done(((bf16[4,192,3584]{2,1,0:T(8,128)(2,1)}), bf16[4,192,3584]{2,1,0:T(8,128)(2,1)}, u32[]{:S(2)}, u32[]{:S(2)}) %all-to-all-start.6) | async-done | bytes 5505056 | tf_op jit(solution)/shard_map/all_to_all | solution.py:38
  358.1 4.3 all-to-all-start.4
  362.4 4.8 %reduce_sum.49 = bf16[192,3584]{1,0:T(8,128)(2,1)} reduce(bf16[4,192,3584]{2,1,0:T(8,128)(2,1)} %all-to-all-done.6, bf16[]{:T(256)} %constant.45.clone.1), dimensions={0}, to_apply=%region_5.6 | reduce | flops 2064384 | bytes 6881282 | tf_op jit(solution)/shard_map/reduce_sum | solution.py:40
  367.3 28.8 %all-to-all-done.4 = bf16[8,24,3584]{2,1,0:T(8,128)(2,1)} async-done(((bf16[8,24,3584]{2,1,0:T(8,128)(2,1)}), bf16[8,24,3584]{2,1,0:T(8,128)(2,1)}, u32[]{:S(2)}, u32[]{:S(2)}) %all-to-all-start.4) | async-done | bytes 1376288 | tf_op jit(solution)/shard_map/all_to_all | solution.py:42
  396.0 3.8 all-to-all-start.7
  399.8 7.6 %fusion.1 = bf16[1,3584,512]{2,1,0:T(8,128)(2,1)} fusion(bf16[768,3584]{1,0:T(8,128)(2,1)} %bitcast.79, bf16[768,512]{1,0:T(8,128)(2,1)} %copy-done.8), kind=kOutput, calls=%fused_computation.11 | convolution fusion | flops 2820407296 | bytes 9961472 | tf_op jit(solution)/shard_map/dot_general | solution.py:24
  407.5 7.2 %fusion = bf16[1,3584,512]{2,1,0:T(8,128)(2,1)} fusion(bf16[768,3584]{1,0:T(8,128)(2,1)} %bitcast.80, bf16[768,512]{1,0:T(8,128)(2,1)S(1)} %get-tuple-element.27), kind=kOutput, calls=%fused_computation.10 | convolution fusion | flops 2820407296 | bytes 9961472 | tf_op jit(solution)/shard_map/dot_general | solution.py:24
  414.7 7.0 %fusion.2 = bf16[1,512,3584]{2,1,0:T(8,128)(2,1)} fusion(bf16[768,512]{1,0:T(8,128)(2,1)S(1)} %copy-done.7, bf16[768,3584]{1,0:T(8,128)(2,1)} %bitcast.14), kind=kOutput, calls=%fused_computation.12 | convolution fusion | flops 2820407296 | bytes 9961472 | tf_op jit(solution)/shard_map/dot_general | solution.py:24
  421.7 1.8 fusion.14
  425.6 3.1 convolution_convert_fusion.5
  428.7 4.5 %all-to-all-done.7 = bf16[8,24,3584]{2,1,0:T(8,128)(2,1)S(1)} async-done(((bf16[8,24,3584]{2,1,0:T(8,128)(2,1)}), bf16[8,24,3584]{2,1,0:T(8,128)(2,1)S(1)}, u32[]{:S(2)}, u32[]{:S(2)}) %all-to-all-start.7) | async-done | bytes 1376288 | tf_op jit(solution)/shard_map/all_to_all | solution.py:42
  (53 shorter events, 11.5 us)
Async XLA Ops:
  11.9 9.0 %copy-start.1 = (f32[128,8]{0,1:T(8,128)S(1)}, f32[128,8]{0,1:T(8,128)}, u32[]{:S(2)}) copy-start(f32[128,8]{0,1:T(8,128)} %param.8) | copy-start | bytes 12292
  14.4 8.2 %copy-start = (bf16[128,3584]{1,0:T(8,128)(2,1)S(1)}, bf16[128,3584]{1,0:T(8,128)(2,1)}, u32[]{:S(2)}) copy-start(bf16[128,3584]{1,0:T(8,128)(2,1)} %param.10) | copy-start | bytes 2752516
  14.4 40.2 %all-to-all-start = ((bf16[8,24,3584]{2,1,0:T(8,128)(2,1)}), bf16[8,24,3584]{2,1,0:T(8,128)(2,1)}, u32[]{:S(2)}, u32[]{:S(2)}) async-start(bf16[8,24,3584]{2,1,0:T(8,128)(2,1)} %bitcast.3), calls=%async_computation | async-start | bytes 2752512 | tf_op jit(solution)/shard_map/all_to_all | solution.py:30
  160.8 65.3 %all-to-all-start.5 = ((bf16[4,192,3584]{2,1,0:T(8,128)(2,1)}), bf16[4,192,3584]{2,1,0:T(8,128)(2,1)}, u32[]{:S(2)}, u32[]{:S(2)}) async-start(bf16[4,192,3584]{2,1,0:T(8,128)(2,1)} %tile.8), calls=%async_computation.5 | async-start | bytes 11010048 | tf_op jit(solution)/shard_map/all_to_all | solution.py:34
  165.9 6.2 %copy-start.4 = (bf16[1,3584,512]{2,1,0:T(8,128)(2,1)S(1)}, bf16[1,3584,512]{2,1,0:T(8,128)(2,1)}, u32[]{:S(2)}) copy-start(bf16[1,3584,512]{2,1,0:T(8,128)(2,1)} %param.12) | copy-start | bytes 11010052
  172.1 7.4 %copy-start.9 = (f32[768,512]{1,0:T(8,128)}, f32[768,512]{1,0:T(8,128)S(1)}, u32[]{:S(2)}) copy-start(f32[768,512]{1,0:T(8,128)S(1)} %fusion.11) | copy-start | bytes 4718596
  172.2 7.4 %copy-start.2 = (bf16[1,512,3584]{2,1,0:T(8,128)(2,1)S(1)}, bf16[1,512,3584]{2,1,0:T(8,128)(2,1)}, u32[]{:S(2)}) copy-start(bf16[1,512,3584]{2,1,0:T(8,128)(2,1)} %param.13) | copy-start | bytes 11010052
  179.6 4.8 %copy-start.6 = (bf16[768,512]{1,0:T(8,128)(2,1)}, bf16[768,512]{1,0:T(8,128)(2,1)S(1)}, u32[]{:S(2)}) copy-start(bf16[768,512]{1,0:T(8,128)(2,1)S(1)} %get-tuple-element.17) | copy-start | bytes 2359300
  226.1 66.0 %all-to-all-start.3 = ((bf16[4,192,3584]{2,1,0:T(8,128)(2,1)}), bf16[4,192,3584]{2,1,0:T(8,128)(2,1)}, u32[]{:S(2)}, u32[]{:S(2)}) async-start(bf16[4,192,3584]{2,1,0:T(8,128)(2,1)} %bitcast.81), calls=%async_computation.3 | async-start | bytes 11010048 | tf_op jit(solution)/shard_map/all_to_all | solution.py:38
  231.4 8.2 %copy-start.3 = (bf16[1,3584,512]{2,1,0:T(8,128)(2,1)S(1)}, bf16[1,3584,512]{2,1,0:T(8,128)(2,1)}, u32[]{:S(2)}) copy-start(bf16[1,3584,512]{2,1,0:T(8,128)(2,1)} %param.11) | copy-start | bytes 11010052
  239.6 5.8 %copy-start.8 = (bf16[768,512]{1,0:T(8,128)(2,1)}, bf16[768,512]{1,0:T(8,128)(2,1)S(1)}, u32[]{:S(2)}) copy-start(bf16[768,512]{1,0:T(8,128)(2,1)S(1)} %get-tuple-element.26) | copy-start | bytes 2359300
  239.6 5.8 %copy-start.5 = (bf16[1,3584,512]{2,1,0:T(8,128)(2,1)S(1)}, bf16[1,3584,512]{2,1,0:T(8,128)(2,1)}, u32[]{:S(2)}) copy-start(bf16[1,3584,512]{2,1,0:T(8,128)(2,1)} %param.12) | copy-start | bytes 11010052
  292.1 66.0 %all-to-all-start.6 = ((bf16[4,192,3584]{2,1,0:T(8,128)(2,1)}), bf16[4,192,3584]{2,1,0:T(8,128)(2,1)}, u32[]{:S(2)}, u32[]{:S(2)}) async-start(bf16[4,192,3584]{2,1,0:T(8,128)(2,1)} %bitcast.82), calls=%async_computation.6 | async-start | bytes 11010048 | tf_op jit(solution)/shard_map/all_to_all | solution.py:38
  358.1 37.9 %all-to-all-start.4 = ((bf16[8,24,3584]{2,1,0:T(8,128)(2,1)}), bf16[8,24,3584]{2,1,0:T(8,128)(2,1)}, u32[]{:S(2)}, u32[]{:S(2)}) async-start(bf16[8,24,3584]{2,1,0:T(8,128)(2,1)} %bitcast.12), calls=%async_computation.4 | async-start | bytes 2752512 | tf_op jit(solution)/shard_map/all_to_all | solution.py:42
  396.0 37.1 %all-to-all-start.7 = ((bf16[8,24,3584]{2,1,0:T(8,128)(2,1)}), bf16[8,24,3584]{2,1,0:T(8,128)(2,1)S(1)}, u32[]{:S(2)}, u32[]{:S(2)}) async-start(bf16[8,24,3584]{2,1,0:T(8,128)(2,1)} %bitcast.16), calls=%async_computation.7 | async-start | bytes 2752512 | tf_op jit(solution)/shard_map/all_to_all | solution.py:42
  407.5 7.2 %copy-start.7 = (bf16[768,512]{1,0:T(8,128)(2,1)S(1)}, bf16[768,512]{1,0:T(8,128)(2,1)}, u32[]{:S(2)}) copy-start(bf16[768,512]{1,0:T(8,128)(2,1)} %copy-done.6) | copy-start | bytes 2359300

commit v6 on v5

--- a/solution.py
+++ b/solution.py
@@ -30,15 +30,42 @@
     return lax.all_to_all(send_rows, "expert", split_axis=0, concat_axis=0, tiled=True)
 
 
+def pairs(groups, bit):
+    return [(g, g ^ bit) for g in range(groups)]
+
+
 def replicate_dp(rows, groups):
-    return lax.all_to_all(jnp.tile(rows, (groups, 1)), "dp", split_axis=0, concat_axis=0, tiled=True)
+    if groups != 4:
+        return lax.all_gather(rows, "dp", axis=0, tiled=True)
+    half = rows.shape[0] // 2
+    from_x = lax.ppermute(rows, "dp", perm=pairs(groups, 1))
+    from_y = lax.ppermute(rows, "dp", perm=pairs(groups, 2))
+    diag_lo = lax.ppermute(from_x[:half], "dp", perm=pairs(groups, 2))
+    diag_hi = lax.ppermute(from_y[half:], "dp", perm=pairs(groups, 1))
+    return jnp.concatenate([rows, from_x, from_y, diag_lo, diag_hi], axis=0)
+
+
+def reduce_dp(partial_rows, groups):
+    if groups != 4:
+        return lax.psum_scatter(partial_rows, "dp", scatter_dimension=0, tiled=True)
+    own, to_x, to_y, to_diag = jnp.split(partial_rows, 4, axis=0)
+    half = own.shape[0] // 2
+    via_x = lax.ppermute(to_diag[:half], "dp", perm=pairs(groups, 1))
+    via_y = lax.ppermute(to_diag[half:], "dp", perm=pairs(groups, 2))
+    to_y = jnp.concatenate(
+        [(to_y[:half].astype(jnp.float32) + via_x.astype(jnp.float32)).astype(jnp.bfloat16), to_y[half:]], 0
+    )
+    to_x = jnp.concatenate(
+        [to_x[:half], (to_x[half:].astype(jnp.float32) + via_y.astype(jnp.float32)).astype(jnp.bfloat16)], 0
+    )
+    from_x = lax.ppermute(to_x, "dp", perm=pairs(groups, 1))
+    from_y = lax.ppermute(to_y, "dp", perm=pairs(groups, 2))
+    total = own.astype(jnp.float32) + from_x.astype(jnp.float32) + from_y.astype(jnp.float32)
+    return total.astype(jnp.bfloat16)
 
 
 def gather_back(partial_rows, groups):
-    by_group = lax.all_to_all(partial_rows, "dp", split_axis=0, concat_axis=0, tiled=True)
-    rows = by_group.shape[0] // groups
-    summed = jnp.sum(by_group.astype(jnp.float32).reshape(groups, rows, -1), axis=0)
-    summed = summed.astype(jnp.bfloat16)
+    summed = reduce_dp(partial_rows, groups)
     return lax.all_to_all(summed, "expert", split_axis=0, concat_axis=0, tiled=True)
 
 

time: 435 us -> 332 us (0.76)
  blocking collectives: 102 us -> 0 us
  waiting for transfers between devices: 200 us -> 189 us
  starting transfers between devices: 30 us -> 38.9 us
  local copies, waits for them, and re-layouts: 19.6 us -> 27.5 us
  matrix products: 66.1 us -> 59.8 us
    ppermute x0 -> x16, waiting for transfers between devices: none -> 139 us  [the longest x2 46.7 us: replicate_dp(): from_y = lax.ppermute(rows, 'dp', perm=pairs(groups, 2))]
    all_to_all x3 -> x0, waiting for transfers between devices: 137 us -> none  [the longest x2 95.3 us: gather_back(): lax.all_to_all(partial_rows, 'dp', split_axis=0, concat_axis=0, tiled=True)]
    all_to_all x2 -> x0, blocking collectives: 102 us -> none  [the longest x1 65.6 us: replicate_dp(): lax.all_to_all(jnp.tile(rows, (groups, 1)), 'dp', split_axis=0, concat_ax...]
    ppermute x0 -> x16, starting transfers between devices: none -> 20.6 us  [the longest x2 3.63 us: replicate_dp(): diag_hi = lax.ppermute(from_y[half:], 'dp', perm=pairs(groups, 1))]
    all_to_all x3 -> x0, starting transfers between devices: 15.5 us -> none  [the longest x2 10.4 us: gather_back(): lax.all_to_all(partial_rows, 'dp', split_axis=0, concat_axis=0, tiled=True)]
    all_to_all x2, waiting for transfers between devices: 33.2 us -> 18.9 us  [gather_back(): lax.all_to_all(summed, 'expert', split_axis=0, concat_axis=0, tiled=True)]
    reduce_sum x2 -> x0, other arithmetic: 9.7 us -> none  [gather_back(): jnp.sum(by_group.astype(jnp.float32).reshape(groups, rows, -1), axis=0)]
    unnamed x23 -> x37, local copies, waits for them, and re-layouts: 1.6 us -> 10.4 us
  transfers between devices with their start and end apart: 6 -> 20, of which waited for: 6 -> 13; matrix products, arithmetic and copies ran while one was open for 19% -> 15% of each run, Pallas kernels for 0% -> 0%
where the time goes in v6:
time: 332 us; the launch traced here: 331 us
  waiting for transfers between devices  189 us (57%)
  matrix products  59.8 us (18%)
  starting transfers between devices  38.9 us (12%)
  local copies, waits for them, and re-layouts  27.5 us (8%)
  other arithmetic  15.2 us (5%)
    ppermute x2, waiting for transfers between devices, replicate_dp(): from_y = lax.ppermute(rows, 'dp', perm=pairs(groups, 2))  46.7 us
    ppermute x2, waiting for transfers between devices, reduce_dp(): from_y = lax.ppermute(to_y, 'dp', perm=pairs(groups, 2))  42.4 us
    all_to_all x2, waiting for transfers between devices, along_expert(): lax.all_to_all(send_rows, 'expert', split_axis=0, concat_axis=0, tiled=True)  30.5 us
    ppermute x2, waiting for transfers between devices, reduce_dp(): via_x = lax.ppermute(to_diag[:half], 'dp', perm=pairs(groups, 1))  28.2 us
    ppermute x2, waiting for transfers between devices, replicate_dp(): diag_lo = lax.ppermute(from_x[:half], 'dp', perm=pairs(groups, 2))  20.4 us
    dot_general x3, matrix products, contract_first(): lax.dot_general(left, right, (((0,), (0,)), ((), ())), preferred_element_...  19.6 us
    all_to_all x2, waiting for transfers between devices, gather_back(): lax.all_to_all(summed, 'expert', split_axis=0, concat_axis=0, tiled=True)  18.9 us
    dot_general x3, matrix products, contract_last(): lax.dot_general(left, right, (((1,), (1,)), ((), ())), preferred_element_...  18.9 us
  transfers between devices with their start and end apart: 20, of which 13 were waited for; matrix products, arithmetic and copies ran while one was open for 15% of the time, Pallas kernels for 0%

profile of v6, /device:TPU:0, one launch (start us, length us, event | category | flops | bytes accessed | tf_op | source)
XLA Modules:
  0.0 331.4 jit_solution(15299521763042145995)
XLA Ops:
  3.4 2.3 reduce-window.6
  6.3 4.3 %scatter_custom_fusion = s32[192]{0:T(256)S(1)} fusion(s32[1024]{0:T(1024)S(1)} %bitcast.81, s32[1024]{0:T(1024)S(1)} %iota.15, s32[]{:T(128)} %constant.15.clone.1), kind=kCustom, calls=%fused_computation.82 | custom fusion | bytes 772 | tf_op jit(solution)/shard_map/scatter | solution.py:14
  11.9 2.5 gather_fusion.1
  14.4 6.5 %all-to-all-start = ((bf16[8,24,3584]{2,1,0:T(8,128)(2,1)}), bf16[8,24,3584]{2,1,0:T(8,128)(2,1)}, u32[]{:S(2)}, u32[]{:S(2)}) async-start(bf16[8,24,3584]{2,1,0:T(8,128)(2,1)} %bitcast.3), calls=%async_computation | async-start | bytes 2752512 | tf_op jit(solution)/shard_map/all_to_all | solution.py:30
  24.1 30.5 %all-to-all-done = bf16[8,24,3584]{2,1,0:T(8,128)(2,1)} async-done(((bf16[8,24,3584]{2,1,0:T(8,128)(2,1)}), bf16[8,24,3584]{2,1,0:T(8,128)(2,1)}, u32[]{:S(2)}, u32[]{:S(2)}) %all-to-all-start) | async-done | bytes 1376288 | tf_op jit(solution)/shard_map/all_to_all | solution.py:30
  59.0 3.8 %all-to-all-start.1 = ((bf16[8,24,3584]{2,1,0:T(8,128)(2,1)}), bf16[8,24,3584]{2,1,0:T(8,128)(2,1)S(1)}, u32[]{:S(2)}, u32[]{:S(2)}) async-start(bf16[8,24,3584]{2,1,0:T(8,128)(2,1)} %fusion.13), calls=%async_computation.1 | async-start | bytes 2752512 | tf_op jit(solution)/shard_map/all_to_all | solution.py:30
  62.7 2.5 constant_dynamic-update-slice_fusion.4
  65.3 21.3 %collective-permute-done.1 = bf16[192,3584]{1,0:T(8,128)(2,1)} collective-permute-done((bf16[192,3584]{1,0:T(8,128)(2,1)}, bf16[192,3584]{1,0:T(8,128)(2,1)}, u32[]{:S(2)}, u32[]{:S(2)}) %collective-permute-start.1) | collective-permute-done | bytes 1376288 | tf_op jit(solution)/shard_map/ppermute | solution.py:42
  92.0 2.5 constant_dynamic-update-slice_fusion.3
  94.6 2.5 constant_dynamic-update-slice_fusion.2
  97.1 9.3 %collective-permute-done.2 = bf16[96,3584]{1,0:T(8,128)(2,1)S(1)} collective-permute-done((bf16[96,3584]{1,0:T(8,128)(2,1)S(1)}, bf16[96,3584]{1,0:T(8,128)(2,1)S(1)}, u32[]{:S(2)}, u32[]{:S(2)}) %collective-permute-start.2) | collective-permute-done | bytes 688160 | tf_op jit(solution)/shard_map/ppermute | solution.py:43
  108.2 6.2 %fusion.11 = f32[768,512]{1,0:T(8,128)S(1)} fusion(bf16[768,3584]{1,0:T(8,128)(2,1)} %constant_dynamic-update-slice_fusion, bf16[1,3584,512]{2,1,0:T(8,128)(2,1)} %param.11), kind=kOutput, calls=%fused_computation.23 | convolution fusion | flops 2818572288 | bytes 10747904 | tf_op jit(solution)/shard_map/dot_general | solution.py:92
  114.4 7.4 %multiply_convert_fusion.2 = (bf16[768,512]{1,0:T(8,128)(2,1)S(1)}, f32[768,512]{1,0:T(8,128)}) fusion(f32[768,512]{1,0:T(8,128)S(1)} %fusion.11, bf16[768,3584]{1,0:T(8,128)(2,1)} %constant_dynamic-update-slice_fusion, bf16[1,3584,512]{2,1,0:T(8,128)(2,1)S(1)} %copy-done.6), kind=kOutput, calls=%fused_computation.34 | convolution fusion | flops 2820931584 | bytes 13107200 | tf_op jit(solution)/shard_map/dot_general | solution.py:93
  121.8 3.2 convolution_convert_fusion
  129.5 14.2 %collective-permute-done.6 = bf16[96,3584]{1,0:T(8,128)(2,1)S(1)} collective-permute-done((bf16[96,3584]{1,0:T(8,128)(2,1)S(1)}, bf16[96,3584]{1,0:T(8,128)(2,1)S(1)}, u32[]{:S(2)}, u32[]{:S(2)}) %collective-permute-start.6) | collective-permute-done | bytes 688160 | tf_op jit(solution)/shard_map/ppermute | solution.py:53
  144.6 25.4 %collective-permute-done.9 = bf16[192,3584]{1,0:T(8,128)(2,1)S(1)} collective-permute-done((bf16[192,3584]{1,0:T(8,128)(2,1)S(1)}, bf16[192,3584]{1,0:T(8,128)(2,1)S(1)}, u32[]{:S(2)}, u32[]{:S(2)}) %collective-permute-start.9) | collective-permute-done | bytes 1376288 | tf_op jit(solution)/shard_map/ppermute | solution.py:42
  173.9 11.2 %collective-permute-done.10 = bf16[96,3584]{1,0:T(8,128)(2,1)S(1)} collective-permute-done((bf16[96,3584]{1,0:T(8,128)(2,1)S(1)}, bf16[96,3584]{1,0:T(8,128)(2,1)S(1)}, u32[]{:S(2)}, u32[]{:S(2)}) %collective-permute-start.10) | collective-permute-done | bytes 688160 | tf_op jit(solution)/shard_map/ppermute | solution.py:43
  185.2 6.2 %multiply_convert_fusion = (bf16[768,512]{1,0:T(8,128)(2,1)S(1)}, bf16[768,512]{1,0:T(8,128)(2,1)S(1)}) fusion(f32[768,512]{1,0:T(8,128)} %copy-done.10, f32[768,512]{1,0:T(8,128)} %get-tuple-element.15, bf16[768,3584]{1,0:T(8,128)(2,1)S(1)} %constant_dynamic-update-slice_fusion.5, bf16[1,512,3584]{2,1,0:T(8,128)(2,1)S(1)} %copy-done.4), kind=kOutput, calls=%fused_computation.31 | convolution fusion | flops 2823684096 | bytes 13893632 | tf_op jit(solution)/shard_map/dot_general | solution.py:18
  191.5 5.7 %fusion.9 = f32[768,3584]{1,0:T(8,128)} fusion(bf16[768,512]{1,0:T(8,128)(2,1)S(1)} %get-tuple-element.39, bf16[1,3584,512]{2,1,0:T(8,128)(2,1)S(1)} %copy-done.5), kind=kOutput, calls=%fused_computation.21 | convolution fusion | flops 2818572288 | bytes 15466496 | tf_op jit(solution)/shard_map/dot_general | solution.py:18
  197.2 7.0 %add_convert_fusion = bf16[768,3584]{1,0:T(8,128)(2,1)S(1)} fusion(f32[768,3584]{1,0:T(8,128)} %fusion.9, bf16[768,512]{1,0:T(8,128)(2,1)S(1)} %get-tuple-element.38, bf16[1,3584,512]{2,1,0:T(8,128)(2,1)} %param.12), kind=kOutput, calls=%fused_computation.5 | convolution fusion | flops 2824077312 | bytes 20971520 | tf_op jit(solution)/shard_map/dot_general | solution.py:18
  208.8 14.0 %collective-permute-done.14 = bf16[96,3584]{1,0:T(8,128)(2,1)S(1)} collective-permute-done((bf16[96,3584]{1,0:T(8,128)(2,1)S(1)}, bf16[96,3584]{1,0:T(8,128)(2,1)S(1)}, u32[]{:S(2)}, u32[]{:S(2)}) %collective-permute-start.14) | collective-permute-done | bytes 688160 | tf_op jit(solution)/shard_map/ppermute | solution.py:53
  229.0 24.4 %collective-permute-done.7 = bf16[192,3584]{1,0:T(8,128)(2,1)S(1)} collective-permute-done((bf16[192,3584]{1,0:T(8,128)(2,1)S(1)}, bf16[192,3584]{1,0:T(8,128)(2,1)S(1)}, u32[]{:S(2)}, u32[]{:S(2)}) %collective-permute-start.7) | collective-permute-done | bytes 1376288 | tf_op jit(solution)/shard_map/ppermute | solution.py:62
  255.0 4.3 %all-to-all-start.2 = ((bf16[8,24,3584]{2,1,0:T(8,128)(2,1)}), bf16[8,24,3584]{2,1,0:T(8,128)(2,1)}, u32[]{:S(2)}, u32[]{:S(2)}) async-start(bf16[8,24,3584]{2,1,0:T(8,128)(2,1)} %bitcast.10), calls=%async_computation.2 | async-start | bytes 2752512 | tf_op jit(solution)/shard_map/all_to_all | solution.py:69
  259.3 18.0 %collective-permute-done.15 = bf16[192,3584]{1,0:T(8,128)(2,1)S(1)} collective-permute-done((bf16[192,3584]{1,0:T(8,128)(2,1)}, bf16[192,3584]{1,0:T(8,128)(2,1)S(1)}, u32[]{:S(2)}, u32[]{:S(2)}) %collective-permute-start.15) | collective-permute-done | bytes 1376288 | tf_op jit(solution)/shard_map/ppermute | solution.py:62
  277.3 3.4 %add_convert_fusion.1 = bf16[192,3584]{1,0:T(8,128)(2,1)} fusion(bf16[192,3584]{1,0:T(8,128)(2,1)S(1)} %collective-permute-done.15, bf16[192,3584]{1,0:T(8,128)(2,1)} %collective-permute-done.13, bf16[768,3584]{1,0:T(8,128)(2,1)} %copy-done), kind=kLoop, calls=%fused_computation.29 | loop fusion | flops 4128768 | bytes 5505024 | tf_op jit(solution)/shard_map/convert_element_type | solution.py:64
  280.7 12.2 %all-to-all-done.2 = bf16[8,24,3584]{2,1,0:T(8,128)(2,1)} async-done(((bf16[8,24,3584]{2,1,0:T(8,128)(2,1)}), bf16[8,24,3584]{2,1,0:T(8,128)(2,1)}, u32[]{:S(2)}, u32[]{:S(2)}) %all-to-all-start.2) | async-done | bytes 1376288 | tf_op jit(solution)/shard_map/all_to_all | solution.py:69
  292.9 3.8 %all-to-all-start.3 = ((bf16[8,24,3584]{2,1,0:T(8,128)(2,1)}), bf16[8,24,3584]{2,1,0:T(8,128)(2,1)S(1)}, u32[]{:S(2)}, u32[]{:S(2)}) async-start(bf16[8,24,3584]{2,1,0:T(8,128)(2,1)} %bitcast.12), calls=%async_computation.3 | async-start | bytes 2752512 | tf_op jit(solution)/shard_map/all_to_all | solution.py:69
  296.7 7.8 %fusion.1 = bf16[1,3584,512]{2,1,0:T(8,128)(2,1)} fusion(bf16[768,3584]{1,0:T(8,128)(2,1)} %constant_dynamic-update-slice_fusion, bf16[768,512]{1,0:T(8,128)(2,1)} %copy-done.9), kind=kOutput, calls=%fused_computation.11 | convolution fusion | flops 2820407296 | bytes 9961472 | tf_op jit(solution)/shard_map/dot_general | solution.py:24
  304.5 7.3 %fusion = bf16[1,3584,512]{2,1,0:T(8,128)(2,1)} fusion(bf16[768,3584]{1,0:T(8,128)(2,1)} %constant_dynamic-update-slice_fusion, bf16[768,512]{1,0:T(8,128)(2,1)S(1)} %get-tuple-element.39), kind=kOutput, calls=%fused_computation.10 | convolution fusion | flops 2820407296 | bytes 9961472 | tf_op jit(solution)/shard_map/dot_general | solution.py:24
  311.8 4.5 %fusion.2 = bf16[1,512,3584]{2,1,0:T(8,128)(2,1)} fusion(bf16[768,512]{1,0:T(8,128)(2,1)S(1)} %copy-done.8, bf16[768,3584]{1,0:T(8,128)(2,1)S(1)} %bitcast.78), kind=kOutput, calls=%fused_computation.12 | convolution fusion | flops 2820407296 | bytes 9961472 | tf_op jit(solution)/shard_map/dot_general | solution.py:24
  320.2 3.1 convolution_convert_fusion.5
  323.3 6.7 %all-to-all-done.3 = bf16[8,24,3584]{2,1,0:T(8,128)(2,1)S(1)} async-done(((bf16[8,24,3584]{2,1,0:T(8,128)(2,1)}), bf16[8,24,3584]{2,1,0:T(8,128)(2,1)S(1)}, u32[]{:S(2)}, u32[]{:S(2)}) %all-to-all-start.3) | async-done | bytes 1376288 | tf_op jit(solution)/shard_map/all_to_all | solution.py:69
  (106 shorter events, 46.4 us)
Async XLA Ops:
  14.4 6.5 %copy-start.3 = (f32[128,8]{0,1:T(8,128)S(1)}, f32[128,8]{0,1:T(8,128)}, u32[]{:S(2)}) copy-start(f32[128,8]{0,1:T(8,128)} %param.8) | copy-start | bytes 12292
  14.4 8.2 %copy-start.1 = (bf16[128,3584]{1,0:T(8,128)(2,1)S(1)}, bf16[128,3584]{1,0:T(8,128)(2,1)}, u32[]{:S(2)}) copy-start(bf16[128,3584]{1,0:T(8,128)(2,1)} %param.10) | copy-start | bytes 2752516
  14.4 40.2 %all-to-all-start = ((bf16[8,24,3584]{2,1,0:T(8,128)(2,1)}), bf16[8,24,3584]{2,1,0:T(8,128)(2,1)}, u32[]{:S(2)}, u32[]{:S(2)}) async-start(bf16[8,24,3584]{2,1,0:T(8,128)(2,1)} %bitcast.3), calls=%async_computation | async-start | bytes 2752512 | tf_op jit(solution)/shard_map/all_to_all | solution.py:30
  54.6 32.0 %collective-permute-start.1 = (bf16[192,3584]{1,0:T(8,128)(2,1)}, bf16[192,3584]{1,0:T(8,128)(2,1)}, u32[]{:S(2)}, u32[]{:S(2)}) collective-permute-start(bf16[192,3584]{1,0:T(8,128)(2,1)} %bitcast.4), channel_id=1, source_target_pairs={{0,16},{8,24},{16,0},{24,8},{1,17},{9,25},{17,1},{25,9},{2,18},{10... | collective-permute-start | bytes 4128776 | tf_op jit(solution)/shard_map/ppermute | solution.py:42
  56.1 33.2 %collective-permute-start = (bf16[192,3584]{1,0:T(8,128)(2,1)}, bf16[192,3584]{1,0:T(8,128)(2,1)}, u32[]{:S(2)}, u32[]{:S(2)}) collective-permute-start(bf16[192,3584]{1,0:T(8,128)(2,1)} %bitcast.4), channel_id=1, source_target_pairs={{0,8},{8,0},{16,24},{24,16},{1,9},{9,1},{17,25},{25,17},{2,10},{10... | collective-permute-start | bytes 4128776 | tf_op jit(solution)/shard_map/ppermute | solution.py:41
  59.0 49.2 %all-to-all-start.1 = ((bf16[8,24,3584]{2,1,0:T(8,128)(2,1)}), bf16[8,24,3584]{2,1,0:T(8,128)(2,1)S(1)}, u32[]{:S(2)}, u32[]{:S(2)}) async-start(bf16[8,24,3584]{2,1,0:T(8,128)(2,1)} %fusion.13), calls=%async_computation.1 | async-start | bytes 2752512 | tf_op jit(solution)/shard_map/all_to_all | solution.py:30
  87.8 19.5 %collective-permute-start.3 = (bf16[96,3584]{1,0:T(8,128)(2,1)S(1)}, bf16[96,3584]{1,0:T(8,128)(2,1)S(1)}, u32[]{:S(2)}, u32[]{:S(2)}) collective-permute-start(bf16[96,3584]{1,0:T(8,128)(2,1)S(1)} %slice.96), channel_id=1, source_target_pairs={{0,8},{8,0},{16,24},{24,16},{1,9},{9,1},{17,25},{25,17},{2,10},{10... | collective-permute-start | bytes 2064392 | tf_op jit(solution)/shard_map/ppermute | solution.py:44
  90.5 15.9 %collective-permute-start.2 = (bf16[96,3584]{1,0:T(8,128)(2,1)S(1)}, bf16[96,3584]{1,0:T(8,128)(2,1)S(1)}, u32[]{:S(2)}, u32[]{:S(2)}) collective-permute-start(bf16[96,3584]{1,0:T(8,128)(2,1)S(1)} %slice.95), channel_id=1, source_target_pairs={{0,16},{8,24},{16,0},{24,8},{1,17},{9,25},{17,1},{25,9},{2,18},{10... | collective-permute-start | bytes 2064392 | tf_op jit(solution)/shard_map/ppermute | solution.py:43
  108.2 6.2 %copy-start.6 = (bf16[1,3584,512]{2,1,0:T(8,128)(2,1)S(1)}, bf16[1,3584,512]{2,1,0:T(8,128)(2,1)}, u32[]{:S(2)}) copy-start(bf16[1,3584,512]{2,1,0:T(8,128)(2,1)} %param.12) | copy-start | bytes 11010052
  114.4 7.4 %copy-start.10 = (f32[768,512]{1,0:T(8,128)}, f32[768,512]{1,0:T(8,128)S(1)}, u32[]{:S(2)}) copy-start(f32[768,512]{1,0:T(8,128)S(1)} %fusion.11) | copy-start | bytes 4718596
  114.4 7.4 %copy-start.4 = (bf16[1,512,3584]{2,1,0:T(8,128)(2,1)S(1)}, bf16[1,512,3584]{2,1,0:T(8,128)(2,1)}, u32[]{:S(2)}) copy-start(bf16[1,512,3584]{2,1,0:T(8,128)(2,1)} %param.13) | copy-start | bytes 11010052
  125.3 18.4 %collective-permute-start.6 = (bf16[96,3584]{1,0:T(8,128)(2,1)S(1)}, bf16[96,3584]{1,0:T(8,128)(2,1)S(1)}, u32[]{:S(2)}, u32[]{:S(2)}) collective-permute-start(bf16[96,3584]{1,0:T(8,128)(2,1)S(1)} %get-tuple-element.34), channel_id=1, source_target_pairs={{0,8},{8,0},{16,24},{24,16},{1,9},{9,1},{17,25},{25,17},{2,10},{10... | collective-permute-start | bytes 2064392 | tf_op jit(solution)/shard_map/ppermute | solution.py:53
  125.9 18.4 %collective-permute-start.4 = (bf16[96,3584]{1,0:T(8,128)(2,1)S(1)}, bf16[96,3584]{1,0:T(8,128)(2,1)S(1)}, u32[]{:S(2)}, u32[]{:S(2)}) collective-permute-start(bf16[96,3584]{1,0:T(8,128)(2,1)S(1)} %get-tuple-element.35), channel_id=1, source_target_pairs={{0,16},{8,24},{16,0},{24,8},{1,17},{9,25},{17,1},{25,9},{2,18},{10... | collective-permute-start | bytes 2064392 | tf_op jit(solution)/shard_map/ppermute | solution.py:54
  127.4 42.6 %collective-permute-start.9 = (bf16[192,3584]{1,0:T(8,128)(2,1)S(1)}, bf16[192,3584]{1,0:T(8,128)(2,1)S(1)}, u32[]{:S(2)}, u32[]{:S(2)}) collective-permute-start(bf16[192,3584]{1,0:T(8,128)(2,1)S(1)} %bitcast.73), channel_id=1, source_target_pairs={{0,16},{8,24},{16,0},{24,8},{1,17},{9,25},{17,1},{25,9},{2,18},{10... | collective-permute-start | bytes 4128776 | tf_op jit(solution)/shard_map/ppermute | solution.py:42
  127.9 44.2 %collective-permute-start.8 = (bf16[192,3584]{1,0:T(8,128)(2,1)S(1)}, bf16[192,3584]{1,0:T(8,128)(2,1)S(1)}, u32[]{:S(2)}, u32[]{:S(2)}) collective-permute-start(bf16[192,3584]{1,0:T(8,128)(2,1)S(1)} %bitcast.74), channel_id=1, source_target_pairs={{0,8},{8,0},{16,24},{24,16},{1,9},{9,1},{17,25},{25,17},{2,10},{10... | collective-permute-start | bytes 4128776 | tf_op jit(solution)/shard_map/ppermute | solution.py:41
  170.0 15.1 %collective-permute-start.11 = (bf16[96,3584]{1,0:T(8,128)(2,1)S(1)}, bf16[96,3584]{1,0:T(8,128)(2,1)S(1)}, u32[]{:S(2)}, u32[]{:S(2)}) collective-permute-start(bf16[96,3584]{1,0:T(8,128)(2,1)S(1)} %slice.98), channel_id=1, source_target_pairs={{0,8},{8,0},{16,24},{24,16},{1,9},{9,1},{17,25},{25,17},{2,10},{10... | collective-permute-start | bytes 2064392 | tf_op jit(solution)/shard_map/ppermute | solution.py:44
  172.2 12.9 %collective-permute-start.10 = (bf16[96,3584]{1,0:T(8,128)(2,1)S(1)}, bf16[96,3584]{1,0:T(8,128)(2,1)S(1)}, u32[]{:S(2)}, u32[]{:S(2)}) collective-permute-start(bf16[96,3584]{1,0:T(8,128)(2,1)S(1)} %slice.97), channel_id=1, source_target_pairs={{0,16},{8,24},{16,0},{24,8},{1,17},{9,25},{17,1},{25,9},{2,18},{10... | collective-permute-start | bytes 2064392 | tf_op jit(solution)/shard_map/ppermute | solution.py:43
  185.2 6.2 %copy-start.2 = (bf16[768,3584]{1,0:T(8,128)(2,1)}, bf16[768,3584]{1,0:T(8,128)(2,1)S(1)}, u32[]{:S(2)}) copy-start(bf16[768,3584]{1,0:T(8,128)(2,1)S(1)} %constant_dynamic-update-slice_fusion.5) | copy-start | bytes 16515076
  185.2 6.2 %copy-start.5 = (bf16[1,3584,512]{2,1,0:T(8,128)(2,1)S(1)}, bf16[1,3584,512]{2,1,0:T(8,128)(2,1)}, u32[]{:S(2)}) copy-start(bf16[1,3584,512]{2,1,0:T(8,128)(2,1)} %param.11) | copy-start | bytes 11010052
  191.5 5.8 %copy-start.9 = (bf16[768,512]{1,0:T(8,128)(2,1)}, bf16[768,512]{1,0:T(8,128)(2,1)S(1)}, u32[]{:S(2)}) copy-start(bf16[768,512]{1,0:T(8,128)(2,1)S(1)} %get-tuple-element.38) | copy-start | bytes 2359300
  204.2 19.7 %copy-start = (bf16[768,3584]{1,0:T(8,128)(2,1)}, bf16[768,3584]{1,0:T(8,128)(2,1)S(1)}, u32[]{:S(2)}) copy-start(bf16[768,3584]{1,0:T(8,128)(2,1)S(1)} %add_convert_fusion) | copy-start | bytes 16515076
  204.4 18.4 %collective-permute-start.14 = (bf16[96,3584]{1,0:T(8,128)(2,1)S(1)}, bf16[96,3584]{1,0:T(8,128)(2,1)S(1)}, u32[]{:S(2)}, u32[]{:S(2)}) collective-permute-start(bf16[96,3584]{1,0:T(8,128)(2,1)S(1)} %get-tuple-element.28), channel_id=1, source_target_pairs={{0,8},{8,0},{16,24},{24,16},{1,9},{9,1},{17,25},{25,17},{2,10},{10... | collective-permute-start | bytes 2064392 | tf_op jit(solution)/shard_map/ppermute | solution.py:53
  205.6 18.4 %collective-permute-start.12 = (bf16[96,3584]{1,0:T(8,128)(2,1)S(1)}, bf16[96,3584]{1,0:T(8,128)(2,1)S(1)}, u32[]{:S(2)}, u32[]{:S(2)}) collective-permute-start(bf16[96,3584]{1,0:T(8,128)(2,1)S(1)} %get-tuple-element.29), channel_id=1, source_target_pairs={{0,16},{8,24},{16,0},{24,8},{1,17},{9,25},{17,1},{25,9},{2,18},{10... | collective-permute-start | bytes 2064392 | tf_op jit(solution)/shard_map/ppermute | solution.py:54
  207.2 46.3 %collective-permute-start.7 = (bf16[192,3584]{1,0:T(8,128)(2,1)S(1)}, bf16[192,3584]{1,0:T(8,128)(2,1)S(1)}, u32[]{:S(2)}, u32[]{:S(2)}) collective-permute-start(bf16[192,3584]{1,0:T(8,128)(2,1)S(1)} %pad_maximum_fusion.1), channel_id=1, source_target_pairs={{0,16},{8,24},{16,0},{24,8},{1,17},{9,25},{17,1},{25,9},{2,18},{10... | collective-permute-start | bytes 4128776 | tf_op jit(solution)/shard_map/ppermute | solution.py:62
  207.9 45.6 %collective-permute-start.5 = (bf16[192,3584]{1,0:T(8,128)(2,1)S(1)}, bf16[192,3584]{1,0:T(8,128)(2,1)S(1)}, u32[]{:S(2)}, u32[]{:S(2)}) collective-permute-start(bf16[192,3584]{1,0:T(8,128)(2,1)S(1)} %pad_maximum_fusion), channel_id=1, source_target_pairs={{0,8},{8,0},{16,24},{24,16},{1,9},{9,1},{17,25},{25,17},{2,10},{10... | collective-permute-start | bytes 4128776 | tf_op jit(solution)/shard_map/ppermute | solution.py:61
  225.4 51.9 %collective-permute-start.15 = (bf16[192,3584]{1,0:T(8,128)(2,1)}, bf16[192,3584]{1,0:T(8,128)(2,1)S(1)}, u32[]{:S(2)}, u32[]{:S(2)}) collective-permute-start(bf16[192,3584]{1,0:T(8,128)(2,1)} %pad_maximum_fusion.3), channel_id=1, source_target_pairs={{0,16},{8,24},{16,0},{24,8},{1,17},{9,25},{17,1},{25,9},{2,18},{10... | collective-permute-start | bytes 4128776 | tf_op jit(solution)/shard_map/ppermute | solution.py:62
  228.1 49.2 %collective-permute-start.13 = (bf16[192,3584]{1,0:T(8,128)(2,1)}, bf16[192,3584]{1,0:T(8,128)(2,1)}, u32[]{:S(2)}, u32[]{:S(2)}) collective-permute-start(bf16[192,3584]{1,0:T(8,128)(2,1)} %pad_maximum_fusion.2), channel_id=1, source_target_pairs={{0,8},{8,0},{16,24},{24,16},{1,9},{9,1},{17,25},{25,17},{2,10},{10... | collective-permute-start | bytes 4128776 | tf_op jit(solution)/shard_map/ppermute | solution.py:61
  255.0 37.9 %all-to-all-start.2 = ((bf16[8,24,3584]{2,1,0:T(8,128)(2,1)}), bf16[8,24,3584]{2,1,0:T(8,128)(2,1)}, u32[]{:S(2)}, u32[]{:S(2)}) async-start(bf16[8,24,3584]{2,1,0:T(8,128)(2,1)} %bitcast.10), calls=%async_computation.2 | async-start | bytes 2752512 | tf_op jit(solution)/shard_map/all_to_all | solution.py:69
  292.9 37.1 %all-to-all-start.3 = ((bf16[8,24,3584]{2,1,0:T(8,128)(2,1)}), bf16[8,24,3584]{2,1,0:T(8,128)(2,1)S(1)}, u32[]{:S(2)}, u32[]{:S(2)}) async-start(bf16[8,24,3584]{2,1,0:T(8,128)(2,1)} %bitcast.12), calls=%async_computation.3 | async-start | bytes 2752512 | tf_op jit(solution)/shard_map/all_to_all | solution.py:69
  296.7 15.1 %slice-start = ((s8[5505024]{0:T(1024)(128)(4,1)}), s8[4194304]{0:T(1024)(128)(4,1)S(1)}, s32[]{:S(2)}) async-start(s8[5505024]{0:T(1024)(128)(4,1)} %bitcast.77), calls=%async_computation.4 | async-start | bytes 8388608
  304.5 7.3 %slice-start.1 = ((s8[5505024]{0:T(1024)(128)(4,1)}), s8[1310720]{0:T(1024)(128)(4,1)S(1)}, s32[]{:S(2)}) async-start(s8[5505024]{0:T(1024)(128)(4,1)} %bitcast.77), calls=%async_computation.5 | async-start | bytes 2621440
  304.5 7.3 %copy-start.8 = (bf16[768,512]{1,0:T(8,128)(2,1)S(1)}, bf16[768,512]{1,0:T(8,128)(2,1)}, u32[]{:S(2)}) copy-start(bf16[768,512]{1,0:T(8,128)(2,1)} %copy-done.7) | copy-start | bytes 2359300
  (1 other events, 3.3 us)

commit v7 on v6

--- a/solution.py
+++ b/solution.py
@@ -34,24 +34,46 @@
     return [(g, g ^ bit) for g in range(groups)]
 
 
-def replicate_dp(rows, groups):
+def swap_halves_first(rows, groups):
+    if groups != 4:
+        return ()
+    return (
+        lax.ppermute(rows, "dp", perm=pairs(groups, 1)),
+        lax.ppermute(rows, "dp", perm=pairs(groups, 2)),
+    )
+
+
+def swap_halves_second(rows, first, groups):
     if groups != 4:
         return lax.all_gather(rows, "dp", axis=0, tiled=True)
+    from_x, from_y = first
     half = rows.shape[0] // 2
-    from_x = lax.ppermute(rows, "dp", perm=pairs(groups, 1))
-    from_y = lax.ppermute(rows, "dp", perm=pairs(groups, 2))
     diag_lo = lax.ppermute(from_x[:half], "dp", perm=pairs(groups, 2))
     diag_hi = lax.ppermute(from_y[half:], "dp", perm=pairs(groups, 1))
     return jnp.concatenate([rows, from_x, from_y, diag_lo, diag_hi], axis=0)
 
 
-def reduce_dp(partial_rows, groups):
+def replicate_dp(rows, groups):
+    return swap_halves_second(rows, swap_halves_first(rows, groups), groups)
+
+
+def reduce_first(partial_rows, groups):
+    if groups != 4:
+        return ()
+    to_diag = jnp.split(partial_rows, 4, axis=0)[3]
+    half = to_diag.shape[0] // 2
+    return (
+        lax.ppermute(to_diag[:half], "dp", perm=pairs(groups, 1)),
+        lax.ppermute(to_diag[half:], "dp", perm=pairs(groups, 2)),
+    )
+
+
+def reduce_second(partial_rows, first, groups):
     if groups != 4:
         return lax.psum_scatter(partial_rows, "dp", scatter_dimension=0, tiled=True)
-    own, to_x, to_y, to_diag = jnp.split(partial_rows, 4, axis=0)
+    own, to_x, to_y, _ = jnp.split(partial_rows, 4, axis=0)
+    via_x, via_y = first
     half = own.shape[0] // 2
-    via_x = lax.ppermute(to_diag[:half], "dp", perm=pairs(groups, 1))
-    via_y = lax.ppermute(to_diag[half:], "dp", perm=pairs(groups, 2))
     to_y = jnp.concatenate(
         [(to_y[:half].astype(jnp.float32) + via_x.astype(jnp.float32)).astype(jnp.bfloat16), to_y[half:]], 0
     )
@@ -62,6 +84,10 @@
     from_y = lax.ppermute(to_y, "dp", perm=pairs(groups, 2))
     total = own.astype(jnp.float32) + from_x.astype(jnp.float32) + from_y.astype(jnp.float32)
     return total.astype(jnp.bfloat16)
+
+
+def reduce_dp(partial_rows, groups):
+    return reduce_second(partial_rows, reduce_first(partial_rows, groups), groups)
 
 
 def gather_back(partial_rows, groups):
@@ -85,7 +111,7 @@
     send_c = (prob_rows[:, None] * rows_dy.astype(jnp.float32)).astype(jnp.bfloat16)
     rows_x = replicate_dp(along_expert(send_x), groups)
     rows_x, c_along = lax.optimization_barrier((rows_x, along_expert(send_c)))
-    rows_c = replicate_dp(c_along, groups)
+    c_first = swap_halves_first(c_along, groups)
     gate_w = w_gate[0]
     up_w = w_up[0]
     down_w = w_down[0]
@@ -95,10 +121,15 @@
     activated = gate_pre * sigmoid_g
     hidden = (activated * up_pre).astype(jnp.bfloat16)
     part_out = jnp.dot(hidden, down_w, preferred_element_type=jnp.float32).astype(jnp.bfloat16)
-    part_out, hidden, gate_pre, up_pre = lax.optimization_barrier((part_out, hidden, gate_pre, up_pre))
+    part_out, hidden, gate_pre, up_pre, c_first = lax.optimization_barrier(
+        (part_out, hidden, gate_pre, up_pre, c_first)
+    )
     sigmoid_g = jax.nn.sigmoid(gate_pre)
     activated = gate_pre * sigmoid_g
-    out_rows = gather_back(part_out, groups).astype(jnp.float32)
+    out_first = reduce_first(part_out, groups)
+    rows_c = swap_halves_second(c_along, c_first, groups)
+    rows_c, out_first = lax.optimization_barrier((rows_c, out_first))
+    out_home = reduce_second(part_out, out_first, groups)
     grad_hidden = contract_last(rows_c, down_w)
     grad_upin = (grad_hidden * activated).astype(jnp.bfloat16)
     grad_gatein = (grad_hidden * up_pre * sigmoid_g * (1.0 + gate_pre * (1.0 - sigmoid_g))).astype(
@@ -107,6 +138,10 @@
     part_dx = (contract_last(grad_gatein, gate_w) + contract_last(grad_upin, up_w)).astype(
         jnp.bfloat16
     )
+    part_dx, grad_upin, grad_gatein, out_home = lax.optimization_barrier(
+        (part_dx, grad_upin, grad_gatein, out_home)
+    )
+    out_rows = along_expert(out_home).astype(jnp.float32)
     dx_rows = gather_back(part_dx, groups).astype(jnp.float32)
     new_gate = contract_first(rows_x, grad_gatein).astype(jnp.bfloat16)[None]
     new_up = contract_first(rows_x, grad_upin).astype(jnp.bfloat16)[None]

time: 332 us -> 300 us (0.904)
  waiting for transfers between devices: 189 us -> 153 us
    ppermute x16, waiting for transfers between devices: 139 us -> 102 us  [the longest x2 34.1 us: swap_halves_first(): lax.ppermute(rows, 'dp', perm=pairs(groups, 1))]
    all_to_all x2 -> x3, waiting for transfers between devices: 30.5 us -> 46 us  [along_expert(): lax.all_to_all(send_rows, 'expert', split_axis=0, concat_axis=0, tiled=True)]
    all_to_all x2 -> x1, waiting for transfers between devices: 18.9 us -> 4.5 us  [gather_back(): lax.all_to_all(summed, 'expert', split_axis=0, concat_axis=0, tiled=True)]
    all_to_all x2 -> x1, starting transfers between devices: 8.07 us -> 3.57 us  [gather_back(): lax.all_to_all(summed, 'expert', split_axis=0, concat_axis=0, tiled=True)]
    all_to_all x2 -> x3, starting transfers between devices: 10.2 us -> 14.5 us  [along_expert(): lax.all_to_all(send_rows, 'expert', split_axis=0, concat_axis=0, tiled=True)]
    unnamed x37 -> x29, local copies, waits for them, and re-layouts: 10.4 us -> 10.4 us
  transfers between devices with their start and end apart: 20 -> 20, of which waited for: 13 -> 17; matrix products, arithmetic and copies ran while one was open for 15% -> 28% of each run, Pallas kernels for 0% -> 0%
where the time goes in v7:
time: 300 us; the launch traced here: 299 us
  waiting for transfers between devices  153 us (51%)
  matrix products  59.7 us (20%)
  starting transfers between devices  41.7 us (14%)
  local copies, waits for them, and re-layouts  27.5 us (9%)
  other arithmetic  16.4 us (5%)
    all_to_all x3, waiting for transfers between devices, along_expert(): lax.all_to_all(send_rows, 'expert', split_axis=0, concat_axis=0, tiled=True)  46 us
    ppermute x2, waiting for transfers between devices, swap_halves_first(): lax.ppermute(rows, 'dp', perm=pairs(groups, 1))  34.1 us
    dot_general x3, matrix products, contract_first(): lax.dot_general(left, right, (((0,), (0,)), ((), ())), preferred_element_...  22 us
    ppermute x2, waiting for transfers between devices, swap_halves_second(): diag_lo = lax.ppermute(from_x[:half], 'dp', perm=pairs(groups, 2))  20.6 us
    ppermute x2, waiting for transfers between devices, reduce_second(): from_x = lax.ppermute(to_x, 'dp', perm=pairs(groups, 1))  19.9 us
    dot_general x3, matrix products, contract_last(): lax.dot_general(left, right, (((1,), (1,)), ((), ())), preferred_element_...  18.6 us
    all_to_all x3, starting transfers between devices, along_expert(): lax.all_to_all(send_rows, 'expert', split_axis=0, concat_axis=0, tiled=True)  14.5 us
    ppermute x2, waiting for transfers between devices, reduce_first(): lax.ppermute(to_diag[:half], 'dp', perm=pairs(groups, 1))  12 us
  transfers between devices with their start and end apart: 20, of which 17 were waited for; matrix products, arithmetic and copies ran while one was open for 28% of the time, Pallas kernels for 0%

profile of v7, /device:TPU:0, one launch (start us, length us, event | category | flops | bytes accessed | tf_op | source)
XLA Modules:
  0.0 299.1 jit_solution(10196500742145359462)
XLA Ops:
  6.3 4.3 %scatter_custom_fusion = s32[192]{0:T(256)S(1)} fusion(s32[1024]{0:T(1024)S(1)} %bitcast.77, s32[1024]{0:T(1024)S(1)} %iota.15, s32[]{:T(128)} %constant.15.clone.1), kind=kCustom, calls=%fused_computation.82 | custom fusion | bytes 772 | tf_op jit(solution)/shard_map/scatter | solution.py:14
  11.9 2.5 gather_fusion.1
  14.4 6.5 %all-to-all-start = ((bf16[8,24,3584]{2,1,0:T(8,128)(2,1)}), bf16[8,24,3584]{2,1,0:T(8,128)(2,1)}, u32[]{:S(2)}, u32[]{:S(2)}) async-start(bf16[8,24,3584]{2,1,0:T(8,128)(2,1)} %bitcast.3), calls=%async_computation | async-start | bytes 2752512 | tf_op jit(solution)/shard_map/all_to_all | solution.py:30
  24.1 30.5 %all-to-all-done = bf16[8,24,3584]{2,1,0:T(8,128)(2,1)} async-done(((bf16[8,24,3584]{2,1,0:T(8,128)(2,1)}), bf16[8,24,3584]{2,1,0:T(8,128)(2,1)}, u32[]{:S(2)}, u32[]{:S(2)}) %all-to-all-start) | async-done | bytes 1376288 | tf_op jit(solution)/shard_map/all_to_all | solution.py:30
  59.0 3.8 %all-to-all-start.1 = ((bf16[8,24,3584]{2,1,0:T(8,128)(2,1)}), bf16[8,24,3584]{2,1,0:T(8,128)(2,1)S(1)}, u32[]{:S(2)}, u32[]{:S(2)}) async-start(bf16[8,24,3584]{2,1,0:T(8,128)(2,1)} %fusion.13), calls=%async_computation.1 | async-start | bytes 2752512 | tf_op jit(solution)/shard_map/all_to_all | solution.py:30
  62.7 2.5 constant_dynamic-update-slice_fusion.4
  65.3 21.3 %collective-permute-done = bf16[192,3584]{1,0:T(8,128)(2,1)} collective-permute-done((bf16[192,3584]{1,0:T(8,128)(2,1)}, bf16[192,3584]{1,0:T(8,128)(2,1)}, u32[]{:S(2)}, u32[]{:S(2)}) %collective-permute-start) | collective-permute-done | bytes 1376288 | tf_op jit(solution)/shard_map/ppermute | solution.py:41
  92.0 2.5 constant_dynamic-update-slice_fusion.3
  94.6 2.5 constant_dynamic-update-slice_fusion.2
  97.1 6.8 %collective-permute-done.2 = bf16[96,3584]{1,0:T(8,128)(2,1)S(1)} collective-permute-done((bf16[96,3584]{1,0:T(8,128)(2,1)S(1)}, bf16[96,3584]{1,0:T(8,128)(2,1)S(1)}, u32[]{:S(2)}, u32[]{:S(2)}) %collective-permute-start.2) | collective-permute-done | bytes 688160 | tf_op jit(solution)/shard_map/ppermute | solution.py:51
  109.4 6.2 %fusion.11 = f32[768,512]{1,0:T(8,128)S(1)} fusion(bf16[768,3584]{1,0:T(8,128)(2,1)} %constant_dynamic-update-slice_fusion, bf16[1,3584,512]{2,1,0:T(8,128)(2,1)} %param.11), kind=kOutput, calls=%fused_computation.23 | convolution fusion | flops 2818572288 | bytes 10747904 | tf_op jit(solution)/shard_map/dot_general | solution.py:118
  115.6 5.2 %multiply_convert_fusion.2 = (bf16[768,512]{1,0:T(8,128)(2,1)S(1)}, f32[768,512]{1,0:T(8,128)S(1)}) fusion(f32[768,512]{1,0:T(8,128)S(1)} %fusion.11, bf16[768,3584]{1,0:T(8,128)(2,1)} %constant_dynamic-update-slice_fusion, bf16[1,3584,512]{2,1,0:T(8,128)(2,1)S(1)} %copy-done.6), kind=kOutput, calls=%fused_computation.34 | convolution fusion | flops 2820931584 | bytes 13107200 | tf_op jit(solution)/shard_map/dot_general | solution.py:119
  120.9 3.2 %convolution_convert_fusion = bf16[768,3584]{1,0:T(8,128)(2,1)S(1)} fusion(bf16[768,512]{1,0:T(8,128)(2,1)S(1)} %get-tuple-element.35, bf16[1,512,3584]{2,1,0:T(8,128)(2,1)S(1)} %copy-done.4), kind=kOutput, calls=%fused_computation.6 | convolution fusion | flops 2821324800 | bytes 9961472 | tf_op jit(solution)/shard_map/dot_general | solution.py:123
  124.1 12.8 %collective-permute-done.4 = bf16[192,3584]{1,0:T(8,128)(2,1)S(1)} collective-permute-done((bf16[192,3584]{1,0:T(8,128)(2,1)S(1)}, bf16[192,3584]{1,0:T(8,128)(2,1)S(1)}, u32[]{:S(2)}, u32[]{:S(2)}) %collective-permute-start.4) | collective-permute-done | bytes 1376288 | tf_op jit(solution)/shard_map/ppermute | solution.py:41
  143.7 13.7 %collective-permute-done.6 = bf16[96,3584]{1,0:T(8,128)(2,1)S(1)} collective-permute-done((bf16[96,3584]{1,0:T(8,128)(2,1)S(1)}, bf16[96,3584]{1,0:T(8,128)(2,1)S(1)}, u32[]{:S(2)}, u32[]{:S(2)}) %collective-permute-start.6) | collective-permute-done | bytes 688160 | tf_op jit(solution)/shard_map/ppermute | solution.py:51
  158.2 9.6 %collective-permute-done.8 = bf16[96,3584]{1,0:T(8,128)(2,1)S(1)} collective-permute-done((bf16[96,3584]{1,0:T(8,128)(2,1)S(1)}, bf16[96,3584]{1,0:T(8,128)(2,1)S(1)}, u32[]{:S(2)}, u32[]{:S(2)}) %collective-permute-start.8) | collective-permute-done | bytes 688160 | tf_op jit(solution)/shard_map/ppermute | solution.py:66
  172.5 4.4 %multiply_convert_fusion = (bf16[768,512]{1,0:T(8,128)(2,1)}, bf16[768,512]{1,0:T(8,128)(2,1)S(1)}) fusion(f32[768,512]{1,0:T(8,128)S(1)} %fusion.11, f32[768,512]{1,0:T(8,128)S(1)} %get-tuple-element.27, bf16[768,3584]{1,0:T(8,128)(2,1)S(1)} %constant_dynamic-update-slice_fusion.5, bf16[1,512,3584]{2,1,0:T(8,128)(2,1)S(1)} %copy-done.4), kind=kOutput, calls=%fused_computation.31 | convolution fusion | flops 2823684096 | bytes 13893632 | tf_op jit(solution)/shard_map/dot_general | solution.py:18
  176.9 5.7 %fusion.9 = f32[768,3584]{1,0:T(8,128)} fusion(bf16[768,512]{1,0:T(8,128)(2,1)S(1)} %get-tuple-element.33, bf16[1,3584,512]{2,1,0:T(8,128)(2,1)S(1)} %copy-done.5), kind=kOutput, calls=%fused_computation.21 | convolution fusion | flops 2818572288 | bytes 15466496 | tf_op jit(solution)/shard_map/dot_general | solution.py:18
  182.6 8.5 %add_convert_fusion = bf16[768,3584]{1,0:T(8,128)(2,1)S(1)} fusion(f32[768,3584]{1,0:T(8,128)} %fusion.9, bf16[768,512]{1,0:T(8,128)(2,1)} %get-tuple-element.34, bf16[1,3584,512]{2,1,0:T(8,128)(2,1)} %param.12), kind=kOutput, calls=%fused_computation.5 | convolution fusion | flops 2824077312 | bytes 20971520 | tf_op jit(solution)/shard_map/dot_general | solution.py:18
  191.1 5.4 %collective-permute-done.10 = bf16[192,3584]{1,0:T(8,128)(2,1)S(1)} collective-permute-done((bf16[192,3584]{1,0:T(8,128)(2,1)S(1)}, bf16[192,3584]{1,0:T(8,128)(2,1)S(1)}, u32[]{:S(2)}, u32[]{:S(2)}) %collective-permute-start.10) | collective-permute-done | bytes 1376288 | tf_op jit(solution)/shard_map/ppermute | solution.py:83
  203.1 9.5 %collective-permute-done.12 = bf16[96,3584]{1,0:T(8,128)(2,1)S(1)} collective-permute-done((bf16[96,3584]{1,0:T(8,128)(2,1)S(1)}, bf16[96,3584]{1,0:T(8,128)(2,1)S(1)}, u32[]{:S(2)}, u32[]{:S(2)}) %collective-permute-start.12) | collective-permute-done | bytes 688160 | tf_op jit(solution)/shard_map/ppermute | solution.py:67
  220.1 2.6 collective-permute-start.15
  222.7 4.3 %all-to-all-start.2 = ((bf16[8,24,3584]{2,1,0:T(8,128)(2,1)}), bf16[8,24,3584]{2,1,0:T(8,128)(2,1)}, u32[]{:S(2)}, u32[]{:S(2)}) async-start(bf16[8,24,3584]{2,1,0:T(8,128)(2,1)} %bitcast.10), calls=%async_computation.2 | async-start | bytes 2752512 | tf_op jit(solution)/shard_map/all_to_all | solution.py:30
  227.0 14.5 %collective-permute-done.13 = bf16[192,3584]{1,0:T(8,128)(2,1)S(1)} collective-permute-done((bf16[192,3584]{1,0:T(8,128)(2,1)}, bf16[192,3584]{1,0:T(8,128)(2,1)S(1)}, u32[]{:S(2)}, u32[]{:S(2)}) %collective-permute-start.13) | collective-permute-done | bytes 1376288 | tf_op jit(solution)/shard_map/ppermute | solution.py:83
  241.7 3.5 %add_convert_fusion.1 = bf16[192,3584]{1,0:T(8,128)(2,1)} fusion(bf16[192,3584]{1,0:T(8,128)(2,1)} %collective-permute-done.15, bf16[192,3584]{1,0:T(8,128)(2,1)S(1)} %collective-permute-done.13, bf16[768,3584]{1,0:T(8,128)(2,1)} %copy-done), kind=kLoop, calls=%fused_computation.29 | loop fusion | flops 4128768 | bytes 5505024 | tf_op jit(solution)/shard_map/convert_element_type | solution.py:86
  245.1 15.5 %all-to-all-done.2 = bf16[8,24,3584]{2,1,0:T(8,128)(2,1)} async-done(((bf16[8,24,3584]{2,1,0:T(8,128)(2,1)}), bf16[8,24,3584]{2,1,0:T(8,128)(2,1)}, u32[]{:S(2)}, u32[]{:S(2)}) %all-to-all-start.2) | async-done | bytes 1376288 | tf_op jit(solution)/shard_map/all_to_all | solution.py:30
  260.6 3.6 %all-to-all-start.3 = ((bf16[8,24,3584]{2,1,0:T(8,128)(2,1)}), bf16[8,24,3584]{2,1,0:T(8,128)(2,1)S(1)}, u32[]{:S(2)}, u32[]{:S(2)}) async-start(bf16[8,24,3584]{2,1,0:T(8,128)(2,1)} %bitcast.12), calls=%async_computation.3 | async-start | bytes 2752512 | tf_op jit(solution)/shard_map/all_to_all | solution.py:95
  264.2 7.8 %fusion.2 = bf16[1,512,3584]{2,1,0:T(8,128)(2,1)} fusion(bf16[768,512]{1,0:T(8,128)(2,1)} %copy-done.7, bf16[768,3584]{1,0:T(8,128)(2,1)} %copy-done.2), kind=kOutput, calls=%fused_computation.12 | convolution fusion | flops 2820407296 | bytes 9961472 | tf_op jit(solution)/shard_map/dot_general | solution.py:24
  272.0 7.1 %fusion.1 = bf16[1,3584,512]{2,1,0:T(8,128)(2,1)} fusion(bf16[768,3584]{1,0:T(8,128)(2,1)} %constant_dynamic-update-slice_fusion, bf16[768,512]{1,0:T(8,128)(2,1)S(1)} %copy-done.8), kind=kOutput, calls=%fused_computation.11 | convolution fusion | flops 2820407296 | bytes 9961472 | tf_op jit(solution)/shard_map/dot_general | solution.py:24
  279.1 7.1 %fusion = bf16[1,3584,512]{2,1,0:T(8,128)(2,1)} fusion(bf16[768,3584]{1,0:T(8,128)(2,1)} %constant_dynamic-update-slice_fusion, bf16[768,512]{1,0:T(8,128)(2,1)S(1)} %get-tuple-element.33), kind=kOutput, calls=%fused_computation.10 | convolution fusion | flops 2820407296 | bytes 9961472 | tf_op jit(solution)/shard_map/dot_general | solution.py:24
  290.1 3.1 %convolution_convert_fusion.5 = bf16[128,3584]{1,0:T(8,128)(2,1)} fusion(bf16[192,3584]{1,0:T(8,128)(2,1)} %bitcast.11, f32[192]{0:T(256)S(1)} %gather_fusion, s32[192]{0:T(256)S(1)} %get-tuple-element.43), kind=kOutput, calls=%fused_computation.14 | convolution fusion | flops 1057472512 | bytes 2295296 | tf_op jit(solution)/shard_map/dot_general | solution.py:152
  293.3 4.5 %all-to-all-done.3 = bf16[8,24,3584]{2,1,0:T(8,128)(2,1)S(1)} async-done(((bf16[8,24,3584]{2,1,0:T(8,128)(2,1)}), bf16[8,24,3584]{2,1,0:T(8,128)(2,1)S(1)}, u32[]{:S(2)}, u32[]{:S(2)}) %all-to-all-start.3) | async-done | bytes 1376288 | tf_op jit(solution)/shard_map/all_to_all | solution.py:95
  (97 shorter events, 57.1 us)
Async XLA Ops:
  14.4 6.5 %copy-start.1 = (bf16[128,3584]{1,0:T(8,128)(2,1)S(1)}, bf16[128,3584]{1,0:T(8,128)(2,1)}, u32[]{:S(2)}) copy-start(bf16[128,3584]{1,0:T(8,128)(2,1)} %param.10) | copy-start | bytes 2752516
  14.4 40.2 %all-to-all-start = ((bf16[8,24,3584]{2,1,0:T(8,128)(2,1)}), bf16[8,24,3584]{2,1,0:T(8,128)(2,1)}, u32[]{:S(2)}, u32[]{:S(2)}) async-start(bf16[8,24,3584]{2,1,0:T(8,128)(2,1)} %bitcast.3), calls=%async_computation | async-start | bytes 2752512 | tf_op jit(solution)/shard_map/all_to_all | solution.py:30
  20.9 1.4 copy-start.3
  54.6 32.0 %collective-permute-start = (bf16[192,3584]{1,0:T(8,128)(2,1)}, bf16[192,3584]{1,0:T(8,128)(2,1)}, u32[]{:S(2)}, u32[]{:S(2)}) collective-permute-start(bf16[192,3584]{1,0:T(8,128)(2,1)} %bitcast.4), channel_id=1, source_target_pairs={{0,8},{8,0},{16,24},{24,16},{1,9},{9,1},{17,25},{25,17},{2,10},{10... | collective-permute-start | bytes 4128776 | tf_op jit(solution)/shard_map/ppermute | solution.py:41
  56.1 33.3 %collective-permute-start.1 = (bf16[192,3584]{1,0:T(8,128)(2,1)}, bf16[192,3584]{1,0:T(8,128)(2,1)}, u32[]{:S(2)}, u32[]{:S(2)}) collective-permute-start(bf16[192,3584]{1,0:T(8,128)(2,1)} %bitcast.4), channel_id=1, source_target_pairs={{0,16},{8,24},{16,0},{24,8},{1,17},{9,25},{17,1},{25,9},{2,18},{10... | collective-permute-start | bytes 4128776 | tf_op jit(solution)/shard_map/ppermute | solution.py:42
  59.0 48.3 %all-to-all-start.1 = ((bf16[8,24,3584]{2,1,0:T(8,128)(2,1)}), bf16[8,24,3584]{2,1,0:T(8,128)(2,1)S(1)}, u32[]{:S(2)}, u32[]{:S(2)}) async-start(bf16[8,24,3584]{2,1,0:T(8,128)(2,1)} %fusion.13), calls=%async_computation.1 | async-start | bytes 2752512 | tf_op jit(solution)/shard_map/all_to_all | solution.py:30
  87.8 16.1 %collective-permute-start.2 = (bf16[96,3584]{1,0:T(8,128)(2,1)S(1)}, bf16[96,3584]{1,0:T(8,128)(2,1)S(1)}, u32[]{:S(2)}, u32[]{:S(2)}) collective-permute-start(bf16[96,3584]{1,0:T(8,128)(2,1)S(1)} %slice.95), channel_id=1, source_target_pairs={{0,16},{8,24},{16,0},{24,8},{1,17},{9,25},{17,1},{25,9},{2,18},{10... | collective-permute-start | bytes 2064392 | tf_op jit(solution)/shard_map/ppermute | solution.py:51
  90.5 15.9 %collective-permute-start.3 = (bf16[96,3584]{1,0:T(8,128)(2,1)S(1)}, bf16[96,3584]{1,0:T(8,128)(2,1)S(1)}, u32[]{:S(2)}, u32[]{:S(2)}) collective-permute-start(bf16[96,3584]{1,0:T(8,128)(2,1)S(1)} %slice.96), channel_id=1, source_target_pairs={{0,8},{8,0},{16,24},{24,16},{1,9},{9,1},{17,25},{25,17},{2,10},{10... | collective-permute-start | bytes 2064392 | tf_op jit(solution)/shard_map/ppermute | solution.py:52
  107.3 29.6 %collective-permute-start.4 = (bf16[192,3584]{1,0:T(8,128)(2,1)S(1)}, bf16[192,3584]{1,0:T(8,128)(2,1)S(1)}, u32[]{:S(2)}, u32[]{:S(2)}) collective-permute-start(bf16[192,3584]{1,0:T(8,128)(2,1)S(1)} %bitcast.71), channel_id=1, source_target_pairs={{0,8},{8,0},{16,24},{24,16},{1,9},{9,1},{17,25},{25,17},{2,10},{10... | collective-permute-start | bytes 4128776 | tf_op jit(solution)/shard_map/ppermute | solution.py:41
  108.8 30.2 %collective-permute-start.5 = (bf16[192,3584]{1,0:T(8,128)(2,1)S(1)}, bf16[192,3584]{1,0:T(8,128)(2,1)S(1)}, u32[]{:S(2)}, u32[]{:S(2)}) collective-permute-start(bf16[192,3584]{1,0:T(8,128)(2,1)S(1)} %bitcast.72), channel_id=1, source_target_pairs={{0,16},{8,24},{16,0},{24,8},{1,17},{9,25},{17,1},{25,9},{2,18},{10... | collective-permute-start | bytes 4128776 | tf_op jit(solution)/shard_map/ppermute | solution.py:42
  109.4 6.2 %copy-start.6 = (bf16[1,3584,512]{2,1,0:T(8,128)(2,1)S(1)}, bf16[1,3584,512]{2,1,0:T(8,128)(2,1)}, u32[]{:S(2)}) copy-start(bf16[1,3584,512]{2,1,0:T(8,128)(2,1)} %param.12) | copy-start | bytes 11010052
  115.6 5.3 %copy-start.4 = (bf16[1,512,3584]{2,1,0:T(8,128)(2,1)S(1)}, bf16[1,512,3584]{2,1,0:T(8,128)(2,1)}, u32[]{:S(2)}) copy-start(bf16[1,512,3584]{2,1,0:T(8,128)(2,1)} %param.13) | copy-start | bytes 11010052
  120.8 3.3 %copy-start.7 = (bf16[768,512]{1,0:T(8,128)(2,1)}, bf16[768,512]{1,0:T(8,128)(2,1)S(1)}, u32[]{:S(2)}) copy-start(bf16[768,512]{1,0:T(8,128)(2,1)S(1)} %get-tuple-element.35) | copy-start | bytes 2359300
  139.0 18.4 %collective-permute-start.6 = (bf16[96,3584]{1,0:T(8,128)(2,1)S(1)}, bf16[96,3584]{1,0:T(8,128)(2,1)S(1)}, u32[]{:S(2)}, u32[]{:S(2)}) collective-permute-start(bf16[96,3584]{1,0:T(8,128)(2,1)S(1)} %slice.73), channel_id=1, source_target_pairs={{0,16},{8,24},{16,0},{24,8},{1,17},{9,25},{17,1},{25,9},{2,18},{10... | collective-permute-start | bytes 2064392 | tf_op jit(solution)/shard_map/ppermute | solution.py:51
  139.7 18.4 %collective-permute-start.7 = (bf16[96,3584]{1,0:T(8,128)(2,1)S(1)}, bf16[96,3584]{1,0:T(8,128)(2,1)S(1)}, u32[]{:S(2)}, u32[]{:S(2)}) collective-permute-start(bf16[96,3584]{1,0:T(8,128)(2,1)S(1)} %slice.74), channel_id=1, source_target_pairs={{0,8},{8,0},{16,24},{24,16},{1,9},{9,1},{17,25},{25,17},{2,10},{10... | collective-permute-start | bytes 2064392 | tf_op jit(solution)/shard_map/ppermute | solution.py:52
  140.6 27.1 %collective-permute-start.8 = (bf16[96,3584]{1,0:T(8,128)(2,1)S(1)}, bf16[96,3584]{1,0:T(8,128)(2,1)S(1)}, u32[]{:S(2)}, u32[]{:S(2)}) collective-permute-start(bf16[96,3584]{1,0:T(8,128)(2,1)S(1)} %get-tuple-element.53), channel_id=1, source_target_pairs={{0,8},{8,0},{16,24},{24,16},{1,9},{9,1},{17,25},{25,17},{2,10},{10... | collective-permute-start | bytes 2064392 | tf_op jit(solution)/shard_map/ppermute | solution.py:66
  142.2 25.5 %collective-permute-start.9 = (bf16[96,3584]{1,0:T(8,128)(2,1)S(1)}, bf16[96,3584]{1,0:T(8,128)(2,1)S(1)}, u32[]{:S(2)}, u32[]{:S(2)}) collective-permute-start(bf16[96,3584]{1,0:T(8,128)(2,1)S(1)} %get-tuple-element.52), channel_id=1, source_target_pairs={{0,16},{8,24},{16,0},{24,8},{1,17},{9,25},{17,1},{25,9},{2,18},{10... | collective-permute-start | bytes 2064392 | tf_op jit(solution)/shard_map/ppermute | solution.py:67
  158.2 14.4 %copy-start.2 = (bf16[768,3584]{1,0:T(8,128)(2,1)}, bf16[768,3584]{1,0:T(8,128)(2,1)S(1)}, u32[]{:S(2)}) copy-start(bf16[768,3584]{1,0:T(8,128)(2,1)S(1)} %constant_dynamic-update-slice_fusion.5) | copy-start | bytes 16515076
  168.2 28.3 %collective-permute-start.10 = (bf16[192,3584]{1,0:T(8,128)(2,1)S(1)}, bf16[192,3584]{1,0:T(8,128)(2,1)S(1)}, u32[]{:S(2)}, u32[]{:S(2)}) collective-permute-start(bf16[192,3584]{1,0:T(8,128)(2,1)S(1)} %pad_maximum_fusion), channel_id=1, source_target_pairs={{0,8},{8,0},{16,24},{24,16},{1,9},{9,1},{17,25},{25,17},{2,10},{10... | collective-permute-start | bytes 4128776 | tf_op jit(solution)/shard_map/ppermute | solution.py:83
  170.6 6.2 %copy-start.5 = (bf16[1,3584,512]{2,1,0:T(8,128)(2,1)S(1)}, bf16[1,3584,512]{2,1,0:T(8,128)(2,1)}, u32[]{:S(2)}) copy-start(bf16[1,3584,512]{2,1,0:T(8,128)(2,1)} %param.11) | copy-start | bytes 11010052
  170.6 27.8 %collective-permute-start.11 = (bf16[192,3584]{1,0:T(8,128)(2,1)}, bf16[192,3584]{1,0:T(8,128)(2,1)S(1)}, u32[]{:S(2)}, u32[]{:S(2)}) collective-permute-start(bf16[192,3584]{1,0:T(8,128)(2,1)} %pad_maximum_fusion.1), channel_id=1, source_target_pairs={{0,16},{8,24},{16,0},{24,8},{1,17},{9,25},{17,1},{25,9},{2,18},{10... | collective-permute-start | bytes 4128776 | tf_op jit(solution)/shard_map/ppermute | solution.py:84
  191.1 23.9 %copy-start = (bf16[768,3584]{1,0:T(8,128)(2,1)}, bf16[768,3584]{1,0:T(8,128)(2,1)S(1)}, u32[]{:S(2)}) copy-start(bf16[768,3584]{1,0:T(8,128)(2,1)S(1)} %add_convert_fusion) | copy-start | bytes 16515076
  200.2 12.4 %collective-permute-start.12 = (bf16[96,3584]{1,0:T(8,128)(2,1)S(1)}, bf16[96,3584]{1,0:T(8,128)(2,1)S(1)}, u32[]{:S(2)}, u32[]{:S(2)}) collective-permute-start(bf16[96,3584]{1,0:T(8,128)(2,1)S(1)} %get-tuple-element.47), channel_id=1, source_target_pairs={{0,16},{8,24},{16,0},{24,8},{1,17},{9,25},{17,1},{25,9},{2,18},{10... | collective-permute-start | bytes 2064392 | tf_op jit(solution)/shard_map/ppermute | solution.py:67
  200.7 14.2 %collective-permute-start.14 = (bf16[96,3584]{1,0:T(8,128)(2,1)S(1)}, bf16[96,3584]{1,0:T(8,128)(2,1)S(1)}, u32[]{:S(2)}, u32[]{:S(2)}) collective-permute-start(bf16[96,3584]{1,0:T(8,128)(2,1)S(1)} %get-tuple-element.46), channel_id=1, source_target_pairs={{0,8},{8,0},{16,24},{24,16},{1,9},{9,1},{17,25},{25,17},{2,10},{10... | collective-permute-start | bytes 2064392 | tf_op jit(solution)/shard_map/ppermute | solution.py:66
  216.5 25.1 %collective-permute-start.13 = (bf16[192,3584]{1,0:T(8,128)(2,1)}, bf16[192,3584]{1,0:T(8,128)(2,1)S(1)}, u32[]{:S(2)}, u32[]{:S(2)}) collective-permute-start(bf16[192,3584]{1,0:T(8,128)(2,1)} %pad_maximum_fusion.2), channel_id=1, source_target_pairs={{0,8},{8,0},{16,24},{24,16},{1,9},{9,1},{17,25},{25,17},{2,10},{10... | collective-permute-start | bytes 4128776 | tf_op jit(solution)/shard_map/ppermute | solution.py:83
  220.1 21.5 %collective-permute-start.15 = (bf16[192,3584]{1,0:T(8,128)(2,1)}, bf16[192,3584]{1,0:T(8,128)(2,1)}, u32[]{:S(2)}, u32[]{:S(2)}) collective-permute-start(bf16[192,3584]{1,0:T(8,128)(2,1)} %pad_maximum_fusion.3), channel_id=1, source_target_pairs={{0,16},{8,24},{16,0},{24,8},{1,17},{9,25},{17,1},{25,9},{2,18},{10... | collective-permute-start | bytes 4128776 | tf_op jit(solution)/shard_map/ppermute | solution.py:84
  222.7 37.9 %all-to-all-start.2 = ((bf16[8,24,3584]{2,1,0:T(8,128)(2,1)}), bf16[8,24,3584]{2,1,0:T(8,128)(2,1)}, u32[]{:S(2)}, u32[]{:S(2)}) async-start(bf16[8,24,3584]{2,1,0:T(8,128)(2,1)} %bitcast.10), calls=%async_computation.2 | async-start | bytes 2752512 | tf_op jit(solution)/shard_map/all_to_all | solution.py:30
  260.6 37.1 %all-to-all-start.3 = ((bf16[8,24,3584]{2,1,0:T(8,128)(2,1)}), bf16[8,24,3584]{2,1,0:T(8,128)(2,1)S(1)}, u32[]{:S(2)}, u32[]{:S(2)}) async-start(bf16[8,24,3584]{2,1,0:T(8,128)(2,1)} %bitcast.12), calls=%async_computation.3 | async-start | bytes 2752512 | tf_op jit(solution)/shard_map/all_to_all | solution.py:95
  264.2 7.8 %copy-start.8 = (bf16[768,512]{1,0:T(8,128)(2,1)S(1)}, bf16[768,512]{1,0:T(8,128)(2,1)}, u32[]{:S(2)}) copy-start(bf16[768,512]{1,0:T(8,128)(2,1)} %get-tuple-element.34) | copy-start | bytes 2359300

commit v8 on v7

--- a/solution.py
+++ b/solution.py
@@ -4,14 +4,12 @@
 from jax.sharding import PartitionSpec as P
 
 
-def slot_table(flat_ids, experts, capacity, sentinel):
+def slot_selection(flat_ids, experts, capacity):
     matches = (flat_ids[:, None] == jnp.arange(experts, dtype=jnp.int32)[None, :]).astype(jnp.int32)
     earlier = jnp.cumsum(matches, axis=0) - matches
     slot_pos = jnp.sum(earlier * matches, axis=1)
-    target = jnp.where(flat_ids < experts, flat_ids * capacity + slot_pos, experts * capacity)
-    flat_index = jnp.arange(flat_ids.shape[0], dtype=jnp.int32)
-    blank_table = jnp.full((experts * capacity,), sentinel, jnp.int32)
-    return blank_table.at[target].set(flat_index, mode="drop")
+    target = jnp.where(flat_ids < experts, flat_ids * capacity + slot_pos, -1)
+    return target[:, None] == jnp.arange(experts * capacity, dtype=jnp.int32)[None, :]
 
 
 def contract_last(left, right):
@@ -101,13 +99,11 @@
     experts = lax.axis_size("expert")
     groups = lax.axis_size("dp")
     capacity = 3 * tok_count * top_k // (16 * experts)
-    flat_count = tok_count * top_k
-    slots = slot_table(expert_ids.reshape(-1), experts, capacity, flat_count)
-    token_of = slots // top_k
-    zero_row = jnp.zeros((1, model_width), jnp.bfloat16)
-    send_x = jnp.concatenate([tokens, zero_row], 0)[token_of]
-    rows_dy = jnp.concatenate([cotangent, zero_row], 0)[token_of]
-    prob_rows = jnp.concatenate([gate_probs.reshape(-1), jnp.zeros((1,), jnp.float32)], 0)[slots]
+    chosen = slot_selection(expert_ids.reshape(-1), experts, capacity)
+    owner = jnp.any(chosen.reshape(tok_count, top_k, -1), axis=1).astype(jnp.bfloat16)
+    send_x = contract_first(owner, tokens).astype(jnp.bfloat16)
+    rows_dy = contract_first(owner, cotangent).astype(jnp.bfloat16)
+    prob_rows = jnp.sum(jnp.where(chosen, gate_probs.reshape(-1)[:, None], 0.0), axis=0)
     send_c = (prob_rows[:, None] * rows_dy.astype(jnp.float32)).astype(jnp.bfloat16)
     rows_x = replicate_dp(along_expert(send_x), groups)
     rows_x, c_along = lax.optimization_barrier((rows_x, along_expert(send_c)))
@@ -142,29 +138,19 @@
         (part_dx, grad_upin, grad_gatein, out_home)
     )
     out_rows = along_expert(out_home).astype(jnp.float32)
-    dx_rows = gather_back(part_dx, groups).astype(jnp.float32)
+    dx_rows = gather_back(part_dx, groups)
     new_gate = contract_first(rows_x, grad_gatein).astype(jnp.bfloat16)[None]
     new_up = contract_first(rows_x, grad_upin).astype(jnp.bfloat16)[None]
     new_down = contract_first(hidden, rows_c).astype(jnp.bfloat16)[None]
-    owner = (token_of[None, :] == jnp.arange(tok_count, dtype=jnp.int32)[:, None]).astype(
-        jnp.float32
-    )
     layer_out = jnp.dot(
-        owner * prob_rows[None, :],
+        owner.astype(jnp.float32) * prob_rows[None, :],
         out_rows,
         precision=lax.Precision.HIGHEST,
         preferred_element_type=jnp.float32,
     ).astype(jnp.bfloat16)
-    grad_tokens = jnp.dot(
-        owner, dx_rows, precision=lax.Precision.HIGHEST, preferred_element_type=jnp.float32
-    ).astype(jnp.bfloat16)
+    grad_tokens = jnp.dot(owner, dx_rows, preferred_element_type=jnp.float32).astype(jnp.bfloat16)
     score_rows = jnp.sum(rows_dy.astype(jnp.float32) * out_rows, axis=1)
-    grad_probs = (
-        jnp.zeros((flat_count + 1,), jnp.float32)
-        .at[slots]
-        .set(score_rows)[:flat_count]
-        .reshape(tok_count, top_k)
-    )
+    grad_probs = jnp.sum(jnp.where(chosen, score_rows[None, :], 0.0), axis=1).reshape(tok_count, top_k)
     return (layer_out, grad_tokens, grad_probs, new_gate, new_up, new_down)
 
 

time: 300 us -> 290 us (0.967)
  blocking collectives: 0 us -> 39.8 us
  waiting for transfers between devices: 153 us -> 125 us
  local copies, waits for them, and re-layouts: 27.5 us -> 15 us
  starting transfers between devices: 41.7 us -> 30.5 us
  matrix products: 59.7 us -> 65.9 us
  other arithmetic: 16.4 us -> 12.6 us
    all_to_all x0 -> x1, blocking collectives: none -> 39.8 us  [along_expert(): lax.all_to_all(send_rows, 'expert', split_axis=0, concat_axis=0, tiled=True)]
    all_to_all x3 -> x2, waiting for transfers between devices: 46 us -> 10.5 us  [along_expert(): lax.all_to_all(send_rows, 'expert', split_axis=0, concat_axis=0, tiled=True)]
    all_to_all x3 -> x2, starting transfers between devices: 14.5 us -> 7.24 us  [along_expert(): lax.all_to_all(send_rows, 'expert', split_axis=0, concat_axis=0, tiled=True)]
    scatter x2 -> x0, local copies, waits for them, and re-layouts: 5.51 us -> none  [the longest x1 4.3 us: slot_table(): return blank_table.at[target].set(flat_index, mode='drop')]
    ppermute x2, waiting for transfers between devices: 19.9 us -> 25.3 us  [reduce_second(): from_x = lax.ppermute(to_x, 'dp', perm=pairs(groups, 1))]
    gather x3 -> x0, local copies, waits for them, and re-layouts: 5.37 us -> none  [the longest x1 2.51 us: on_device(): send_x = jnp.concatenate([tokens, zero_row], 0)[token_of]]
    all_to_all x1, waiting for transfers between devices: 4.5 us -> 8.8 us  [gather_back(): lax.all_to_all(summed, 'expert', split_axis=0, concat_axis=0, tiled=True)]
    dot_general x3 -> x5, matrix products: 22 us -> 25.7 us  [contract_first(): lax.dot_general(left, right, (((0,), (0,)), ((), ())), preferred_element_...]
  transfers between devices with their start and end apart: 20 -> 19, of which waited for: 17 -> 17; matrix products, arithmetic and copies ran while one was open for 28% -> 28% of each run, Pallas kernels for 0% -> 0%
where the time goes in v8:
time: 290 us; the launch traced here: 289 us
  waiting for transfers between devices  125 us (43%)
  matrix products  65.9 us (23%)
  blocking collectives  39.8 us (14%)
  starting transfers between devices  30.5 us (11%)
  local copies, waits for them, and re-layouts  15 us (5%)
  other arithmetic  12.6 us (4%)
    all_to_all x1, blocking collectives, along_expert(): lax.all_to_all(send_rows, 'expert', split_axis=0, concat_axis=0, tiled=True)  39.8 us
    ppermute x2, waiting for transfers between devices, swap_halves_first(): lax.ppermute(rows, 'dp', perm=pairs(groups, 1))  30.9 us
    dot_general x5, matrix products, contract_first(): lax.dot_general(left, right, (((0,), (0,)), ((), ())), preferred_element_...  25.7 us
    ppermute x2, waiting for transfers between devices, reduce_second(): from_x = lax.ppermute(to_x, 'dp', perm=pairs(groups, 1))  25.3 us
    ppermute x2, waiting for transfers between devices, swap_halves_second(): diag_lo = lax.ppermute(from_x[:half], 'dp', perm=pairs(groups, 2))  20.7 us
    dot_general x3, matrix products, contract_last(): lax.dot_general(left, right, (((1,), (1,)), ((), ())), preferred_element_...  18.6 us
    ppermute x2, waiting for transfers between devices, reduce_first(): lax.ppermute(to_diag[half:], 'dp', perm=pairs(groups, 2))  11.7 us
    ppermute x2, waiting for transfers between devices, reduce_first(): lax.ppermute(to_diag[:half], 'dp', perm=pairs(groups, 1))  10.7 us
  transfers between devices with their start and end apart: 19, of which 17 were waited for; matrix products, arithmetic and copies ran while one was open for 28% of the time, Pallas kernels for 0%

profile of v8, /device:TPU:0, one launch (start us, length us, event | category | flops | bytes accessed | tf_op | source)
XLA Modules:
  0.0 289.2 jit_solution(1376235701750989313)
XLA Ops:
  1.7 2.3 reduce-window.6
  7.2 39.8 %all_to_all.48 = bf16[8,24,3584]{2,1,0:T(8,128)(2,1)} all-to-all(bf16[8,24,3584]{2,1,0:T(8,128)(2,1)S(1)} %bitcast.79), channel_id=1, replica_groups=mesh['dp'=4,'expert'=8] {'expert'}, dimensions={0} | all-to-all | bytes 2752512 | tf_op jit(solution)/shard_map/all_to_all | solution.py:28
  50.4 2.5 multiply_convert_fusion
  52.9 3.6 %all-to-all-start.1 = ((bf16[8,24,3584]{2,1,0:T(8,128)(2,1)}), bf16[8,24,3584]{2,1,0:T(8,128)(2,1)S(1)}, u32[]{:S(2)}, u32[]{:S(2)}) async-start(bf16[8,24,3584]{2,1,0:T(8,128)(2,1)} %bitcast.77), calls=%async_computation.1 | async-start | bytes 2752512 | tf_op jit(solution)/shard_map/all_to_all | solution.py:28
  56.5 2.5 constant_dynamic-update-slice_fusion.4
  59.1 20.2 %collective-permute-done = bf16[192,3584]{1,0:T(8,128)(2,1)} collective-permute-done((bf16[192,3584]{1,0:T(8,128)(2,1)}, bf16[192,3584]{1,0:T(8,128)(2,1)}, u32[]{:S(2)}, u32[]{:S(2)}) %collective-permute-start) | collective-permute-done | bytes 1376288 | tf_op jit(solution)/shard_map/ppermute | solution.py:39
  84.7 2.5 constant_dynamic-update-slice_fusion.3
  87.2 2.5 constant_dynamic-update-slice_fusion.2
  89.7 7.0 %collective-permute-done.2 = bf16[96,3584]{1,0:T(8,128)(2,1)S(1)} collective-permute-done((bf16[96,3584]{1,0:T(8,128)(2,1)S(1)}, bf16[96,3584]{1,0:T(8,128)(2,1)S(1)}, u32[]{:S(2)}, u32[]{:S(2)}) %collective-permute-start.2) | collective-permute-done | bytes 688160 | tf_op jit(solution)/shard_map/ppermute | solution.py:49
  102.1 6.2 %fusion.12 = f32[768,512]{1,0:T(8,128)S(1)} fusion(bf16[768,3584]{1,0:T(8,128)(2,1)} %constant_dynamic-update-slice_fusion, bf16[1,3584,512]{2,1,0:T(8,128)(2,1)} %param.11), kind=kOutput, calls=%fused_computation.21 | convolution fusion | flops 2818572288 | bytes 10747904 | tf_op jit(solution)/shard_map/dot_general | solution.py:114
  108.4 7.4 %multiply_convert_fusion.3 = (bf16[768,512]{1,0:T(8,128)(2,1)S(1)}, f32[768,512]{1,0:T(8,128)}) fusion(f32[768,512]{1,0:T(8,128)S(1)} %fusion.12, bf16[768,3584]{1,0:T(8,128)(2,1)} %constant_dynamic-update-slice_fusion, bf16[1,3584,512]{2,1,0:T(8,128)(2,1)S(1)} %copy-done.8), kind=kOutput, calls=%fused_computation.30 | convolution fusion | flops 2820931584 | bytes 13107200 | tf_op jit(solution)/shard_map/dot_general | solution.py:115
  115.8 3.2 %convolution_convert_fusion = bf16[768,3584]{1,0:T(8,128)(2,1)S(1)} fusion(bf16[768,512]{1,0:T(8,128)(2,1)S(1)} %get-tuple-element.35, bf16[1,512,3584]{2,1,0:T(8,128)(2,1)S(1)} %copy-done.6), kind=kOutput, calls=%fused_computation.1 | convolution fusion | flops 2821324800 | bytes 9961472 | tf_op jit(solution)/shard_map/dot_general | solution.py:119
  119.1 10.7 %collective-permute-done.4 = bf16[192,3584]{1,0:T(8,128)(2,1)S(1)} collective-permute-done((bf16[192,3584]{1,0:T(8,128)(2,1)S(1)}, bf16[192,3584]{1,0:T(8,128)(2,1)S(1)}, u32[]{:S(2)}, u32[]{:S(2)}) %collective-permute-start.4) | collective-permute-done | bytes 1376288 | tf_op jit(solution)/shard_map/ppermute | solution.py:39
  136.5 13.7 %collective-permute-done.6 = bf16[96,3584]{1,0:T(8,128)(2,1)S(1)} collective-permute-done((bf16[96,3584]{1,0:T(8,128)(2,1)S(1)}, bf16[96,3584]{1,0:T(8,128)(2,1)S(1)}, u32[]{:S(2)}, u32[]{:S(2)}) %collective-permute-start.6) | collective-permute-done | bytes 688160 | tf_op jit(solution)/shard_map/ppermute | solution.py:49
  150.9 9.8 %collective-permute-done.8 = bf16[96,3584]{1,0:T(8,128)(2,1)S(1)} collective-permute-done((bf16[96,3584]{1,0:T(8,128)(2,1)S(1)}, bf16[96,3584]{1,0:T(8,128)(2,1)S(1)}, u32[]{:S(2)}, u32[]{:S(2)}) %collective-permute-start.8) | collective-permute-done | bytes 688160 | tf_op jit(solution)/shard_map/ppermute | solution.py:64
  162.3 2.2 collective-permute-start.11
  164.6 4.4 %multiply_convert_fusion.1 = (bf16[768,512]{1,0:T(8,128)(2,1)}, bf16[768,512]{1,0:T(8,128)(2,1)S(1)}) fusion(f32[768,512]{1,0:T(8,128)S(1)} %copy-done.15, f32[768,512]{1,0:T(8,128)S(1)} %copy-done.16, bf16[768,3584]{1,0:T(8,128)(2,1)S(1)} %constant_dynamic-update-slice_fusion.5, bf16[1,512,3584]{2,1,0:T(8,128)(2,1)S(1)} %copy-done.6), kind=kOutput, calls=%fused_computation.27 | convolution fusion | flops 2823684096 | bytes 13893632 | tf_op jit(solution)/shard_map/dot_general | solution.py:16
  169.0 5.7 %fusion.10 = f32[768,3584]{1,0:T(8,128)} fusion(bf16[768,512]{1,0:T(8,128)(2,1)S(1)} %get-tuple-element.33, bf16[1,3584,512]{2,1,0:T(8,128)(2,1)S(1)} %copy-done.7), kind=kOutput, calls=%fused_computation.19 | convolution fusion | flops 2818572288 | bytes 15466496 | tf_op jit(solution)/shard_map/dot_general | solution.py:16
  174.7 8.5 %add_convert_fusion = bf16[768,3584]{1,0:T(8,128)(2,1)S(1)} fusion(f32[768,3584]{1,0:T(8,128)} %fusion.10, bf16[768,512]{1,0:T(8,128)(2,1)} %get-tuple-element.34, bf16[1,3584,512]{2,1,0:T(8,128)(2,1)} %param.12), kind=kOutput, calls=%fused_computation | convolution fusion | flops 2824077312 | bytes 20971520 | tf_op jit(solution)/shard_map/dot_general | solution.py:16
  183.2 6.3 %collective-permute-done.10 = bf16[192,3584]{1,0:T(8,128)(2,1)S(1)} collective-permute-done((bf16[192,3584]{1,0:T(8,128)(2,1)S(1)}, bf16[192,3584]{1,0:T(8,128)(2,1)S(1)}, u32[]{:S(2)}, u32[]{:S(2)}) %collective-permute-start.10) | collective-permute-done | bytes 1376288 | tf_op jit(solution)/shard_map/ppermute | solution.py:81
  193.8 11.2 %collective-permute-done.12 = bf16[96,3584]{1,0:T(8,128)(2,1)S(1)} collective-permute-done((bf16[96,3584]{1,0:T(8,128)(2,1)S(1)}, bf16[96,3584]{1,0:T(8,128)(2,1)S(1)}, u32[]{:S(2)}, u32[]{:S(2)}) %collective-permute-start.12) | collective-permute-done | bytes 688160 | tf_op jit(solution)/shard_map/ppermute | solution.py:65
  209.1 2.2 collective-permute-start.15
  211.3 3.7 %all-to-all-start.2 = ((bf16[8,24,3584]{2,1,0:T(8,128)(2,1)}), bf16[8,24,3584]{2,1,0:T(8,128)(2,1)S(1)}, u32[]{:S(2)}, u32[]{:S(2)}) async-start(bf16[8,24,3584]{2,1,0:T(8,128)(2,1)} %bitcast.76), calls=%async_computation.2 | async-start | bytes 2752512 | tf_op jit(solution)/shard_map/all_to_all | solution.py:28
  214.9 18.9 %collective-permute-done.13 = bf16[192,3584]{1,0:T(8,128)(2,1)} collective-permute-done((bf16[192,3584]{1,0:T(8,128)(2,1)}, bf16[192,3584]{1,0:T(8,128)(2,1)}, u32[]{:S(2)}, u32[]{:S(2)}) %collective-permute-start.13) | collective-permute-done | bytes 1376288 | tf_op jit(solution)/shard_map/ppermute | solution.py:81
  234.3 3.8 %add_convert_fusion.1 = bf16[192,3584]{1,0:T(8,128)(2,1)} fusion(bf16[192,3584]{1,0:T(8,128)(2,1)} %collective-permute-done.15, bf16[192,3584]{1,0:T(8,128)(2,1)} %collective-permute-done.13, bf16[768,3584]{1,0:T(8,128)(2,1)} %copy-done.3), kind=kLoop, calls=%fused_computation.24 | loop fusion | flops 4128768 | bytes 5505024 | tf_op jit(solution)/shard_map/convert_element_type | solution.py:84
  238.1 10.5 %all-to-all-done.2 = bf16[8,24,3584]{2,1,0:T(8,128)(2,1)S(1)} async-done(((bf16[8,24,3584]{2,1,0:T(8,128)(2,1)}), bf16[8,24,3584]{2,1,0:T(8,128)(2,1)S(1)}, u32[]{:S(2)}, u32[]{:S(2)}) %all-to-all-start.2) | async-done | bytes 1376288 | tf_op jit(solution)/shard_map/all_to_all | solution.py:28
  248.6 4.3 %all-to-all-start.3 = ((bf16[8,24,3584]{2,1,0:T(8,128)(2,1)}), bf16[8,24,3584]{2,1,0:T(8,128)(2,1)}, u32[]{:S(2)}, u32[]{:S(2)}) async-start(bf16[8,24,3584]{2,1,0:T(8,128)(2,1)} %bitcast.78), calls=%async_computation.3 | async-start | bytes 2752512 | tf_op jit(solution)/shard_map/all_to_all | solution.py:93
  252.9 7.1 %fusion.2 = bf16[1,512,3584]{2,1,0:T(8,128)(2,1)} fusion(bf16[768,512]{1,0:T(8,128)(2,1)S(1)} %copy-done.12, bf16[768,3584]{1,0:T(8,128)(2,1)} %copy-done.4), kind=kOutput, calls=%fused_computation.7 | convolution fusion | flops 2820407296 | bytes 9961472 | tf_op jit(solution)/shard_map/dot_general | solution.py:22
  260.0 7.2 %fusion.1 = bf16[1,3584,512]{2,1,0:T(8,128)(2,1)} fusion(bf16[768,3584]{1,0:T(8,128)(2,1)} %constant_dynamic-update-slice_fusion, bf16[768,512]{1,0:T(8,128)(2,1)S(1)} %copy-done.13), kind=kOutput, calls=%fused_computation.6 | convolution fusion | flops 2820407296 | bytes 9961472 | tf_op jit(solution)/shard_map/dot_general | solution.py:22
  267.2 7.3 %fusion = bf16[1,3584,512]{2,1,0:T(8,128)(2,1)} fusion(bf16[768,3584]{1,0:T(8,128)(2,1)} %constant_dynamic-update-slice_fusion, bf16[768,512]{1,0:T(8,128)(2,1)S(1)} %copy-done.10), kind=kOutput, calls=%fused_computation.5 | convolution fusion | flops 2820407296 | bytes 9961472 | tf_op jit(solution)/shard_map/dot_general | solution.py:22
  277.7 8.8 %all-to-all-done.3 = bf16[8,24,3584]{2,1,0:T(8,128)(2,1)} async-done(((bf16[8,24,3584]{2,1,0:T(8,128)(2,1)}), bf16[8,24,3584]{2,1,0:T(8,128)(2,1)}, u32[]{:S(2)}, u32[]{:S(2)}) %all-to-all-start.3) | async-done | bytes 1376288 | tf_op jit(solution)/shard_map/all_to_all | solution.py:93
  286.5 2.7 convolution_convert_fusion.6
  (99 shorter events, 39.5 us)
Async XLA Ops:
  0.6 49.8 %copy-start = (bf16[128,3584]{1,0:T(8,128)(2,1)S(1)}, bf16[128,3584]{1,0:T(8,128)(2,1)}, u32[]{:S(2)}) copy-start(bf16[128,3584]{1,0:T(8,128)(2,1)} %param.10) | copy-start | bytes 2752516
  1.7 48.4 %copy-start.5 = (f32[128,8]{0,1:T(8,128)S(1)}, f32[128,8]{0,1:T(8,128)}, u32[]{:S(2)}) copy-start(f32[128,8]{0,1:T(8,128)} %param.8) | copy-start | bytes 12292
  47.1 32.2 %collective-permute-start = (bf16[192,3584]{1,0:T(8,128)(2,1)}, bf16[192,3584]{1,0:T(8,128)(2,1)}, u32[]{:S(2)}, u32[]{:S(2)}) collective-permute-start(bf16[192,3584]{1,0:T(8,128)(2,1)} %bitcast.2), channel_id=1, source_target_pairs={{0,8},{8,0},{16,24},{24,16},{1,9},{9,1},{17,25},{25,17},{2,10},{10... | collective-permute-start | bytes 4128776 | tf_op jit(solution)/shard_map/ppermute | solution.py:39
  48.5 33.4 %collective-permute-start.1 = (bf16[192,3584]{1,0:T(8,128)(2,1)}, bf16[192,3584]{1,0:T(8,128)(2,1)}, u32[]{:S(2)}, u32[]{:S(2)}) collective-permute-start(bf16[192,3584]{1,0:T(8,128)(2,1)} %bitcast.2), channel_id=1, source_target_pairs={{0,16},{8,24},{16,0},{24,8},{1,17},{9,25},{17,1},{25,9},{2,18},{10... | collective-permute-start | bytes 4128776 | tf_op jit(solution)/shard_map/ppermute | solution.py:40
  52.9 47.1 %all-to-all-start.1 = ((bf16[8,24,3584]{2,1,0:T(8,128)(2,1)}), bf16[8,24,3584]{2,1,0:T(8,128)(2,1)S(1)}, u32[]{:S(2)}, u32[]{:S(2)}) async-start(bf16[8,24,3584]{2,1,0:T(8,128)(2,1)} %bitcast.77), calls=%async_computation.1 | async-start | bytes 2752512 | tf_op jit(solution)/shard_map/all_to_all | solution.py:28
  80.4 16.3 %collective-permute-start.2 = (bf16[96,3584]{1,0:T(8,128)(2,1)S(1)}, bf16[96,3584]{1,0:T(8,128)(2,1)S(1)}, u32[]{:S(2)}, u32[]{:S(2)}) collective-permute-start(bf16[96,3584]{1,0:T(8,128)(2,1)S(1)} %slice.85), channel_id=1, source_target_pairs={{0,16},{8,24},{16,0},{24,8},{1,17},{9,25},{17,1},{25,9},{2,18},{10... | collective-permute-start | bytes 2064392 | tf_op jit(solution)/shard_map/ppermute | solution.py:49
  83.1 16.0 %collective-permute-start.3 = (bf16[96,3584]{1,0:T(8,128)(2,1)S(1)}, bf16[96,3584]{1,0:T(8,128)(2,1)S(1)}, u32[]{:S(2)}, u32[]{:S(2)}) collective-permute-start(bf16[96,3584]{1,0:T(8,128)(2,1)S(1)} %slice.86), channel_id=1, source_target_pairs={{0,8},{8,0},{16,24},{24,16},{1,9},{9,1},{17,25},{25,17},{2,10},{10... | collective-permute-start | bytes 2064392 | tf_op jit(solution)/shard_map/ppermute | solution.py:50
  100.0 29.8 %collective-permute-start.4 = (bf16[192,3584]{1,0:T(8,128)(2,1)S(1)}, bf16[192,3584]{1,0:T(8,128)(2,1)S(1)}, u32[]{:S(2)}, u32[]{:S(2)}) collective-permute-start(bf16[192,3584]{1,0:T(8,128)(2,1)S(1)} %bitcast.73), channel_id=1, source_target_pairs={{0,8},{8,0},{16,24},{24,16},{1,9},{9,1},{17,25},{25,17},{2,10},{10... | collective-permute-start | bytes 4128776 | tf_op jit(solution)/shard_map/ppermute | solution.py:39
  101.5 30.2 %collective-permute-start.5 = (bf16[192,3584]{1,0:T(8,128)(2,1)S(1)}, bf16[192,3584]{1,0:T(8,128)(2,1)S(1)}, u32[]{:S(2)}, u32[]{:S(2)}) collective-permute-start(bf16[192,3584]{1,0:T(8,128)(2,1)S(1)} %bitcast.74), channel_id=1, source_target_pairs={{0,16},{8,24},{16,0},{24,8},{1,17},{9,25},{17,1},{25,9},{2,18},{10... | collective-permute-start | bytes 4128776 | tf_op jit(solution)/shard_map/ppermute | solution.py:40
  102.1 6.2 %copy-start.8 = (bf16[1,3584,512]{2,1,0:T(8,128)(2,1)S(1)}, bf16[1,3584,512]{2,1,0:T(8,128)(2,1)}, u32[]{:S(2)}) copy-start(bf16[1,3584,512]{2,1,0:T(8,128)(2,1)} %param.12) | copy-start | bytes 11010052
  108.4 7.4 %copy-start.14 = (f32[768,512]{1,0:T(8,128)}, f32[768,512]{1,0:T(8,128)S(1)}, u32[]{:S(2)}) copy-start(f32[768,512]{1,0:T(8,128)S(1)} %fusion.12) | copy-start | bytes 4718596
  108.4 7.4 %copy-start.6 = (bf16[1,512,3584]{2,1,0:T(8,128)(2,1)S(1)}, bf16[1,512,3584]{2,1,0:T(8,128)(2,1)}, u32[]{:S(2)}) copy-start(bf16[1,512,3584]{2,1,0:T(8,128)(2,1)} %param.13) | copy-start | bytes 11010052
  131.8 18.4 %collective-permute-start.6 = (bf16[96,3584]{1,0:T(8,128)(2,1)S(1)}, bf16[96,3584]{1,0:T(8,128)(2,1)S(1)}, u32[]{:S(2)}, u32[]{:S(2)}) collective-permute-start(bf16[96,3584]{1,0:T(8,128)(2,1)S(1)} %slice.70), channel_id=1, source_target_pairs={{0,16},{8,24},{16,0},{24,8},{1,17},{9,25},{17,1},{25,9},{2,18},{10... | collective-permute-start | bytes 2064392 | tf_op jit(solution)/shard_map/ppermute | solution.py:49
  132.4 18.4 %collective-permute-start.7 = (bf16[96,3584]{1,0:T(8,128)(2,1)S(1)}, bf16[96,3584]{1,0:T(8,128)(2,1)S(1)}, u32[]{:S(2)}, u32[]{:S(2)}) collective-permute-start(bf16[96,3584]{1,0:T(8,128)(2,1)S(1)} %slice.71), channel_id=1, source_target_pairs={{0,8},{8,0},{16,24},{24,16},{1,9},{9,1},{17,25},{25,17},{2,10},{10... | collective-permute-start | bytes 2064392 | tf_op jit(solution)/shard_map/ppermute | solution.py:50
  133.4 27.4 %collective-permute-start.8 = (bf16[96,3584]{1,0:T(8,128)(2,1)S(1)}, bf16[96,3584]{1,0:T(8,128)(2,1)S(1)}, u32[]{:S(2)}, u32[]{:S(2)}) collective-permute-start(bf16[96,3584]{1,0:T(8,128)(2,1)S(1)} %get-tuple-element.63), channel_id=1, source_target_pairs={{0,8},{8,0},{16,24},{24,16},{1,9},{9,1},{17,25},{25,17},{2,10},{10... | collective-permute-start | bytes 2064392 | tf_op jit(solution)/shard_map/ppermute | solution.py:64
  135.0 26.3 %collective-permute-start.9 = (bf16[96,3584]{1,0:T(8,128)(2,1)S(1)}, bf16[96,3584]{1,0:T(8,128)(2,1)S(1)}, u32[]{:S(2)}, u32[]{:S(2)}) collective-permute-start(bf16[96,3584]{1,0:T(8,128)(2,1)S(1)} %get-tuple-element.62), channel_id=1, source_target_pairs={{0,16},{8,24},{16,0},{24,8},{1,17},{9,25},{17,1},{25,9},{2,18},{10... | collective-permute-start | bytes 2064392 | tf_op jit(solution)/shard_map/ppermute | solution.py:65
  150.9 13.6 %copy-start.4 = (bf16[768,3584]{1,0:T(8,128)(2,1)}, bf16[768,3584]{1,0:T(8,128)(2,1)S(1)}, u32[]{:S(2)}) copy-start(bf16[768,3584]{1,0:T(8,128)(2,1)S(1)} %constant_dynamic-update-slice_fusion.5) | copy-start | bytes 16515076
  161.7 27.9 %collective-permute-start.10 = (bf16[192,3584]{1,0:T(8,128)(2,1)S(1)}, bf16[192,3584]{1,0:T(8,128)(2,1)S(1)}, u32[]{:S(2)}, u32[]{:S(2)}) collective-permute-start(bf16[192,3584]{1,0:T(8,128)(2,1)S(1)} %pad_maximum_fusion), channel_id=1, source_target_pairs={{0,8},{8,0},{16,24},{24,16},{1,9},{9,1},{17,25},{25,17},{2,10},{10... | collective-permute-start | bytes 4128776 | tf_op jit(solution)/shard_map/ppermute | solution.py:81
  162.3 6.6 %copy-start.7 = (bf16[1,3584,512]{2,1,0:T(8,128)(2,1)S(1)}, bf16[1,3584,512]{2,1,0:T(8,128)(2,1)}, u32[]{:S(2)}) copy-start(bf16[1,3584,512]{2,1,0:T(8,128)(2,1)} %param.11) | copy-start | bytes 11010052
  162.3 28.7 %collective-permute-start.11 = (bf16[192,3584]{1,0:T(8,128)(2,1)S(1)}, bf16[192,3584]{1,0:T(8,128)(2,1)S(1)}, u32[]{:S(2)}, u32[]{:S(2)}) collective-permute-start(bf16[192,3584]{1,0:T(8,128)(2,1)S(1)} %pad_maximum_fusion.1), channel_id=1, source_target_pairs={{0,16},{8,24},{16,0},{24,8},{1,17},{9,25},{17,1},{25,9},{2,18},{10... | collective-permute-start | bytes 4128776 | tf_op jit(solution)/shard_map/ppermute | solution.py:82
  183.2 22.6 %copy-start.3 = (bf16[768,3584]{1,0:T(8,128)(2,1)}, bf16[768,3584]{1,0:T(8,128)(2,1)S(1)}, u32[]{:S(2)}) copy-start(bf16[768,3584]{1,0:T(8,128)(2,1)S(1)} %add_convert_fusion) | copy-start | bytes 16515076
  192.8 12.2 %collective-permute-start.12 = (bf16[96,3584]{1,0:T(8,128)(2,1)S(1)}, bf16[96,3584]{1,0:T(8,128)(2,1)S(1)}, u32[]{:S(2)}, u32[]{:S(2)}) collective-permute-start(bf16[96,3584]{1,0:T(8,128)(2,1)S(1)} %get-tuple-element.57), channel_id=1, source_target_pairs={{0,16},{8,24},{16,0},{24,8},{1,17},{9,25},{17,1},{25,9},{2,18},{10... | collective-permute-start | bytes 2064392 | tf_op jit(solution)/shard_map/ppermute | solution.py:65
  193.2 12.6 %collective-permute-start.14 = (bf16[96,3584]{1,0:T(8,128)(2,1)S(1)}, bf16[96,3584]{1,0:T(8,128)(2,1)S(1)}, u32[]{:S(2)}, u32[]{:S(2)}) collective-permute-start(bf16[96,3584]{1,0:T(8,128)(2,1)S(1)} %get-tuple-element.56), channel_id=1, source_target_pairs={{0,8},{8,0},{16,24},{24,16},{1,9},{9,1},{17,25},{25,17},{2,10},{10... | collective-permute-start | bytes 2064392 | tf_op jit(solution)/shard_map/ppermute | solution.py:64
  207.3 26.6 %collective-permute-start.13 = (bf16[192,3584]{1,0:T(8,128)(2,1)}, bf16[192,3584]{1,0:T(8,128)(2,1)}, u32[]{:S(2)}, u32[]{:S(2)}) collective-permute-start(bf16[192,3584]{1,0:T(8,128)(2,1)} %pad_maximum_fusion.2), channel_id=1, source_target_pairs={{0,8},{8,0},{16,24},{24,16},{1,9},{9,1},{17,25},{25,17},{2,10},{10... | collective-permute-start | bytes 4128776 | tf_op jit(solution)/shard_map/ppermute | solution.py:81
  209.1 25.2 %collective-permute-start.15 = (bf16[192,3584]{1,0:T(8,128)(2,1)}, bf16[192,3584]{1,0:T(8,128)(2,1)}, u32[]{:S(2)}, u32[]{:S(2)}) collective-permute-start(bf16[192,3584]{1,0:T(8,128)(2,1)} %pad_maximum_fusion.3), channel_id=1, source_target_pairs={{0,16},{8,24},{16,0},{24,8},{1,17},{9,25},{17,1},{25,9},{2,18},{10... | collective-permute-start | bytes 4128776 | tf_op jit(solution)/shard_map/ppermute | solution.py:82
  211.3 37.3 %all-to-all-start.2 = ((bf16[8,24,3584]{2,1,0:T(8,128)(2,1)}), bf16[8,24,3584]{2,1,0:T(8,128)(2,1)S(1)}, u32[]{:S(2)}, u32[]{:S(2)}) async-start(bf16[8,24,3584]{2,1,0:T(8,128)(2,1)} %bitcast.76), calls=%async_computation.2 | async-start | bytes 2752512 | tf_op jit(solution)/shard_map/all_to_all | solution.py:28
  238.1 14.7 %copy-start.12 = (bf16[768,512]{1,0:T(8,128)(2,1)S(1)}, bf16[768,512]{1,0:T(8,128)(2,1)}, u32[]{:S(2)}) copy-start(bf16[768,512]{1,0:T(8,128)(2,1)} %copy-done.11) | copy-start | bytes 2359300
  248.6 37.9 %all-to-all-start.3 = ((bf16[8,24,3584]{2,1,0:T(8,128)(2,1)}), bf16[8,24,3584]{2,1,0:T(8,128)(2,1)}, u32[]{:S(2)}, u32[]{:S(2)}) async-start(bf16[8,24,3584]{2,1,0:T(8,128)(2,1)} %bitcast.78), calls=%async_computation.3 | async-start | bytes 2752512 | tf_op jit(solution)/shard_map/all_to_all | solution.py:93
  252.9 7.2 %copy-start.13 = (bf16[768,512]{1,0:T(8,128)(2,1)S(1)}, bf16[768,512]{1,0:T(8,128)(2,1)}, u32[]{:S(2)}) copy-start(bf16[768,512]{1,0:T(8,128)(2,1)} %get-tuple-element.34) | copy-start | bytes 2359300
  260.0 7.2 %copy-start.10 = (bf16[768,512]{1,0:T(8,128)(2,1)S(1)}, bf16[768,512]{1,0:T(8,128)(2,1)}, u32[]{:S(2)}) copy-start(bf16[768,512]{1,0:T(8,128)(2,1)} %copy-done.9) | copy-start | bytes 2359300
  267.2 7.3 %copy-start.2 = (f32[192,3584]{1,0:T(8,128)S(1)}, f32[192,3584]{1,0:T(8,128)}, u32[]{:S(2)}) copy-start(f32[192,3584]{1,0:T(8,128)} %get-tuple-element.69) | copy-start | bytes 8257540
  274.4 14.7 %copy-start.1 = (bf16[128,3584]{1,0:T(8,128)(2,1)S(1)}, bf16[128,3584]{1,0:T(8,128)(2,1)}, u32[]{:S(2)}) copy-start(bf16[128,3584]{1,0:T(8,128)(2,1)} %param.10) | copy-start | bytes 2752516
  (4 other events, 14.9 us)

commit v9 on v8

--- a/solution.py
+++ b/solution.py
@@ -24,8 +24,21 @@
     )
 
 
-def along_expert(send_rows):
-    return lax.all_to_all(send_rows, "expert", split_axis=0, concat_axis=0, tiled=True)
+def along_expert(send_rows, by_shifts=False):
+    experts = lax.axis_size("expert")
+    if experts != 8 or not by_shifts:
+        return lax.all_to_all(send_rows, "expert", split_axis=0, concat_axis=0, tiled=True)
+    blocks = send_rows.reshape(experts, -1, send_rows.shape[-1])
+    me = lax.axis_index("expert")
+    shifts = jnp.arange(experts, dtype=jnp.int32)
+    outgoing = jnp.take(blocks, (me + shifts) % experts, axis=0)
+    received = [outgoing[0]]
+    for shift in range(1, experts):
+        perm = [(i, (i + shift) % experts) for i in range(experts)]
+        received.append(lax.ppermute(outgoing[shift], "expert", perm=perm))
+    by_shift = jnp.stack(received, axis=0)
+    by_source = jnp.take(by_shift, (me - shifts) % experts, axis=0)
+    return by_source.reshape(send_rows.shape)
 
 
 def pairs(groups, bit):
@@ -105,7 +118,7 @@
     rows_dy = contract_first(owner, cotangent).astype(jnp.bfloat16)
     prob_rows = jnp.sum(jnp.where(chosen, gate_probs.reshape(-1)[:, None], 0.0), axis=0)
     send_c = (prob_rows[:, None] * rows_dy.astype(jnp.float32)).astype(jnp.bfloat16)
-    rows_x = replicate_dp(along_expert(send_x), groups)
+    rows_x = replicate_dp(along_expert(send_x, by_shifts=True), groups)
     rows_x, c_along = lax.optimization_barrier((rows_x, along_expert(send_c)))
     c_first = swap_halves_first(c_along, groups)
     gate_w = w_gate[0]

time: 290 us -> 300 us (1.034)
  blocking collectives: 39.8 us -> 0 us
  starting transfers between devices: 30.5 us -> 59.6 us
  local copies, waits for them, and re-layouts: 15 us -> 24.5 us
  waiting for transfers between devices: 125 us -> 133 us
    all_to_all x1 -> x0, blocking collectives: 39.8 us -> none  [along_expert(): lax.all_to_all(send_rows, 'expert', split_axis=0, concat_axis=0, tiled=True)]
    all_to_all x2, starting transfers between devices: 7.24 us -> 21.7 us  [along_expert(): lax.all_to_all(send_rows, 'expert', split_axis=0, concat_axis=0, tiled=True)]
    ppermute x0 -> x7, starting transfers between devices: none -> 12.9 us  [along_expert(): received.append(lax.ppermute(outgoing[shift], 'expert', perm=perm))]
    ppermute x0 -> x7, waiting for transfers between devices: none -> 9.79 us  [along_expert(): received.append(lax.ppermute(outgoing[shift], 'expert', perm=perm))]
    ppermute x2, waiting for transfers between devices: 30.9 us -> 24.1 us  [swap_halves_first(): lax.ppermute(rows, 'dp', perm=pairs(groups, 1))]
    unnamed x45 -> x51, local copies, waits for them, and re-layouts: 10.5 us -> 14.6 us
    gather x0 -> x2, local copies, waits for them, and re-layouts: none -> 3.94 us  [the longest x1 1.97 us: along_expert(): by_source = jnp.take(by_shift, (me - shifts) % experts, axis=0)]
    ppermute x2, waiting for transfers between devices: 10.7 us -> 14.1 us  [reduce_first(): lax.ppermute(to_diag[:half], 'dp', perm=pairs(groups, 1))]
  transfers between devices with their start and end apart: 19 -> 26, of which waited for: 17 -> 18; matrix products, arithmetic and copies ran while one was open for 28% -> 28% of each run, Pallas kernels for 0% -> 0%
where the time goes in v9:
time: 300 us
  waiting for transfers between devices  133 us (44%)
  matrix products  67.1 us (22%)
  starting transfers between devices  59.6 us (20%)
  local copies, waits for them, and re-layouts  24.5 us (8%)
  other arithmetic  14.1 us (5%)
    dot_general x5, matrix products, contract_first(): lax.dot_general(left, right, (((0,), (0,)), ((), ())), preferred_element_...  26.8 us
    ppermute x2, waiting for transfers between devices, reduce_second(): from_x = lax.ppermute(to_x, 'dp', perm=pairs(groups, 1))  24.4 us
    ppermute x2, waiting for transfers between devices, swap_halves_first(): lax.ppermute(rows, 'dp', perm=pairs(groups, 1))  24.1 us
    all_to_all x2, starting transfers between devices, along_expert(): lax.all_to_all(send_rows, 'expert', split_axis=0, concat_axis=0, tiled=True)  21.7 us
    ppermute x2, waiting for transfers between devices, swap_halves_second(): diag_lo = lax.ppermute(from_x[:half], 'dp', perm=pairs(groups, 2))  21 us
    dot_general x3, matrix products, contract_last(): lax.dot_general(left, right, (((1,), (1,)), ((), ())), preferred_element_...  18.7 us
    unnamed x51, local copies, waits for them, and re-layouts  14.6 us
    ppermute x2, waiting for transfers between devices, reduce_first(): lax.ppermute(to_diag[:half], 'dp', perm=pairs(groups, 1))  14.1 us
  transfers between devices with their start and end apart: 26, of which 18 were waited for; matrix products, arithmetic and copies ran while one was open for 28% of the time, Pallas kernels for 0%

profile of v9, /device:TPU:0, one launch (start us, length us, event | category | flops | bytes accessed | tf_op | source)
XLA Modules:
  0.0 299.6 jit_solution(15430779352078475288)
XLA Ops:
  5.6 2.8 convolution_convert_fusion.5
  11.7 2.6 collective-permute-start.1
  14.3 2.6 collective-permute-start.2
  26.2 9.1 %collective-permute-done.2 = bf16[24,3584]{1,0:T(8,128)(2,1)S(1)} collective-permute-done((bf16[24,3584]{1,0:T(8,128)(2,1)S(1)}, bf16[24,3584]{1,0:T(8,128)(2,1)S(1)}, u32[]{:S(2)}, u32[]{:S(2)}) %collective-permute-start.2) | collective-permute-done | bytes 172064 | tf_op jit(solution)/shard_map/ppermute | solution.py:38
  46.0 2.5 multiply_convert_fusion
  48.5 11.7 %all-to-all-start = ((bf16[8,24,3584]{2,1,0:T(8,128)(2,1)}), bf16[8,24,3584]{2,1,0:T(8,128)(2,1)S(1)}, u32[]{:S(2)}, u32[]{:S(2)}) async-start(bf16[8,24,3584]{2,1,0:T(8,128)(2,1)} %bitcast.105), calls=%async_computation | async-start | bytes 2752512 | tf_op jit(solution)/shard_map/all_to_all | solution.py:30
  60.2 2.5 constant_dynamic-update-slice_fusion.4
  62.7 10.6 %collective-permute-done.7 = bf16[192,3584]{1,0:T(8,128)(2,1)} collective-permute-done((bf16[192,3584]{1,0:T(8,128)(2,1)}, bf16[192,3584]{1,0:T(8,128)(2,1)}, u32[]{:S(2)}, u32[]{:S(2)}) %collective-permute-start.7) | collective-permute-done | bytes 1376288 | tf_op jit(solution)/shard_map/ppermute | solution.py:52
  82.0 2.5 constant_dynamic-update-slice_fusion.2
  84.5 7.3 %collective-permute-done.9 = bf16[96,3584]{1,0:T(8,128)(2,1)S(1)} collective-permute-done((bf16[96,3584]{1,0:T(8,128)(2,1)S(1)}, bf16[96,3584]{1,0:T(8,128)(2,1)S(1)}, u32[]{:S(2)}, u32[]{:S(2)}) %collective-permute-start.9) | collective-permute-done | bytes 688160 | tf_op jit(solution)/shard_map/ppermute | solution.py:62
  92.7 3.0 collective-permute-done.10
  98.7 6.2 %fusion.12 = f32[768,512]{1,0:T(8,128)S(1)} fusion(bf16[768,3584]{1,0:T(8,128)(2,1)} %constant_dynamic-update-slice_fusion, bf16[1,3584,512]{2,1,0:T(8,128)(2,1)} %param.13), kind=kOutput, calls=%fused_computation.23 | convolution fusion | flops 2818572288 | bytes 10747904 | tf_op jit(solution)/shard_map/dot_general | solution.py:127
  104.9 7.4 %multiply_convert_fusion.3 = (bf16[768,512]{1,0:T(8,128)(2,1)S(1)}, f32[768,512]{1,0:T(8,128)}) fusion(f32[768,512]{1,0:T(8,128)S(1)} %fusion.12, bf16[768,3584]{1,0:T(8,128)(2,1)} %constant_dynamic-update-slice_fusion, bf16[1,3584,512]{2,1,0:T(8,128)(2,1)S(1)} %copy-done.8), kind=kOutput, calls=%fused_computation.32 | convolution fusion | flops 2820931584 | bytes 13107200 | tf_op jit(solution)/shard_map/dot_general | solution.py:128
  112.3 3.2 %convolution_convert_fusion = bf16[768,3584]{1,0:T(8,128)(2,1)S(1)} fusion(bf16[768,512]{1,0:T(8,128)(2,1)S(1)} %get-tuple-element.36, bf16[1,512,3584]{2,1,0:T(8,128)(2,1)S(1)} %copy-done.6), kind=kOutput, calls=%fused_computation.3 | convolution fusion | flops 2821324800 | bytes 9961472 | tf_op jit(solution)/shard_map/dot_general | solution.py:132
  115.6 13.5 %collective-permute-done.11 = bf16[192,3584]{1,0:T(8,128)(2,1)S(1)} collective-permute-done((bf16[192,3584]{1,0:T(8,128)(2,1)S(1)}, bf16[192,3584]{1,0:T(8,128)(2,1)S(1)}, u32[]{:S(2)}, u32[]{:S(2)}) %collective-permute-start.11) | collective-permute-done | bytes 1376288 | tf_op jit(solution)/shard_map/ppermute | solution.py:52
  135.1 13.7 %collective-permute-done.13 = bf16[96,3584]{1,0:T(8,128)(2,1)S(1)} collective-permute-done((bf16[96,3584]{1,0:T(8,128)(2,1)S(1)}, bf16[96,3584]{1,0:T(8,128)(2,1)S(1)}, u32[]{:S(2)}, u32[]{:S(2)}) %collective-permute-start.13) | collective-permute-done | bytes 688160 | tf_op jit(solution)/shard_map/ppermute | solution.py:62
  149.5 12.7 %collective-permute-done.15 = bf16[96,3584]{1,0:T(8,128)(2,1)S(1)} collective-permute-done((bf16[96,3584]{1,0:T(8,128)(2,1)S(1)}, bf16[96,3584]{1,0:T(8,128)(2,1)S(1)}, u32[]{:S(2)}, u32[]{:S(2)}) %collective-permute-start.15) | collective-permute-done | bytes 688160 | tf_op jit(solution)/shard_map/ppermute | solution.py:77
  165.0 4.4 %multiply_convert_fusion.1 = (bf16[768,512]{1,0:T(8,128)(2,1)}, bf16[768,512]{1,0:T(8,128)(2,1)S(1)}) fusion(f32[768,512]{1,0:T(8,128)S(1)} %copy-done.15, f32[768,512]{1,0:T(8,128)S(1)} %copy-done.16, bf16[768,3584]{1,0:T(8,128)(2,1)S(1)} %constant_dynamic-update-slice_fusion.5, bf16[1,512,3584]{2,1,0:T(8,128)(2,1)S(1)} %copy-done.6), kind=kOutput, calls=%fused_computation.29 | convolution fusion | flops 2823684096 | bytes 13893632 | tf_op jit(solution)/shard_map/dot_general | solution.py:16
  169.4 5.8 %fusion.10 = f32[768,3584]{1,0:T(8,128)} fusion(bf16[768,512]{1,0:T(8,128)(2,1)S(1)} %get-tuple-element.34, bf16[1,3584,512]{2,1,0:T(8,128)(2,1)S(1)} %copy-done.7), kind=kOutput, calls=%fused_computation.21 | convolution fusion | flops 2818572288 | bytes 15466496 | tf_op jit(solution)/shard_map/dot_general | solution.py:16
  175.3 8.5 %add_convert_fusion = bf16[768,3584]{1,0:T(8,128)(2,1)S(1)} fusion(f32[768,3584]{1,0:T(8,128)} %fusion.10, bf16[768,512]{1,0:T(8,128)(2,1)} %get-tuple-element.35, bf16[1,3584,512]{2,1,0:T(8,128)(2,1)} %param.14), kind=kOutput, calls=%fused_computation.2 | convolution fusion | flops 2824077312 | bytes 20971520 | tf_op jit(solution)/shard_map/dot_general | solution.py:16
  183.8 9.2 %collective-permute-done.17 = bf16[192,3584]{1,0:T(8,128)(2,1)S(1)} collective-permute-done((bf16[192,3584]{1,0:T(8,128)(2,1)S(1)}, bf16[192,3584]{1,0:T(8,128)(2,1)S(1)}, u32[]{:S(2)}, u32[]{:S(2)}) %collective-permute-start.17) | collective-permute-done | bytes 1376288 | tf_op jit(solution)/shard_map/ppermute | solution.py:94
  198.2 11.4 %collective-permute-done.19 = bf16[96,3584]{1,0:T(8,128)(2,1)S(1)} collective-permute-done((bf16[96,3584]{1,0:T(8,128)(2,1)S(1)}, bf16[96,3584]{1,0:T(8,128)(2,1)S(1)}, u32[]{:S(2)}, u32[]{:S(2)}) %collective-permute-start.19) | collective-permute-done | bytes 688160 | tf_op jit(solution)/shard_map/ppermute | solution.py:78
  215.4 10.0 %all-to-all-start.1 = ((bf16[8,24,3584]{2,1,0:T(8,128)(2,1)}), bf16[8,24,3584]{2,1,0:T(8,128)(2,1)S(1)}, u32[]{:S(2)}, u32[]{:S(2)}) async-start(bf16[8,24,3584]{2,1,0:T(8,128)(2,1)} %bitcast.104), calls=%async_computation.1 | async-start | bytes 2752512 | tf_op jit(solution)/shard_map/all_to_all | solution.py:30
  225.4 15.3 %collective-permute-done.20 = bf16[192,3584]{1,0:T(8,128)(2,1)} collective-permute-done((bf16[192,3584]{1,0:T(8,128)(2,1)}, bf16[192,3584]{1,0:T(8,128)(2,1)}, u32[]{:S(2)}, u32[]{:S(2)}) %collective-permute-start.20) | collective-permute-done | bytes 1376288 | tf_op jit(solution)/shard_map/ppermute | solution.py:94
  242.8 3.8 %add_convert_fusion.1 = bf16[192,3584]{1,0:T(8,128)(2,1)} fusion(bf16[192,3584]{1,0:T(8,128)(2,1)} %collective-permute-done.22, bf16[192,3584]{1,0:T(8,128)(2,1)} %collective-permute-done.20, bf16[768,3584]{1,0:T(8,128)(2,1)} %copy-done.3), kind=kLoop, calls=%fused_computation.26 | loop fusion | flops 4128768 | bytes 5505024 | tf_op jit(solution)/shard_map/convert_element_type | solution.py:97
  246.6 12.5 %all-to-all-done.1 = bf16[8,24,3584]{2,1,0:T(8,128)(2,1)S(1)} async-done(((bf16[8,24,3584]{2,1,0:T(8,128)(2,1)}), bf16[8,24,3584]{2,1,0:T(8,128)(2,1)S(1)}, u32[]{:S(2)}, u32[]{:S(2)}) %all-to-all-start.1) | async-done | bytes 1376288 | tf_op jit(solution)/shard_map/all_to_all | solution.py:30
  259.0 4.3 %all-to-all-start.2 = ((bf16[8,24,3584]{2,1,0:T(8,128)(2,1)}), bf16[8,24,3584]{2,1,0:T(8,128)(2,1)}, u32[]{:S(2)}, u32[]{:S(2)}) async-start(bf16[8,24,3584]{2,1,0:T(8,128)(2,1)} %bitcast.106), calls=%async_computation.2 | async-start | bytes 2752512 | tf_op jit(solution)/shard_map/all_to_all | solution.py:106
  263.3 7.1 %fusion.2 = bf16[1,512,3584]{2,1,0:T(8,128)(2,1)} fusion(bf16[768,512]{1,0:T(8,128)(2,1)S(1)} %copy-done.12, bf16[768,3584]{1,0:T(8,128)(2,1)} %copy-done.4), kind=kOutput, calls=%fused_computation.9 | convolution fusion | flops 2820407296 | bytes 9961472 | tf_op jit(solution)/shard_map/dot_general | solution.py:22
  270.5 7.2 %fusion.1 = bf16[1,3584,512]{2,1,0:T(8,128)(2,1)} fusion(bf16[768,3584]{1,0:T(8,128)(2,1)} %constant_dynamic-update-slice_fusion, bf16[768,512]{1,0:T(8,128)(2,1)S(1)} %copy-done.13), kind=kOutput, calls=%fused_computation.8 | convolution fusion | flops 2820407296 | bytes 9961472 | tf_op jit(solution)/shard_map/dot_general | solution.py:22
  277.6 7.3 %fusion = bf16[1,3584,512]{2,1,0:T(8,128)(2,1)} fusion(bf16[768,3584]{1,0:T(8,128)(2,1)} %constant_dynamic-update-slice_fusion, bf16[768,512]{1,0:T(8,128)(2,1)S(1)} %copy-done.10), kind=kOutput, calls=%fused_computation.7 | convolution fusion | flops 2820407296 | bytes 9961472 | tf_op jit(solution)/shard_map/dot_general | solution.py:22
  288.1 8.8 %all-to-all-done.2 = bf16[8,24,3584]{2,1,0:T(8,128)(2,1)} async-done(((bf16[8,24,3584]{2,1,0:T(8,128)(2,1)}), bf16[8,24,3584]{2,1,0:T(8,128)(2,1)}, u32[]{:S(2)}, u32[]{:S(2)}) %all-to-all-start.2) | async-done | bytes 1376288 | tf_op jit(solution)/shard_map/all_to_all | solution.py:106
  296.9 2.7 convolution_convert_fusion.6
  (130 shorter events, 66.5 us)
Async XLA Ops:
  0.6 45.3 %copy-start = (bf16[128,3584]{1,0:T(8,128)(2,1)S(1)}, bf16[128,3584]{1,0:T(8,128)(2,1)}, u32[]{:S(2)}) copy-start(bf16[128,3584]{1,0:T(8,128)(2,1)} %param.12) | copy-start | bytes 2752516
  11.3 8.7 %collective-permute-start = (bf16[24,3584]{1,0:T(8,128)(2,1)S(1)}, bf16[24,3584]{1,0:T(8,128)(2,1)S(1)}, u32[]{:S(2)}, u32[]{:S(2)}) collective-permute-start(bf16[24,3584]{1,0:T(8,128)(2,1)S(1)} %get-tuple-element.75), channel_id=1, source_target_pairs={{0,1},{1,2},{2,3},{3,4},{4,5},{5,6},{6,7},{7,0},{8,9},{9,10},{10,1... | collective-permute-start | bytes 516104 | tf_op jit(solution)/shard_map/ppermute | solution.py:38
  11.7 11.4 %collective-permute-start.1 = (bf16[24,3584]{1,0:T(8,128)(2,1)S(1)}, bf16[24,3584]{1,0:T(8,128)(2,1)S(1)}, u32[]{:S(2)}, u32[]{:S(2)}) collective-permute-start(bf16[24,3584]{1,0:T(8,128)(2,1)S(1)} %get-tuple-element.74), channel_id=1, source_target_pairs={{0,2},{1,3},{2,4},{3,5},{4,6},{5,7},{6,0},{7,1},{8,10},{9,11},{10,... | collective-permute-start | bytes 516104 | tf_op jit(solution)/shard_map/ppermute | solution.py:38
  14.3 21.1 %collective-permute-start.2 = (bf16[24,3584]{1,0:T(8,128)(2,1)S(1)}, bf16[24,3584]{1,0:T(8,128)(2,1)S(1)}, u32[]{:S(2)}, u32[]{:S(2)}) collective-permute-start(bf16[24,3584]{1,0:T(8,128)(2,1)S(1)} %get-tuple-element.73), channel_id=1, source_target_pairs={{0,3},{1,4},{2,5},{3,6},{4,7},{5,0},{6,1},{7,2},{8,11},{9,12},{10,... | collective-permute-start | bytes 516104 | tf_op jit(solution)/shard_map/ppermute | solution.py:38
  16.9 19.2 %collective-permute-start.3 = (bf16[24,3584]{1,0:T(8,128)(2,1)S(1)}, bf16[24,3584]{1,0:T(8,128)(2,1)S(1)}, u32[]{:S(2)}, u32[]{:S(2)}) collective-permute-start(bf16[24,3584]{1,0:T(8,128)(2,1)S(1)} %get-tuple-element.72), channel_id=1, source_target_pairs={{0,4},{1,5},{2,6},{3,7},{4,0},{5,1},{6,2},{7,3},{8,12},{9,13},{10,... | collective-permute-start | bytes 516104 | tf_op jit(solution)/shard_map/ppermute | solution.py:38
  18.1 18.6 %collective-permute-start.4 = (bf16[24,3584]{1,0:T(8,128)(2,1)S(1)}, bf16[24,3584]{1,0:T(8,128)(2,1)S(1)}, u32[]{:S(2)}, u32[]{:S(2)}) collective-permute-start(bf16[24,3584]{1,0:T(8,128)(2,1)S(1)} %get-tuple-element.71), channel_id=1, source_target_pairs={{0,5},{1,6},{2,7},{3,0},{4,1},{5,2},{6,3},{7,4},{8,13},{9,14},{10,... | collective-permute-start | bytes 516104 | tf_op jit(solution)/shard_map/ppermute | solution.py:38
  20.0 17.5 %collective-permute-start.5 = (bf16[24,3584]{1,0:T(8,128)(2,1)S(1)}, bf16[24,3584]{1,0:T(8,128)(2,1)S(1)}, u32[]{:S(2)}, u32[]{:S(2)}) collective-permute-start(bf16[24,3584]{1,0:T(8,128)(2,1)S(1)} %get-tuple-element.70), channel_id=1, source_target_pairs={{0,6},{1,7},{2,0},{3,1},{4,2},{5,3},{6,4},{7,5},{8,14},{9,15},{10,... | collective-permute-start | bytes 516104 | tf_op jit(solution)/shard_map/ppermute | solution.py:38
  23.1 15.0 %collective-permute-start.6 = (bf16[24,3584]{1,0:T(8,128)(2,1)S(1)}, bf16[24,3584]{1,0:T(8,128)(2,1)S(1)}, u32[]{:S(2)}, u32[]{:S(2)}) collective-permute-start(bf16[24,3584]{1,0:T(8,128)(2,1)S(1)} %get-tuple-element.69), channel_id=1, source_target_pairs={{0,7},{1,0},{2,1},{3,2},{4,3},{5,4},{6,5},{7,6},{8,15},{9,8},{10,9... | collective-permute-start | bytes 516104 | tf_op jit(solution)/shard_map/ppermute | solution.py:38
  42.1 31.2 %collective-permute-start.7 = (bf16[192,3584]{1,0:T(8,128)(2,1)}, bf16[192,3584]{1,0:T(8,128)(2,1)}, u32[]{:S(2)}, u32[]{:S(2)}) collective-permute-start(bf16[192,3584]{1,0:T(8,128)(2,1)} %bitcast.16), channel_id=1, source_target_pairs={{0,8},{8,0},{16,24},{24,16},{1,9},{9,1},{17,25},{25,17},{2,10},{10... | collective-permute-start | bytes 4128776 | tf_op jit(solution)/shard_map/ppermute | solution.py:52
  44.1 32.7 %collective-permute-start.8 = (bf16[192,3584]{1,0:T(8,128)(2,1)}, bf16[192,3584]{1,0:T(8,128)(2,1)}, u32[]{:S(2)}, u32[]{:S(2)}) collective-permute-start(bf16[192,3584]{1,0:T(8,128)(2,1)} %bitcast.16), channel_id=1, source_target_pairs={{0,16},{8,24},{16,0},{24,8},{1,17},{9,25},{17,1},{25,9},{2,18},{10... | collective-permute-start | bytes 4128776 | tf_op jit(solution)/shard_map/ppermute | solution.py:53
  48.5 48.1 %all-to-all-start = ((bf16[8,24,3584]{2,1,0:T(8,128)(2,1)}), bf16[8,24,3584]{2,1,0:T(8,128)(2,1)S(1)}, u32[]{:S(2)}, u32[]{:S(2)}) async-start(bf16[8,24,3584]{2,1,0:T(8,128)(2,1)} %bitcast.105), calls=%async_computation | async-start | bytes 2752512 | tf_op jit(solution)/shard_map/all_to_all | solution.py:30
  74.4 17.3 %collective-permute-start.9 = (bf16[96,3584]{1,0:T(8,128)(2,1)S(1)}, bf16[96,3584]{1,0:T(8,128)(2,1)S(1)}, u32[]{:S(2)}, u32[]{:S(2)}) collective-permute-start(bf16[96,3584]{1,0:T(8,128)(2,1)S(1)} %slice.129), channel_id=1, source_target_pairs={{0,16},{8,24},{16,0},{24,8},{1,17},{9,25},{17,1},{25,9},{2,18},{10... | collective-permute-start | bytes 2064392 | tf_op jit(solution)/shard_map/ppermute | solution.py:62
  77.9 17.7 %collective-permute-start.10 = (bf16[96,3584]{1,0:T(8,128)(2,1)S(1)}, bf16[96,3584]{1,0:T(8,128)(2,1)S(1)}, u32[]{:S(2)}, u32[]{:S(2)}) collective-permute-start(bf16[96,3584]{1,0:T(8,128)(2,1)S(1)} %slice.130), channel_id=1, source_target_pairs={{0,8},{8,0},{16,24},{24,16},{1,9},{9,1},{17,25},{25,17},{2,10},{10... | collective-permute-start | bytes 2064392 | tf_op jit(solution)/shard_map/ppermute | solution.py:63
  96.6 32.5 %collective-permute-start.11 = (bf16[192,3584]{1,0:T(8,128)(2,1)S(1)}, bf16[192,3584]{1,0:T(8,128)(2,1)S(1)}, u32[]{:S(2)}, u32[]{:S(2)}) collective-permute-start(bf16[192,3584]{1,0:T(8,128)(2,1)S(1)} %bitcast.101), channel_id=1, source_target_pairs={{0,8},{8,0},{16,24},{24,16},{1,9},{9,1},{17,25},{25,17},{2,10},{10... | collective-permute-start | bytes 4128776 | tf_op jit(solution)/shard_map/ppermute | solution.py:52
  98.1 32.3 %collective-permute-start.12 = (bf16[192,3584]{1,0:T(8,128)(2,1)S(1)}, bf16[192,3584]{1,0:T(8,128)(2,1)S(1)}, u32[]{:S(2)}, u32[]{:S(2)}) collective-permute-start(bf16[192,3584]{1,0:T(8,128)(2,1)S(1)} %bitcast.102), channel_id=1, source_target_pairs={{0,16},{8,24},{16,0},{24,8},{1,17},{9,25},{17,1},{25,9},{2,18},{10... | collective-permute-start | bytes 4128776 | tf_op jit(solution)/shard_map/ppermute | solution.py:53
  104.9 7.4 %copy-start.14 = (f32[768,512]{1,0:T(8,128)}, f32[768,512]{1,0:T(8,128)S(1)}, u32[]{:S(2)}) copy-start(f32[768,512]{1,0:T(8,128)S(1)} %fusion.12) | copy-start | bytes 4718596
  130.4 18.4 %collective-permute-start.13 = (bf16[96,3584]{1,0:T(8,128)(2,1)S(1)}, bf16[96,3584]{1,0:T(8,128)(2,1)S(1)}, u32[]{:S(2)}, u32[]{:S(2)}) collective-permute-start(bf16[96,3584]{1,0:T(8,128)(2,1)S(1)} %slice.102), channel_id=1, source_target_pairs={{0,16},{8,24},{16,0},{24,8},{1,17},{9,25},{17,1},{25,9},{2,18},{10... | collective-permute-start | bytes 2064392 | tf_op jit(solution)/shard_map/ppermute | solution.py:62
  131.0 18.4 %collective-permute-start.14 = (bf16[96,3584]{1,0:T(8,128)(2,1)S(1)}, bf16[96,3584]{1,0:T(8,128)(2,1)S(1)}, u32[]{:S(2)}, u32[]{:S(2)}) collective-permute-start(bf16[96,3584]{1,0:T(8,128)(2,1)S(1)} %slice.103), channel_id=1, source_target_pairs={{0,8},{8,0},{16,24},{24,16},{1,9},{9,1},{17,25},{25,17},{2,10},{10... | collective-permute-start | bytes 2064392 | tf_op jit(solution)/shard_map/ppermute | solution.py:63
  132.0 30.2 %collective-permute-start.15 = (bf16[96,3584]{1,0:T(8,128)(2,1)S(1)}, bf16[96,3584]{1,0:T(8,128)(2,1)S(1)}, u32[]{:S(2)}, u32[]{:S(2)}) collective-permute-start(bf16[96,3584]{1,0:T(8,128)(2,1)S(1)} %get-tuple-element.64), channel_id=1, source_target_pairs={{0,8},{8,0},{16,24},{24,16},{1,9},{9,1},{17,25},{25,17},{2,10},{10... | collective-permute-start | bytes 2064392 | tf_op jit(solution)/shard_map/ppermute | solution.py:77
  133.5 28.7 %collective-permute-start.16 = (bf16[96,3584]{1,0:T(8,128)(2,1)S(1)}, bf16[96,3584]{1,0:T(8,128)(2,1)S(1)}, u32[]{:S(2)}, u32[]{:S(2)}) collective-permute-start(bf16[96,3584]{1,0:T(8,128)(2,1)S(1)} %get-tuple-element.63), channel_id=1, source_target_pairs={{0,16},{8,24},{16,0},{24,8},{1,17},{9,25},{17,1},{25,9},{2,18},{10... | collective-permute-start | bytes 2064392 | tf_op jit(solution)/shard_map/ppermute | solution.py:78
  149.5 15.5 %copy-start.4 = (bf16[768,3584]{1,0:T(8,128)(2,1)}, bf16[768,3584]{1,0:T(8,128)(2,1)S(1)}, u32[]{:S(2)}) copy-start(bf16[768,3584]{1,0:T(8,128)(2,1)S(1)} %constant_dynamic-update-slice_fusion.5) | copy-start | bytes 16515076
  162.7 30.3 %collective-permute-start.17 = (bf16[192,3584]{1,0:T(8,128)(2,1)S(1)}, bf16[192,3584]{1,0:T(8,128)(2,1)S(1)}, u32[]{:S(2)}, u32[]{:S(2)}) collective-permute-start(bf16[192,3584]{1,0:T(8,128)(2,1)S(1)} %pad_maximum_fusion), channel_id=1, source_target_pairs={{0,8},{8,0},{16,24},{24,16},{1,9},{9,1},{17,25},{25,17},{2,10},{10... | collective-permute-start | bytes 4128776 | tf_op jit(solution)/shard_map/ppermute | solution.py:94
  163.4 30.0 %collective-permute-start.18 = (bf16[192,3584]{1,0:T(8,128)(2,1)S(1)}, bf16[192,3584]{1,0:T(8,128)(2,1)S(1)}, u32[]{:S(2)}, u32[]{:S(2)}) collective-permute-start(bf16[192,3584]{1,0:T(8,128)(2,1)S(1)} %pad_maximum_fusion.1), channel_id=1, source_target_pairs={{0,16},{8,24},{16,0},{24,8},{1,17},{9,25},{17,1},{25,9},{2,18},{10... | collective-permute-start | bytes 4128776 | tf_op jit(solution)/shard_map/ppermute | solution.py:95
  183.8 27.2 %copy-start.3 = (bf16[768,3584]{1,0:T(8,128)(2,1)}, bf16[768,3584]{1,0:T(8,128)(2,1)S(1)}, u32[]{:S(2)}) copy-start(bf16[768,3584]{1,0:T(8,128)(2,1)S(1)} %add_convert_fusion) | copy-start | bytes 16515076
  195.2 14.4 %collective-permute-start.19 = (bf16[96,3584]{1,0:T(8,128)(2,1)S(1)}, bf16[96,3584]{1,0:T(8,128)(2,1)S(1)}, u32[]{:S(2)}, u32[]{:S(2)}) collective-permute-start(bf16[96,3584]{1,0:T(8,128)(2,1)S(1)} %get-tuple-element.58), channel_id=1, source_target_pairs={{0,16},{8,24},{16,0},{24,8},{1,17},{9,25},{17,1},{25,9},{2,18},{10... | collective-permute-start | bytes 2064392 | tf_op jit(solution)/shard_map/ppermute | solution.py:78
  196.9 14.1 %collective-permute-start.21 = (bf16[96,3584]{1,0:T(8,128)(2,1)S(1)}, bf16[96,3584]{1,0:T(8,128)(2,1)S(1)}, u32[]{:S(2)}, u32[]{:S(2)}) collective-permute-start(bf16[96,3584]{1,0:T(8,128)(2,1)S(1)} %get-tuple-element.57), channel_id=1, source_target_pairs={{0,8},{8,0},{16,24},{24,16},{1,9},{9,1},{17,25},{25,17},{2,10},{10... | collective-permute-start | bytes 2064392 | tf_op jit(solution)/shard_map/ppermute | solution.py:77
  212.4 28.2 %collective-permute-start.20 = (bf16[192,3584]{1,0:T(8,128)(2,1)}, bf16[192,3584]{1,0:T(8,128)(2,1)}, u32[]{:S(2)}, u32[]{:S(2)}) collective-permute-start(bf16[192,3584]{1,0:T(8,128)(2,1)} %pad_maximum_fusion.2), channel_id=1, source_target_pairs={{0,8},{8,0},{16,24},{24,16},{1,9},{9,1},{17,25},{25,17},{2,10},{10... | collective-permute-start | bytes 4128776 | tf_op jit(solution)/shard_map/ppermute | solution.py:94
  214.9 27.9 %collective-permute-start.22 = (bf16[192,3584]{1,0:T(8,128)(2,1)}, bf16[192,3584]{1,0:T(8,128)(2,1)}, u32[]{:S(2)}, u32[]{:S(2)}) collective-permute-start(bf16[192,3584]{1,0:T(8,128)(2,1)} %pad_maximum_fusion.3), channel_id=1, source_target_pairs={{0,16},{8,24},{16,0},{24,8},{1,17},{9,25},{17,1},{25,9},{2,18},{10... | collective-permute-start | bytes 4128776 | tf_op jit(solution)/shard_map/ppermute | solution.py:95
  215.4 43.6 %all-to-all-start.1 = ((bf16[8,24,3584]{2,1,0:T(8,128)(2,1)}), bf16[8,24,3584]{2,1,0:T(8,128)(2,1)S(1)}, u32[]{:S(2)}, u32[]{:S(2)}) async-start(bf16[8,24,3584]{2,1,0:T(8,128)(2,1)} %bitcast.104), calls=%async_computation.1 | async-start | bytes 2752512 | tf_op jit(solution)/shard_map/all_to_all | solution.py:30
  246.6 16.7 %copy-start.12 = (bf16[768,512]{1,0:T(8,128)(2,1)S(1)}, bf16[768,512]{1,0:T(8,128)(2,1)}, u32[]{:S(2)}) copy-start(bf16[768,512]{1,0:T(8,128)(2,1)} %copy-done.11) | copy-start | bytes 2359300
  259.0 37.9 %all-to-all-start.2 = ((bf16[8,24,3584]{2,1,0:T(8,128)(2,1)}), bf16[8,24,3584]{2,1,0:T(8,128)(2,1)}, u32[]{:S(2)}, u32[]{:S(2)}) async-start(bf16[8,24,3584]{2,1,0:T(8,128)(2,1)} %bitcast.106), calls=%async_computation.2 | async-start | bytes 2752512 | tf_op jit(solution)/shard_map/all_to_all | solution.py:106
  286.2 13.4 %copy-start.1 = (bf16[128,3584]{1,0:T(8,128)(2,1)S(1)}, bf16[128,3584]{1,0:T(8,128)(2,1)}, u32[]{:S(2)}) copy-start(bf16[128,3584]{1,0:T(8,128)(2,1)} %param.12) | copy-start | bytes 2752516
  (11 other events, 60.0 us)

commit v10 on v8

--- a/solution.py
+++ b/solution.py
@@ -105,6 +105,7 @@
     rows_dy = contract_first(owner, cotangent).astype(jnp.bfloat16)
     prob_rows = jnp.sum(jnp.where(chosen, gate_probs.reshape(-1)[:, None], 0.0), axis=0)
     send_c = (prob_rows[:, None] * rows_dy.astype(jnp.float32)).astype(jnp.bfloat16)
+    send_x, send_c = lax.optimization_barrier((send_x, send_c))
     rows_x = replicate_dp(along_expert(send_x), groups)
     rows_x, c_along = lax.optimization_barrier((rows_x, along_expert(send_c)))
     c_first = swap_halves_first(c_along, groups)

time: 290 us -> 293 us (1.010)
    unnamed x45 -> x43, local copies, waits for them, and re-layouts: 10.5 us -> 11.2 us
  transfers between devices with their start and end apart: 19 -> 19, of which waited for: 17 -> 17; matrix products, arithmetic and copies ran while one was open for 28% -> 26% of each run, Pallas kernels for 0% -> 0%
where the time goes in v10:
time: 293 us
  waiting for transfers between devices  127 us (43%)
  matrix products  65.9 us (22%)
  blocking collectives  39.8 us (14%)
  starting transfers between devices  30.5 us (10%)
  local copies, waits for them, and re-layouts  15.6 us (5%)
  other arithmetic  12.6 us (4%)
    all_to_all x1, blocking collectives, along_expert(): lax.all_to_all(send_rows, 'expert', split_axis=0, concat_axis=0, tiled=True)  39.8 us
    ppermute x2, waiting for transfers between devices, swap_halves_first(): lax.ppermute(rows, 'dp', perm=pairs(groups, 1))  33.8 us
    dot_general x5, matrix products, contract_first(): lax.dot_general(left, right, (((0,), (0,)), ((), ())), preferred_element_...  25.8 us
    ppermute x2, waiting for transfers between devices, reduce_second(): from_x = lax.ppermute(to_x, 'dp', perm=pairs(groups, 1))  25.2 us
    ppermute x2, waiting for transfers between devices, swap_halves_second(): diag_lo = lax.ppermute(from_x[:half], 'dp', perm=pairs(groups, 2))  20.7 us
    dot_general x3, matrix products, contract_last(): lax.dot_general(left, right, (((1,), (1,)), ((), ())), preferred_element_...  18.6 us
    ppermute x2, waiting for transfers between devices, reduce_first(): lax.ppermute(to_diag[half:], 'dp', perm=pairs(groups, 2))  11.7 us
    unnamed x43, local copies, waits for them, and re-layouts  11.2 us
  transfers between devices with their start and end apart: 19, of which 17 were waited for; matrix products, arithmetic and copies ran while one was open for 26% of the time, Pallas kernels for 0%

profile of v10, /device:TPU:0, one launch (start us, length us, event | category | flops | bytes accessed | tf_op | source)
XLA Modules:
  0.0 292.7 jit_solution(4474561125744877895)
XLA Ops:
  1.7 2.3 reduce-window.6
  8.3 2.5 multiply_convert_fusion
  10.8 39.8 %all_to_all.48 = bf16[8,24,3584]{2,1,0:T(8,128)(2,1)} all-to-all(bf16[8,24,3584]{2,1,0:T(8,128)(2,1)S(1)} %bitcast.79), channel_id=1, replica_groups=mesh['dp'=4,'expert'=8] {'expert'}, dimensions={0} | all-to-all | bytes 2752512 | tf_op jit(solution)/shard_map/all_to_all | solution.py:28
  53.6 3.6 %all-to-all-start.1 = ((bf16[8,24,3584]{2,1,0:T(8,128)(2,1)}), bf16[8,24,3584]{2,1,0:T(8,128)(2,1)S(1)}, u32[]{:S(2)}, u32[]{:S(2)}) async-start(bf16[8,24,3584]{2,1,0:T(8,128)(2,1)} %bitcast.77), calls=%async_computation.1 | async-start | bytes 2752512 | tf_op jit(solution)/shard_map/all_to_all | solution.py:28
  57.2 2.5 constant_dynamic-update-slice_fusion.4
  59.7 23.0 %collective-permute-done = bf16[192,3584]{1,0:T(8,128)(2,1)} collective-permute-done((bf16[192,3584]{1,0:T(8,128)(2,1)}, bf16[192,3584]{1,0:T(8,128)(2,1)}, u32[]{:S(2)}, u32[]{:S(2)}) %collective-permute-start) | collective-permute-done | bytes 1376288 | tf_op jit(solution)/shard_map/ppermute | solution.py:39
  88.2 2.5 constant_dynamic-update-slice_fusion.3
  90.7 2.5 constant_dynamic-update-slice_fusion.2
  93.2 7.0 %collective-permute-done.2 = bf16[96,3584]{1,0:T(8,128)(2,1)S(1)} collective-permute-done((bf16[96,3584]{1,0:T(8,128)(2,1)S(1)}, bf16[96,3584]{1,0:T(8,128)(2,1)S(1)}, u32[]{:S(2)}, u32[]{:S(2)}) %collective-permute-start.2) | collective-permute-done | bytes 688160 | tf_op jit(solution)/shard_map/ppermute | solution.py:49
  105.7 6.2 %fusion.12 = f32[768,512]{1,0:T(8,128)S(1)} fusion(bf16[768,3584]{1,0:T(8,128)(2,1)} %constant_dynamic-update-slice_fusion, bf16[1,3584,512]{2,1,0:T(8,128)(2,1)} %param.11), kind=kOutput, calls=%fused_computation.21 | convolution fusion | flops 2818572288 | bytes 10747904 | tf_op jit(solution)/shard_map/dot_general | solution.py:115
  111.9 7.4 %multiply_convert_fusion.3 = (bf16[768,512]{1,0:T(8,128)(2,1)S(1)}, f32[768,512]{1,0:T(8,128)}) fusion(f32[768,512]{1,0:T(8,128)S(1)} %fusion.12, bf16[768,3584]{1,0:T(8,128)(2,1)} %constant_dynamic-update-slice_fusion, bf16[1,3584,512]{2,1,0:T(8,128)(2,1)S(1)} %copy-done.7), kind=kOutput, calls=%fused_computation.30 | convolution fusion | flops 2820931584 | bytes 13107200 | tf_op jit(solution)/shard_map/dot_general | solution.py:116
  119.3 3.2 %convolution_convert_fusion = bf16[768,3584]{1,0:T(8,128)(2,1)S(1)} fusion(bf16[768,512]{1,0:T(8,128)(2,1)S(1)} %get-tuple-element.39, bf16[1,512,3584]{2,1,0:T(8,128)(2,1)S(1)} %copy-done.5), kind=kOutput, calls=%fused_computation.1 | convolution fusion | flops 2821324800 | bytes 9961472 | tf_op jit(solution)/shard_map/dot_general | solution.py:120
  122.6 10.7 %collective-permute-done.4 = bf16[192,3584]{1,0:T(8,128)(2,1)S(1)} collective-permute-done((bf16[192,3584]{1,0:T(8,128)(2,1)S(1)}, bf16[192,3584]{1,0:T(8,128)(2,1)S(1)}, u32[]{:S(2)}, u32[]{:S(2)}) %collective-permute-start.4) | collective-permute-done | bytes 1376288 | tf_op jit(solution)/shard_map/ppermute | solution.py:39
  140.0 13.7 %collective-permute-done.6 = bf16[96,3584]{1,0:T(8,128)(2,1)S(1)} collective-permute-done((bf16[96,3584]{1,0:T(8,128)(2,1)S(1)}, bf16[96,3584]{1,0:T(8,128)(2,1)S(1)}, u32[]{:S(2)}, u32[]{:S(2)}) %collective-permute-start.6) | collective-permute-done | bytes 688160 | tf_op jit(solution)/shard_map/ppermute | solution.py:49
  154.4 9.8 %collective-permute-done.8 = bf16[96,3584]{1,0:T(8,128)(2,1)S(1)} collective-permute-done((bf16[96,3584]{1,0:T(8,128)(2,1)S(1)}, bf16[96,3584]{1,0:T(8,128)(2,1)S(1)}, u32[]{:S(2)}, u32[]{:S(2)}) %collective-permute-start.8) | collective-permute-done | bytes 688160 | tf_op jit(solution)/shard_map/ppermute | solution.py:64
  165.9 2.2 collective-permute-start.11
  168.1 4.4 %multiply_convert_fusion.1 = (bf16[768,512]{1,0:T(8,128)(2,1)}, bf16[768,512]{1,0:T(8,128)(2,1)S(1)}) fusion(f32[768,512]{1,0:T(8,128)S(1)} %copy-done.14, f32[768,512]{1,0:T(8,128)S(1)} %copy-done.15, bf16[768,3584]{1,0:T(8,128)(2,1)S(1)} %constant_dynamic-update-slice_fusion.5, bf16[1,512,3584]{2,1,0:T(8,128)(2,1)S(1)} %copy-done.5), kind=kOutput, calls=%fused_computation.27 | convolution fusion | flops 2823684096 | bytes 13893632 | tf_op jit(solution)/shard_map/dot_general | solution.py:16
  172.5 5.7 %fusion.10 = f32[768,3584]{1,0:T(8,128)} fusion(bf16[768,512]{1,0:T(8,128)(2,1)S(1)} %get-tuple-element.37, bf16[1,3584,512]{2,1,0:T(8,128)(2,1)S(1)} %copy-done.6), kind=kOutput, calls=%fused_computation.19 | convolution fusion | flops 2818572288 | bytes 15466496 | tf_op jit(solution)/shard_map/dot_general | solution.py:16
  178.2 8.5 %add_convert_fusion = bf16[768,3584]{1,0:T(8,128)(2,1)S(1)} fusion(f32[768,3584]{1,0:T(8,128)} %fusion.10, bf16[768,512]{1,0:T(8,128)(2,1)} %get-tuple-element.38, bf16[1,3584,512]{2,1,0:T(8,128)(2,1)} %param.12), kind=kOutput, calls=%fused_computation | convolution fusion | flops 2824077312 | bytes 20971520 | tf_op jit(solution)/shard_map/dot_general | solution.py:16
  186.8 6.3 %collective-permute-done.10 = bf16[192,3584]{1,0:T(8,128)(2,1)S(1)} collective-permute-done((bf16[192,3584]{1,0:T(8,128)(2,1)S(1)}, bf16[192,3584]{1,0:T(8,128)(2,1)S(1)}, u32[]{:S(2)}, u32[]{:S(2)}) %collective-permute-start.10) | collective-permute-done | bytes 1376288 | tf_op jit(solution)/shard_map/ppermute | solution.py:81
  197.3 11.2 %collective-permute-done.12 = bf16[96,3584]{1,0:T(8,128)(2,1)S(1)} collective-permute-done((bf16[96,3584]{1,0:T(8,128)(2,1)S(1)}, bf16[96,3584]{1,0:T(8,128)(2,1)S(1)}, u32[]{:S(2)}, u32[]{:S(2)}) %collective-permute-start.12) | collective-permute-done | bytes 688160 | tf_op jit(solution)/shard_map/ppermute | solution.py:65
  212.6 2.2 collective-permute-start.15
  214.8 3.6 %all-to-all-start.2 = ((bf16[8,24,3584]{2,1,0:T(8,128)(2,1)}), bf16[8,24,3584]{2,1,0:T(8,128)(2,1)S(1)}, u32[]{:S(2)}, u32[]{:S(2)}) async-start(bf16[8,24,3584]{2,1,0:T(8,128)(2,1)} %bitcast.76), calls=%async_computation.2 | async-start | bytes 2752512 | tf_op jit(solution)/shard_map/all_to_all | solution.py:28
  218.5 18.9 %collective-permute-done.13 = bf16[192,3584]{1,0:T(8,128)(2,1)} collective-permute-done((bf16[192,3584]{1,0:T(8,128)(2,1)}, bf16[192,3584]{1,0:T(8,128)(2,1)}, u32[]{:S(2)}, u32[]{:S(2)}) %collective-permute-start.13) | collective-permute-done | bytes 1376288 | tf_op jit(solution)/shard_map/ppermute | solution.py:81
  237.9 3.8 %add_convert_fusion.1 = bf16[192,3584]{1,0:T(8,128)(2,1)} fusion(bf16[192,3584]{1,0:T(8,128)(2,1)} %collective-permute-done.15, bf16[192,3584]{1,0:T(8,128)(2,1)} %collective-permute-done.13, bf16[768,3584]{1,0:T(8,128)(2,1)} %copy-done.3), kind=kLoop, calls=%fused_computation.24 | loop fusion | flops 4128768 | bytes 5505024 | tf_op jit(solution)/shard_map/convert_element_type | solution.py:84
  241.6 10.4 %all-to-all-done.2 = bf16[8,24,3584]{2,1,0:T(8,128)(2,1)S(1)} async-done(((bf16[8,24,3584]{2,1,0:T(8,128)(2,1)}), bf16[8,24,3584]{2,1,0:T(8,128)(2,1)S(1)}, u32[]{:S(2)}, u32[]{:S(2)}) %all-to-all-start.2) | async-done | bytes 1376288 | tf_op jit(solution)/shard_map/all_to_all | solution.py:28
  252.1 4.3 %all-to-all-start.3 = ((bf16[8,24,3584]{2,1,0:T(8,128)(2,1)}), bf16[8,24,3584]{2,1,0:T(8,128)(2,1)}, u32[]{:S(2)}, u32[]{:S(2)}) async-start(bf16[8,24,3584]{2,1,0:T(8,128)(2,1)} %bitcast.78), calls=%async_computation.3 | async-start | bytes 2752512 | tf_op jit(solution)/shard_map/all_to_all | solution.py:93
  256.4 7.1 %fusion.2 = bf16[1,512,3584]{2,1,0:T(8,128)(2,1)} fusion(bf16[768,512]{1,0:T(8,128)(2,1)S(1)} %copy-done.11, bf16[768,3584]{1,0:T(8,128)(2,1)} %copy-done.4), kind=kOutput, calls=%fused_computation.7 | convolution fusion | flops 2820407296 | bytes 9961472 | tf_op jit(solution)/shard_map/dot_general | solution.py:22
  263.5 7.2 %fusion.1 = bf16[1,3584,512]{2,1,0:T(8,128)(2,1)} fusion(bf16[768,3584]{1,0:T(8,128)(2,1)} %constant_dynamic-update-slice_fusion, bf16[768,512]{1,0:T(8,128)(2,1)S(1)} %copy-done.12), kind=kOutput, calls=%fused_computation.6 | convolution fusion | flops 2820407296 | bytes 9961472 | tf_op jit(solution)/shard_map/dot_general | solution.py:22
  270.7 7.3 %fusion = bf16[1,3584,512]{2,1,0:T(8,128)(2,1)} fusion(bf16[768,3584]{1,0:T(8,128)(2,1)} %constant_dynamic-update-slice_fusion, bf16[768,512]{1,0:T(8,128)(2,1)S(1)} %copy-done.9), kind=kOutput, calls=%fused_computation.5 | convolution fusion | flops 2820407296 | bytes 9961472 | tf_op jit(solution)/shard_map/dot_general | solution.py:22
  281.2 8.8 %all-to-all-done.3 = bf16[8,24,3584]{2,1,0:T(8,128)(2,1)} async-done(((bf16[8,24,3584]{2,1,0:T(8,128)(2,1)}), bf16[8,24,3584]{2,1,0:T(8,128)(2,1)}, u32[]{:S(2)}, u32[]{:S(2)}) %all-to-all-start.3) | async-done | bytes 1376288 | tf_op jit(solution)/shard_map/all_to_all | solution.py:93
  290.0 2.7 convolution_convert_fusion.6
  (97 shorter events, 40.2 us)
Async XLA Ops:
  0.6 7.6 %copy-start = (bf16[128,3584]{1,0:T(8,128)(2,1)S(1)}, bf16[128,3584]{1,0:T(8,128)(2,1)}, u32[]{:S(2)}) copy-start(bf16[128,3584]{1,0:T(8,128)(2,1)} %param.10) | copy-start | bytes 2752516
  50.6 32.2 %collective-permute-start = (bf16[192,3584]{1,0:T(8,128)(2,1)}, bf16[192,3584]{1,0:T(8,128)(2,1)}, u32[]{:S(2)}, u32[]{:S(2)}) collective-permute-start(bf16[192,3584]{1,0:T(8,128)(2,1)} %bitcast.2), channel_id=1, source_target_pairs={{0,8},{8,0},{16,24},{24,16},{1,9},{9,1},{17,25},{25,17},{2,10},{10... | collective-permute-start | bytes 4128776 | tf_op jit(solution)/shard_map/ppermute | solution.py:39
  52.1 33.4 %collective-permute-start.1 = (bf16[192,3584]{1,0:T(8,128)(2,1)}, bf16[192,3584]{1,0:T(8,128)(2,1)}, u32[]{:S(2)}, u32[]{:S(2)}) collective-permute-start(bf16[192,3584]{1,0:T(8,128)(2,1)} %bitcast.2), channel_id=1, source_target_pairs={{0,16},{8,24},{16,0},{24,8},{1,17},{9,25},{17,1},{25,9},{2,18},{10... | collective-permute-start | bytes 4128776 | tf_op jit(solution)/shard_map/ppermute | solution.py:40
  53.6 49.9 %all-to-all-start.1 = ((bf16[8,24,3584]{2,1,0:T(8,128)(2,1)}), bf16[8,24,3584]{2,1,0:T(8,128)(2,1)S(1)}, u32[]{:S(2)}, u32[]{:S(2)}) async-start(bf16[8,24,3584]{2,1,0:T(8,128)(2,1)} %bitcast.77), calls=%async_computation.1 | async-start | bytes 2752512 | tf_op jit(solution)/shard_map/all_to_all | solution.py:28
  83.9 16.3 %collective-permute-start.2 = (bf16[96,3584]{1,0:T(8,128)(2,1)S(1)}, bf16[96,3584]{1,0:T(8,128)(2,1)S(1)}, u32[]{:S(2)}, u32[]{:S(2)}) collective-permute-start(bf16[96,3584]{1,0:T(8,128)(2,1)S(1)} %slice.85), channel_id=1, source_target_pairs={{0,16},{8,24},{16,0},{24,8},{1,17},{9,25},{17,1},{25,9},{2,18},{10... | collective-permute-start | bytes 2064392 | tf_op jit(solution)/shard_map/ppermute | solution.py:49
  86.6 16.0 %collective-permute-start.3 = (bf16[96,3584]{1,0:T(8,128)(2,1)S(1)}, bf16[96,3584]{1,0:T(8,128)(2,1)S(1)}, u32[]{:S(2)}, u32[]{:S(2)}) collective-permute-start(bf16[96,3584]{1,0:T(8,128)(2,1)S(1)} %slice.86), channel_id=1, source_target_pairs={{0,8},{8,0},{16,24},{24,16},{1,9},{9,1},{17,25},{25,17},{2,10},{10... | collective-permute-start | bytes 2064392 | tf_op jit(solution)/shard_map/ppermute | solution.py:50
  103.5 29.8 %collective-permute-start.4 = (bf16[192,3584]{1,0:T(8,128)(2,1)S(1)}, bf16[192,3584]{1,0:T(8,128)(2,1)S(1)}, u32[]{:S(2)}, u32[]{:S(2)}) collective-permute-start(bf16[192,3584]{1,0:T(8,128)(2,1)S(1)} %bitcast.73), channel_id=1, source_target_pairs={{0,8},{8,0},{16,24},{24,16},{1,9},{9,1},{17,25},{25,17},{2,10},{10... | collective-permute-start | bytes 4128776 | tf_op jit(solution)/shard_map/ppermute | solution.py:39
  105.1 30.2 %collective-permute-start.5 = (bf16[192,3584]{1,0:T(8,128)(2,1)S(1)}, bf16[192,3584]{1,0:T(8,128)(2,1)S(1)}, u32[]{:S(2)}, u32[]{:S(2)}) collective-permute-start(bf16[192,3584]{1,0:T(8,128)(2,1)S(1)} %bitcast.74), channel_id=1, source_target_pairs={{0,16},{8,24},{16,0},{24,8},{1,17},{9,25},{17,1},{25,9},{2,18},{10... | collective-permute-start | bytes 4128776 | tf_op jit(solution)/shard_map/ppermute | solution.py:40
  105.6 6.2 %copy-start.7 = (bf16[1,3584,512]{2,1,0:T(8,128)(2,1)S(1)}, bf16[1,3584,512]{2,1,0:T(8,128)(2,1)}, u32[]{:S(2)}) copy-start(bf16[1,3584,512]{2,1,0:T(8,128)(2,1)} %param.12) | copy-start | bytes 11010052
  111.9 7.4 %copy-start.13 = (f32[768,512]{1,0:T(8,128)}, f32[768,512]{1,0:T(8,128)S(1)}, u32[]{:S(2)}) copy-start(f32[768,512]{1,0:T(8,128)S(1)} %fusion.12) | copy-start | bytes 4718596
  111.9 7.4 %copy-start.5 = (bf16[1,512,3584]{2,1,0:T(8,128)(2,1)S(1)}, bf16[1,512,3584]{2,1,0:T(8,128)(2,1)}, u32[]{:S(2)}) copy-start(bf16[1,512,3584]{2,1,0:T(8,128)(2,1)} %param.13) | copy-start | bytes 11010052
  135.3 18.4 %collective-permute-start.6 = (bf16[96,3584]{1,0:T(8,128)(2,1)S(1)}, bf16[96,3584]{1,0:T(8,128)(2,1)S(1)}, u32[]{:S(2)}, u32[]{:S(2)}) collective-permute-start(bf16[96,3584]{1,0:T(8,128)(2,1)S(1)} %slice.70), channel_id=1, source_target_pairs={{0,16},{8,24},{16,0},{24,8},{1,17},{9,25},{17,1},{25,9},{2,18},{10... | collective-permute-start | bytes 2064392 | tf_op jit(solution)/shard_map/ppermute | solution.py:49
  135.9 18.4 %collective-permute-start.7 = (bf16[96,3584]{1,0:T(8,128)(2,1)S(1)}, bf16[96,3584]{1,0:T(8,128)(2,1)S(1)}, u32[]{:S(2)}, u32[]{:S(2)}) collective-permute-start(bf16[96,3584]{1,0:T(8,128)(2,1)S(1)} %slice.71), channel_id=1, source_target_pairs={{0,8},{8,0},{16,24},{24,16},{1,9},{9,1},{17,25},{25,17},{2,10},{10... | collective-permute-start | bytes 2064392 | tf_op jit(solution)/shard_map/ppermute | solution.py:50
  136.9 27.3 %collective-permute-start.8 = (bf16[96,3584]{1,0:T(8,128)(2,1)S(1)}, bf16[96,3584]{1,0:T(8,128)(2,1)S(1)}, u32[]{:S(2)}, u32[]{:S(2)}) collective-permute-start(bf16[96,3584]{1,0:T(8,128)(2,1)S(1)} %get-tuple-element.67), channel_id=1, source_target_pairs={{0,8},{8,0},{16,24},{24,16},{1,9},{9,1},{17,25},{25,17},{2,10},{10... | collective-permute-start | bytes 2064392 | tf_op jit(solution)/shard_map/ppermute | solution.py:64
  138.5 26.3 %collective-permute-start.9 = (bf16[96,3584]{1,0:T(8,128)(2,1)S(1)}, bf16[96,3584]{1,0:T(8,128)(2,1)S(1)}, u32[]{:S(2)}, u32[]{:S(2)}) collective-permute-start(bf16[96,3584]{1,0:T(8,128)(2,1)S(1)} %get-tuple-element.66), channel_id=1, source_target_pairs={{0,16},{8,24},{16,0},{24,8},{1,17},{9,25},{17,1},{25,9},{2,18},{10... | collective-permute-start | bytes 2064392 | tf_op jit(solution)/shard_map/ppermute | solution.py:65
  154.4 13.7 %copy-start.4 = (bf16[768,3584]{1,0:T(8,128)(2,1)}, bf16[768,3584]{1,0:T(8,128)(2,1)S(1)}, u32[]{:S(2)}) copy-start(bf16[768,3584]{1,0:T(8,128)(2,1)S(1)} %constant_dynamic-update-slice_fusion.5) | copy-start | bytes 16515076
  165.2 27.9 %collective-permute-start.10 = (bf16[192,3584]{1,0:T(8,128)(2,1)S(1)}, bf16[192,3584]{1,0:T(8,128)(2,1)S(1)}, u32[]{:S(2)}, u32[]{:S(2)}) collective-permute-start(bf16[192,3584]{1,0:T(8,128)(2,1)S(1)} %pad_maximum_fusion), channel_id=1, source_target_pairs={{0,8},{8,0},{16,24},{24,16},{1,9},{9,1},{17,25},{25,17},{2,10},{10... | collective-permute-start | bytes 4128776 | tf_op jit(solution)/shard_map/ppermute | solution.py:81
  165.8 6.6 %copy-start.6 = (bf16[1,3584,512]{2,1,0:T(8,128)(2,1)S(1)}, bf16[1,3584,512]{2,1,0:T(8,128)(2,1)}, u32[]{:S(2)}) copy-start(bf16[1,3584,512]{2,1,0:T(8,128)(2,1)} %param.11) | copy-start | bytes 11010052
  165.9 28.7 %collective-permute-start.11 = (bf16[192,3584]{1,0:T(8,128)(2,1)S(1)}, bf16[192,3584]{1,0:T(8,128)(2,1)S(1)}, u32[]{:S(2)}, u32[]{:S(2)}) collective-permute-start(bf16[192,3584]{1,0:T(8,128)(2,1)S(1)} %pad_maximum_fusion.1), channel_id=1, source_target_pairs={{0,16},{8,24},{16,0},{24,8},{1,17},{9,25},{17,1},{25,9},{2,18},{10... | collective-permute-start | bytes 4128776 | tf_op jit(solution)/shard_map/ppermute | solution.py:82
  172.5 5.7 %copy-start.8 = (bf16[768,512]{1,0:T(8,128)(2,1)}, bf16[768,512]{1,0:T(8,128)(2,1)S(1)}, u32[]{:S(2)}) copy-start(bf16[768,512]{1,0:T(8,128)(2,1)S(1)} %get-tuple-element.37) | copy-start | bytes 2359300
  186.8 22.6 %copy-start.3 = (bf16[768,3584]{1,0:T(8,128)(2,1)}, bf16[768,3584]{1,0:T(8,128)(2,1)S(1)}, u32[]{:S(2)}) copy-start(bf16[768,3584]{1,0:T(8,128)(2,1)S(1)} %add_convert_fusion) | copy-start | bytes 16515076
  196.3 12.2 %collective-permute-start.12 = (bf16[96,3584]{1,0:T(8,128)(2,1)S(1)}, bf16[96,3584]{1,0:T(8,128)(2,1)S(1)}, u32[]{:S(2)}, u32[]{:S(2)}) collective-permute-start(bf16[96,3584]{1,0:T(8,128)(2,1)S(1)} %get-tuple-element.61), channel_id=1, source_target_pairs={{0,16},{8,24},{16,0},{24,8},{1,17},{9,25},{17,1},{25,9},{2,18},{10... | collective-permute-start | bytes 2064392 | tf_op jit(solution)/shard_map/ppermute | solution.py:65
  196.8 12.6 %collective-permute-start.14 = (bf16[96,3584]{1,0:T(8,128)(2,1)S(1)}, bf16[96,3584]{1,0:T(8,128)(2,1)S(1)}, u32[]{:S(2)}, u32[]{:S(2)}) collective-permute-start(bf16[96,3584]{1,0:T(8,128)(2,1)S(1)} %get-tuple-element.60), channel_id=1, source_target_pairs={{0,8},{8,0},{16,24},{24,16},{1,9},{9,1},{17,25},{25,17},{2,10},{10... | collective-permute-start | bytes 2064392 | tf_op jit(solution)/shard_map/ppermute | solution.py:64
  210.8 26.6 %collective-permute-start.13 = (bf16[192,3584]{1,0:T(8,128)(2,1)}, bf16[192,3584]{1,0:T(8,128)(2,1)}, u32[]{:S(2)}, u32[]{:S(2)}) collective-permute-start(bf16[192,3584]{1,0:T(8,128)(2,1)} %pad_maximum_fusion.2), channel_id=1, source_target_pairs={{0,8},{8,0},{16,24},{24,16},{1,9},{9,1},{17,25},{25,17},{2,10},{10... | collective-permute-start | bytes 4128776 | tf_op jit(solution)/shard_map/ppermute | solution.py:81
  212.6 25.2 %collective-permute-start.15 = (bf16[192,3584]{1,0:T(8,128)(2,1)}, bf16[192,3584]{1,0:T(8,128)(2,1)}, u32[]{:S(2)}, u32[]{:S(2)}) collective-permute-start(bf16[192,3584]{1,0:T(8,128)(2,1)} %pad_maximum_fusion.3), channel_id=1, source_target_pairs={{0,16},{8,24},{16,0},{24,8},{1,17},{9,25},{17,1},{25,9},{2,18},{10... | collective-permute-start | bytes 4128776 | tf_op jit(solution)/shard_map/ppermute | solution.py:82
  214.8 37.3 %all-to-all-start.2 = ((bf16[8,24,3584]{2,1,0:T(8,128)(2,1)}), bf16[8,24,3584]{2,1,0:T(8,128)(2,1)S(1)}, u32[]{:S(2)}, u32[]{:S(2)}) async-start(bf16[8,24,3584]{2,1,0:T(8,128)(2,1)} %bitcast.76), calls=%async_computation.2 | async-start | bytes 2752512 | tf_op jit(solution)/shard_map/all_to_all | solution.py:28
  241.6 14.7 %copy-start.11 = (bf16[768,512]{1,0:T(8,128)(2,1)S(1)}, bf16[768,512]{1,0:T(8,128)(2,1)}, u32[]{:S(2)}) copy-start(bf16[768,512]{1,0:T(8,128)(2,1)} %copy-done.10) | copy-start | bytes 2359300
  252.1 37.9 %all-to-all-start.3 = ((bf16[8,24,3584]{2,1,0:T(8,128)(2,1)}), bf16[8,24,3584]{2,1,0:T(8,128)(2,1)}, u32[]{:S(2)}, u32[]{:S(2)}) async-start(bf16[8,24,3584]{2,1,0:T(8,128)(2,1)} %bitcast.78), calls=%async_computation.3 | async-start | bytes 2752512 | tf_op jit(solution)/shard_map/all_to_all | solution.py:93
  256.4 7.2 %copy-start.12 = (bf16[768,512]{1,0:T(8,128)(2,1)S(1)}, bf16[768,512]{1,0:T(8,128)(2,1)}, u32[]{:S(2)}) copy-start(bf16[768,512]{1,0:T(8,128)(2,1)} %get-tuple-element.38) | copy-start | bytes 2359300
  263.5 7.2 %copy-start.9 = (bf16[768,512]{1,0:T(8,128)(2,1)S(1)}, bf16[768,512]{1,0:T(8,128)(2,1)}, u32[]{:S(2)}) copy-start(bf16[768,512]{1,0:T(8,128)(2,1)} %copy-done.8) | copy-start | bytes 2359300
  270.7 7.3 %copy-start.2 = (f32[192,3584]{1,0:T(8,128)S(1)}, f32[192,3584]{1,0:T(8,128)}, u32[]{:S(2)}) copy-start(f32[192,3584]{1,0:T(8,128)} %get-tuple-element.73) | copy-start | bytes 8257540
  278.0 14.7 %copy-start.1 = (bf16[128,3584]{1,0:T(8,128)(2,1)S(1)}, bf16[128,3584]{1,0:T(8,128)(2,1)}, u32[]{:S(2)}) copy-start(bf16[128,3584]{1,0:T(8,128)(2,1)} %param.10) | copy-start | bytes 2752516
  (3 other events, 9.2 us)

commit v11 on v8

--- a/solution.py
+++ b/solution.py
@@ -138,10 +138,13 @@
         (part_dx, grad_upin, grad_gatein, out_home)
     )
     out_rows = along_expert(out_home).astype(jnp.float32)
-    dx_rows = gather_back(part_dx, groups)
     new_gate = contract_first(rows_x, grad_gatein).astype(jnp.bfloat16)[None]
     new_up = contract_first(rows_x, grad_upin).astype(jnp.bfloat16)[None]
     new_down = contract_first(hidden, rows_c).astype(jnp.bfloat16)[None]
+    dx_home, new_gate, new_up, new_down = lax.optimization_barrier(
+        (reduce_dp(part_dx, groups), new_gate, new_up, new_down)
+    )
+    dx_rows = along_expert(dx_home)
     layer_out = jnp.dot(
         owner.astype(jnp.float32) * prob_rows[None, :],
         out_rows,

time: 290 us -> 284 us (0.979)
  waiting for transfers between devices: 125 us -> 119 us
  matrix products: 65.9 us -> 63 us
    all_to_all x2 -> x3, waiting for transfers between devices: 10.5 us -> 28.7 us  [along_expert(): lax.all_to_all(send_rows, 'expert', split_axis=0, concat_axis=0, tiled=True)]
    ppermute x2, waiting for transfers between devices: 11.7 us -> 2.55 us  [reduce_first(): lax.ppermute(to_diag[half:], 'dp', perm=pairs(groups, 2))]
    all_to_all x1 -> x0, waiting for transfers between devices: 8.8 us -> none  [gather_back(): lax.all_to_all(summed, 'expert', split_axis=0, concat_axis=0, tiled=True)]
    ppermute x2, waiting for transfers between devices: 25.3 us -> 19.8 us  [reduce_second(): from_x = lax.ppermute(to_x, 'dp', perm=pairs(groups, 1))]
    all_to_all x2 -> x3, starting transfers between devices: 7.24 us -> 12 us  [along_expert(): lax.all_to_all(send_rows, 'expert', split_axis=0, concat_axis=0, tiled=True)]
    all_to_all x1 -> x0, starting transfers between devices: 4.28 us -> none  [gather_back(): lax.all_to_all(summed, 'expert', split_axis=0, concat_axis=0, tiled=True)]
  transfers between devices with their start and end apart: 19 -> 19, of which waited for: 17 -> 16; matrix products, arithmetic and copies ran while one was open for 28% -> 28% of each run, Pallas kernels for 0% -> 0%
where the time goes in v11:
time: 284 us; the launch traced here: 283 us
  waiting for transfers between devices  119 us (42%)
  matrix products  63 us (22%)
  blocking collectives  39.8 us (14%)
  starting transfers between devices  31 us (11%)
  local copies, waits for them, and re-layouts  16.2 us (6%)
  other arithmetic  13.2 us (5%)
    all_to_all x1, blocking collectives, along_expert(): lax.all_to_all(send_rows, 'expert', split_axis=0, concat_axis=0, tiled=True)  39.8 us
    ppermute x2, waiting for transfers between devices, swap_halves_first(): lax.ppermute(rows, 'dp', perm=pairs(groups, 1))  30.9 us
    all_to_all x3, waiting for transfers between devices, along_expert(): lax.all_to_all(send_rows, 'expert', split_axis=0, concat_axis=0, tiled=True)  28.7 us
    dot_general x5, matrix products, contract_first(): lax.dot_general(left, right, (((0,), (0,)), ((), ())), preferred_element_...  22.9 us
    ppermute x2, waiting for transfers between devices, swap_halves_second(): diag_lo = lax.ppermute(from_x[:half], 'dp', perm=pairs(groups, 2))  20.7 us
    ppermute x2, waiting for transfers between devices, reduce_second(): from_x = lax.ppermute(to_x, 'dp', perm=pairs(groups, 1))  19.8 us
    dot_general x3, matrix products, contract_last(): lax.dot_general(left, right, (((1,), (1,)), ((), ())), preferred_element_...  18.6 us
    all_to_all x3, starting transfers between devices, along_expert(): lax.all_to_all(send_rows, 'expert', split_axis=0, concat_axis=0, tiled=True)  12 us
  transfers between devices with their start and end apart: 19, of which 16 were waited for; matrix products, arithmetic and copies ran while one was open for 28% of the time, Pallas kernels for 0%

profile of v11, /device:TPU:0, one launch (start us, length us, event | category | flops | bytes accessed | tf_op | source)
XLA Modules:
  0.0 283.2 jit_solution(7608056007320497532)
XLA Ops:
  1.7 2.3 reduce-window.6
  7.2 39.8 %all_to_all.48 = bf16[8,24,3584]{2,1,0:T(8,128)(2,1)} all-to-all(bf16[8,24,3584]{2,1,0:T(8,128)(2,1)S(1)} %bitcast.79), channel_id=1, replica_groups=mesh['dp'=4,'expert'=8] {'expert'}, dimensions={0} | all-to-all | bytes 2752512 | tf_op jit(solution)/shard_map/all_to_all | solution.py:28
  50.4 2.5 multiply_convert_fusion
  52.9 3.6 %all-to-all-start.1 = ((bf16[8,24,3584]{2,1,0:T(8,128)(2,1)}), bf16[8,24,3584]{2,1,0:T(8,128)(2,1)S(1)}, u32[]{:S(2)}, u32[]{:S(2)}) async-start(bf16[8,24,3584]{2,1,0:T(8,128)(2,1)} %bitcast.77), calls=%async_computation.1 | async-start | bytes 2752512 | tf_op jit(solution)/shard_map/all_to_all | solution.py:28
  56.5 2.5 constant_dynamic-update-slice_fusion.4
  59.1 20.2 %collective-permute-done = bf16[192,3584]{1,0:T(8,128)(2,1)} collective-permute-done((bf16[192,3584]{1,0:T(8,128)(2,1)}, bf16[192,3584]{1,0:T(8,128)(2,1)}, u32[]{:S(2)}, u32[]{:S(2)}) %collective-permute-start) | collective-permute-done | bytes 1376288 | tf_op jit(solution)/shard_map/ppermute | solution.py:39
  84.7 2.5 constant_dynamic-update-slice_fusion.3
  87.2 2.5 constant_dynamic-update-slice_fusion.2
  89.7 7.0 %collective-permute-done.2 = bf16[96,3584]{1,0:T(8,128)(2,1)S(1)} collective-permute-done((bf16[96,3584]{1,0:T(8,128)(2,1)S(1)}, bf16[96,3584]{1,0:T(8,128)(2,1)S(1)}, u32[]{:S(2)}, u32[]{:S(2)}) %collective-permute-start.2) | collective-permute-done | bytes 688160 | tf_op jit(solution)/shard_map/ppermute | solution.py:49
  102.1 6.2 %fusion.12 = f32[768,512]{1,0:T(8,128)S(1)} fusion(bf16[768,3584]{1,0:T(8,128)(2,1)} %constant_dynamic-update-slice_fusion, bf16[1,3584,512]{2,1,0:T(8,128)(2,1)} %param.11), kind=kOutput, calls=%fused_computation.21 | convolution fusion | flops 2818572288 | bytes 10747904 | tf_op jit(solution)/shard_map/dot_general | solution.py:114
  108.4 7.4 %multiply_convert_fusion.3 = (bf16[768,512]{1,0:T(8,128)(2,1)S(1)}, f32[768,512]{1,0:T(8,128)}) fusion(f32[768,512]{1,0:T(8,128)S(1)} %fusion.12, bf16[768,3584]{1,0:T(8,128)(2,1)} %constant_dynamic-update-slice_fusion, bf16[1,3584,512]{2,1,0:T(8,128)(2,1)S(1)} %copy-done.8), kind=kOutput, calls=%fused_computation.30 | convolution fusion | flops 2820931584 | bytes 13107200 | tf_op jit(solution)/shard_map/dot_general | solution.py:115
  115.8 3.2 %convolution_convert_fusion = bf16[768,3584]{1,0:T(8,128)(2,1)S(1)} fusion(bf16[768,512]{1,0:T(8,128)(2,1)S(1)} %get-tuple-element.39, bf16[1,512,3584]{2,1,0:T(8,128)(2,1)S(1)} %copy-done.6), kind=kOutput, calls=%fused_computation.1 | convolution fusion | flops 2821324800 | bytes 9961472 | tf_op jit(solution)/shard_map/dot_general | solution.py:119
  119.1 10.7 %collective-permute-done.4 = bf16[192,3584]{1,0:T(8,128)(2,1)S(1)} collective-permute-done((bf16[192,3584]{1,0:T(8,128)(2,1)S(1)}, bf16[192,3584]{1,0:T(8,128)(2,1)S(1)}, u32[]{:S(2)}, u32[]{:S(2)}) %collective-permute-start.4) | collective-permute-done | bytes 1376288 | tf_op jit(solution)/shard_map/ppermute | solution.py:39
  136.5 13.7 %collective-permute-done.6 = bf16[96,3584]{1,0:T(8,128)(2,1)S(1)} collective-permute-done((bf16[96,3584]{1,0:T(8,128)(2,1)S(1)}, bf16[96,3584]{1,0:T(8,128)(2,1)S(1)}, u32[]{:S(2)}, u32[]{:S(2)}) %collective-permute-start.6) | collective-permute-done | bytes 688160 | tf_op jit(solution)/shard_map/ppermute | solution.py:49
  150.9 9.8 %collective-permute-done.8 = bf16[96,3584]{1,0:T(8,128)(2,1)S(1)} collective-permute-done((bf16[96,3584]{1,0:T(8,128)(2,1)S(1)}, bf16[96,3584]{1,0:T(8,128)(2,1)S(1)}, u32[]{:S(2)}, u32[]{:S(2)}) %collective-permute-start.8) | collective-permute-done | bytes 688160 | tf_op jit(solution)/shard_map/ppermute | solution.py:64
  162.3 2.2 collective-permute-start.11
  164.6 4.4 %multiply_convert_fusion.1 = (bf16[768,512]{1,0:T(8,128)(2,1)}, bf16[768,512]{1,0:T(8,128)(2,1)S(1)}) fusion(f32[768,512]{1,0:T(8,128)S(1)} %copy-done.15, f32[768,512]{1,0:T(8,128)S(1)} %copy-done.16, bf16[768,3584]{1,0:T(8,128)(2,1)S(1)} %constant_dynamic-update-slice_fusion.5, bf16[1,512,3584]{2,1,0:T(8,128)(2,1)S(1)} %copy-done.6), kind=kOutput, calls=%fused_computation.27 | convolution fusion | flops 2823684096 | bytes 13893632 | tf_op jit(solution)/shard_map/dot_general | solution.py:16
  169.0 5.7 %fusion.10 = f32[768,3584]{1,0:T(8,128)} fusion(bf16[768,512]{1,0:T(8,128)(2,1)S(1)} %get-tuple-element.37, bf16[1,3584,512]{2,1,0:T(8,128)(2,1)S(1)} %copy-done.7), kind=kOutput, calls=%fused_computation.19 | convolution fusion | flops 2818572288 | bytes 15466496 | tf_op jit(solution)/shard_map/dot_general | solution.py:16
  174.7 8.5 %add_convert_fusion = bf16[768,3584]{1,0:T(8,128)(2,1)S(1)} fusion(f32[768,3584]{1,0:T(8,128)} %fusion.10, bf16[768,512]{1,0:T(8,128)(2,1)} %get-tuple-element.38, bf16[1,3584,512]{2,1,0:T(8,128)(2,1)} %param.12), kind=kOutput, calls=%fused_computation | convolution fusion | flops 2824077312 | bytes 20971520 | tf_op jit(solution)/shard_map/dot_general | solution.py:16
  183.2 6.3 %collective-permute-done.10 = bf16[192,3584]{1,0:T(8,128)(2,1)S(1)} collective-permute-done((bf16[192,3584]{1,0:T(8,128)(2,1)S(1)}, bf16[192,3584]{1,0:T(8,128)(2,1)S(1)}, u32[]{:S(2)}, u32[]{:S(2)}) %collective-permute-start.10) | collective-permute-done | bytes 1376288 | tf_op jit(solution)/shard_map/ppermute | solution.py:81
  194.7 4.5 %fusion.2 = bf16[1,512,3584]{2,1,0:T(8,128)(2,1)} fusion(bf16[768,512]{1,0:T(8,128)(2,1)S(1)} %copy-done.12, bf16[768,3584]{1,0:T(8,128)(2,1)S(1)} %copy-done.4), kind=kOutput, calls=%fused_computation.7 | convolution fusion | flops 2820407296 | bytes 9961472 | tf_op jit(solution)/shard_map/dot_general | solution.py:22
  199.2 3.7 %all-to-all-start.2 = ((bf16[8,24,3584]{2,1,0:T(8,128)(2,1)}), bf16[8,24,3584]{2,1,0:T(8,128)(2,1)S(1)}, u32[]{:S(2)}, u32[]{:S(2)}) async-start(bf16[8,24,3584]{2,1,0:T(8,128)(2,1)} %bitcast.73), calls=%async_computation.2 | async-start | bytes 2752512 | tf_op jit(solution)/shard_map/all_to_all | solution.py:28
  202.9 2.1 collective-permute-done.12
  205.5 2.0 add_convert_fusion.4
  210.0 7.1 %fusion.1 = bf16[1,3584,512]{2,1,0:T(8,128)(2,1)} fusion(bf16[768,3584]{1,0:T(8,128)(2,1)} %constant_dynamic-update-slice_fusion, bf16[768,512]{1,0:T(8,128)(2,1)S(1)} %copy-done.13), kind=kOutput, calls=%fused_computation.6 | convolution fusion | flops 2820407296 | bytes 9961472 | tf_op jit(solution)/shard_map/dot_general | solution.py:22
  217.1 7.1 %fusion = bf16[1,3584,512]{2,1,0:T(8,128)(2,1)} fusion(bf16[768,3584]{1,0:T(8,128)(2,1)} %constant_dynamic-update-slice_fusion, bf16[768,512]{1,0:T(8,128)(2,1)S(1)} %copy-done.10), kind=kOutput, calls=%fused_computation.5 | convolution fusion | flops 2820407296 | bytes 9961472 | tf_op jit(solution)/shard_map/dot_general | solution.py:22
  224.2 13.5 %collective-permute-done.13 = bf16[192,3584]{1,0:T(8,128)(2,1)S(1)} collective-permute-done((bf16[192,3584]{1,0:T(8,128)(2,1)S(1)}, bf16[192,3584]{1,0:T(8,128)(2,1)S(1)}, u32[]{:S(2)}, u32[]{:S(2)}) %collective-permute-start.13) | collective-permute-done | bytes 1376288 | tf_op jit(solution)/shard_map/ppermute | solution.py:81
  239.1 3.0 %add_convert_fusion.1 = bf16[192,3584]{1,0:T(8,128)(2,1)} fusion(bf16[192,3584]{1,0:T(8,128)(2,1)S(1)} %collective-permute-done.15, bf16[192,3584]{1,0:T(8,128)(2,1)S(1)} %collective-permute-done.13, bf16[768,3584]{1,0:T(8,128)(2,1)} %copy-done.2), kind=kLoop, calls=%fused_computation.24 | loop fusion | flops 4128768 | bytes 5505024 | tf_op jit(solution)/shard_map/convert_element_type | solution.py:84
  242.0 4.7 %all-to-all-start.3 = ((bf16[8,24,3584]{2,1,0:T(8,128)(2,1)}), bf16[8,24,3584]{2,1,0:T(8,128)(2,1)}, u32[]{:S(2)}, u32[]{:S(2)}) async-start(bf16[8,24,3584]{2,1,0:T(8,128)(2,1)} %bitcast.78), calls=%async_computation.3 | async-start | bytes 2752512 | tf_op jit(solution)/shard_map/all_to_all | solution.py:28
  246.8 2.2 multiply_reduce_fusion
  251.8 28.7 %all-to-all-done.3 = bf16[8,24,3584]{2,1,0:T(8,128)(2,1)} async-done(((bf16[8,24,3584]{2,1,0:T(8,128)(2,1)}), bf16[8,24,3584]{2,1,0:T(8,128)(2,1)}, u32[]{:S(2)}, u32[]{:S(2)}) %all-to-all-start.3) | async-done | bytes 1376288 | tf_op jit(solution)/shard_map/all_to_all | solution.py:28
  280.5 2.7 convolution_convert_fusion.6
  (99 shorter events, 39.7 us)
Async XLA Ops:
  0.6 49.8 %copy-start = (bf16[128,3584]{1,0:T(8,128)(2,1)S(1)}, bf16[128,3584]{1,0:T(8,128)(2,1)}, u32[]{:S(2)}) copy-start(bf16[128,3584]{1,0:T(8,128)(2,1)} %param.10) | copy-start | bytes 2752516
  1.7 48.4 %copy-start.5 = (f32[128,8]{0,1:T(8,128)S(1)}, f32[128,8]{0,1:T(8,128)}, u32[]{:S(2)}) copy-start(f32[128,8]{0,1:T(8,128)} %param.8) | copy-start | bytes 12292
  47.1 32.2 %collective-permute-start = (bf16[192,3584]{1,0:T(8,128)(2,1)}, bf16[192,3584]{1,0:T(8,128)(2,1)}, u32[]{:S(2)}, u32[]{:S(2)}) collective-permute-start(bf16[192,3584]{1,0:T(8,128)(2,1)} %bitcast.2), channel_id=1, source_target_pairs={{0,8},{8,0},{16,24},{24,16},{1,9},{9,1},{17,25},{25,17},{2,10},{10... | collective-permute-start | bytes 4128776 | tf_op jit(solution)/shard_map/ppermute | solution.py:39
  48.5 33.4 %collective-permute-start.1 = (bf16[192,3584]{1,0:T(8,128)(2,1)}, bf16[192,3584]{1,0:T(8,128)(2,1)}, u32[]{:S(2)}, u32[]{:S(2)}) collective-permute-start(bf16[192,3584]{1,0:T(8,128)(2,1)} %bitcast.2), channel_id=1, source_target_pairs={{0,16},{8,24},{16,0},{24,8},{1,17},{9,25},{17,1},{25,9},{2,18},{10... | collective-permute-start | bytes 4128776 | tf_op jit(solution)/shard_map/ppermute | solution.py:40
  52.9 47.1 %all-to-all-start.1 = ((bf16[8,24,3584]{2,1,0:T(8,128)(2,1)}), bf16[8,24,3584]{2,1,0:T(8,128)(2,1)S(1)}, u32[]{:S(2)}, u32[]{:S(2)}) async-start(bf16[8,24,3584]{2,1,0:T(8,128)(2,1)} %bitcast.77), calls=%async_computation.1 | async-start | bytes 2752512 | tf_op jit(solution)/shard_map/all_to_all | solution.py:28
  80.4 16.3 %collective-permute-start.2 = (bf16[96,3584]{1,0:T(8,128)(2,1)S(1)}, bf16[96,3584]{1,0:T(8,128)(2,1)S(1)}, u32[]{:S(2)}, u32[]{:S(2)}) collective-permute-start(bf16[96,3584]{1,0:T(8,128)(2,1)S(1)} %slice.85), channel_id=1, source_target_pairs={{0,16},{8,24},{16,0},{24,8},{1,17},{9,25},{17,1},{25,9},{2,18},{10... | collective-permute-start | bytes 2064392 | tf_op jit(solution)/shard_map/ppermute | solution.py:49
  83.1 16.0 %collective-permute-start.3 = (bf16[96,3584]{1,0:T(8,128)(2,1)S(1)}, bf16[96,3584]{1,0:T(8,128)(2,1)S(1)}, u32[]{:S(2)}, u32[]{:S(2)}) collective-permute-start(bf16[96,3584]{1,0:T(8,128)(2,1)S(1)} %slice.86), channel_id=1, source_target_pairs={{0,8},{8,0},{16,24},{24,16},{1,9},{9,1},{17,25},{25,17},{2,10},{10... | collective-permute-start | bytes 2064392 | tf_op jit(solution)/shard_map/ppermute | solution.py:50
  100.0 29.8 %collective-permute-start.4 = (bf16[192,3584]{1,0:T(8,128)(2,1)S(1)}, bf16[192,3584]{1,0:T(8,128)(2,1)S(1)}, u32[]{:S(2)}, u32[]{:S(2)}) collective-permute-start(bf16[192,3584]{1,0:T(8,128)(2,1)S(1)} %bitcast.74), channel_id=1, source_target_pairs={{0,8},{8,0},{16,24},{24,16},{1,9},{9,1},{17,25},{25,17},{2,10},{10... | collective-permute-start | bytes 4128776 | tf_op jit(solution)/shard_map/ppermute | solution.py:39
  101.5 30.2 %collective-permute-start.5 = (bf16[192,3584]{1,0:T(8,128)(2,1)S(1)}, bf16[192,3584]{1,0:T(8,128)(2,1)S(1)}, u32[]{:S(2)}, u32[]{:S(2)}) collective-permute-start(bf16[192,3584]{1,0:T(8,128)(2,1)S(1)} %bitcast.75), channel_id=1, source_target_pairs={{0,16},{8,24},{16,0},{24,8},{1,17},{9,25},{17,1},{25,9},{2,18},{10... | collective-permute-start | bytes 4128776 | tf_op jit(solution)/shard_map/ppermute | solution.py:40
  102.1 6.2 %copy-start.8 = (bf16[1,3584,512]{2,1,0:T(8,128)(2,1)S(1)}, bf16[1,3584,512]{2,1,0:T(8,128)(2,1)}, u32[]{:S(2)}) copy-start(bf16[1,3584,512]{2,1,0:T(8,128)(2,1)} %param.12) | copy-start | bytes 11010052
  108.4 7.4 %copy-start.14 = (f32[768,512]{1,0:T(8,128)}, f32[768,512]{1,0:T(8,128)S(1)}, u32[]{:S(2)}) copy-start(f32[768,512]{1,0:T(8,128)S(1)} %fusion.12) | copy-start | bytes 4718596
  108.4 7.4 %copy-start.6 = (bf16[1,512,3584]{2,1,0:T(8,128)(2,1)S(1)}, bf16[1,512,3584]{2,1,0:T(8,128)(2,1)}, u32[]{:S(2)}) copy-start(bf16[1,512,3584]{2,1,0:T(8,128)(2,1)} %param.13) | copy-start | bytes 11010052
  115.8 3.3 %copy-start.11 = (bf16[768,512]{1,0:T(8,128)(2,1)}, bf16[768,512]{1,0:T(8,128)(2,1)S(1)}, u32[]{:S(2)}) copy-start(bf16[768,512]{1,0:T(8,128)(2,1)S(1)} %get-tuple-element.39) | copy-start | bytes 2359300
  131.8 18.4 %collective-permute-start.6 = (bf16[96,3584]{1,0:T(8,128)(2,1)S(1)}, bf16[96,3584]{1,0:T(8,128)(2,1)S(1)}, u32[]{:S(2)}, u32[]{:S(2)}) collective-permute-start(bf16[96,3584]{1,0:T(8,128)(2,1)S(1)} %slice.70), channel_id=1, source_target_pairs={{0,16},{8,24},{16,0},{24,8},{1,17},{9,25},{17,1},{25,9},{2,18},{10... | collective-permute-start | bytes 2064392 | tf_op jit(solution)/shard_map/ppermute | solution.py:49
  132.4 18.4 %collective-permute-start.7 = (bf16[96,3584]{1,0:T(8,128)(2,1)S(1)}, bf16[96,3584]{1,0:T(8,128)(2,1)S(1)}, u32[]{:S(2)}, u32[]{:S(2)}) collective-permute-start(bf16[96,3584]{1,0:T(8,128)(2,1)S(1)} %slice.71), channel_id=1, source_target_pairs={{0,8},{8,0},{16,24},{24,16},{1,9},{9,1},{17,25},{25,17},{2,10},{10... | collective-permute-start | bytes 2064392 | tf_op jit(solution)/shard_map/ppermute | solution.py:50
  133.4 27.4 %collective-permute-start.8 = (bf16[96,3584]{1,0:T(8,128)(2,1)S(1)}, bf16[96,3584]{1,0:T(8,128)(2,1)S(1)}, u32[]{:S(2)}, u32[]{:S(2)}) collective-permute-start(bf16[96,3584]{1,0:T(8,128)(2,1)S(1)} %get-tuple-element.71), channel_id=1, source_target_pairs={{0,8},{8,0},{16,24},{24,16},{1,9},{9,1},{17,25},{25,17},{2,10},{10... | collective-permute-start | bytes 2064392 | tf_op jit(solution)/shard_map/ppermute | solution.py:64
  135.0 26.3 %collective-permute-start.9 = (bf16[96,3584]{1,0:T(8,128)(2,1)S(1)}, bf16[96,3584]{1,0:T(8,128)(2,1)S(1)}, u32[]{:S(2)}, u32[]{:S(2)}) collective-permute-start(bf16[96,3584]{1,0:T(8,128)(2,1)S(1)} %get-tuple-element.70), channel_id=1, source_target_pairs={{0,16},{8,24},{16,0},{24,8},{1,17},{9,25},{17,1},{25,9},{2,18},{10... | collective-permute-start | bytes 2064392 | tf_op jit(solution)/shard_map/ppermute | solution.py:65
  150.9 13.6 %copy-start.3 = (bf16[768,3584]{1,0:T(8,128)(2,1)}, bf16[768,3584]{1,0:T(8,128)(2,1)S(1)}, u32[]{:S(2)}) copy-start(bf16[768,3584]{1,0:T(8,128)(2,1)S(1)} %constant_dynamic-update-slice_fusion.5) | copy-start | bytes 16515076
  161.7 27.8 %collective-permute-start.10 = (bf16[192,3584]{1,0:T(8,128)(2,1)S(1)}, bf16[192,3584]{1,0:T(8,128)(2,1)S(1)}, u32[]{:S(2)}, u32[]{:S(2)}) collective-permute-start(bf16[192,3584]{1,0:T(8,128)(2,1)S(1)} %pad_maximum_fusion), channel_id=1, source_target_pairs={{0,8},{8,0},{16,24},{24,16},{1,9},{9,1},{17,25},{25,17},{2,10},{10... | collective-permute-start | bytes 4128776 | tf_op jit(solution)/shard_map/ppermute | solution.py:81
  162.3 6.6 %copy-start.7 = (bf16[1,3584,512]{2,1,0:T(8,128)(2,1)S(1)}, bf16[1,3584,512]{2,1,0:T(8,128)(2,1)}, u32[]{:S(2)}) copy-start(bf16[1,3584,512]{2,1,0:T(8,128)(2,1)} %param.11) | copy-start | bytes 11010052
  162.3 27.7 %collective-permute-start.11 = (bf16[192,3584]{1,0:T(8,128)(2,1)S(1)}, bf16[192,3584]{1,0:T(8,128)(2,1)S(1)}, u32[]{:S(2)}, u32[]{:S(2)}) collective-permute-start(bf16[192,3584]{1,0:T(8,128)(2,1)S(1)} %pad_maximum_fusion.1), channel_id=1, source_target_pairs={{0,16},{8,24},{16,0},{24,8},{1,17},{9,25},{17,1},{25,9},{2,18},{10... | collective-permute-start | bytes 4128776 | tf_op jit(solution)/shard_map/ppermute | solution.py:82
  168.9 5.7 %copy-start.9 = (bf16[768,512]{1,0:T(8,128)(2,1)}, bf16[768,512]{1,0:T(8,128)(2,1)S(1)}, u32[]{:S(2)}) copy-start(bf16[768,512]{1,0:T(8,128)(2,1)S(1)} %get-tuple-element.37) | copy-start | bytes 2359300
  183.2 8.4 %copy-start.2 = (bf16[768,3584]{1,0:T(8,128)(2,1)}, bf16[768,3584]{1,0:T(8,128)(2,1)S(1)}, u32[]{:S(2)}) copy-start(bf16[768,3584]{1,0:T(8,128)(2,1)S(1)} %add_convert_fusion) | copy-start | bytes 16515076
  190.0 4.5 %copy-start.12 = (bf16[768,512]{1,0:T(8,128)(2,1)S(1)}, bf16[768,512]{1,0:T(8,128)(2,1)}, u32[]{:S(2)}) copy-start(bf16[768,512]{1,0:T(8,128)(2,1)} %copy-done.11) | copy-start | bytes 2359300
  192.9 12.1 %collective-permute-start.12 = (bf16[96,3584]{1,0:T(8,128)(2,1)}, bf16[96,3584]{1,0:T(8,128)(2,1)}, u32[]{:S(2)}, u32[]{:S(2)}) collective-permute-start(bf16[96,3584]{1,0:T(8,128)(2,1)} %get-tuple-element.65), channel_id=1, source_target_pairs={{0,16},{8,24},{16,0},{24,8},{1,17},{9,25},{17,1},{25,9},{2,18},{10... | collective-permute-start | bytes 2064392 | tf_op jit(solution)/shard_map/ppermute | solution.py:65
  193.9 11.6 %collective-permute-start.14 = (bf16[96,3584]{1,0:T(8,128)(2,1)}, bf16[96,3584]{1,0:T(8,128)(2,1)}, u32[]{:S(2)}, u32[]{:S(2)}) collective-permute-start(bf16[96,3584]{1,0:T(8,128)(2,1)} %get-tuple-element.64), channel_id=1, source_target_pairs={{0,8},{8,0},{16,24},{24,16},{1,9},{9,1},{17,25},{25,17},{2,10},{10... | collective-permute-start | bytes 2064392 | tf_op jit(solution)/shard_map/ppermute | solution.py:64
  199.2 42.8 %all-to-all-start.2 = ((bf16[8,24,3584]{2,1,0:T(8,128)(2,1)}), bf16[8,24,3584]{2,1,0:T(8,128)(2,1)S(1)}, u32[]{:S(2)}, u32[]{:S(2)}) async-start(bf16[8,24,3584]{2,1,0:T(8,128)(2,1)} %bitcast.73), calls=%async_computation.2 | async-start | bytes 2752512 | tf_op jit(solution)/shard_map/all_to_all | solution.py:28
  207.7 30.1 %collective-permute-start.13 = (bf16[192,3584]{1,0:T(8,128)(2,1)S(1)}, bf16[192,3584]{1,0:T(8,128)(2,1)S(1)}, u32[]{:S(2)}, u32[]{:S(2)}) collective-permute-start(bf16[192,3584]{1,0:T(8,128)(2,1)S(1)} %pad_maximum_fusion.2), channel_id=1, source_target_pairs={{0,8},{8,0},{16,24},{24,16},{1,9},{9,1},{17,25},{25,17},{2,10},{10... | collective-permute-start | bytes 4128776 | tf_op jit(solution)/shard_map/ppermute | solution.py:81
  208.4 8.7 %copy-start.10 = (bf16[768,512]{1,0:T(8,128)(2,1)S(1)}, bf16[768,512]{1,0:T(8,128)(2,1)}, u32[]{:S(2)}) copy-start(bf16[768,512]{1,0:T(8,128)(2,1)} %copy-done.9) | copy-start | bytes 2359300
  208.4 30.7 %collective-permute-start.15 = (bf16[192,3584]{1,0:T(8,128)(2,1)S(1)}, bf16[192,3584]{1,0:T(8,128)(2,1)S(1)}, u32[]{:S(2)}, u32[]{:S(2)}) collective-permute-start(bf16[192,3584]{1,0:T(8,128)(2,1)S(1)} %pad_maximum_fusion.3), channel_id=1, source_target_pairs={{0,16},{8,24},{16,0},{24,8},{1,17},{9,25},{17,1},{25,9},{2,18},{10... | collective-permute-start | bytes 4128776 | tf_op jit(solution)/shard_map/ppermute | solution.py:82
  242.0 38.5 %all-to-all-start.3 = ((bf16[8,24,3584]{2,1,0:T(8,128)(2,1)}), bf16[8,24,3584]{2,1,0:T(8,128)(2,1)}, u32[]{:S(2)}, u32[]{:S(2)}) async-start(bf16[8,24,3584]{2,1,0:T(8,128)(2,1)} %bitcast.78), calls=%async_computation.3 | async-start | bytes 2752512 | tf_op jit(solution)/shard_map/all_to_all | solution.py:28
  246.8 36.4 %copy-start.1 = (bf16[128,3584]{1,0:T(8,128)(2,1)S(1)}, bf16[128,3584]{1,0:T(8,128)(2,1)}, u32[]{:S(2)}) copy-start(bf16[128,3584]{1,0:T(8,128)(2,1)} %param.10) | copy-start | bytes 2752516
  (4 other events, 11.5 us)

commit v12 on v11

--- a/solution.py
+++ b/solution.py
@@ -80,12 +80,19 @@
     )
     from_x = lax.ppermute(to_x, "dp", perm=pairs(groups, 1))
     from_y = lax.ppermute(to_y, "dp", perm=pairs(groups, 2))
+    return own, from_x, from_y
+
+
+def add_parts(parts):
+    if not isinstance(parts, tuple):
+        return parts
+    own, from_x, from_y = parts
     total = own.astype(jnp.float32) + from_x.astype(jnp.float32) + from_y.astype(jnp.float32)
     return total.astype(jnp.bfloat16)
 
 
 def reduce_dp(partial_rows, groups):
-    return reduce_second(partial_rows, reduce_first(partial_rows, groups), groups)
+    return add_parts(reduce_second(partial_rows, reduce_first(partial_rows, groups), groups))
 
 
 def gather_back(partial_rows, groups):
@@ -125,7 +132,7 @@
     out_first = reduce_first(part_out, groups)
     rows_c = swap_halves_second(c_along, c_first, groups)
     rows_c, out_first = lax.optimization_barrier((rows_c, out_first))
-    out_home = reduce_second(part_out, out_first, groups)
+    out_parts = reduce_second(part_out, out_first, groups)
     grad_hidden = contract_last(rows_c, down_w)
     grad_upin = (grad_hidden * activated).astype(jnp.bfloat16)
     grad_gatein = (grad_hidden * up_pre * sigmoid_g * (1.0 + gate_pre * (1.0 - sigmoid_g))).astype(
@@ -134,10 +141,10 @@
     part_dx = (contract_last(grad_gatein, gate_w) + contract_last(grad_upin, up_w)).astype(
         jnp.bfloat16
     )
-    part_dx, grad_upin, grad_gatein, out_home = lax.optimization_barrier(
-        (part_dx, grad_upin, grad_gatein, out_home)
+    part_dx, grad_upin, grad_gatein, out_parts = lax.optimization_barrier(
+        (part_dx, grad_upin, grad_gatein, out_parts)
     )
-    out_rows = along_expert(out_home).astype(jnp.float32)
+    out_rows = along_expert(add_parts(out_parts)).astype(jnp.float32)
     new_gate = contract_first(rows_x, grad_gatein).astype(jnp.bfloat16)[None]
     new_up = contract_first(rows_x, grad_upin).astype(jnp.bfloat16)[None]
     new_down = contract_first(hidden, rows_c).astype(jnp.bfloat16)[None]

time: 284 us -> 281 us (0.989)
  matrix products: 63 us -> 59 us
  waiting for transfers between devices: 119 us -> 122 us
    ppermute x2, waiting for transfers between devices: 1.96 us -> 33 us  [swap_halves_first(): lax.ppermute(rows, 'dp', perm=pairs(groups, 2))]
    ppermute x2, waiting for transfers between devices: 30.9 us -> 1.71 us  [swap_halves_first(): lax.ppermute(rows, 'dp', perm=pairs(groups, 1))]
    ppermute x2, waiting for transfers between devices: 19.8 us -> 7.59 us  [reduce_second(): from_x = lax.ppermute(to_x, 'dp', perm=pairs(groups, 1))]
    ppermute x2, waiting for transfers between devices: 1.83 us -> 10.6 us  [reduce_second(): from_y = lax.ppermute(to_y, 'dp', perm=pairs(groups, 2))]
    ppermute x2, waiting for transfers between devices: 2.55 us -> 9.86 us  [reduce_first(): lax.ppermute(to_diag[half:], 'dp', perm=pairs(groups, 2))]
    ppermute x2, waiting for transfers between devices: 10.4 us -> 6.76 us  [reduce_first(): lax.ppermute(to_diag[:half], 'dp', perm=pairs(groups, 1))]
    ppermute x2, waiting for transfers between devices: 20.7 us -> 24.1 us  [swap_halves_second(): diag_lo = lax.ppermute(from_x[:half], 'dp', perm=pairs(groups, 2))]
    unnamed x45 -> x35, local copies, waits for them, and re-layouts: 10.7 us -> 10.5 us
  transfers between devices with their start and end apart: 19 -> 19, of which waited for: 16 -> 12; matrix products, arithmetic and copies ran while one was open for 28% -> 27% of each run, Pallas kernels for 0% -> 0%
where the time goes in v12:
time: 281 us; the launch traced here: 280 us
  waiting for transfers between devices  122 us (43%)
  matrix products  59 us (21%)
  blocking collectives  39.8 us (14%)
  starting transfers between devices  29 us (10%)
  local copies, waits for them, and re-layouts  16 us (6%)
  other arithmetic  13.2 us (5%)
    all_to_all x1, blocking collectives, along_expert(): lax.all_to_all(send_rows, 'expert', split_axis=0, concat_axis=0, tiled=True)  39.8 us
    ppermute x2, waiting for transfers between devices, swap_halves_first(): lax.ppermute(rows, 'dp', perm=pairs(groups, 2))  33 us
    all_to_all x3, waiting for transfers between devices, along_expert(): lax.all_to_all(send_rows, 'expert', split_axis=0, concat_axis=0, tiled=True)  28.7 us
    ppermute x2, waiting for transfers between devices, swap_halves_second(): diag_lo = lax.ppermute(from_x[:half], 'dp', perm=pairs(groups, 2))  24.1 us
    dot_general x5, matrix products, contract_first(): lax.dot_general(left, right, (((0,), (0,)), ((), ())), preferred_element_...  22.9 us
    dot_general x3, matrix products, contract_last(): lax.dot_general(left, right, (((1,), (1,)), ((), ())), preferred_element_...  16.7 us
    all_to_all x3, starting transfers between devices, along_expert(): lax.all_to_all(send_rows, 'expert', split_axis=0, concat_axis=0, tiled=True)  12.2 us
    ppermute x2, waiting for transfers between devices, reduce_second(): from_y = lax.ppermute(to_y, 'dp', perm=pairs(groups, 2))  10.6 us
  transfers between devices with their start and end apart: 19, of which 12 were waited for; matrix products, arithmetic and copies ran while one was open for 27% of the time, Pallas kernels for 0%

profile of v12, /device:TPU:0, one launch (start us, length us, event | category | flops | bytes accessed | tf_op | source)
XLA Modules:
  0.0 280.3 jit_solution(3361070730494901314)
XLA Ops:
  1.7 2.3 reduce-window.6
  7.2 39.8 %all_to_all.48 = bf16[8,24,3584]{2,1,0:T(8,128)(2,1)} all-to-all(bf16[8,24,3584]{2,1,0:T(8,128)(2,1)S(1)} %bitcast.79), channel_id=1, replica_groups=mesh['dp'=4,'expert'=8] {'expert'}, dimensions={0} | all-to-all | bytes 2752512 | tf_op jit(solution)/shard_map/all_to_all | solution.py:28
  50.4 2.5 multiply_convert_fusion
  52.9 3.6 %all-to-all-start.1 = ((bf16[8,24,3584]{2,1,0:T(8,128)(2,1)}), bf16[8,24,3584]{2,1,0:T(8,128)(2,1)S(1)}, u32[]{:S(2)}, u32[]{:S(2)}) async-start(bf16[8,24,3584]{2,1,0:T(8,128)(2,1)} %bitcast.77), calls=%async_computation.1 | async-start | bytes 2752512 | tf_op jit(solution)/shard_map/all_to_all | solution.py:28
  56.5 2.5 constant_dynamic-update-slice_fusion.4
  59.0 20.2 %collective-permute-done.1 = bf16[192,3584]{1,0:T(8,128)(2,1)} collective-permute-done((bf16[192,3584]{1,0:T(8,128)(2,1)}, bf16[192,3584]{1,0:T(8,128)(2,1)}, u32[]{:S(2)}, u32[]{:S(2)}) %collective-permute-start.1) | collective-permute-done | bytes 1376288 | tf_op jit(solution)/shard_map/ppermute | solution.py:40
  84.7 2.5 constant_dynamic-update-slice_fusion.3
  87.2 2.5 constant_dynamic-update-slice_fusion.2
  89.7 9.4 %collective-permute-done.2 = bf16[96,3584]{1,0:T(8,128)(2,1)S(1)} collective-permute-done((bf16[96,3584]{1,0:T(8,128)(2,1)S(1)}, bf16[96,3584]{1,0:T(8,128)(2,1)S(1)}, u32[]{:S(2)}, u32[]{:S(2)}) %collective-permute-start.2) | collective-permute-done | bytes 688160 | tf_op jit(solution)/shard_map/ppermute | solution.py:49
  103.1 6.2 %fusion.12 = f32[768,512]{1,0:T(8,128)S(1)} fusion(bf16[768,3584]{1,0:T(8,128)(2,1)} %constant_dynamic-update-slice_fusion, bf16[1,3584,512]{2,1,0:T(8,128)(2,1)} %param.11), kind=kOutput, calls=%fused_computation.21 | convolution fusion | flops 2818572288 | bytes 10747904 | tf_op jit(solution)/shard_map/dot_general | solution.py:121
  109.3 5.2 %multiply_convert_fusion.3 = (bf16[768,512]{1,0:T(8,128)(2,1)S(1)}, f32[768,512]{1,0:T(8,128)S(1)}) fusion(f32[768,512]{1,0:T(8,128)S(1)} %fusion.12, bf16[768,3584]{1,0:T(8,128)(2,1)} %constant_dynamic-update-slice_fusion, bf16[1,3584,512]{2,1,0:T(8,128)(2,1)S(1)} %copy-done.7), kind=kOutput, calls=%fused_computation.30 | convolution fusion | flops 2820931584 | bytes 13107200 | tf_op jit(solution)/shard_map/dot_general | solution.py:122
  114.6 3.2 %convolution_convert_fusion = bf16[768,3584]{1,0:T(8,128)(2,1)S(1)} fusion(bf16[768,512]{1,0:T(8,128)(2,1)S(1)} %get-tuple-element.43, bf16[1,512,3584]{2,1,0:T(8,128)(2,1)S(1)} %copy-done.5), kind=kOutput, calls=%fused_computation.1 | convolution fusion | flops 2821324800 | bytes 9961472 | tf_op jit(solution)/shard_map/dot_general | solution.py:126
  117.8 12.8 %collective-permute-done.5 = bf16[192,3584]{1,0:T(8,128)(2,1)S(1)} collective-permute-done((bf16[192,3584]{1,0:T(8,128)(2,1)S(1)}, bf16[192,3584]{1,0:T(8,128)(2,1)S(1)}, u32[]{:S(2)}, u32[]{:S(2)}) %collective-permute-start.5) | collective-permute-done | bytes 1376288 | tf_op jit(solution)/shard_map/ppermute | solution.py:40
  137.0 14.7 %collective-permute-done.6 = bf16[96,3584]{1,0:T(8,128)(2,1)S(1)} collective-permute-done((bf16[96,3584]{1,0:T(8,128)(2,1)S(1)}, bf16[96,3584]{1,0:T(8,128)(2,1)S(1)}, u32[]{:S(2)}, u32[]{:S(2)}) %collective-permute-start.6) | collective-permute-done | bytes 688160 | tf_op jit(solution)/shard_map/ppermute | solution.py:49
  151.8 9.9 %collective-permute-done.9 = bf16[96,3584]{1,0:T(8,128)(2,1)S(1)} collective-permute-done((bf16[96,3584]{1,0:T(8,128)(2,1)S(1)}, bf16[96,3584]{1,0:T(8,128)(2,1)S(1)}, u32[]{:S(2)}, u32[]{:S(2)}) %collective-permute-start.9) | collective-permute-done | bytes 688160 | tf_op jit(solution)/shard_map/ppermute | solution.py:65
  164.4 4.5 %fusion.2 = bf16[1,512,3584]{2,1,0:T(8,128)(2,1)} fusion(bf16[768,512]{1,0:T(8,128)(2,1)S(1)} %get-tuple-element.43, bf16[768,3584]{1,0:T(8,128)(2,1)S(1)} %constant_dynamic-update-slice_fusion.5), kind=kOutput, calls=%fused_computation.7 | convolution fusion | flops 2820407296 | bytes 9961472 | tf_op jit(solution)/shard_map/dot_general | solution.py:22
  168.9 3.5 %multiply_convert_fusion.1 = (bf16[768,512]{1,0:T(8,128)(2,1)S(1)}, bf16[768,512]{1,0:T(8,128)(2,1)S(1)}) fusion(f32[768,512]{1,0:T(8,128)S(1)} %fusion.12, f32[768,512]{1,0:T(8,128)S(1)} %get-tuple-element.33, bf16[768,3584]{1,0:T(8,128)(2,1)S(1)} %constant_dynamic-update-slice_fusion.5, bf16[1,512,3584]{2,1,0:T(8,128)(2,1)S(1)} %copy-done.5), kind=kOutput, calls=%fused_computation.27 | convolution fusion | flops 2823684096 | bytes 13893632 | tf_op jit(solution)/shard_map/dot_general | solution.py:16
  172.5 5.8 %fusion.10 = f32[768,3584]{1,0:T(8,128)} fusion(bf16[768,512]{1,0:T(8,128)(2,1)S(1)} %get-tuple-element.41, bf16[1,3584,512]{2,1,0:T(8,128)(2,1)S(1)} %copy-done.6), kind=kOutput, calls=%fused_computation.19 | convolution fusion | flops 2818572288 | bytes 15466496 | tf_op jit(solution)/shard_map/dot_general | solution.py:16
  178.3 7.4 %add_convert_fusion = bf16[768,3584]{1,0:T(8,128)(2,1)S(1)} fusion(f32[768,3584]{1,0:T(8,128)} %fusion.10, bf16[768,512]{1,0:T(8,128)(2,1)S(1)} %get-tuple-element.42, bf16[1,3584,512]{2,1,0:T(8,128)(2,1)} %param.12), kind=kOutput, calls=%fused_computation | convolution fusion | flops 2824077312 | bytes 20971520 | tf_op jit(solution)/shard_map/dot_general | solution.py:16
  185.7 6.3 %collective-permute-done.10 = bf16[192,3584]{1,0:T(8,128)(2,1)S(1)} collective-permute-done((bf16[192,3584]{1,0:T(8,128)(2,1)S(1)}, bf16[192,3584]{1,0:T(8,128)(2,1)S(1)}, u32[]{:S(2)}, u32[]{:S(2)}) %collective-permute-start.10) | collective-permute-done | bytes 1376288 | tf_op jit(solution)/shard_map/ppermute | solution.py:81
  196.1 3.9 %all-to-all-start.2 = ((bf16[8,24,3584]{2,1,0:T(8,128)(2,1)}), bf16[8,24,3584]{2,1,0:T(8,128)(2,1)S(1)}, u32[]{:S(2)}, u32[]{:S(2)}) async-start(bf16[8,24,3584]{2,1,0:T(8,128)(2,1)} %bitcast.76), calls=%async_computation.2 | async-start | bytes 2752512 | tf_op jit(solution)/shard_map/all_to_all | solution.py:28
  200.0 5.8 %collective-permute-done.14 = bf16[96,3584]{1,0:T(8,128)(2,1)} collective-permute-done((bf16[96,3584]{1,0:T(8,128)(2,1)}, bf16[96,3584]{1,0:T(8,128)(2,1)}, u32[]{:S(2)}, u32[]{:S(2)}) %collective-permute-start.14) | collective-permute-done | bytes 688160 | tf_op jit(solution)/shard_map/ppermute | solution.py:64
  205.7 2.0 add_convert_fusion.4
  210.0 7.1 %fusion = bf16[1,3584,512]{2,1,0:T(8,128)(2,1)} fusion(bf16[768,3584]{1,0:T(8,128)(2,1)} %constant_dynamic-update-slice_fusion, bf16[768,512]{1,0:T(8,128)(2,1)S(1)} %copy-done.9), kind=kOutput, calls=%fused_computation.5 | convolution fusion | flops 2820407296 | bytes 9961472 | tf_op jit(solution)/shard_map/dot_general | solution.py:22
  217.1 7.1 %fusion.1 = bf16[1,3584,512]{2,1,0:T(8,128)(2,1)} fusion(bf16[768,3584]{1,0:T(8,128)(2,1)} %constant_dynamic-update-slice_fusion, bf16[768,512]{1,0:T(8,128)(2,1)S(1)} %copy-done.11), kind=kOutput, calls=%fused_computation.6 | convolution fusion | flops 2820407296 | bytes 9961472 | tf_op jit(solution)/shard_map/dot_general | solution.py:22
  224.2 10.6 %collective-permute-done.15 = bf16[192,3584]{1,0:T(8,128)(2,1)S(1)} collective-permute-done((bf16[192,3584]{1,0:T(8,128)(2,1)S(1)}, bf16[192,3584]{1,0:T(8,128)(2,1)S(1)}, u32[]{:S(2)}, u32[]{:S(2)}) %collective-permute-start.15) | collective-permute-done | bytes 1376288 | tf_op jit(solution)/shard_map/ppermute | solution.py:82
  236.1 2.9 %add_convert_fusion.1 = bf16[192,3584]{1,0:T(8,128)(2,1)} fusion(bf16[192,3584]{1,0:T(8,128)(2,1)S(1)} %collective-permute-done.15, bf16[192,3584]{1,0:T(8,128)(2,1)S(1)} %collective-permute-done.13, bf16[768,3584]{1,0:T(8,128)(2,1)} %copy-done.2), kind=kLoop, calls=%fused_computation.24 | loop fusion | flops 4128768 | bytes 5505024 | tf_op jit(solution)/shard_map/convert_element_type | solution.py:91
  239.1 4.7 %all-to-all-start.3 = ((bf16[8,24,3584]{2,1,0:T(8,128)(2,1)}), bf16[8,24,3584]{2,1,0:T(8,128)(2,1)}, u32[]{:S(2)}, u32[]{:S(2)}) async-start(bf16[8,24,3584]{2,1,0:T(8,128)(2,1)} %bitcast.78), calls=%async_computation.3 | async-start | bytes 2752512 | tf_op jit(solution)/shard_map/all_to_all | solution.py:28
  243.8 2.2 multiply_reduce_fusion
  247.0 1.9 convolution_convert_fusion.7
  248.9 28.6 %all-to-all-done.3 = bf16[8,24,3584]{2,1,0:T(8,128)(2,1)} async-done(((bf16[8,24,3584]{2,1,0:T(8,128)(2,1)}), bf16[8,24,3584]{2,1,0:T(8,128)(2,1)}, u32[]{:S(2)}, u32[]{:S(2)}) %all-to-all-start.3) | async-done | bytes 1376288 | tf_op jit(solution)/shard_map/all_to_all | solution.py:28
  277.5 2.7 convolution_convert_fusion.6
  (91 shorter events, 34.7 us)
Async XLA Ops:
  0.6 49.8 %copy-start = (bf16[128,3584]{1,0:T(8,128)(2,1)S(1)}, bf16[128,3584]{1,0:T(8,128)(2,1)}, u32[]{:S(2)}) copy-start(bf16[128,3584]{1,0:T(8,128)(2,1)} %param.10) | copy-start | bytes 2752516
  1.7 48.4 %copy-start.4 = (f32[128,8]{0,1:T(8,128)S(1)}, f32[128,8]{0,1:T(8,128)}, u32[]{:S(2)}) copy-start(f32[128,8]{0,1:T(8,128)} %param.8) | copy-start | bytes 12292
  47.1 32.2 %collective-permute-start.1 = (bf16[192,3584]{1,0:T(8,128)(2,1)}, bf16[192,3584]{1,0:T(8,128)(2,1)}, u32[]{:S(2)}, u32[]{:S(2)}) collective-permute-start(bf16[192,3584]{1,0:T(8,128)(2,1)} %bitcast.2), channel_id=1, source_target_pairs={{0,16},{8,24},{16,0},{24,8},{1,17},{9,25},{17,1},{25,9},{2,18},{10... | collective-permute-start | bytes 4128776 | tf_op jit(solution)/shard_map/ppermute | solution.py:40
  48.6 33.4 %collective-permute-start = (bf16[192,3584]{1,0:T(8,128)(2,1)}, bf16[192,3584]{1,0:T(8,128)(2,1)}, u32[]{:S(2)}, u32[]{:S(2)}) collective-permute-start(bf16[192,3584]{1,0:T(8,128)(2,1)} %bitcast.2), channel_id=1, source_target_pairs={{0,8},{8,0},{16,24},{24,16},{1,9},{9,1},{17,25},{25,17},{2,10},{10... | collective-permute-start | bytes 4128776 | tf_op jit(solution)/shard_map/ppermute | solution.py:39
  52.9 48.0 %all-to-all-start.1 = ((bf16[8,24,3584]{2,1,0:T(8,128)(2,1)}), bf16[8,24,3584]{2,1,0:T(8,128)(2,1)S(1)}, u32[]{:S(2)}, u32[]{:S(2)}) async-start(bf16[8,24,3584]{2,1,0:T(8,128)(2,1)} %bitcast.77), calls=%async_computation.1 | async-start | bytes 2752512 | tf_op jit(solution)/shard_map/all_to_all | solution.py:28
  80.4 19.6 %collective-permute-start.3 = (bf16[96,3584]{1,0:T(8,128)(2,1)S(1)}, bf16[96,3584]{1,0:T(8,128)(2,1)S(1)}, u32[]{:S(2)}, u32[]{:S(2)}) collective-permute-start(bf16[96,3584]{1,0:T(8,128)(2,1)S(1)} %slice.86), channel_id=1, source_target_pairs={{0,8},{8,0},{16,24},{24,16},{1,9},{9,1},{17,25},{25,17},{2,10},{10... | collective-permute-start | bytes 2064392 | tf_op jit(solution)/shard_map/ppermute | solution.py:50
  83.1 16.0 %collective-permute-start.2 = (bf16[96,3584]{1,0:T(8,128)(2,1)S(1)}, bf16[96,3584]{1,0:T(8,128)(2,1)S(1)}, u32[]{:S(2)}, u32[]{:S(2)}) collective-permute-start(bf16[96,3584]{1,0:T(8,128)(2,1)S(1)} %slice.85), channel_id=1, source_target_pairs={{0,16},{8,24},{16,0},{24,8},{1,17},{9,25},{17,1},{25,9},{2,18},{10... | collective-permute-start | bytes 2064392 | tf_op jit(solution)/shard_map/ppermute | solution.py:49
  100.9 29.8 %collective-permute-start.5 = (bf16[192,3584]{1,0:T(8,128)(2,1)S(1)}, bf16[192,3584]{1,0:T(8,128)(2,1)S(1)}, u32[]{:S(2)}, u32[]{:S(2)}) collective-permute-start(bf16[192,3584]{1,0:T(8,128)(2,1)S(1)} %bitcast.73), channel_id=1, source_target_pairs={{0,16},{8,24},{16,0},{24,8},{1,17},{9,25},{17,1},{25,9},{2,18},{10... | collective-permute-start | bytes 4128776 | tf_op jit(solution)/shard_map/ppermute | solution.py:40
  102.4 30.0 %collective-permute-start.4 = (bf16[192,3584]{1,0:T(8,128)(2,1)S(1)}, bf16[192,3584]{1,0:T(8,128)(2,1)S(1)}, u32[]{:S(2)}, u32[]{:S(2)}) collective-permute-start(bf16[192,3584]{1,0:T(8,128)(2,1)S(1)} %bitcast.74), channel_id=1, source_target_pairs={{0,8},{8,0},{16,24},{24,16},{1,9},{9,1},{17,25},{25,17},{2,10},{10... | collective-permute-start | bytes 4128776 | tf_op jit(solution)/shard_map/ppermute | solution.py:39
  103.0 6.2 %copy-start.7 = (bf16[1,3584,512]{2,1,0:T(8,128)(2,1)S(1)}, bf16[1,3584,512]{2,1,0:T(8,128)(2,1)}, u32[]{:S(2)}) copy-start(bf16[1,3584,512]{2,1,0:T(8,128)(2,1)} %param.12) | copy-start | bytes 11010052
  109.3 5.3 %copy-start.5 = (bf16[1,512,3584]{2,1,0:T(8,128)(2,1)S(1)}, bf16[1,512,3584]{2,1,0:T(8,128)(2,1)}, u32[]{:S(2)}) copy-start(bf16[1,512,3584]{2,1,0:T(8,128)(2,1)} %param.13) | copy-start | bytes 11010052
  117.8 44.8 %copy-start.3 = (bf16[768,3584]{1,0:T(8,128)(2,1)}, bf16[768,3584]{1,0:T(8,128)(2,1)S(1)}, u32[]{:S(2)}) copy-start(bf16[768,3584]{1,0:T(8,128)(2,1)S(1)} %convolution_convert_fusion) | copy-start | bytes 16515076
  132.7 19.0 %collective-permute-start.7 = (bf16[96,3584]{1,0:T(8,128)(2,1)S(1)}, bf16[96,3584]{1,0:T(8,128)(2,1)S(1)}, u32[]{:S(2)}, u32[]{:S(2)}) collective-permute-start(bf16[96,3584]{1,0:T(8,128)(2,1)S(1)} %slice.71), channel_id=1, source_target_pairs={{0,8},{8,0},{16,24},{24,16},{1,9},{9,1},{17,25},{25,17},{2,10},{10... | collective-permute-start | bytes 2064392 | tf_op jit(solution)/shard_map/ppermute | solution.py:50
  133.3 18.4 %collective-permute-start.6 = (bf16[96,3584]{1,0:T(8,128)(2,1)S(1)}, bf16[96,3584]{1,0:T(8,128)(2,1)S(1)}, u32[]{:S(2)}, u32[]{:S(2)}) collective-permute-start(bf16[96,3584]{1,0:T(8,128)(2,1)S(1)} %slice.70), channel_id=1, source_target_pairs={{0,16},{8,24},{16,0},{24,8},{1,17},{9,25},{17,1},{25,9},{2,18},{10... | collective-permute-start | bytes 2064392 | tf_op jit(solution)/shard_map/ppermute | solution.py:49
  133.7 27.9 %collective-permute-start.9 = (bf16[96,3584]{1,0:T(8,128)(2,1)S(1)}, bf16[96,3584]{1,0:T(8,128)(2,1)S(1)}, u32[]{:S(2)}, u32[]{:S(2)}) collective-permute-start(bf16[96,3584]{1,0:T(8,128)(2,1)S(1)} %get-tuple-element.76), channel_id=1, source_target_pairs={{0,16},{8,24},{16,0},{24,8},{1,17},{9,25},{17,1},{25,9},{2,18},{10... | collective-permute-start | bytes 2064392 | tf_op jit(solution)/shard_map/ppermute | solution.py:65
  135.3 27.3 %collective-permute-start.8 = (bf16[96,3584]{1,0:T(8,128)(2,1)S(1)}, bf16[96,3584]{1,0:T(8,128)(2,1)S(1)}, u32[]{:S(2)}, u32[]{:S(2)}) collective-permute-start(bf16[96,3584]{1,0:T(8,128)(2,1)S(1)} %get-tuple-element.77), channel_id=1, source_target_pairs={{0,8},{8,0},{16,24},{24,16},{1,9},{9,1},{17,25},{25,17},{2,10},{10... | collective-permute-start | bytes 2064392 | tf_op jit(solution)/shard_map/ppermute | solution.py:64
  163.0 28.9 %collective-permute-start.10 = (bf16[192,3584]{1,0:T(8,128)(2,1)S(1)}, bf16[192,3584]{1,0:T(8,128)(2,1)S(1)}, u32[]{:S(2)}, u32[]{:S(2)}) collective-permute-start(bf16[192,3584]{1,0:T(8,128)(2,1)S(1)} %pad_maximum_fusion), channel_id=1, source_target_pairs={{0,8},{8,0},{16,24},{24,16},{1,9},{9,1},{17,25},{25,17},{2,10},{10... | collective-permute-start | bytes 4128776 | tf_op jit(solution)/shard_map/ppermute | solution.py:81
  163.7 28.2 %collective-permute-start.11 = (bf16[192,3584]{1,0:T(8,128)(2,1)S(1)}, bf16[192,3584]{1,0:T(8,128)(2,1)S(1)}, u32[]{:S(2)}, u32[]{:S(2)}) collective-permute-start(bf16[192,3584]{1,0:T(8,128)(2,1)S(1)} %pad_maximum_fusion.1), channel_id=1, source_target_pairs={{0,16},{8,24},{16,0},{24,8},{1,17},{9,25},{17,1},{25,9},{2,18},{10... | collective-permute-start | bytes 4128776 | tf_op jit(solution)/shard_map/ppermute | solution.py:82
  168.9 3.5 %copy-start.6 = (bf16[1,3584,512]{2,1,0:T(8,128)(2,1)S(1)}, bf16[1,3584,512]{2,1,0:T(8,128)(2,1)}, u32[]{:S(2)}) copy-start(bf16[1,3584,512]{2,1,0:T(8,128)(2,1)} %param.11) | copy-start | bytes 11010052
  172.4 5.8 %copy-start.8 = (bf16[768,512]{1,0:T(8,128)(2,1)}, bf16[768,512]{1,0:T(8,128)(2,1)S(1)}, u32[]{:S(2)}) copy-start(bf16[768,512]{1,0:T(8,128)(2,1)S(1)} %get-tuple-element.41) | copy-start | bytes 2359300
  172.4 5.8 %copy-start.10 = (bf16[768,512]{1,0:T(8,128)(2,1)}, bf16[768,512]{1,0:T(8,128)(2,1)S(1)}, u32[]{:S(2)}) copy-start(bf16[768,512]{1,0:T(8,128)(2,1)S(1)} %get-tuple-element.42) | copy-start | bytes 2359300
  185.7 7.6 %copy-start.2 = (bf16[768,3584]{1,0:T(8,128)(2,1)}, bf16[768,3584]{1,0:T(8,128)(2,1)S(1)}, u32[]{:S(2)}) copy-start(bf16[768,3584]{1,0:T(8,128)(2,1)S(1)} %add_convert_fusion) | copy-start | bytes 16515076
  185.7 8.8 %slice-start = ((bf16[768,3584]{1,0:T(8,128)(2,1)}), bf16[192,3584]{1,0:T(8,128)(2,1)S(1)}, s32[]{:S(2)}) async-start(bf16[768,3584]{1,0:T(8,128)(2,1)} %copy-done.3), calls=%async_computation.4 | async-start | bytes 2752512 | tf_op jit(solution)/shard_map/split | solution.py:72
  193.2 12.5 %collective-permute-start.14 = (bf16[96,3584]{1,0:T(8,128)(2,1)}, bf16[96,3584]{1,0:T(8,128)(2,1)}, u32[]{:S(2)}, u32[]{:S(2)}) collective-permute-start(bf16[96,3584]{1,0:T(8,128)(2,1)} %get-tuple-element.68), channel_id=1, source_target_pairs={{0,8},{8,0},{16,24},{24,16},{1,9},{9,1},{17,25},{25,17},{2,10},{10... | collective-permute-start | bytes 2064392 | tf_op jit(solution)/shard_map/ppermute | solution.py:64
  193.9 11.8 %collective-permute-start.12 = (bf16[96,3584]{1,0:T(8,128)(2,1)}, bf16[96,3584]{1,0:T(8,128)(2,1)}, u32[]{:S(2)}, u32[]{:S(2)}) collective-permute-start(bf16[96,3584]{1,0:T(8,128)(2,1)} %get-tuple-element.69), channel_id=1, source_target_pairs={{0,16},{8,24},{16,0},{24,8},{1,17},{9,25},{17,1},{25,9},{2,18},{10... | collective-permute-start | bytes 2064392 | tf_op jit(solution)/shard_map/ppermute | solution.py:65
  196.1 43.0 %all-to-all-start.2 = ((bf16[8,24,3584]{2,1,0:T(8,128)(2,1)}), bf16[8,24,3584]{2,1,0:T(8,128)(2,1)S(1)}, u32[]{:S(2)}, u32[]{:S(2)}) async-start(bf16[8,24,3584]{2,1,0:T(8,128)(2,1)} %bitcast.76), calls=%async_computation.2 | async-start | bytes 2752512 | tf_op jit(solution)/shard_map/all_to_all | solution.py:28
  207.8 2.2 copy-start.9
  207.9 27.0 %collective-permute-start.15 = (bf16[192,3584]{1,0:T(8,128)(2,1)S(1)}, bf16[192,3584]{1,0:T(8,128)(2,1)S(1)}, u32[]{:S(2)}, u32[]{:S(2)}) collective-permute-start(bf16[192,3584]{1,0:T(8,128)(2,1)S(1)} %pad_maximum_fusion.3), channel_id=1, source_target_pairs={{0,16},{8,24},{16,0},{24,8},{1,17},{9,25},{17,1},{25,9},{2,18},{10... | collective-permute-start | bytes 4128776 | tf_op jit(solution)/shard_map/ppermute | solution.py:82
  208.6 8.5 %copy-start.11 = (bf16[768,512]{1,0:T(8,128)(2,1)S(1)}, bf16[768,512]{1,0:T(8,128)(2,1)}, u32[]{:S(2)}) copy-start(bf16[768,512]{1,0:T(8,128)(2,1)} %copy-done.10) | copy-start | bytes 2359300
  208.6 27.6 %collective-permute-start.13 = (bf16[192,3584]{1,0:T(8,128)(2,1)S(1)}, bf16[192,3584]{1,0:T(8,128)(2,1)S(1)}, u32[]{:S(2)}, u32[]{:S(2)}) collective-permute-start(bf16[192,3584]{1,0:T(8,128)(2,1)S(1)} %pad_maximum_fusion.2), channel_id=1, source_target_pairs={{0,8},{8,0},{16,24},{24,16},{1,9},{9,1},{17,25},{25,17},{2,10},{10... | collective-permute-start | bytes 4128776 | tf_op jit(solution)/shard_map/ppermute | solution.py:81
  239.1 38.5 %all-to-all-start.3 = ((bf16[8,24,3584]{2,1,0:T(8,128)(2,1)}), bf16[8,24,3584]{2,1,0:T(8,128)(2,1)}, u32[]{:S(2)}, u32[]{:S(2)}) async-start(bf16[8,24,3584]{2,1,0:T(8,128)(2,1)} %bitcast.78), calls=%async_computation.3 | async-start | bytes 2752512 | tf_op jit(solution)/shard_map/all_to_all | solution.py:28
  243.8 36.4 %copy-start.1 = (bf16[128,3584]{1,0:T(8,128)(2,1)S(1)}, bf16[128,3584]{1,0:T(8,128)(2,1)}, u32[]{:S(2)}) copy-start(bf16[128,3584]{1,0:T(8,128)(2,1)} %param.10) | copy-start | bytes 2752516

commit v13 on v12

--- a/solution.py
+++ b/solution.py
@@ -141,15 +141,14 @@
     part_dx = (contract_last(grad_gatein, gate_w) + contract_last(grad_upin, up_w)).astype(
         jnp.bfloat16
     )
-    part_dx, grad_upin, grad_gatein, out_parts = lax.optimization_barrier(
-        (part_dx, grad_upin, grad_gatein, out_parts)
-    )
+    dx_first = reduce_first(part_dx, groups)
+    dx_first, out_parts = lax.optimization_barrier((dx_first, out_parts))
     out_rows = along_expert(add_parts(out_parts)).astype(jnp.float32)
     new_gate = contract_first(rows_x, grad_gatein).astype(jnp.bfloat16)[None]
     new_up = contract_first(rows_x, grad_upin).astype(jnp.bfloat16)[None]
     new_down = contract_first(hidden, rows_c).astype(jnp.bfloat16)[None]
     dx_home, new_gate, new_up, new_down = lax.optimization_barrier(
-        (reduce_dp(part_dx, groups), new_gate, new_up, new_down)
+        (add_parts(reduce_second(part_dx, dx_first, groups)), new_gate, new_up, new_down)
     )
     dx_rows = along_expert(dx_home)
     layer_out = jnp.dot(

time: 281 us -> 291 us (1.036)
  waiting for transfers between devices: 122 us -> 129 us
    ppermute x2, waiting for transfers between devices: 9.86 us -> 21.8 us  [reduce_first(): lax.ppermute(to_diag[half:], 'dp', perm=pairs(groups, 2))]
    ppermute x2, waiting for transfers between devices: 10.6 us -> 18.4 us  [reduce_second(): from_y = lax.ppermute(to_y, 'dp', perm=pairs(groups, 2))]
    ppermute x2, waiting for transfers between devices: 7.59 us -> 0.56 us  [reduce_second(): from_x = lax.ppermute(to_x, 'dp', perm=pairs(groups, 1))]
    ppermute x2, waiting for transfers between devices: 6.76 us -> 1.27 us  [reduce_first(): lax.ppermute(to_diag[:half], 'dp', perm=pairs(groups, 1))]
    unnamed x35 -> x45, local copies, waits for them, and re-layouts: 10.5 us -> 12.7 us
  transfers between devices with their start and end apart: 19 -> 19, of which waited for: 12 -> 12; matrix products, arithmetic and copies ran while one was open for 27% -> 26% of each run, Pallas kernels for 0% -> 0%
where the time goes in v13:
time: 291 us; the launch traced here: 290 us
  waiting for transfers between devices  129 us (44%)
  matrix products  59 us (20%)
  blocking collectives  39.8 us (14%)
  starting transfers between devices  30.6 us (11%)
  local copies, waits for them, and re-layouts  17.2 us (6%)
  other arithmetic  13.2 us (5%)
    all_to_all x1, blocking collectives, along_expert(): lax.all_to_all(send_rows, 'expert', split_axis=0, concat_axis=0, tiled=True)  39.8 us
    ppermute x2, waiting for transfers between devices, swap_halves_first(): lax.ppermute(rows, 'dp', perm=pairs(groups, 2))  33 us
    all_to_all x3, waiting for transfers between devices, along_expert(): lax.all_to_all(send_rows, 'expert', split_axis=0, concat_axis=0, tiled=True)  28.7 us
    ppermute x2, waiting for transfers between devices, swap_halves_second(): diag_lo = lax.ppermute(from_x[:half], 'dp', perm=pairs(groups, 2))  24 us
    dot_general x5, matrix products, contract_first(): lax.dot_general(left, right, (((0,), (0,)), ((), ())), preferred_element_...  23.2 us
    ppermute x2, waiting for transfers between devices, reduce_first(): lax.ppermute(to_diag[half:], 'dp', perm=pairs(groups, 2))  21.8 us
    ppermute x2, waiting for transfers between devices, reduce_second(): from_y = lax.ppermute(to_y, 'dp', perm=pairs(groups, 2))  18.4 us
    dot_general x3, matrix products, contract_last(): lax.dot_general(left, right, (((1,), (1,)), ((), ())), preferred_element_...  16.5 us
  transfers between devices with their start and end apart: 19, of which 12 were waited for; matrix products, arithmetic and copies ran while one was open for 26% of the time, Pallas kernels for 0%

profile of v13, /device:TPU:0, one launch (start us, length us, event | category | flops | bytes accessed | tf_op | source)
XLA Modules:
  0.0 290.4 jit_solution(14053732581336756745)
XLA Ops:
  1.7 2.3 reduce-window.6
  7.2 39.8 %all_to_all.48 = bf16[8,24,3584]{2,1,0:T(8,128)(2,1)} all-to-all(bf16[8,24,3584]{2,1,0:T(8,128)(2,1)S(1)} %bitcast.79), channel_id=1, replica_groups=mesh['dp'=4,'expert'=8] {'expert'}, dimensions={0} | all-to-all | bytes 2752512 | tf_op jit(solution)/shard_map/all_to_all | solution.py:28
  50.4 2.5 multiply_convert_fusion
  52.9 3.6 %all-to-all-start.1 = ((bf16[8,24,3584]{2,1,0:T(8,128)(2,1)}), bf16[8,24,3584]{2,1,0:T(8,128)(2,1)S(1)}, u32[]{:S(2)}, u32[]{:S(2)}) async-start(bf16[8,24,3584]{2,1,0:T(8,128)(2,1)} %bitcast.77), calls=%async_computation.1 | async-start | bytes 2752512 | tf_op jit(solution)/shard_map/all_to_all | solution.py:28
  56.5 2.5 constant_dynamic-update-slice_fusion.4
  59.0 20.2 %collective-permute-done.1 = bf16[192,3584]{1,0:T(8,128)(2,1)} collective-permute-done((bf16[192,3584]{1,0:T(8,128)(2,1)}, bf16[192,3584]{1,0:T(8,128)(2,1)}, u32[]{:S(2)}, u32[]{:S(2)}) %collective-permute-start.1) | collective-permute-done | bytes 1376288 | tf_op jit(solution)/shard_map/ppermute | solution.py:40
  84.7 2.5 constant_dynamic-update-slice_fusion.3
  87.2 2.6 constant_dynamic-update-slice_fusion.2
  89.8 9.3 %collective-permute-done.2 = bf16[96,3584]{1,0:T(8,128)(2,1)S(1)} collective-permute-done((bf16[96,3584]{1,0:T(8,128)(2,1)S(1)}, bf16[96,3584]{1,0:T(8,128)(2,1)S(1)}, u32[]{:S(2)}, u32[]{:S(2)}) %collective-permute-start.2) | collective-permute-done | bytes 688160 | tf_op jit(solution)/shard_map/ppermute | solution.py:49
  103.0 6.2 %fusion.12 = f32[768,512]{1,0:T(8,128)S(1)} fusion(bf16[768,3584]{1,0:T(8,128)(2,1)} %constant_dynamic-update-slice_fusion, bf16[1,3584,512]{2,1,0:T(8,128)(2,1)} %param.11), kind=kOutput, calls=%fused_computation.21 | convolution fusion | flops 2818572288 | bytes 10747904 | tf_op jit(solution)/shard_map/dot_general | solution.py:121
  109.3 5.2 %multiply_convert_fusion.3 = (bf16[768,512]{1,0:T(8,128)(2,1)S(1)}, f32[768,512]{1,0:T(8,128)S(1)}) fusion(f32[768,512]{1,0:T(8,128)S(1)} %fusion.12, bf16[768,3584]{1,0:T(8,128)(2,1)} %constant_dynamic-update-slice_fusion, bf16[1,3584,512]{2,1,0:T(8,128)(2,1)S(1)} %copy-done.10), kind=kOutput, calls=%fused_computation.30 | convolution fusion | flops 2820931584 | bytes 13107200 | tf_op jit(solution)/shard_map/dot_general | solution.py:122
  114.6 3.2 %convolution_convert_fusion = bf16[768,3584]{1,0:T(8,128)(2,1)S(1)} fusion(bf16[768,512]{1,0:T(8,128)(2,1)S(1)} %get-tuple-element.41, bf16[1,512,3584]{2,1,0:T(8,128)(2,1)S(1)} %copy-done.8), kind=kOutput, calls=%fused_computation.1 | convolution fusion | flops 2821324800 | bytes 9961472 | tf_op jit(solution)/shard_map/dot_general | solution.py:126
  117.8 12.8 %collective-permute-done.5 = bf16[192,3584]{1,0:T(8,128)(2,1)S(1)} collective-permute-done((bf16[192,3584]{1,0:T(8,128)(2,1)S(1)}, bf16[192,3584]{1,0:T(8,128)(2,1)S(1)}, u32[]{:S(2)}, u32[]{:S(2)}) %collective-permute-start.5) | collective-permute-done | bytes 1376288 | tf_op jit(solution)/shard_map/ppermute | solution.py:40
  137.0 14.7 %collective-permute-done.6 = bf16[96,3584]{1,0:T(8,128)(2,1)S(1)} collective-permute-done((bf16[96,3584]{1,0:T(8,128)(2,1)S(1)}, bf16[96,3584]{1,0:T(8,128)(2,1)S(1)}, u32[]{:S(2)}, u32[]{:S(2)}) %collective-permute-start.6) | collective-permute-done | bytes 688160 | tf_op jit(solution)/shard_map/ppermute | solution.py:49
  151.8 9.8 %collective-permute-done.9 = bf16[96,3584]{1,0:T(8,128)(2,1)S(1)} collective-permute-done((bf16[96,3584]{1,0:T(8,128)(2,1)S(1)}, bf16[96,3584]{1,0:T(8,128)(2,1)S(1)}, u32[]{:S(2)}, u32[]{:S(2)}) %collective-permute-start.9) | collective-permute-done | bytes 688160 | tf_op jit(solution)/shard_map/ppermute | solution.py:65
  164.4 3.5 %multiply_convert_fusion.1 = (bf16[768,512]{1,0:T(8,128)(2,1)S(1)}, bf16[768,512]{1,0:T(8,128)(2,1)S(1)}) fusion(f32[768,512]{1,0:T(8,128)S(1)} %fusion.12, f32[768,512]{1,0:T(8,128)S(1)} %get-tuple-element.32, bf16[768,3584]{1,0:T(8,128)(2,1)S(1)} %constant_dynamic-update-slice_fusion.5, bf16[1,512,3584]{2,1,0:T(8,128)(2,1)S(1)} %copy-done.8), kind=kOutput, calls=%fused_computation.27 | convolution fusion | flops 2823684096 | bytes 13893632 | tf_op jit(solution)/shard_map/dot_general | solution.py:16
  167.9 5.8 %fusion.10 = f32[768,3584]{1,0:T(8,128)} fusion(bf16[768,512]{1,0:T(8,128)(2,1)S(1)} %get-tuple-element.77, bf16[1,3584,512]{2,1,0:T(8,128)(2,1)S(1)} %copy-done.9), kind=kOutput, calls=%fused_computation.19 | convolution fusion | flops 2818572288 | bytes 15466496 | tf_op jit(solution)/shard_map/dot_general | solution.py:16
  173.7 7.2 %add_convert_fusion = bf16[768,3584]{1,0:T(8,128)(2,1)S(1)} fusion(f32[768,3584]{1,0:T(8,128)} %fusion.10, bf16[768,512]{1,0:T(8,128)(2,1)S(1)} %get-tuple-element.76, bf16[1,3584,512]{2,1,0:T(8,128)(2,1)} %param.12), kind=kOutput, calls=%fused_computation | convolution fusion | flops 2824077312 | bytes 20971520 | tf_op jit(solution)/shard_map/dot_general | solution.py:16
  181.1 2.2 copy-done.2
  186.3 7.1 %fusion.1 = bf16[1,3584,512]{2,1,0:T(8,128)(2,1)} fusion(bf16[768,3584]{1,0:T(8,128)(2,1)} %constant_dynamic-update-slice_fusion, bf16[768,512]{1,0:T(8,128)(2,1)S(1)} %get-tuple-element.76), kind=kOutput, calls=%fused_computation.6 | convolution fusion | flops 2820407296 | bytes 9961472 | tf_op jit(solution)/shard_map/dot_general | solution.py:22
  193.4 11.9 %collective-permute-done.11 = bf16[96,3584]{1,0:T(8,128)(2,1)S(1)} collective-permute-done((bf16[96,3584]{1,0:T(8,128)(2,1)S(1)}, bf16[96,3584]{1,0:T(8,128)(2,1)S(1)}, u32[]{:S(2)}, u32[]{:S(2)}) %collective-permute-start.11) | collective-permute-done | bytes 688160 | tf_op jit(solution)/shard_map/ppermute | solution.py:65
  207.3 3.6 %all-to-all-start.2 = ((bf16[8,24,3584]{2,1,0:T(8,128)(2,1)}), bf16[8,24,3584]{2,1,0:T(8,128)(2,1)S(1)}, u32[]{:S(2)}, u32[]{:S(2)}) async-start(bf16[8,24,3584]{2,1,0:T(8,128)(2,1)} %bitcast.76), calls=%async_computation.2 | async-start | bytes 2752512 | tf_op jit(solution)/shard_map/all_to_all | solution.py:28
  210.9 2.0 add_convert_fusion.4
  215.3 7.4 %fusion = bf16[1,3584,512]{2,1,0:T(8,128)(2,1)} fusion(bf16[768,3584]{1,0:T(8,128)(2,1)} %constant_dynamic-update-slice_fusion, bf16[768,512]{1,0:T(8,128)(2,1)S(1)} %copy-done.12), kind=kOutput, calls=%fused_computation.5 | convolution fusion | flops 2820407296 | bytes 9961472 | tf_op jit(solution)/shard_map/dot_general | solution.py:22
  222.7 4.5 %fusion.2 = bf16[1,512,3584]{2,1,0:T(8,128)(2,1)} fusion(bf16[768,512]{1,0:T(8,128)(2,1)S(1)} %copy-done.14, bf16[768,3584]{1,0:T(8,128)(2,1)S(1)} %bitcast.81), kind=kOutput, calls=%fused_computation.7 | convolution fusion | flops 2820407296 | bytes 9961472 | tf_op jit(solution)/shard_map/dot_general | solution.py:22
  227.2 18.4 %collective-permute-done.15 = bf16[192,3584]{1,0:T(8,128)(2,1)S(1)} collective-permute-done((bf16[192,3584]{1,0:T(8,128)(2,1)S(1)}, bf16[192,3584]{1,0:T(8,128)(2,1)S(1)}, u32[]{:S(2)}, u32[]{:S(2)}) %collective-permute-start.15) | collective-permute-done | bytes 1376288 | tf_op jit(solution)/shard_map/ppermute | solution.py:82
  246.2 3.0 %add_convert_fusion.1 = bf16[192,3584]{1,0:T(8,128)(2,1)} fusion(bf16[192,3584]{1,0:T(8,128)(2,1)S(1)} %collective-permute-done.15, bf16[192,3584]{1,0:T(8,128)(2,1)S(1)} %collective-permute-done.14, bf16[768,3584]{1,0:T(8,128)(2,1)} %copy-done.2), kind=kLoop, calls=%fused_computation.24 | loop fusion | flops 4128768 | bytes 5505024 | tf_op jit(solution)/shard_map/convert_element_type | solution.py:91
  249.2 4.7 %all-to-all-start.3 = ((bf16[8,24,3584]{2,1,0:T(8,128)(2,1)}), bf16[8,24,3584]{2,1,0:T(8,128)(2,1)}, u32[]{:S(2)}, u32[]{:S(2)}) async-start(bf16[8,24,3584]{2,1,0:T(8,128)(2,1)} %bitcast.78), calls=%async_computation.3 | async-start | bytes 2752512 | tf_op jit(solution)/shard_map/all_to_all | solution.py:28
  254.0 2.2 multiply_reduce_fusion
  257.1 1.9 convolution_convert_fusion.7
  259.0 28.6 %all-to-all-done.3 = bf16[8,24,3584]{2,1,0:T(8,128)(2,1)} async-done(((bf16[8,24,3584]{2,1,0:T(8,128)(2,1)}), bf16[8,24,3584]{2,1,0:T(8,128)(2,1)}, u32[]{:S(2)}, u32[]{:S(2)}) %all-to-all-start.3) | async-done | bytes 1376288 | tf_op jit(solution)/shard_map/all_to_all | solution.py:28
  287.7 2.7 convolution_convert_fusion.6
  (102 shorter events, 35.1 us)
Async XLA Ops:
  0.6 49.8 %copy-start = (bf16[128,3584]{1,0:T(8,128)(2,1)S(1)}, bf16[128,3584]{1,0:T(8,128)(2,1)}, u32[]{:S(2)}) copy-start(bf16[128,3584]{1,0:T(8,128)(2,1)} %param.10) | copy-start | bytes 2752516
  1.7 48.4 %copy-start.7 = (f32[128,8]{0,1:T(8,128)S(1)}, f32[128,8]{0,1:T(8,128)}, u32[]{:S(2)}) copy-start(f32[128,8]{0,1:T(8,128)} %param.8) | copy-start | bytes 12292
  47.1 32.2 %collective-permute-start.1 = (bf16[192,3584]{1,0:T(8,128)(2,1)}, bf16[192,3584]{1,0:T(8,128)(2,1)}, u32[]{:S(2)}, u32[]{:S(2)}) collective-permute-start(bf16[192,3584]{1,0:T(8,128)(2,1)} %bitcast.2), channel_id=1, source_target_pairs={{0,16},{8,24},{16,0},{24,8},{1,17},{9,25},{17,1},{25,9},{2,18},{10... | collective-permute-start | bytes 4128776 | tf_op jit(solution)/shard_map/ppermute | solution.py:40
  48.6 33.4 %collective-permute-start = (bf16[192,3584]{1,0:T(8,128)(2,1)}, bf16[192,3584]{1,0:T(8,128)(2,1)}, u32[]{:S(2)}, u32[]{:S(2)}) collective-permute-start(bf16[192,3584]{1,0:T(8,128)(2,1)} %bitcast.2), channel_id=1, source_target_pairs={{0,8},{8,0},{16,24},{24,16},{1,9},{9,1},{17,25},{25,17},{2,10},{10... | collective-permute-start | bytes 4128776 | tf_op jit(solution)/shard_map/ppermute | solution.py:39
  52.9 47.9 %all-to-all-start.1 = ((bf16[8,24,3584]{2,1,0:T(8,128)(2,1)}), bf16[8,24,3584]{2,1,0:T(8,128)(2,1)S(1)}, u32[]{:S(2)}, u32[]{:S(2)}) async-start(bf16[8,24,3584]{2,1,0:T(8,128)(2,1)} %bitcast.77), calls=%async_computation.1 | async-start | bytes 2752512 | tf_op jit(solution)/shard_map/all_to_all | solution.py:28
  80.4 19.6 %collective-permute-start.3 = (bf16[96,3584]{1,0:T(8,128)(2,1)S(1)}, bf16[96,3584]{1,0:T(8,128)(2,1)S(1)}, u32[]{:S(2)}, u32[]{:S(2)}) collective-permute-start(bf16[96,3584]{1,0:T(8,128)(2,1)S(1)} %slice.86), channel_id=1, source_target_pairs={{0,8},{8,0},{16,24},{24,16},{1,9},{9,1},{17,25},{25,17},{2,10},{10... | collective-permute-start | bytes 2064392 | tf_op jit(solution)/shard_map/ppermute | solution.py:50
  83.1 16.0 %collective-permute-start.2 = (bf16[96,3584]{1,0:T(8,128)(2,1)S(1)}, bf16[96,3584]{1,0:T(8,128)(2,1)S(1)}, u32[]{:S(2)}, u32[]{:S(2)}) collective-permute-start(bf16[96,3584]{1,0:T(8,128)(2,1)S(1)} %slice.85), channel_id=1, source_target_pairs={{0,16},{8,24},{16,0},{24,8},{1,17},{9,25},{17,1},{25,9},{2,18},{10... | collective-permute-start | bytes 2064392 | tf_op jit(solution)/shard_map/ppermute | solution.py:49
  100.9 29.8 %collective-permute-start.5 = (bf16[192,3584]{1,0:T(8,128)(2,1)S(1)}, bf16[192,3584]{1,0:T(8,128)(2,1)S(1)}, u32[]{:S(2)}, u32[]{:S(2)}) collective-permute-start(bf16[192,3584]{1,0:T(8,128)(2,1)S(1)} %bitcast.73), channel_id=1, source_target_pairs={{0,16},{8,24},{16,0},{24,8},{1,17},{9,25},{17,1},{25,9},{2,18},{10... | collective-permute-start | bytes 4128776 | tf_op jit(solution)/shard_map/ppermute | solution.py:40
  102.4 30.0 %collective-permute-start.4 = (bf16[192,3584]{1,0:T(8,128)(2,1)S(1)}, bf16[192,3584]{1,0:T(8,128)(2,1)S(1)}, u32[]{:S(2)}, u32[]{:S(2)}) collective-permute-start(bf16[192,3584]{1,0:T(8,128)(2,1)S(1)} %bitcast.74), channel_id=1, source_target_pairs={{0,8},{8,0},{16,24},{24,16},{1,9},{9,1},{17,25},{25,17},{2,10},{10... | collective-permute-start | bytes 4128776 | tf_op jit(solution)/shard_map/ppermute | solution.py:39
  103.0 6.2 %copy-start.10 = (bf16[1,3584,512]{2,1,0:T(8,128)(2,1)S(1)}, bf16[1,3584,512]{2,1,0:T(8,128)(2,1)}, u32[]{:S(2)}) copy-start(bf16[1,3584,512]{2,1,0:T(8,128)(2,1)} %param.12) | copy-start | bytes 11010052
  109.3 5.3 %copy-start.8 = (bf16[1,512,3584]{2,1,0:T(8,128)(2,1)S(1)}, bf16[1,512,3584]{2,1,0:T(8,128)(2,1)}, u32[]{:S(2)}) copy-start(bf16[1,512,3584]{2,1,0:T(8,128)(2,1)} %param.13) | copy-start | bytes 11010052
  117.8 44.8 %copy-start.3 = (bf16[768,3584]{1,0:T(8,128)(2,1)}, bf16[768,3584]{1,0:T(8,128)(2,1)S(1)}, u32[]{:S(2)}) copy-start(bf16[768,3584]{1,0:T(8,128)(2,1)S(1)} %convolution_convert_fusion) | copy-start | bytes 16515076
  132.7 19.0 %collective-permute-start.7 = (bf16[96,3584]{1,0:T(8,128)(2,1)S(1)}, bf16[96,3584]{1,0:T(8,128)(2,1)S(1)}, u32[]{:S(2)}, u32[]{:S(2)}) collective-permute-start(bf16[96,3584]{1,0:T(8,128)(2,1)S(1)} %slice.71), channel_id=1, source_target_pairs={{0,8},{8,0},{16,24},{24,16},{1,9},{9,1},{17,25},{25,17},{2,10},{10... | collective-permute-start | bytes 2064392 | tf_op jit(solution)/shard_map/ppermute | solution.py:50
  133.3 18.4 %collective-permute-start.6 = (bf16[96,3584]{1,0:T(8,128)(2,1)S(1)}, bf16[96,3584]{1,0:T(8,128)(2,1)S(1)}, u32[]{:S(2)}, u32[]{:S(2)}) collective-permute-start(bf16[96,3584]{1,0:T(8,128)(2,1)S(1)} %slice.70), channel_id=1, source_target_pairs={{0,16},{8,24},{16,0},{24,8},{1,17},{9,25},{17,1},{25,9},{2,18},{10... | collective-permute-start | bytes 2064392 | tf_op jit(solution)/shard_map/ppermute | solution.py:49
  133.7 27.9 %collective-permute-start.9 = (bf16[96,3584]{1,0:T(8,128)(2,1)S(1)}, bf16[96,3584]{1,0:T(8,128)(2,1)S(1)}, u32[]{:S(2)}, u32[]{:S(2)}) collective-permute-start(bf16[96,3584]{1,0:T(8,128)(2,1)S(1)} %get-tuple-element.74), channel_id=1, source_target_pairs={{0,16},{8,24},{16,0},{24,8},{1,17},{9,25},{17,1},{25,9},{2,18},{10... | collective-permute-start | bytes 2064392 | tf_op jit(solution)/shard_map/ppermute | solution.py:65
  135.3 27.3 %collective-permute-start.8 = (bf16[96,3584]{1,0:T(8,128)(2,1)S(1)}, bf16[96,3584]{1,0:T(8,128)(2,1)S(1)}, u32[]{:S(2)}, u32[]{:S(2)}) collective-permute-start(bf16[96,3584]{1,0:T(8,128)(2,1)S(1)} %get-tuple-element.75), channel_id=1, source_target_pairs={{0,8},{8,0},{16,24},{24,16},{1,9},{9,1},{17,25},{25,17},{2,10},{10... | collective-permute-start | bytes 2064392 | tf_op jit(solution)/shard_map/ppermute | solution.py:64
  151.8 12.6 %copy-start.6 = (bf16[768,3584]{1,0:T(8,128)(2,1)}, bf16[768,3584]{1,0:T(8,128)(2,1)S(1)}, u32[]{:S(2)}) copy-start(bf16[768,3584]{1,0:T(8,128)(2,1)S(1)} %constant_dynamic-update-slice_fusion.5) | copy-start | bytes 16515076
  163.0 42.6 %collective-permute-start.12 = (bf16[192,3584]{1,0:T(8,128)(2,1)S(1)}, bf16[192,3584]{1,0:T(8,128)(2,1)S(1)}, u32[]{:S(2)}, u32[]{:S(2)}) collective-permute-start(bf16[192,3584]{1,0:T(8,128)(2,1)S(1)} %pad_maximum_fusion), channel_id=1, source_target_pairs={{0,8},{8,0},{16,24},{24,16},{1,9},{9,1},{17,25},{25,17},{2,10},{10... | collective-permute-start | bytes 4128776 | tf_op jit(solution)/shard_map/ppermute | solution.py:81
  163.7 4.1 %copy-start.9 = (bf16[1,3584,512]{2,1,0:T(8,128)(2,1)S(1)}, bf16[1,3584,512]{2,1,0:T(8,128)(2,1)}, u32[]{:S(2)}) copy-start(bf16[1,3584,512]{2,1,0:T(8,128)(2,1)} %param.11) | copy-start | bytes 11010052
  163.7 41.9 %collective-permute-start.13 = (bf16[192,3584]{1,0:T(8,128)(2,1)S(1)}, bf16[192,3584]{1,0:T(8,128)(2,1)S(1)}, u32[]{:S(2)}, u32[]{:S(2)}) collective-permute-start(bf16[192,3584]{1,0:T(8,128)(2,1)S(1)} %pad_maximum_fusion.1), channel_id=1, source_target_pairs={{0,16},{8,24},{16,0},{24,8},{1,17},{9,25},{17,1},{25,9},{2,18},{10... | collective-permute-start | bytes 4128776 | tf_op jit(solution)/shard_map/ppermute | solution.py:82
  167.9 5.8 %copy-start.11 = (bf16[768,512]{1,0:T(8,128)(2,1)}, bf16[768,512]{1,0:T(8,128)(2,1)S(1)}, u32[]{:S(2)}) copy-start(bf16[768,512]{1,0:T(8,128)(2,1)S(1)} %get-tuple-element.77) | copy-start | bytes 2359300
  183.3 22.0 %collective-permute-start.11 = (bf16[96,3584]{1,0:T(8,128)(2,1)S(1)}, bf16[96,3584]{1,0:T(8,128)(2,1)S(1)}, u32[]{:S(2)}, u32[]{:S(2)}) collective-permute-start(bf16[96,3584]{1,0:T(8,128)(2,1)S(1)} %get-tuple-element.66), channel_id=1, source_target_pairs={{0,16},{8,24},{16,0},{24,8},{1,17},{9,25},{17,1},{25,9},{2,18},{10... | collective-permute-start | bytes 2064392 | tf_op jit(solution)/shard_map/ppermute | solution.py:65
  184.8 20.8 %slice-start = ((bf16[768,3584]{1,0:T(8,128)(2,1)}), bf16[192,3584]{1,0:T(8,128)(2,1)S(1)}, s32[]{:S(2)}) async-start(bf16[768,3584]{1,0:T(8,128)(2,1)} %copy-done.3), calls=%async_computation.4 | async-start | bytes 2752512 | tf_op jit(solution)/shard_map/split | solution.py:72
  184.8 20.8 %collective-permute-start.10 = (bf16[96,3584]{1,0:T(8,128)(2,1)S(1)}, bf16[96,3584]{1,0:T(8,128)(2,1)S(1)}, u32[]{:S(2)}, u32[]{:S(2)}) collective-permute-start(bf16[96,3584]{1,0:T(8,128)(2,1)S(1)} %get-tuple-element.67), channel_id=1, source_target_pairs={{0,8},{8,0},{16,24},{24,16},{1,9},{9,1},{17,25},{25,17},{2,10},{10... | collective-permute-start | bytes 2064392 | tf_op jit(solution)/shard_map/ppermute | solution.py:64
  207.3 42.0 %all-to-all-start.2 = ((bf16[8,24,3584]{2,1,0:T(8,128)(2,1)}), bf16[8,24,3584]{2,1,0:T(8,128)(2,1)S(1)}, u32[]{:S(2)}, u32[]{:S(2)}) async-start(bf16[8,24,3584]{2,1,0:T(8,128)(2,1)} %bitcast.76), calls=%async_computation.2 | async-start | bytes 2752512 | tf_op jit(solution)/shard_map/all_to_all | solution.py:28
  213.0 32.7 %collective-permute-start.15 = (bf16[192,3584]{1,0:T(8,128)(2,1)S(1)}, bf16[192,3584]{1,0:T(8,128)(2,1)S(1)}, u32[]{:S(2)}, u32[]{:S(2)}) collective-permute-start(bf16[192,3584]{1,0:T(8,128)(2,1)S(1)} %pad_maximum_fusion.3), channel_id=1, source_target_pairs={{0,16},{8,24},{16,0},{24,8},{1,17},{9,25},{17,1},{25,9},{2,18},{10... | collective-permute-start | bytes 4128776 | tf_op jit(solution)/shard_map/ppermute | solution.py:82
  213.7 9.0 %slice-start.1 = ((s8[5505024]{0:T(1024)(128)(4,1)}), s8[4194304]{0:T(1024)(128)(4,1)S(1)}, s32[]{:S(2)}) async-start(s8[5505024]{0:T(1024)(128)(4,1)} %bitcast.80), calls=%async_computation.5 | async-start | bytes 8388608
  213.8 8.9 %slice-start.2 = ((s8[5505024]{0:T(1024)(128)(4,1)}), s8[1310720]{0:T(1024)(128)(4,1)S(1)}, s32[]{:S(2)}) async-start(s8[5505024]{0:T(1024)(128)(4,1)} %bitcast.80), calls=%async_computation.6 | async-start | bytes 2621440
  213.8 8.8 %copy-start.14 = (bf16[768,512]{1,0:T(8,128)(2,1)S(1)}, bf16[768,512]{1,0:T(8,128)(2,1)}, u32[]{:S(2)}) copy-start(bf16[768,512]{1,0:T(8,128)(2,1)} %copy-done.13) | copy-start | bytes 2359300
  213.9 32.4 %collective-permute-start.14 = (bf16[192,3584]{1,0:T(8,128)(2,1)S(1)}, bf16[192,3584]{1,0:T(8,128)(2,1)S(1)}, u32[]{:S(2)}, u32[]{:S(2)}) collective-permute-start(bf16[192,3584]{1,0:T(8,128)(2,1)S(1)} %pad_maximum_fusion.2), channel_id=1, source_target_pairs={{0,8},{8,0},{16,24},{24,16},{1,9},{9,1},{17,25},{25,17},{2,10},{10... | collective-permute-start | bytes 4128776 | tf_op jit(solution)/shard_map/ppermute | solution.py:81
  249.2 38.5 %all-to-all-start.3 = ((bf16[8,24,3584]{2,1,0:T(8,128)(2,1)}), bf16[8,24,3584]{2,1,0:T(8,128)(2,1)}, u32[]{:S(2)}, u32[]{:S(2)}) async-start(bf16[8,24,3584]{2,1,0:T(8,128)(2,1)} %bitcast.78), calls=%async_computation.3 | async-start | bytes 2752512 | tf_op jit(solution)/shard_map/all_to_all | solution.py:28
  254.0 36.4 %copy-start.1 = (bf16[128,3584]{1,0:T(8,128)(2,1)S(1)}, bf16[128,3584]{1,0:T(8,128)(2,1)}, u32[]{:S(2)}) copy-start(bf16[128,3584]{1,0:T(8,128)(2,1)} %param.10) | copy-start | bytes 2752516
  (5 other events, 11.7 us)

commit v14 on v12

--- a/solution.py
+++ b/solution.py
@@ -35,20 +35,21 @@
 def swap_halves_first(rows, groups):
     if groups != 4:
         return ()
-    return (
-        lax.ppermute(rows, "dp", perm=pairs(groups, 1)),
-        lax.ppermute(rows, "dp", perm=pairs(groups, 2)),
+    half = rows.shape[0] // 2
+    return tuple(
+        lax.ppermute(part, "dp", perm=pairs(groups, bit))
+        for bit in (1, 2)
+        for part in (rows[:half], rows[half:])
     )
 
 
 def swap_halves_second(rows, first, groups):
     if groups != 4:
         return lax.all_gather(rows, "dp", axis=0, tiled=True)
-    from_x, from_y = first
-    half = rows.shape[0] // 2
-    diag_lo = lax.ppermute(from_x[:half], "dp", perm=pairs(groups, 2))
-    diag_hi = lax.ppermute(from_y[half:], "dp", perm=pairs(groups, 1))
-    return jnp.concatenate([rows, from_x, from_y, diag_lo, diag_hi], axis=0)
+    x_lo, x_hi, y_lo, y_hi = first
+    diag_lo = lax.ppermute(x_lo, "dp", perm=pairs(groups, 2))
+    diag_hi = lax.ppermute(y_hi, "dp", perm=pairs(groups, 1))
+    return jnp.concatenate([rows, x_lo, x_hi, y_lo, y_hi, diag_lo, diag_hi], axis=0)
 
 
 def replicate_dp(rows, groups):

time: 281 us -> 280 us (level)
  blocking collectives: 39.8 us -> 0 us
  waiting for transfers between devices: 122 us -> 150 us
  starting transfers between devices: 29 us -> 42 us
    all_to_all x1 -> x0, blocking collectives: 39.8 us -> none  [along_expert(): lax.all_to_all(send_rows, 'expert', split_axis=0, concat_axis=0, tiled=True)]
    all_to_all x3 -> x4, waiting for transfers between devices: 28.7 us -> 61.9 us  [along_expert(): lax.all_to_all(send_rows, 'expert', split_axis=0, concat_axis=0, tiled=True)]
    all_to_all x3 -> x4, starting transfers between devices: 12.2 us -> 19 us  [along_expert(): lax.all_to_all(send_rows, 'expert', split_axis=0, concat_axis=0, tiled=True)]
    ppermute x8 -> x12, starting transfers between devices: 9.26 us -> 12.4 us  [the longest x8 8.25 us: swap_halves_first(): lax.ppermute(part, 'dp', perm=pairs(groups, bit))]
    ppermute x8 -> x12, waiting for transfers between devices: 58.8 us -> 56 us  [the longest x8 30.3 us: swap_halves_first(): lax.ppermute(part, 'dp', perm=pairs(groups, bit))]
    unnamed x35 -> x39, local copies, waits for them, and re-layouts: 10.5 us -> 8.8 us
  transfers between devices with their start and end apart: 19 -> 24, of which waited for: 12 -> 17; matrix products, arithmetic and copies ran while one was open for 27% -> 26% of each run, Pallas kernels for 0% -> 0%
where the time goes in v14:
time: 280 us; the launch traced here: 279 us
  waiting for transfers between devices  150 us (54%)
  matrix products  59.9 us (21%)
  starting transfers between devices  42 us (15%)
  local copies, waits for them, and re-layouts  13.2 us (5%)
  other arithmetic  13.2 us (5%)
    all_to_all x4, waiting for transfers between devices, along_expert(): lax.all_to_all(send_rows, 'expert', split_axis=0, concat_axis=0, tiled=True)  61.9 us
    ppermute x8, waiting for transfers between devices, swap_halves_first(): lax.ppermute(part, 'dp', perm=pairs(groups, bit))  30.3 us
    ppermute x2, waiting for transfers between devices, swap_halves_second(): diag_lo = lax.ppermute(x_lo, 'dp', perm=pairs(groups, 2))  25 us
    dot_general x5, matrix products, contract_first(): lax.dot_general(left, right, (((0,), (0,)), ((), ())), preferred_element_...  24 us
    all_to_all x4, starting transfers between devices, along_expert(): lax.all_to_all(send_rows, 'expert', split_axis=0, concat_axis=0, tiled=True)  19 us
    dot_general x3, matrix products, contract_last(): lax.dot_general(left, right, (((1,), (1,)), ((), ())), preferred_element_...  16.8 us
    ppermute x2, waiting for transfers between devices, reduce_first(): lax.ppermute(to_diag[half:], 'dp', perm=pairs(groups, 2))  10.3 us
    ppermute x2, waiting for transfers between devices, reduce_second(): from_y = lax.ppermute(to_y, 'dp', perm=pairs(groups, 2))  9.86 us
  transfers between devices with their start and end apart: 24, of which 17 were waited for; matrix products, arithmetic and copies ran while one was open for 26% of the time, Pallas kernels for 0%

profile of v14, /device:TPU:0, one launch (start us, length us, event | category | flops | bytes accessed | tf_op | source)
XLA Modules:
  0.0 279.5 jit_solution(14273013781887477950)
XLA Ops:
  1.7 2.3 reduce-window.6
  5.5 2.8 convolution_convert_fusion.5
  8.3 6.3 %all-to-all-start = ((bf16[8,24,3584]{2,1,0:T(8,128)(2,1)}), bf16[8,24,3584]{2,1,0:T(8,128)(2,1)S(1)}, u32[]{:S(2)}, u32[]{:S(2)}) async-start(bf16[8,24,3584]{2,1,0:T(8,128)(2,1)} %bitcast.81), calls=%async_computation | async-start | bytes 2752512 | tf_op jit(solution)/shard_map/all_to_all | solution.py:28
  15.0 33.2 %all-to-all-done = bf16[8,24,3584]{2,1,0:T(8,128)(2,1)S(1)} async-done(((bf16[8,24,3584]{2,1,0:T(8,128)(2,1)}), bf16[8,24,3584]{2,1,0:T(8,128)(2,1)S(1)}, u32[]{:S(2)}, u32[]{:S(2)}) %all-to-all-start) | async-done | bytes 1376288 | tf_op jit(solution)/shard_map/all_to_all | solution.py:28
  52.4 2.5 multiply_convert_fusion
  54.9 3.8 %all-to-all-start.1 = ((bf16[8,24,3584]{2,1,0:T(8,128)(2,1)}), bf16[8,24,3584]{2,1,0:T(8,128)(2,1)S(1)}, u32[]{:S(2)}, u32[]{:S(2)}) async-start(bf16[8,24,3584]{2,1,0:T(8,128)(2,1)} %bitcast.78), calls=%async_computation.1 | async-start | bytes 2752512 | tf_op jit(solution)/shard_map/all_to_all | solution.py:28
  61.0 7.1 %collective-permute-done = bf16[96,3584]{1,0:T(8,128)(2,1)} collective-permute-done((bf16[96,3584]{1,0:T(8,128)(2,1)}, bf16[96,3584]{1,0:T(8,128)(2,1)}, u32[]{:S(2)}, u32[]{:S(2)}) %collective-permute-start) | collective-permute-done | bytes 688160 | tf_op jit(solution)/shard_map/ppermute | solution.py:40
  71.1 2.0 constant_dynamic-update-slice_fusion.5
  73.1 9.6 %collective-permute-done.1 = bf16[96,3584]{1,0:T(8,128)(2,1)S(1)} collective-permute-done((bf16[96,3584]{1,0:T(8,128)(2,1)}, bf16[96,3584]{1,0:T(8,128)(2,1)S(1)}, u32[]{:S(2)}, u32[]{:S(2)}) %collective-permute-start.1) | collective-permute-done | bytes 688160 | tf_op jit(solution)/shard_map/ppermute | solution.py:40
  86.0 11.3 %collective-permute-done.4 = bf16[96,3584]{1,0:T(8,128)(2,1)S(1)} collective-permute-done((bf16[96,3584]{1,0:T(8,128)(2,1)}, bf16[96,3584]{1,0:T(8,128)(2,1)S(1)}, u32[]{:S(2)}, u32[]{:S(2)}) %collective-permute-start.4) | collective-permute-done | bytes 688160 | tf_op jit(solution)/shard_map/ppermute | solution.py:50
  103.3 6.1 %fusion.12 = f32[768,512]{1,0:T(8,128)S(1)} fusion(bf16[768,3584]{1,0:T(8,128)(2,1)} %constant_dynamic-update-slice_fusion, bf16[1,3584,512]{2,1,0:T(8,128)(2,1)} %param.11), kind=kOutput, calls=%fused_computation.21 | convolution fusion | flops 2818572288 | bytes 10747904 | tf_op jit(solution)/shard_map/dot_general | solution.py:122
  109.4 5.2 %multiply_convert_fusion.3 = (bf16[768,512]{1,0:T(8,128)(2,1)S(1)}, f32[768,512]{1,0:T(8,128)S(1)}) fusion(f32[768,512]{1,0:T(8,128)S(1)} %fusion.12, bf16[768,3584]{1,0:T(8,128)(2,1)} %constant_dynamic-update-slice_fusion, bf16[1,3584,512]{2,1,0:T(8,128)(2,1)S(1)} %copy-done.7), kind=kOutput, calls=%fused_computation.30 | convolution fusion | flops 2820931584 | bytes 13107200 | tf_op jit(solution)/shard_map/dot_general | solution.py:123
  114.8 3.2 %convolution_convert_fusion = bf16[768,3584]{1,0:T(8,128)(2,1)S(1)} fusion(bf16[768,512]{1,0:T(8,128)(2,1)S(1)} %get-tuple-element.47, bf16[1,512,3584]{2,1,0:T(8,128)(2,1)S(1)} %copy-done.5), kind=kOutput, calls=%fused_computation.1 | convolution fusion | flops 2821324800 | bytes 9961472 | tf_op jit(solution)/shard_map/dot_general | solution.py:127
  119.1 10.6 %collective-permute-done.8 = bf16[96,3584]{1,0:T(8,128)(2,1)S(1)} collective-permute-done((bf16[96,3584]{1,0:T(8,128)(2,1)S(1)}, bf16[96,3584]{1,0:T(8,128)(2,1)S(1)}, u32[]{:S(2)}, u32[]{:S(2)}) %collective-permute-start.8) | collective-permute-done | bytes 688160 | tf_op jit(solution)/shard_map/ppermute | solution.py:40
  135.6 13.8 %collective-permute-done.10 = bf16[96,3584]{1,0:T(8,128)(2,1)S(1)} collective-permute-done((bf16[96,3584]{1,0:T(8,128)(2,1)S(1)}, bf16[96,3584]{1,0:T(8,128)(2,1)S(1)}, u32[]{:S(2)}, u32[]{:S(2)}) %collective-permute-start.10) | collective-permute-done | bytes 688160 | tf_op jit(solution)/shard_map/ppermute | solution.py:50
  150.1 10.3 %collective-permute-done.13 = bf16[96,3584]{1,0:T(8,128)(2,1)S(1)} collective-permute-done((bf16[96,3584]{1,0:T(8,128)(2,1)S(1)}, bf16[96,3584]{1,0:T(8,128)(2,1)S(1)}, u32[]{:S(2)}, u32[]{:S(2)}) %collective-permute-start.13) | collective-permute-done | bytes 688160 | tf_op jit(solution)/shard_map/ppermute | solution.py:66
  164.2 4.5 %fusion.2 = bf16[1,512,3584]{2,1,0:T(8,128)(2,1)} fusion(bf16[768,512]{1,0:T(8,128)(2,1)S(1)} %get-tuple-element.47, bf16[768,3584]{1,0:T(8,128)(2,1)S(1)} %constant_dynamic-update-slice_fusion.7), kind=kOutput, calls=%fused_computation.7 | convolution fusion | flops 2820407296 | bytes 9961472 | tf_op jit(solution)/shard_map/dot_general | solution.py:22
  168.7 3.5 %multiply_convert_fusion.1 = (bf16[768,512]{1,0:T(8,128)(2,1)S(1)}, bf16[768,512]{1,0:T(8,128)(2,1)S(1)}) fusion(f32[768,512]{1,0:T(8,128)S(1)} %fusion.12, f32[768,512]{1,0:T(8,128)S(1)} %get-tuple-element.37, bf16[768,3584]{1,0:T(8,128)(2,1)S(1)} %constant_dynamic-update-slice_fusion.7, bf16[1,512,3584]{2,1,0:T(8,128)(2,1)S(1)} %copy-done.5), kind=kOutput, calls=%fused_computation.27 | convolution fusion | flops 2823684096 | bytes 13893632 | tf_op jit(solution)/shard_map/dot_general | solution.py:16
  172.3 5.8 %fusion.10 = f32[768,3584]{1,0:T(8,128)} fusion(bf16[768,512]{1,0:T(8,128)(2,1)S(1)} %get-tuple-element.45, bf16[1,3584,512]{2,1,0:T(8,128)(2,1)S(1)} %copy-done.6), kind=kOutput, calls=%fused_computation.19 | convolution fusion | flops 2818572288 | bytes 15466496 | tf_op jit(solution)/shard_map/dot_general | solution.py:16
  178.1 7.4 %add_convert_fusion = bf16[768,3584]{1,0:T(8,128)(2,1)S(1)} fusion(f32[768,3584]{1,0:T(8,128)} %fusion.10, bf16[768,512]{1,0:T(8,128)(2,1)S(1)} %get-tuple-element.46, bf16[1,3584,512]{2,1,0:T(8,128)(2,1)} %param.12), kind=kOutput, calls=%fused_computation | convolution fusion | flops 2824077312 | bytes 20971520 | tf_op jit(solution)/shard_map/dot_general | solution.py:16
  185.5 5.3 %collective-permute-done.14 = bf16[192,3584]{1,0:T(8,128)(2,1)S(1)} collective-permute-done((bf16[192,3584]{1,0:T(8,128)(2,1)S(1)}, bf16[192,3584]{1,0:T(8,128)(2,1)S(1)}, u32[]{:S(2)}, u32[]{:S(2)}) %collective-permute-start.14) | collective-permute-done | bytes 1376288 | tf_op jit(solution)/shard_map/ppermute | solution.py:82
  195.8 4.2 %all-to-all-start.2 = ((bf16[8,24,3584]{2,1,0:T(8,128)(2,1)}), bf16[8,24,3584]{2,1,0:T(8,128)(2,1)S(1)}, u32[]{:S(2)}, u32[]{:S(2)}) async-start(bf16[8,24,3584]{2,1,0:T(8,128)(2,1)} %bitcast.79), calls=%async_computation.2 | async-start | bytes 2752512 | tf_op jit(solution)/shard_map/all_to_all | solution.py:28
  200.0 5.1 %collective-permute-done.18 = bf16[96,3584]{1,0:T(8,128)(2,1)} collective-permute-done((bf16[96,3584]{1,0:T(8,128)(2,1)}, bf16[96,3584]{1,0:T(8,128)(2,1)}, u32[]{:S(2)}, u32[]{:S(2)}) %collective-permute-start.18) | collective-permute-done | bytes 688160 | tf_op jit(solution)/shard_map/ppermute | solution.py:65
  205.1 2.0 add_convert_fusion.4
  210.7 7.1 %fusion = bf16[1,3584,512]{2,1,0:T(8,128)(2,1)} fusion(bf16[768,3584]{1,0:T(8,128)(2,1)} %constant_dynamic-update-slice_fusion, bf16[768,512]{1,0:T(8,128)(2,1)S(1)} %copy-done.9), kind=kOutput, calls=%fused_computation.5 | convolution fusion | flops 2820407296 | bytes 9961472 | tf_op jit(solution)/shard_map/dot_general | solution.py:22
  217.8 7.1 %fusion.1 = bf16[1,3584,512]{2,1,0:T(8,128)(2,1)} fusion(bf16[768,3584]{1,0:T(8,128)(2,1)} %constant_dynamic-update-slice_fusion, bf16[768,512]{1,0:T(8,128)(2,1)S(1)} %copy-done.11), kind=kOutput, calls=%fused_computation.6 | convolution fusion | flops 2820407296 | bytes 9961472 | tf_op jit(solution)/shard_map/dot_general | solution.py:22
  224.9 9.9 %collective-permute-done.19 = bf16[192,3584]{1,0:T(8,128)(2,1)S(1)} collective-permute-done((bf16[192,3584]{1,0:T(8,128)(2,1)S(1)}, bf16[192,3584]{1,0:T(8,128)(2,1)S(1)}, u32[]{:S(2)}, u32[]{:S(2)}) %collective-permute-start.19) | collective-permute-done | bytes 1376288 | tf_op jit(solution)/shard_map/ppermute | solution.py:83
  235.3 3.0 %add_convert_fusion.1 = bf16[192,3584]{1,0:T(8,128)(2,1)} fusion(bf16[192,3584]{1,0:T(8,128)(2,1)S(1)} %collective-permute-done.19, bf16[192,3584]{1,0:T(8,128)(2,1)S(1)} %collective-permute-done.17, bf16[768,3584]{1,0:T(8,128)(2,1)} %copy-done.2), kind=kLoop, calls=%fused_computation.24 | loop fusion | flops 4128768 | bytes 5505024 | tf_op jit(solution)/shard_map/convert_element_type | solution.py:92
  238.3 4.7 %all-to-all-start.3 = ((bf16[8,24,3584]{2,1,0:T(8,128)(2,1)}), bf16[8,24,3584]{2,1,0:T(8,128)(2,1)}, u32[]{:S(2)}, u32[]{:S(2)}) async-start(bf16[8,24,3584]{2,1,0:T(8,128)(2,1)} %bitcast.80), calls=%async_computation.3 | async-start | bytes 2752512 | tf_op jit(solution)/shard_map/all_to_all | solution.py:28
  243.0 2.2 multiply_reduce_fusion
  248.1 28.6 %all-to-all-done.3 = bf16[8,24,3584]{2,1,0:T(8,128)(2,1)} async-done(((bf16[8,24,3584]{2,1,0:T(8,128)(2,1)}), bf16[8,24,3584]{2,1,0:T(8,128)(2,1)}, u32[]{:S(2)}, u32[]{:S(2)}) %all-to-all-start.3) | async-done | bytes 1376288 | tf_op jit(solution)/shard_map/all_to_all | solution.py:28
  276.8 2.7 convolution_convert_fusion.6
  (102 shorter events, 45.2 us)
Async XLA Ops:
  0.6 51.8 %copy-start = (bf16[128,3584]{1,0:T(8,128)(2,1)S(1)}, bf16[128,3584]{1,0:T(8,128)(2,1)}, u32[]{:S(2)}) copy-start(bf16[128,3584]{1,0:T(8,128)(2,1)} %param.10) | copy-start | bytes 2752516
  1.7 12.9 %copy-start.4 = (f32[128,8]{0,1:T(8,128)S(1)}, f32[128,8]{0,1:T(8,128)}, u32[]{:S(2)}) copy-start(f32[128,8]{0,1:T(8,128)} %param.8) | copy-start | bytes 12292
  8.3 39.9 %all-to-all-start = ((bf16[8,24,3584]{2,1,0:T(8,128)(2,1)}), bf16[8,24,3584]{2,1,0:T(8,128)(2,1)S(1)}, u32[]{:S(2)}, u32[]{:S(2)}) async-start(bf16[8,24,3584]{2,1,0:T(8,128)(2,1)} %bitcast.81), calls=%async_computation | async-start | bytes 2752512 | tf_op jit(solution)/shard_map/all_to_all | solution.py:28
  49.4 18.7 %collective-permute-start = (bf16[96,3584]{1,0:T(8,128)(2,1)}, bf16[96,3584]{1,0:T(8,128)(2,1)}, u32[]{:S(2)}, u32[]{:S(2)}) collective-permute-start(bf16[96,3584]{1,0:T(8,128)(2,1)} %bitcast.3), channel_id=1, source_target_pairs={{0,8},{8,0},{16,24},{24,16},{1,9},{9,1},{17,25},{25,17},{2,10},{10... | collective-permute-start | bytes 2064392 | tf_op jit(solution)/shard_map/ppermute | solution.py:40
  50.9 18.7 %collective-permute-start.3 = (bf16[96,3584]{1,0:T(8,128)(2,1)}, bf16[96,3584]{1,0:T(8,128)(2,1)S(1)}, u32[]{:S(2)}, u32[]{:S(2)}) collective-permute-start(bf16[96,3584]{1,0:T(8,128)(2,1)} %bitcast.4), channel_id=1, source_target_pairs={{0,16},{8,24},{16,0},{24,8},{1,17},{9,25},{17,1},{25,9},{2,18},{10... | collective-permute-start | bytes 2064392 | tf_op jit(solution)/shard_map/ppermute | solution.py:40
  54.9 44.2 %all-to-all-start.1 = ((bf16[8,24,3584]{2,1,0:T(8,128)(2,1)}), bf16[8,24,3584]{2,1,0:T(8,128)(2,1)S(1)}, u32[]{:S(2)}, u32[]{:S(2)}) async-start(bf16[8,24,3584]{2,1,0:T(8,128)(2,1)} %bitcast.78), calls=%async_computation.1 | async-start | bytes 2752512 | tf_op jit(solution)/shard_map/all_to_all | solution.py:28
  58.7 25.6 %collective-permute-start.2 = (bf16[96,3584]{1,0:T(8,128)(2,1)}, bf16[96,3584]{1,0:T(8,128)(2,1)S(1)}, u32[]{:S(2)}, u32[]{:S(2)}) collective-permute-start(bf16[96,3584]{1,0:T(8,128)(2,1)} %bitcast.3), channel_id=1, source_target_pairs={{0,16},{8,24},{16,0},{24,8},{1,17},{9,25},{17,1},{25,9},{2,18},{10... | collective-permute-start | bytes 2064392 | tf_op jit(solution)/shard_map/ppermute | solution.py:40
  59.2 23.5 %collective-permute-start.1 = (bf16[96,3584]{1,0:T(8,128)(2,1)}, bf16[96,3584]{1,0:T(8,128)(2,1)S(1)}, u32[]{:S(2)}, u32[]{:S(2)}) collective-permute-start(bf16[96,3584]{1,0:T(8,128)(2,1)} %bitcast.4), channel_id=1, source_target_pairs={{0,8},{8,0},{16,24},{24,16},{1,9},{9,1},{17,25},{25,17},{2,10},{10... | collective-permute-start | bytes 2064392 | tf_op jit(solution)/shard_map/ppermute | solution.py:40
  68.1 29.2 %collective-permute-start.4 = (bf16[96,3584]{1,0:T(8,128)(2,1)}, bf16[96,3584]{1,0:T(8,128)(2,1)S(1)}, u32[]{:S(2)}, u32[]{:S(2)}) collective-permute-start(bf16[96,3584]{1,0:T(8,128)(2,1)} %collective-permute-done), channel_id=1, source_target_pairs={{0,16},{8,24},{16,0},{24,8},{1,17},{9,25},{17,1},{25,9},{2,18},{10... | collective-permute-start | bytes 2064392 | tf_op jit(solution)/shard_map/ppermute | solution.py:50
  69.6 28.6 %collective-permute-start.5 = (bf16[96,3584]{1,0:T(8,128)(2,1)S(1)}, bf16[96,3584]{1,0:T(8,128)(2,1)S(1)}, u32[]{:S(2)}, u32[]{:S(2)}) collective-permute-start(bf16[96,3584]{1,0:T(8,128)(2,1)S(1)} %collective-permute-done.3), channel_id=1, source_target_pairs={{0,8},{8,0},{16,24},{24,16},{1,9},{9,1},{17,25},{25,17},{2,10},{10... | collective-permute-start | bytes 2064392 | tf_op jit(solution)/shard_map/ppermute | solution.py:51
  99.2 18.8 %collective-permute-start.9 = (bf16[96,3584]{1,0:T(8,128)(2,1)S(1)}, bf16[96,3584]{1,0:T(8,128)(2,1)S(1)}, u32[]{:S(2)}, u32[]{:S(2)}) collective-permute-start(bf16[96,3584]{1,0:T(8,128)(2,1)S(1)} %get-tuple-element.84), channel_id=1, source_target_pairs={{0,16},{8,24},{16,0},{24,8},{1,17},{9,25},{17,1},{25,9},{2,18},{10... | collective-permute-start | bytes 2064392 | tf_op jit(solution)/shard_map/ppermute | solution.py:40
  100.8 18.4 %collective-permute-start.7 = (bf16[96,3584]{1,0:T(8,128)(2,1)S(1)}, bf16[96,3584]{1,0:T(8,128)(2,1)S(1)}, u32[]{:S(2)}, u32[]{:S(2)}) collective-permute-start(bf16[96,3584]{1,0:T(8,128)(2,1)S(1)} %get-tuple-element.84), channel_id=1, source_target_pairs={{0,8},{8,0},{16,24},{24,16},{1,9},{9,1},{17,25},{25,17},{2,10},{10... | collective-permute-start | bytes 2064392 | tf_op jit(solution)/shard_map/ppermute | solution.py:40
  101.3 8.1 %copy-start.7 = (bf16[1,3584,512]{2,1,0:T(8,128)(2,1)S(1)}, bf16[1,3584,512]{2,1,0:T(8,128)(2,1)}, u32[]{:S(2)}) copy-start(bf16[1,3584,512]{2,1,0:T(8,128)(2,1)} %param.12) | copy-start | bytes 11010052
  101.3 28.5 %collective-permute-start.8 = (bf16[96,3584]{1,0:T(8,128)(2,1)S(1)}, bf16[96,3584]{1,0:T(8,128)(2,1)S(1)}, u32[]{:S(2)}, u32[]{:S(2)}) collective-permute-start(bf16[96,3584]{1,0:T(8,128)(2,1)S(1)} %get-tuple-element.85), channel_id=1, source_target_pairs={{0,16},{8,24},{16,0},{24,8},{1,17},{9,25},{17,1},{25,9},{2,18},{10... | collective-permute-start | bytes 2064392 | tf_op jit(solution)/shard_map/ppermute | solution.py:40
  101.8 29.2 %collective-permute-start.6 = (bf16[96,3584]{1,0:T(8,128)(2,1)S(1)}, bf16[96,3584]{1,0:T(8,128)(2,1)S(1)}, u32[]{:S(2)}, u32[]{:S(2)}) collective-permute-start(bf16[96,3584]{1,0:T(8,128)(2,1)S(1)} %get-tuple-element.85), channel_id=1, source_target_pairs={{0,8},{8,0},{16,24},{24,16},{1,9},{9,1},{17,25},{25,17},{2,10},{10... | collective-permute-start | bytes 2064392 | tf_op jit(solution)/shard_map/ppermute | solution.py:40
  118.0 43.5 %copy-start.3 = (bf16[768,3584]{1,0:T(8,128)(2,1)}, bf16[768,3584]{1,0:T(8,128)(2,1)S(1)}, u32[]{:S(2)}) copy-start(bf16[768,3584]{1,0:T(8,128)(2,1)S(1)} %convolution_convert_fusion) | copy-start | bytes 16515076
  131.0 18.4 %collective-permute-start.10 = (bf16[96,3584]{1,0:T(8,128)(2,1)S(1)}, bf16[96,3584]{1,0:T(8,128)(2,1)S(1)}, u32[]{:S(2)}, u32[]{:S(2)}) collective-permute-start(bf16[96,3584]{1,0:T(8,128)(2,1)S(1)} %collective-permute-done.6), channel_id=1, source_target_pairs={{0,16},{8,24},{16,0},{24,8},{1,17},{9,25},{17,1},{25,9},{2,18},{10... | collective-permute-start | bytes 2064392 | tf_op jit(solution)/shard_map/ppermute | solution.py:50
  131.6 18.4 %collective-permute-start.11 = (bf16[96,3584]{1,0:T(8,128)(2,1)S(1)}, bf16[96,3584]{1,0:T(8,128)(2,1)S(1)}, u32[]{:S(2)}, u32[]{:S(2)}) collective-permute-start(bf16[96,3584]{1,0:T(8,128)(2,1)S(1)} %collective-permute-done.9), channel_id=1, source_target_pairs={{0,8},{8,0},{16,24},{24,16},{1,9},{9,1},{17,25},{25,17},{2,10},{10... | collective-permute-start | bytes 2064392 | tf_op jit(solution)/shard_map/ppermute | solution.py:51
  132.5 27.8 %collective-permute-start.13 = (bf16[96,3584]{1,0:T(8,128)(2,1)S(1)}, bf16[96,3584]{1,0:T(8,128)(2,1)S(1)}, u32[]{:S(2)}, u32[]{:S(2)}) collective-permute-start(bf16[96,3584]{1,0:T(8,128)(2,1)S(1)} %get-tuple-element.80), channel_id=1, source_target_pairs={{0,16},{8,24},{16,0},{24,8},{1,17},{9,25},{17,1},{25,9},{2,18},{10... | collective-permute-start | bytes 2064392 | tf_op jit(solution)/shard_map/ppermute | solution.py:66
  134.1 27.4 %collective-permute-start.12 = (bf16[96,3584]{1,0:T(8,128)(2,1)S(1)}, bf16[96,3584]{1,0:T(8,128)(2,1)S(1)}, u32[]{:S(2)}, u32[]{:S(2)}) collective-permute-start(bf16[96,3584]{1,0:T(8,128)(2,1)S(1)} %get-tuple-element.81), channel_id=1, source_target_pairs={{0,8},{8,0},{16,24},{24,16},{1,9},{9,1},{17,25},{25,17},{2,10},{10... | collective-permute-start | bytes 2064392 | tf_op jit(solution)/shard_map/ppermute | solution.py:65
  161.9 28.9 %collective-permute-start.14 = (bf16[192,3584]{1,0:T(8,128)(2,1)S(1)}, bf16[192,3584]{1,0:T(8,128)(2,1)S(1)}, u32[]{:S(2)}, u32[]{:S(2)}) collective-permute-start(bf16[192,3584]{1,0:T(8,128)(2,1)S(1)} %pad_maximum_fusion), channel_id=1, source_target_pairs={{0,8},{8,0},{16,24},{24,16},{1,9},{9,1},{17,25},{25,17},{2,10},{10... | collective-permute-start | bytes 4128776 | tf_op jit(solution)/shard_map/ppermute | solution.py:82
  162.6 28.3 %collective-permute-start.15 = (bf16[192,3584]{1,0:T(8,128)(2,1)S(1)}, bf16[192,3584]{1,0:T(8,128)(2,1)S(1)}, u32[]{:S(2)}, u32[]{:S(2)}) collective-permute-start(bf16[192,3584]{1,0:T(8,128)(2,1)S(1)} %pad_maximum_fusion.1), channel_id=1, source_target_pairs={{0,16},{8,24},{16,0},{24,8},{1,17},{9,25},{17,1},{25,9},{2,18},{10... | collective-permute-start | bytes 4128776 | tf_op jit(solution)/shard_map/ppermute | solution.py:83
  172.2 5.9 %copy-start.8 = (bf16[768,512]{1,0:T(8,128)(2,1)}, bf16[768,512]{1,0:T(8,128)(2,1)S(1)}, u32[]{:S(2)}) copy-start(bf16[768,512]{1,0:T(8,128)(2,1)S(1)} %get-tuple-element.45) | copy-start | bytes 2359300
  185.5 8.6 %slice-start = ((bf16[768,3584]{1,0:T(8,128)(2,1)}), bf16[192,3584]{1,0:T(8,128)(2,1)S(1)}, s32[]{:S(2)}) async-start(bf16[768,3584]{1,0:T(8,128)(2,1)} %copy-done.3), calls=%async_computation.4 | async-start | bytes 2752512 | tf_op jit(solution)/shard_map/split | solution.py:73
  192.1 13.0 %collective-permute-start.18 = (bf16[96,3584]{1,0:T(8,128)(2,1)}, bf16[96,3584]{1,0:T(8,128)(2,1)}, u32[]{:S(2)}, u32[]{:S(2)}) collective-permute-start(bf16[96,3584]{1,0:T(8,128)(2,1)} %get-tuple-element.72), channel_id=1, source_target_pairs={{0,8},{8,0},{16,24},{24,16},{1,9},{9,1},{17,25},{25,17},{2,10},{10... | collective-permute-start | bytes 2064392 | tf_op jit(solution)/shard_map/ppermute | solution.py:65
  192.7 12.4 %collective-permute-start.16 = (bf16[96,3584]{1,0:T(8,128)(2,1)}, bf16[96,3584]{1,0:T(8,128)(2,1)}, u32[]{:S(2)}, u32[]{:S(2)}) collective-permute-start(bf16[96,3584]{1,0:T(8,128)(2,1)} %get-tuple-element.73), channel_id=1, source_target_pairs={{0,16},{8,24},{16,0},{24,8},{1,17},{9,25},{17,1},{25,9},{2,18},{10... | collective-permute-start | bytes 2064392 | tf_op jit(solution)/shard_map/ppermute | solution.py:66
  195.8 42.5 %all-to-all-start.2 = ((bf16[8,24,3584]{2,1,0:T(8,128)(2,1)}), bf16[8,24,3584]{2,1,0:T(8,128)(2,1)S(1)}, u32[]{:S(2)}, u32[]{:S(2)}) async-start(bf16[8,24,3584]{2,1,0:T(8,128)(2,1)} %bitcast.79), calls=%async_computation.2 | async-start | bytes 2752512 | tf_op jit(solution)/shard_map/all_to_all | solution.py:28
  207.2 27.6 %collective-permute-start.19 = (bf16[192,3584]{1,0:T(8,128)(2,1)S(1)}, bf16[192,3584]{1,0:T(8,128)(2,1)S(1)}, u32[]{:S(2)}, u32[]{:S(2)}) collective-permute-start(bf16[192,3584]{1,0:T(8,128)(2,1)S(1)} %pad_maximum_fusion.3), channel_id=1, source_target_pairs={{0,16},{8,24},{16,0},{24,8},{1,17},{9,25},{17,1},{25,9},{2,18},{10... | collective-permute-start | bytes 4128776 | tf_op jit(solution)/shard_map/ppermute | solution.py:83
  208.9 9.0 %copy-start.11 = (bf16[768,512]{1,0:T(8,128)(2,1)S(1)}, bf16[768,512]{1,0:T(8,128)(2,1)}, u32[]{:S(2)}) copy-start(bf16[768,512]{1,0:T(8,128)(2,1)} %copy-done.10) | copy-start | bytes 2359300
  208.9 26.4 %collective-permute-start.17 = (bf16[192,3584]{1,0:T(8,128)(2,1)S(1)}, bf16[192,3584]{1,0:T(8,128)(2,1)S(1)}, u32[]{:S(2)}, u32[]{:S(2)}) collective-permute-start(bf16[192,3584]{1,0:T(8,128)(2,1)S(1)} %pad_maximum_fusion.2), channel_id=1, source_target_pairs={{0,8},{8,0},{16,24},{24,16},{1,9},{9,1},{17,25},{25,17},{2,10},{10... | collective-permute-start | bytes 4128776 | tf_op jit(solution)/shard_map/ppermute | solution.py:82
  238.3 38.5 %all-to-all-start.3 = ((bf16[8,24,3584]{2,1,0:T(8,128)(2,1)}), bf16[8,24,3584]{2,1,0:T(8,128)(2,1)}, u32[]{:S(2)}, u32[]{:S(2)}) async-start(bf16[8,24,3584]{2,1,0:T(8,128)(2,1)} %bitcast.80), calls=%async_computation.3 | async-start | bytes 2752512 | tf_op jit(solution)/shard_map/all_to_all | solution.py:28
  243.0 36.4 %copy-start.1 = (bf16[128,3584]{1,0:T(8,128)(2,1)S(1)}, bf16[128,3584]{1,0:T(8,128)(2,1)}, u32[]{:S(2)}) copy-start(bf16[128,3584]{1,0:T(8,128)(2,1)} %param.10) | copy-start | bytes 2752516
  (5 other events, 23.7 us)

commit v15 on v14

--- a/solution.py
+++ b/solution.py
@@ -59,11 +59,13 @@
 def reduce_first(partial_rows, groups):
     if groups != 4:
         return ()
-    to_diag = jnp.split(partial_rows, 4, axis=0)[3]
+    _, to_x, to_y, to_diag = jnp.split(partial_rows, 4, axis=0)
     half = to_diag.shape[0] // 2
     return (
         lax.ppermute(to_diag[:half], "dp", perm=pairs(groups, 1)),
         lax.ppermute(to_diag[half:], "dp", perm=pairs(groups, 2)),
+        lax.ppermute(to_x[:half], "dp", perm=pairs(groups, 1)),
+        lax.ppermute(to_y[half:], "dp", perm=pairs(groups, 2)),
     )
 
 
@@ -71,25 +73,23 @@
     if groups != 4:
         return lax.psum_scatter(partial_rows, "dp", scatter_dimension=0, tiled=True)
     own, to_x, to_y, _ = jnp.split(partial_rows, 4, axis=0)
-    via_x, via_y = first
+    via_x, via_y, from_x_lo, from_y_hi = first
     half = own.shape[0] // 2
-    to_y = jnp.concatenate(
-        [(to_y[:half].astype(jnp.float32) + via_x.astype(jnp.float32)).astype(jnp.bfloat16), to_y[half:]], 0
-    )
-    to_x = jnp.concatenate(
-        [to_x[:half], (to_x[half:].astype(jnp.float32) + via_y.astype(jnp.float32)).astype(jnp.bfloat16)], 0
-    )
-    from_x = lax.ppermute(to_x, "dp", perm=pairs(groups, 1))
-    from_y = lax.ppermute(to_y, "dp", perm=pairs(groups, 2))
-    return own, from_x, from_y
+    to_y_lo = (to_y[:half].astype(jnp.float32) + via_x.astype(jnp.float32)).astype(jnp.bfloat16)
+    to_x_hi = (to_x[half:].astype(jnp.float32) + via_y.astype(jnp.float32)).astype(jnp.bfloat16)
+    from_x_hi = lax.ppermute(to_x_hi, "dp", perm=pairs(groups, 1))
+    from_y_lo = lax.ppermute(to_y_lo, "dp", perm=pairs(groups, 2))
+    return own, from_x_lo, from_x_hi, from_y_lo, from_y_hi
 
 
 def add_parts(parts):
     if not isinstance(parts, tuple):
         return parts
-    own, from_x, from_y = parts
-    total = own.astype(jnp.float32) + from_x.astype(jnp.float32) + from_y.astype(jnp.float32)
-    return total.astype(jnp.bfloat16)
+    own, from_x_lo, from_x_hi, from_y_lo, from_y_hi = [part.astype(jnp.float32) for part in parts]
+    half = from_x_lo.shape[0]
+    low = own[:half] + from_x_lo + from_y_lo
+    high = own[half:] + from_x_hi + from_y_hi
+    return jnp.concatenate([low, high], axis=0).astype(jnp.bfloat16)
 
 
 def reduce_dp(partial_rows, groups):

time: 280 us -> 307 us (1.096)
  waiting for transfers between devices: 150 us -> 173 us
  matrix products: 59.9 us -> 63.1 us
    ppermute x2, waiting for transfers between devices: 10.3 us -> 32.7 us  [reduce_first(): lax.ppermute(to_diag[half:], 'dp', perm=pairs(groups, 2))]
    ppermute x4 -> x8, waiting for transfers between devices: 15.7 us -> 23.3 us  [the longest x2 14.1 us: reduce_first(): lax.ppermute(to_y[half:], 'dp', perm=pairs(groups, 2))]
    ppermute x2, waiting for transfers between devices: 6.26 us -> 0.01 us  [reduce_first(): lax.ppermute(to_diag[:half], 'dp', perm=pairs(groups, 1))]
    convert_element_type x3 -> x2, other arithmetic: 6.63 us -> 2.19 us  [add_parts(): part.astype(jnp.float32)]
    ppermute x4 -> x8, starting transfers between devices: 5.56 us -> 8.47 us  [the longest x2 3.05 us: reduce_first(): lax.ppermute(to_x[:half], 'dp', perm=pairs(groups, 1))]
    unnamed x39 -> x47, local copies, waits for them, and re-layouts: 8.8 us -> 8.9 us
  transfers between devices with their start and end apart: 24 -> 28, of which waited for: 17 -> 16; matrix products, arithmetic and copies ran while one was open for 26% -> 24% of each run, Pallas kernels for 0% -> 0%
where the time goes in v15:
time: 307 us; the launch traced here: 306 us
  waiting for transfers between devices  173 us (56%)
  matrix products  63.1 us (21%)
  starting transfers between devices  42.2 us (14%)
  local copies, waits for them, and re-layouts  13.9 us (5%)
  other arithmetic  13.4 us (4%)
    all_to_all x4, waiting for transfers between devices, along_expert(): lax.all_to_all(send_rows, 'expert', split_axis=0, concat_axis=0, tiled=True)  61.9 us
    ppermute x2, waiting for transfers between devices, reduce_first(): lax.ppermute(to_diag[half:], 'dp', perm=pairs(groups, 2))  32.7 us
    ppermute x8, waiting for transfers between devices, swap_halves_first(): lax.ppermute(part, 'dp', perm=pairs(groups, bit))  30.3 us
    dot_general x5, matrix products, contract_first(): lax.dot_general(left, right, (((0,), (0,)), ((), ())), preferred_element_...  25.1 us
    ppermute x2, waiting for transfers between devices, swap_halves_second(): diag_lo = lax.ppermute(x_lo, 'dp', perm=pairs(groups, 2))  24.5 us
    dot_general x3, matrix products, contract_last(): lax.dot_general(left, right, (((1,), (1,)), ((), ())), preferred_element_...  18.9 us
    all_to_all x4, starting transfers between devices, along_expert(): lax.all_to_all(send_rows, 'expert', split_axis=0, concat_axis=0, tiled=True)  18 us
    ppermute x2, waiting for transfers between devices, reduce_first(): lax.ppermute(to_y[half:], 'dp', perm=pairs(groups, 2))  14.1 us
  transfers between devices with their start and end apart: 28, of which 16 were waited for; matrix products, arithmetic and copies ran while one was open for 24% of the time, Pallas kernels for 0%

profile of v15, /device:TPU:0, one launch (start us, length us, event | category | flops | bytes accessed | tf_op | source)
XLA Modules:
  0.0 306.3 jit_solution(17899262088286057823)
XLA Ops:
  1.7 2.3 reduce-window.6
  5.5 2.8 convolution_convert_fusion.5
  8.3 6.3 %all-to-all-start = ((bf16[8,24,3584]{2,1,0:T(8,128)(2,1)}), bf16[8,24,3584]{2,1,0:T(8,128)(2,1)S(1)}, u32[]{:S(2)}, u32[]{:S(2)}) async-start(bf16[8,24,3584]{2,1,0:T(8,128)(2,1)} %bitcast.81), calls=%async_computation | async-start | bytes 2752512 | tf_op jit(solution)/shard_map/all_to_all | solution.py:28
  15.0 33.2 %all-to-all-done = bf16[8,24,3584]{2,1,0:T(8,128)(2,1)S(1)} async-done(((bf16[8,24,3584]{2,1,0:T(8,128)(2,1)}), bf16[8,24,3584]{2,1,0:T(8,128)(2,1)S(1)}, u32[]{:S(2)}, u32[]{:S(2)}) %all-to-all-start) | async-done | bytes 1376288 | tf_op jit(solution)/shard_map/all_to_all | solution.py:28
  52.4 2.5 multiply_convert_fusion
  54.9 3.8 %all-to-all-start.1 = ((bf16[8,24,3584]{2,1,0:T(8,128)(2,1)}), bf16[8,24,3584]{2,1,0:T(8,128)(2,1)S(1)}, u32[]{:S(2)}, u32[]{:S(2)}) async-start(bf16[8,24,3584]{2,1,0:T(8,128)(2,1)} %bitcast.79), calls=%async_computation.1 | async-start | bytes 2752512 | tf_op jit(solution)/shard_map/all_to_all | solution.py:28
  61.0 7.1 %collective-permute-done = bf16[96,3584]{1,0:T(8,128)(2,1)} collective-permute-done((bf16[96,3584]{1,0:T(8,128)(2,1)}, bf16[96,3584]{1,0:T(8,128)(2,1)}, u32[]{:S(2)}, u32[]{:S(2)}) %collective-permute-start) | collective-permute-done | bytes 688160 | tf_op jit(solution)/shard_map/ppermute | solution.py:40
  71.1 2.0 constant_dynamic-update-slice_fusion.5
  73.0 9.6 %collective-permute-done.1 = bf16[96,3584]{1,0:T(8,128)(2,1)S(1)} collective-permute-done((bf16[96,3584]{1,0:T(8,128)(2,1)}, bf16[96,3584]{1,0:T(8,128)(2,1)S(1)}, u32[]{:S(2)}, u32[]{:S(2)}) %collective-permute-start.1) | collective-permute-done | bytes 688160 | tf_op jit(solution)/shard_map/ppermute | solution.py:40
  86.1 11.2 %collective-permute-done.4 = bf16[96,3584]{1,0:T(8,128)(2,1)S(1)} collective-permute-done((bf16[96,3584]{1,0:T(8,128)(2,1)}, bf16[96,3584]{1,0:T(8,128)(2,1)S(1)}, u32[]{:S(2)}, u32[]{:S(2)}) %collective-permute-start.4) | collective-permute-done | bytes 688160 | tf_op jit(solution)/shard_map/ppermute | solution.py:50
  103.3 6.1 %fusion.12 = f32[768,512]{1,0:T(8,128)S(1)} fusion(bf16[768,3584]{1,0:T(8,128)(2,1)} %constant_dynamic-update-slice_fusion, bf16[1,3584,512]{2,1,0:T(8,128)(2,1)} %param.11), kind=kOutput, calls=%fused_computation.21 | convolution fusion | flops 2818572288 | bytes 10747904 | tf_op jit(solution)/shard_map/dot_general | solution.py:122
  109.4 5.2 %multiply_convert_fusion.3 = (bf16[768,512]{1,0:T(8,128)(2,1)S(1)}, f32[768,512]{1,0:T(8,128)S(1)}) fusion(f32[768,512]{1,0:T(8,128)S(1)} %fusion.12, bf16[768,3584]{1,0:T(8,128)(2,1)} %constant_dynamic-update-slice_fusion, bf16[1,3584,512]{2,1,0:T(8,128)(2,1)S(1)} %copy-done.9), kind=kOutput, calls=%fused_computation.28 | convolution fusion | flops 2820931584 | bytes 13107200 | tf_op jit(solution)/shard_map/dot_general | solution.py:123
  114.8 3.2 %convolution_convert_fusion = bf16[768,3584]{1,0:T(8,128)(2,1)S(1)} fusion(bf16[768,512]{1,0:T(8,128)(2,1)S(1)} %get-tuple-element.55, bf16[1,512,3584]{2,1,0:T(8,128)(2,1)S(1)} %copy-done.7), kind=kOutput, calls=%fused_computation.1 | convolution fusion | flops 2821324800 | bytes 9961472 | tf_op jit(solution)/shard_map/dot_general | solution.py:127
  119.1 10.6 %collective-permute-done.8 = bf16[96,3584]{1,0:T(8,128)(2,1)S(1)} collective-permute-done((bf16[96,3584]{1,0:T(8,128)(2,1)S(1)}, bf16[96,3584]{1,0:T(8,128)(2,1)S(1)}, u32[]{:S(2)}, u32[]{:S(2)}) %collective-permute-start.8) | collective-permute-done | bytes 688160 | tf_op jit(solution)/shard_map/ppermute | solution.py:40
  136.1 13.3 %collective-permute-done.10 = bf16[96,3584]{1,0:T(8,128)(2,1)S(1)} collective-permute-done((bf16[96,3584]{1,0:T(8,128)(2,1)S(1)}, bf16[96,3584]{1,0:T(8,128)(2,1)S(1)}, u32[]{:S(2)}, u32[]{:S(2)}) %collective-permute-start.10) | collective-permute-done | bytes 688160 | tf_op jit(solution)/shard_map/ppermute | solution.py:50
  150.1 14.1 %collective-permute-done.15 = bf16[96,3584]{1,0:T(8,128)(2,1)S(1)} collective-permute-done((bf16[96,3584]{1,0:T(8,128)(2,1)S(1)}, bf16[96,3584]{1,0:T(8,128)(2,1)S(1)}, u32[]{:S(2)}, u32[]{:S(2)}) %collective-permute-start.15) | collective-permute-done | bytes 688160 | tf_op jit(solution)/shard_map/ppermute | solution.py:68
  164.7 10.8 %collective-permute-done.13 = bf16[96,3584]{1,0:T(8,128)(2,1)S(1)} collective-permute-done((bf16[96,3584]{1,0:T(8,128)(2,1)S(1)}, bf16[96,3584]{1,0:T(8,128)(2,1)S(1)}, u32[]{:S(2)}, u32[]{:S(2)}) %collective-permute-start.13) | collective-permute-done | bytes 688160 | tf_op jit(solution)/shard_map/ppermute | solution.py:66
  175.9 2.0 collective-permute-start.17
  178.4 4.4 %multiply_convert_fusion.1 = (bf16[768,512]{1,0:T(8,128)(2,1)}, bf16[768,512]{1,0:T(8,128)(2,1)S(1)}) fusion(f32[768,512]{1,0:T(8,128)S(1)} %fusion.12, f32[768,512]{1,0:T(8,128)S(1)} %get-tuple-element.41, bf16[768,3584]{1,0:T(8,128)(2,1)S(1)} %constant_dynamic-update-slice_fusion.7, bf16[1,512,3584]{2,1,0:T(8,128)(2,1)S(1)} %copy-done.7), kind=kOutput, calls=%fused_computation.25 | convolution fusion | flops 2823684096 | bytes 13893632 | tf_op jit(solution)/shard_map/dot_general | solution.py:16
  182.8 5.8 %fusion.10 = f32[768,3584]{1,0:T(8,128)} fusion(bf16[768,512]{1,0:T(8,128)(2,1)S(1)} %get-tuple-element.53, bf16[1,3584,512]{2,1,0:T(8,128)(2,1)S(1)} %copy-done.8), kind=kOutput, calls=%fused_computation.19 | convolution fusion | flops 2818572288 | bytes 15466496 | tf_op jit(solution)/shard_map/dot_general | solution.py:16
  188.7 8.7 %add_convert_fusion = bf16[768,3584]{1,0:T(8,128)(2,1)S(1)} fusion(f32[768,3584]{1,0:T(8,128)} %fusion.10, bf16[768,512]{1,0:T(8,128)(2,1)} %get-tuple-element.54, bf16[1,3584,512]{2,1,0:T(8,128)(2,1)} %param.12), kind=kOutput, calls=%fused_computation | convolution fusion | flops 2824077312 | bytes 20971520 | tf_op jit(solution)/shard_map/dot_general | solution.py:16
  197.4 4.8 %fusion.2 = bf16[1,512,3584]{2,1,0:T(8,128)(2,1)} fusion(bf16[768,512]{1,0:T(8,128)(2,1)S(1)} %copy-done.12, bf16[768,3584]{1,0:T(8,128)(2,1)S(1)} %bitcast.83), kind=kOutput, calls=%fused_computation.7 | convolution fusion | flops 2820407296 | bytes 9961472 | tf_op jit(solution)/shard_map/dot_general | solution.py:22
  208.0 3.6 %all-to-all-start.2 = ((bf16[8,24,3584]{2,1,0:T(8,128)(2,1)}), bf16[8,24,3584]{2,1,0:T(8,128)(2,1)S(1)}, u32[]{:S(2)}, u32[]{:S(2)}) async-start(bf16[8,24,3584]{2,1,0:T(8,128)(2,1)} %bitcast.78), calls=%async_computation.2 | async-start | bytes 2752512 | tf_op jit(solution)/shard_map/all_to_all | solution.py:28
  215.7 7.6 %fusion = bf16[1,3584,512]{2,1,0:T(8,128)(2,1)} fusion(bf16[768,3584]{1,0:T(8,128)(2,1)} %constant_dynamic-update-slice_fusion, bf16[768,512]{1,0:T(8,128)(2,1)} %copy-done.10), kind=kOutput, calls=%fused_computation.5 | convolution fusion | flops 2820407296 | bytes 9961472 | tf_op jit(solution)/shard_map/dot_general | solution.py:22
  223.3 21.9 %collective-permute-done.21 = bf16[96,3584]{1,0:T(8,128)(2,1)S(1)} collective-permute-done((bf16[96,3584]{1,0:T(8,128)(2,1)}, bf16[96,3584]{1,0:T(8,128)(2,1)S(1)}, u32[]{:S(2)}, u32[]{:S(2)}) %collective-permute-start.21) | collective-permute-done | bytes 688160 | tf_op jit(solution)/shard_map/ppermute | solution.py:66
  247.9 7.4 %fusion.1 = bf16[1,3584,512]{2,1,0:T(8,128)(2,1)} fusion(bf16[768,3584]{1,0:T(8,128)(2,1)} %constant_dynamic-update-slice_fusion, bf16[768,512]{1,0:T(8,128)(2,1)S(1)} %copy-done.13), kind=kOutput, calls=%fused_computation.6 | convolution fusion | flops 2820407296 | bytes 9961472 | tf_op jit(solution)/shard_map/dot_general | solution.py:22
  255.3 8.2 %collective-permute-done.20 = bf16[96,3584]{1,0:T(8,128)(2,1)S(1)} collective-permute-done((bf16[96,3584]{1,0:T(8,128)(2,1)S(1)}, bf16[96,3584]{1,0:T(8,128)(2,1)S(1)}, u32[]{:S(2)}, u32[]{:S(2)}) %collective-permute-start.20) | collective-permute-done | bytes 688160 | tf_op jit(solution)/shard_map/ppermute | solution.py:81
  265.5 4.3 %all-to-all-start.3 = ((bf16[8,24,3584]{2,1,0:T(8,128)(2,1)}), bf16[8,24,3584]{2,1,0:T(8,128)(2,1)}, u32[]{:S(2)}, u32[]{:S(2)}) async-start(bf16[8,24,3584]{2,1,0:T(8,128)(2,1)} %bitcast.80), calls=%async_computation.3 | async-start | bytes 2752512 | tf_op jit(solution)/shard_map/all_to_all | solution.py:28
  269.8 2.2 multiply_reduce_fusion
  273.0 1.9 convolution_convert_fusion.7
  274.9 28.6 %all-to-all-done.3 = bf16[8,24,3584]{2,1,0:T(8,128)(2,1)} async-done(((bf16[8,24,3584]{2,1,0:T(8,128)(2,1)}), bf16[8,24,3584]{2,1,0:T(8,128)(2,1)}, u32[]{:S(2)}, u32[]{:S(2)}) %all-to-all-start.3) | async-done | bytes 1376288 | tf_op jit(solution)/shard_map/all_to_all | solution.py:28
  303.5 2.7 convolution_convert_fusion.6
  (119 shorter events, 46.9 us)
Async XLA Ops:
  0.6 51.8 %copy-start = (bf16[128,3584]{1,0:T(8,128)(2,1)S(1)}, bf16[128,3584]{1,0:T(8,128)(2,1)}, u32[]{:S(2)}) copy-start(bf16[128,3584]{1,0:T(8,128)(2,1)} %param.10) | copy-start | bytes 2752516
  8.3 39.9 %all-to-all-start = ((bf16[8,24,3584]{2,1,0:T(8,128)(2,1)}), bf16[8,24,3584]{2,1,0:T(8,128)(2,1)S(1)}, u32[]{:S(2)}, u32[]{:S(2)}) async-start(bf16[8,24,3584]{2,1,0:T(8,128)(2,1)} %bitcast.81), calls=%async_computation | async-start | bytes 2752512 | tf_op jit(solution)/shard_map/all_to_all | solution.py:28
  49.4 18.7 %collective-permute-start = (bf16[96,3584]{1,0:T(8,128)(2,1)}, bf16[96,3584]{1,0:T(8,128)(2,1)}, u32[]{:S(2)}, u32[]{:S(2)}) collective-permute-start(bf16[96,3584]{1,0:T(8,128)(2,1)} %bitcast.3), channel_id=1, source_target_pairs={{0,8},{8,0},{16,24},{24,16},{1,9},{9,1},{17,25},{25,17},{2,10},{10... | collective-permute-start | bytes 2064392 | tf_op jit(solution)/shard_map/ppermute | solution.py:40
  50.9 18.7 %collective-permute-start.3 = (bf16[96,3584]{1,0:T(8,128)(2,1)}, bf16[96,3584]{1,0:T(8,128)(2,1)S(1)}, u32[]{:S(2)}, u32[]{:S(2)}) collective-permute-start(bf16[96,3584]{1,0:T(8,128)(2,1)} %bitcast.4), channel_id=1, source_target_pairs={{0,16},{8,24},{16,0},{24,8},{1,17},{9,25},{17,1},{25,9},{2,18},{10... | collective-permute-start | bytes 2064392 | tf_op jit(solution)/shard_map/ppermute | solution.py:40
  54.9 44.2 %all-to-all-start.1 = ((bf16[8,24,3584]{2,1,0:T(8,128)(2,1)}), bf16[8,24,3584]{2,1,0:T(8,128)(2,1)S(1)}, u32[]{:S(2)}, u32[]{:S(2)}) async-start(bf16[8,24,3584]{2,1,0:T(8,128)(2,1)} %bitcast.79), calls=%async_computation.1 | async-start | bytes 2752512 | tf_op jit(solution)/shard_map/all_to_all | solution.py:28
  58.7 25.6 %collective-permute-start.2 = (bf16[96,3584]{1,0:T(8,128)(2,1)}, bf16[96,3584]{1,0:T(8,128)(2,1)S(1)}, u32[]{:S(2)}, u32[]{:S(2)}) collective-permute-start(bf16[96,3584]{1,0:T(8,128)(2,1)} %bitcast.3), channel_id=1, source_target_pairs={{0,16},{8,24},{16,0},{24,8},{1,17},{9,25},{17,1},{25,9},{2,18},{10... | collective-permute-start | bytes 2064392 | tf_op jit(solution)/shard_map/ppermute | solution.py:40
  59.2 23.5 %collective-permute-start.1 = (bf16[96,3584]{1,0:T(8,128)(2,1)}, bf16[96,3584]{1,0:T(8,128)(2,1)S(1)}, u32[]{:S(2)}, u32[]{:S(2)}) collective-permute-start(bf16[96,3584]{1,0:T(8,128)(2,1)} %bitcast.4), channel_id=1, source_target_pairs={{0,8},{8,0},{16,24},{24,16},{1,9},{9,1},{17,25},{25,17},{2,10},{10... | collective-permute-start | bytes 2064392 | tf_op jit(solution)/shard_map/ppermute | solution.py:40
  68.1 29.2 %collective-permute-start.4 = (bf16[96,3584]{1,0:T(8,128)(2,1)}, bf16[96,3584]{1,0:T(8,128)(2,1)S(1)}, u32[]{:S(2)}, u32[]{:S(2)}) collective-permute-start(bf16[96,3584]{1,0:T(8,128)(2,1)} %collective-permute-done), channel_id=1, source_target_pairs={{0,16},{8,24},{16,0},{24,8},{1,17},{9,25},{17,1},{25,9},{2,18},{10... | collective-permute-start | bytes 2064392 | tf_op jit(solution)/shard_map/ppermute | solution.py:50
  69.6 28.6 %collective-permute-start.5 = (bf16[96,3584]{1,0:T(8,128)(2,1)S(1)}, bf16[96,3584]{1,0:T(8,128)(2,1)S(1)}, u32[]{:S(2)}, u32[]{:S(2)}) collective-permute-start(bf16[96,3584]{1,0:T(8,128)(2,1)S(1)} %collective-permute-done.3), channel_id=1, source_target_pairs={{0,8},{8,0},{16,24},{24,16},{1,9},{9,1},{17,25},{25,17},{2,10},{10... | collective-permute-start | bytes 2064392 | tf_op jit(solution)/shard_map/ppermute | solution.py:51
  99.2 18.9 %collective-permute-start.9 = (bf16[96,3584]{1,0:T(8,128)(2,1)S(1)}, bf16[96,3584]{1,0:T(8,128)(2,1)S(1)}, u32[]{:S(2)}, u32[]{:S(2)}) collective-permute-start(bf16[96,3584]{1,0:T(8,128)(2,1)S(1)} %get-tuple-element.96), channel_id=1, source_target_pairs={{0,16},{8,24},{16,0},{24,8},{1,17},{9,25},{17,1},{25,9},{2,18},{10... | collective-permute-start | bytes 2064392 | tf_op jit(solution)/shard_map/ppermute | solution.py:40
  100.8 18.4 %collective-permute-start.7 = (bf16[96,3584]{1,0:T(8,128)(2,1)S(1)}, bf16[96,3584]{1,0:T(8,128)(2,1)S(1)}, u32[]{:S(2)}, u32[]{:S(2)}) collective-permute-start(bf16[96,3584]{1,0:T(8,128)(2,1)S(1)} %get-tuple-element.96), channel_id=1, source_target_pairs={{0,8},{8,0},{16,24},{24,16},{1,9},{9,1},{17,25},{25,17},{2,10},{10... | collective-permute-start | bytes 2064392 | tf_op jit(solution)/shard_map/ppermute | solution.py:40
  101.3 28.5 %collective-permute-start.8 = (bf16[96,3584]{1,0:T(8,128)(2,1)S(1)}, bf16[96,3584]{1,0:T(8,128)(2,1)S(1)}, u32[]{:S(2)}, u32[]{:S(2)}) collective-permute-start(bf16[96,3584]{1,0:T(8,128)(2,1)S(1)} %get-tuple-element.97), channel_id=1, source_target_pairs={{0,16},{8,24},{16,0},{24,8},{1,17},{9,25},{17,1},{25,9},{2,18},{10... | collective-permute-start | bytes 2064392 | tf_op jit(solution)/shard_map/ppermute | solution.py:40
  101.8 29.2 %collective-permute-start.6 = (bf16[96,3584]{1,0:T(8,128)(2,1)S(1)}, bf16[96,3584]{1,0:T(8,128)(2,1)S(1)}, u32[]{:S(2)}, u32[]{:S(2)}) collective-permute-start(bf16[96,3584]{1,0:T(8,128)(2,1)S(1)} %get-tuple-element.97), channel_id=1, source_target_pairs={{0,8},{8,0},{16,24},{24,16},{1,9},{9,1},{17,25},{25,17},{2,10},{10... | collective-permute-start | bytes 2064392 | tf_op jit(solution)/shard_map/ppermute | solution.py:40
  118.0 57.5 %copy-start.3 = (bf16[768,3584]{1,0:T(8,128)(2,1)}, bf16[768,3584]{1,0:T(8,128)(2,1)S(1)}, u32[]{:S(2)}) copy-start(bf16[768,3584]{1,0:T(8,128)(2,1)S(1)} %convolution_convert_fusion) | copy-start | bytes 16515076
  131.0 18.4 %collective-permute-start.10 = (bf16[96,3584]{1,0:T(8,128)(2,1)S(1)}, bf16[96,3584]{1,0:T(8,128)(2,1)S(1)}, u32[]{:S(2)}, u32[]{:S(2)}) collective-permute-start(bf16[96,3584]{1,0:T(8,128)(2,1)S(1)} %collective-permute-done.6), channel_id=1, source_target_pairs={{0,16},{8,24},{16,0},{24,8},{1,17},{9,25},{17,1},{25,9},{2,18},{10... | collective-permute-start | bytes 2064392 | tf_op jit(solution)/shard_map/ppermute | solution.py:50
  131.6 18.4 %collective-permute-start.11 = (bf16[96,3584]{1,0:T(8,128)(2,1)S(1)}, bf16[96,3584]{1,0:T(8,128)(2,1)S(1)}, u32[]{:S(2)}, u32[]{:S(2)}) collective-permute-start(bf16[96,3584]{1,0:T(8,128)(2,1)S(1)} %collective-permute-done.9), channel_id=1, source_target_pairs={{0,8},{8,0},{16,24},{24,16},{1,9},{9,1},{17,25},{25,17},{2,10},{10... | collective-permute-start | bytes 2064392 | tf_op jit(solution)/shard_map/ppermute | solution.py:51
  132.5 31.6 %collective-permute-start.15 = (bf16[96,3584]{1,0:T(8,128)(2,1)S(1)}, bf16[96,3584]{1,0:T(8,128)(2,1)S(1)}, u32[]{:S(2)}, u32[]{:S(2)}) collective-permute-start(bf16[96,3584]{1,0:T(8,128)(2,1)S(1)} %get-tuple-element.86), channel_id=1, source_target_pairs={{0,16},{8,24},{16,0},{24,8},{1,17},{9,25},{17,1},{25,9},{2,18},{10... | collective-permute-start | bytes 2064392 | tf_op jit(solution)/shard_map/ppermute | solution.py:68
  134.1 30.6 %collective-permute-start.14 = (bf16[96,3584]{1,0:T(8,128)(2,1)S(1)}, bf16[96,3584]{1,0:T(8,128)(2,1)S(1)}, u32[]{:S(2)}, u32[]{:S(2)}) collective-permute-start(bf16[96,3584]{1,0:T(8,128)(2,1)S(1)} %get-tuple-element.87), channel_id=1, source_target_pairs={{0,8},{8,0},{16,24},{24,16},{1,9},{9,1},{17,25},{25,17},{2,10},{10... | collective-permute-start | bytes 2064392 | tf_op jit(solution)/shard_map/ppermute | solution.py:67
  135.6 39.9 %collective-permute-start.13 = (bf16[96,3584]{1,0:T(8,128)(2,1)S(1)}, bf16[96,3584]{1,0:T(8,128)(2,1)S(1)}, u32[]{:S(2)}, u32[]{:S(2)}) collective-permute-start(bf16[96,3584]{1,0:T(8,128)(2,1)S(1)} %get-tuple-element.88), channel_id=1, source_target_pairs={{0,16},{8,24},{16,0},{24,8},{1,17},{9,25},{17,1},{25,9},{2,18},{10... | collective-permute-start | bytes 2064392 | tf_op jit(solution)/shard_map/ppermute | solution.py:66
  149.4 26.2 %collective-permute-start.12 = (bf16[96,3584]{1,0:T(8,128)(2,1)S(1)}, bf16[96,3584]{1,0:T(8,128)(2,1)S(1)}, u32[]{:S(2)}, u32[]{:S(2)}) collective-permute-start(bf16[96,3584]{1,0:T(8,128)(2,1)S(1)} %get-tuple-element.89), channel_id=1, source_target_pairs={{0,8},{8,0},{16,24},{24,16},{1,9},{9,1},{17,25},{25,17},{2,10},{10... | collective-permute-start | bytes 2064392 | tf_op jit(solution)/shard_map/ppermute | solution.py:65
  150.0 32.8 %copy-start.5 = (bf16[768,3584]{1,0:T(8,128)(2,1)}, bf16[768,3584]{1,0:T(8,128)(2,1)S(1)}, u32[]{:S(2)}) copy-start(bf16[768,3584]{1,0:T(8,128)(2,1)S(1)} %constant_dynamic-update-slice_fusion.7) | copy-start | bytes 16515076
  175.9 26.3 %collective-permute-start.17 = (bf16[96,3584]{1,0:T(8,128)(2,1)S(1)}, bf16[96,3584]{1,0:T(8,128)(2,1)S(1)}, u32[]{:S(2)}, u32[]{:S(2)}) collective-permute-start(bf16[96,3584]{1,0:T(8,128)(2,1)S(1)} %get-tuple-element.84), channel_id=1, source_target_pairs={{0,16},{8,24},{16,0},{24,8},{1,17},{9,25},{17,1},{25,9},{2,18},{10... | collective-permute-start | bytes 2064392 | tf_op jit(solution)/shard_map/ppermute | solution.py:81
  177.9 24.3 %collective-permute-start.16 = (bf16[96,3584]{1,0:T(8,128)(2,1)S(1)}, bf16[96,3584]{1,0:T(8,128)(2,1)S(1)}, u32[]{:S(2)}, u32[]{:S(2)}) collective-permute-start(bf16[96,3584]{1,0:T(8,128)(2,1)S(1)} %get-tuple-element.85), channel_id=1, source_target_pairs={{0,8},{8,0},{16,24},{24,16},{1,9},{9,1},{17,25},{25,17},{2,10},{10... | collective-permute-start | bytes 2064392 | tf_op jit(solution)/shard_map/ppermute | solution.py:80
  208.0 57.5 %all-to-all-start.2 = ((bf16[8,24,3584]{2,1,0:T(8,128)(2,1)}), bf16[8,24,3584]{2,1,0:T(8,128)(2,1)S(1)}, u32[]{:S(2)}, u32[]{:S(2)}) async-start(bf16[8,24,3584]{2,1,0:T(8,128)(2,1)} %bitcast.78), calls=%async_computation.2 | async-start | bytes 2752512 | tf_op jit(solution)/shard_map/all_to_all | solution.py:28
  211.5 43.7 %collective-permute-start.18 = (bf16[96,3584]{1,0:T(8,128)(2,1)S(1)}, bf16[96,3584]{1,0:T(8,128)(2,1)S(1)}, u32[]{:S(2)}, u32[]{:S(2)}) collective-permute-start(bf16[96,3584]{1,0:T(8,128)(2,1)S(1)} %get-tuple-element.78), channel_id=1, source_target_pairs={{0,8},{8,0},{16,24},{24,16},{1,9},{9,1},{17,25},{25,17},{2,10},{10... | collective-permute-start | bytes 2064392 | tf_op jit(solution)/shard_map/ppermute | solution.py:67
  213.1 42.2 %collective-permute-start.23 = (bf16[96,3584]{1,0:T(8,128)(2,1)S(1)}, bf16[96,3584]{1,0:T(8,128)(2,1)S(1)}, u32[]{:S(2)}, u32[]{:S(2)}) collective-permute-start(bf16[96,3584]{1,0:T(8,128)(2,1)S(1)} %get-tuple-element.79), channel_id=1, source_target_pairs={{0,16},{8,24},{16,0},{24,8},{1,17},{9,25},{17,1},{25,9},{2,18},{10... | collective-permute-start | bytes 2064392 | tf_op jit(solution)/shard_map/ppermute | solution.py:68
  213.3 31.9 %collective-permute-start.21 = (bf16[96,3584]{1,0:T(8,128)(2,1)}, bf16[96,3584]{1,0:T(8,128)(2,1)S(1)}, u32[]{:S(2)}, u32[]{:S(2)}) collective-permute-start(bf16[96,3584]{1,0:T(8,128)(2,1)} %get-tuple-element.80), channel_id=1, source_target_pairs={{0,16},{8,24},{16,0},{24,8},{1,17},{9,25},{17,1},{25,9},{2,18},{10... | collective-permute-start | bytes 2064392 | tf_op jit(solution)/shard_map/ppermute | solution.py:66
  215.1 30.1 %collective-permute-start.19 = (bf16[96,3584]{1,0:T(8,128)(2,1)}, bf16[96,3584]{1,0:T(8,128)(2,1)S(1)}, u32[]{:S(2)}, u32[]{:S(2)}) collective-permute-start(bf16[96,3584]{1,0:T(8,128)(2,1)} %get-tuple-element.81), channel_id=1, source_target_pairs={{0,8},{8,0},{16,24},{24,16},{1,9},{9,1},{17,25},{25,17},{2,10},{10... | collective-permute-start | bytes 2064392 | tf_op jit(solution)/shard_map/ppermute | solution.py:65
  246.9 16.6 %collective-permute-start.20 = (bf16[96,3584]{1,0:T(8,128)(2,1)S(1)}, bf16[96,3584]{1,0:T(8,128)(2,1)S(1)}, u32[]{:S(2)}, u32[]{:S(2)}) collective-permute-start(bf16[96,3584]{1,0:T(8,128)(2,1)S(1)} %get-tuple-element.82), channel_id=1, source_target_pairs={{0,16},{8,24},{16,0},{24,8},{1,17},{9,25},{17,1},{25,9},{2,18},{10... | collective-permute-start | bytes 2064392 | tf_op jit(solution)/shard_map/ppermute | solution.py:81
  247.4 16.5 %collective-permute-start.22 = (bf16[96,3584]{1,0:T(8,128)(2,1)S(1)}, bf16[96,3584]{1,0:T(8,128)(2,1)S(1)}, u32[]{:S(2)}, u32[]{:S(2)}) collective-permute-start(bf16[96,3584]{1,0:T(8,128)(2,1)S(1)} %get-tuple-element.83), channel_id=1, source_target_pairs={{0,8},{8,0},{16,24},{24,16},{1,9},{9,1},{17,25},{25,17},{2,10},{10... | collective-permute-start | bytes 2064392 | tf_op jit(solution)/shard_map/ppermute | solution.py:80
  265.5 38.1 %all-to-all-start.3 = ((bf16[8,24,3584]{2,1,0:T(8,128)(2,1)}), bf16[8,24,3584]{2,1,0:T(8,128)(2,1)}, u32[]{:S(2)}, u32[]{:S(2)}) async-start(bf16[8,24,3584]{2,1,0:T(8,128)(2,1)} %bitcast.80), calls=%async_computation.3 | async-start | bytes 2752512 | tf_op jit(solution)/shard_map/all_to_all | solution.py:28
  269.8 36.4 %copy-start.1 = (bf16[128,3584]{1,0:T(8,128)(2,1)S(1)}, bf16[128,3584]{1,0:T(8,128)(2,1)}, u32[]{:S(2)}) copy-start(bf16[128,3584]{1,0:T(8,128)(2,1)} %param.10) | copy-start | bytes 2752516
  (13 other events, 122.0 us)

commit v16 on v14

--- a/solution.py
+++ b/solution.py
@@ -59,18 +59,25 @@
 def reduce_first(partial_rows, groups):
     if groups != 4:
         return ()
-    to_diag = jnp.split(partial_rows, 4, axis=0)[3]
-    half = to_diag.shape[0] // 2
+    if isinstance(partial_rows, tuple):
+        diag_lo, diag_hi = partial_rows[1:]
+    else:
+        to_diag = jnp.split(partial_rows, 4, axis=0)[3]
+        half = to_diag.shape[0] // 2
+        diag_lo, diag_hi = to_diag[:half], to_diag[half:]
     return (
-        lax.ppermute(to_diag[:half], "dp", perm=pairs(groups, 1)),
-        lax.ppermute(to_diag[half:], "dp", perm=pairs(groups, 2)),
+        lax.ppermute(diag_lo, "dp", perm=pairs(groups, 1)),
+        lax.ppermute(diag_hi, "dp", perm=pairs(groups, 2)),
     )
 
 
 def reduce_second(partial_rows, first, groups):
     if groups != 4:
         return lax.psum_scatter(partial_rows, "dp", scatter_dimension=0, tiled=True)
-    own, to_x, to_y, _ = jnp.split(partial_rows, 4, axis=0)
+    if isinstance(partial_rows, tuple):
+        own, to_x, to_y = jnp.split(partial_rows[0], 3, axis=0)
+    else:
+        own, to_x, to_y, _ = jnp.split(partial_rows, 4, axis=0)
     via_x, via_y = first
     half = own.shape[0] // 2
     to_y = jnp.concatenate(
@@ -124,7 +131,19 @@
     sigmoid_g = jax.nn.sigmoid(gate_pre)
     activated = gate_pre * sigmoid_g
     hidden = (activated * up_pre).astype(jnp.bfloat16)
-    part_out = jnp.dot(hidden, down_w, preferred_element_type=jnp.float32).astype(jnp.bfloat16)
+    def output_part(lo, hi):
+        return jnp.dot(hidden[lo:hi], down_w, preferred_element_type=jnp.float32).astype(jnp.bfloat16)
+
+    rows = hidden.shape[0]
+    if groups == 4:
+        block = rows // 4
+        part_out = (
+            output_part(0, 3 * block),
+            output_part(3 * block, 3 * block + block // 2),
+            output_part(3 * block + block // 2, rows),
+        )
+    else:
+        part_out = output_part(0, rows)
     part_out, hidden, gate_pre, up_pre, c_first = lax.optimization_barrier(
         (part_out, hidden, gate_pre, up_pre, c_first)
     )

time: 280 us -> 280 us (level)
  waiting for transfers between devices: 150 us -> 155 us
  starting transfers between devices: 42 us -> 38.3 us
    ppermute x2, waiting for transfers between devices: 25 us -> 36.4 us  [swap_halves_second(): diag_lo = lax.ppermute(x_lo, 'dp', perm=pairs(groups, 2))]
    ppermute x4, waiting for transfers between devices: 16.5 us -> 7.22 us  [the longest x2 5.75 us: reduce_first(): lax.ppermute(diag_lo, 'dp', perm=pairs(groups, 1))]
    unnamed x39 -> x40, local copies, waits for them, and re-layouts: 8.8 us -> 8.89 us
where the time goes in v16:
time: 280 us; the launch traced here: 279 us
  waiting for transfers between devices  155 us (55%)
  matrix products  58.3 us (21%)
  starting transfers between devices  38.3 us (14%)
  local copies, waits for them, and re-layouts  13.3 us (5%)
  other arithmetic  13.2 us (5%)
    all_to_all x4, waiting for transfers between devices, along_expert(): lax.all_to_all(send_rows, 'expert', split_axis=0, concat_axis=0, tiled=True)  61.9 us
    ppermute x2, waiting for transfers between devices, swap_halves_second(): diag_lo = lax.ppermute(x_lo, 'dp', perm=pairs(groups, 2))  36.4 us
    ppermute x8, waiting for transfers between devices, swap_halves_first(): lax.ppermute(part, 'dp', perm=pairs(groups, bit))  30.7 us
    dot_general x5, matrix products, contract_first(): lax.dot_general(left, right, (((0,), (0,)), ((), ())), preferred_element_...  24 us
    all_to_all x4, starting transfers between devices, along_expert(): lax.all_to_all(send_rows, 'expert', split_axis=0, concat_axis=0, tiled=True)  18.8 us
    dot_general x3, matrix products, contract_last(): lax.dot_general(left, right, (((1,), (1,)), ((), ())), preferred_element_...  15.4 us
    ppermute x2, waiting for transfers between devices, reduce_second(): from_y = lax.ppermute(to_y, 'dp', perm=pairs(groups, 2))  11.7 us
    unnamed x40, local copies, waits for them, and re-layouts  8.89 us
  transfers between devices with their start and end apart: 24, of which 17 were waited for; matrix products, arithmetic and copies ran while one was open for 26% of the time, Pallas kernels for 0%

profile of v16, /device:TPU:0, one launch (start us, length us, event | category | flops | bytes accessed | tf_op | source)
XLA Modules:
  0.0 279.5 jit_solution(1237999113831445656)
XLA Ops:
  1.7 2.3 reduce-window.6
  5.5 2.8 convolution_convert_fusion.5
  8.3 6.3 %all-to-all-start = ((bf16[8,24,3584]{2,1,0:T(8,128)(2,1)}), bf16[8,24,3584]{2,1,0:T(8,128)(2,1)S(1)}, u32[]{:S(2)}, u32[]{:S(2)}) async-start(bf16[8,24,3584]{2,1,0:T(8,128)(2,1)} %bitcast.84), calls=%async_computation | async-start | bytes 2752512 | tf_op jit(solution)/shard_map/all_to_all | solution.py:28
  15.0 33.2 %all-to-all-done = bf16[8,24,3584]{2,1,0:T(8,128)(2,1)S(1)} async-done(((bf16[8,24,3584]{2,1,0:T(8,128)(2,1)}), bf16[8,24,3584]{2,1,0:T(8,128)(2,1)S(1)}, u32[]{:S(2)}, u32[]{:S(2)}) %all-to-all-start) | async-done | bytes 1376288 | tf_op jit(solution)/shard_map/all_to_all | solution.py:28
  52.4 2.5 multiply_convert_fusion
  54.9 3.8 %all-to-all-start.1 = ((bf16[8,24,3584]{2,1,0:T(8,128)(2,1)}), bf16[8,24,3584]{2,1,0:T(8,128)(2,1)S(1)}, u32[]{:S(2)}, u32[]{:S(2)}) async-start(bf16[8,24,3584]{2,1,0:T(8,128)(2,1)} %bitcast.81), calls=%async_computation.1 | async-start | bytes 2752512 | tf_op jit(solution)/shard_map/all_to_all | solution.py:28
  61.0 7.1 %collective-permute-done = bf16[96,3584]{1,0:T(8,128)(2,1)} collective-permute-done((bf16[96,3584]{1,0:T(8,128)(2,1)}, bf16[96,3584]{1,0:T(8,128)(2,1)}, u32[]{:S(2)}, u32[]{:S(2)}) %collective-permute-start) | collective-permute-done | bytes 688160 | tf_op jit(solution)/shard_map/ppermute | solution.py:40
  71.1 2.1 constant_dynamic-update-slice_fusion.5
  73.1 9.6 %collective-permute-done.1 = bf16[96,3584]{1,0:T(8,128)(2,1)S(1)} collective-permute-done((bf16[96,3584]{1,0:T(8,128)(2,1)}, bf16[96,3584]{1,0:T(8,128)(2,1)S(1)}, u32[]{:S(2)}, u32[]{:S(2)}) %collective-permute-start.1) | collective-permute-done | bytes 688160 | tf_op jit(solution)/shard_map/ppermute | solution.py:40
  86.0 11.3 %collective-permute-done.4 = bf16[96,3584]{1,0:T(8,128)(2,1)S(1)} collective-permute-done((bf16[96,3584]{1,0:T(8,128)(2,1)}, bf16[96,3584]{1,0:T(8,128)(2,1)S(1)}, u32[]{:S(2)}, u32[]{:S(2)}) %collective-permute-start.4) | collective-permute-done | bytes 688160 | tf_op jit(solution)/shard_map/ppermute | solution.py:50
  103.4 5.1 %fusion.14 = f32[768,512]{1,0:T(8,128)S(1)} fusion(bf16[768,3584]{1,0:T(8,128)(2,1)} %constant_dynamic-update-slice_fusion, bf16[1,3584,512]{2,1,0:T(8,128)(2,1)S(1)} %copy-done.6), kind=kOutput, calls=%fused_computation.25 | convolution fusion | flops 2818572288 | bytes 10747904 | tf_op jit(solution)/shard_map/dot_general | solution.py:129
  108.6 5.2 %multiply_convert_fusion.3 = (bf16[768,512]{1,0:T(8,128)(2,1)S(1)}, f32[768,512]{1,0:T(8,128)S(1)}) fusion(f32[768,512]{1,0:T(8,128)S(1)} %fusion.14, bf16[768,3584]{1,0:T(8,128)(2,1)} %constant_dynamic-update-slice_fusion, bf16[1,3584,512]{2,1,0:T(8,128)(2,1)S(1)} %copy-done.7), kind=kOutput, calls=%fused_computation.34 | convolution fusion | flops 2820931584 | bytes 13107200 | tf_op jit(solution)/shard_map/dot_general | solution.py:130
  115.3 2.3 convolution_convert_fusion
  119.1 10.6 %collective-permute-done.8 = bf16[96,3584]{1,0:T(8,128)(2,1)S(1)} collective-permute-done((bf16[96,3584]{1,0:T(8,128)(2,1)S(1)}, bf16[96,3584]{1,0:T(8,128)(2,1)S(1)}, u32[]{:S(2)}, u32[]{:S(2)}) %collective-permute-start.8) | collective-permute-done | bytes 688160 | tf_op jit(solution)/shard_map/ppermute | solution.py:40
  135.5 25.1 %collective-permute-done.10 = bf16[96,3584]{1,0:T(8,128)(2,1)S(1)} collective-permute-done((bf16[96,3584]{1,0:T(8,128)(2,1)S(1)}, bf16[96,3584]{1,0:T(8,128)(2,1)S(1)}, u32[]{:S(2)}, u32[]{:S(2)}) %collective-permute-start.10) | collective-permute-done | bytes 688160 | tf_op jit(solution)/shard_map/ppermute | solution.py:50
  163.5 4.6 %fusion.2 = bf16[1,512,3584]{2,1,0:T(8,128)(2,1)} fusion(bf16[768,512]{1,0:T(8,128)(2,1)S(1)} %get-tuple-element.51, bf16[768,3584]{1,0:T(8,128)(2,1)S(1)} %constant_dynamic-update-slice_fusion.7), kind=kOutput, calls=%fused_computation.7 | convolution fusion | flops 2820407296 | bytes 9961472 | tf_op jit(solution)/shard_map/dot_general | solution.py:22
  168.1 3.5 %multiply_convert_fusion.1 = (bf16[768,512]{1,0:T(8,128)(2,1)S(1)}, bf16[768,512]{1,0:T(8,128)(2,1)S(1)}) fusion(f32[768,512]{1,0:T(8,128)S(1)} %fusion.14, f32[768,512]{1,0:T(8,128)S(1)} %get-tuple-element.40, bf16[768,3584]{1,0:T(8,128)(2,1)S(1)} %constant_dynamic-update-slice_fusion.7, bf16[1,512,3584]{2,1,0:T(8,128)(2,1)S(1)} %copy-done.2), kind=kOutput, calls=%fused_computation.31 | convolution fusion | flops 2823684096 | bytes 13893632 | tf_op jit(solution)/shard_map/dot_general | solution.py:16
  171.6 5.7 %fusion.12 = f32[768,3584]{1,0:T(8,128)} fusion(bf16[768,512]{1,0:T(8,128)(2,1)S(1)} %get-tuple-element.49, bf16[1,3584,512]{2,1,0:T(8,128)(2,1)S(1)} %copy-done.6), kind=kOutput, calls=%fused_computation.23 | convolution fusion | flops 2818572288 | bytes 15466496 | tf_op jit(solution)/shard_map/dot_general | solution.py:16
  177.3 6.2 %add_convert_fusion = bf16[768,3584]{1,0:T(8,128)(2,1)S(1)} fusion(f32[768,3584]{1,0:T(8,128)} %fusion.12, bf16[768,512]{1,0:T(8,128)(2,1)S(1)} %get-tuple-element.50, bf16[1,3584,512]{2,1,0:T(8,128)(2,1)S(1)} %copy-done.8), kind=kOutput, calls=%fused_computation | convolution fusion | flops 2824077312 | bytes 20971520 | tf_op jit(solution)/shard_map/dot_general | solution.py:16
  183.6 6.8 %collective-permute-done.14 = bf16[192,3584]{1,0:T(8,128)(2,1)S(1)} collective-permute-done((bf16[192,3584]{1,0:T(8,128)(2,1)S(1)}, bf16[192,3584]{1,0:T(8,128)(2,1)S(1)}, u32[]{:S(2)}, u32[]{:S(2)}) %collective-permute-start.14) | collective-permute-done | bytes 1376288 | tf_op jit(solution)/shard_map/ppermute | solution.py:89
  195.2 3.9 %all-to-all-start.2 = ((bf16[8,24,3584]{2,1,0:T(8,128)(2,1)}), bf16[8,24,3584]{2,1,0:T(8,128)(2,1)S(1)}, u32[]{:S(2)}, u32[]{:S(2)}) async-start(bf16[8,24,3584]{2,1,0:T(8,128)(2,1)} %bitcast.82), calls=%async_computation.2 | async-start | bytes 2752512 | tf_op jit(solution)/shard_map/all_to_all | solution.py:28
  199.1 5.7 %collective-permute-done.18 = bf16[96,3584]{1,0:T(8,128)(2,1)} collective-permute-done((bf16[96,3584]{1,0:T(8,128)(2,1)}, bf16[96,3584]{1,0:T(8,128)(2,1)}, u32[]{:S(2)}, u32[]{:S(2)}) %collective-permute-start.18) | collective-permute-done | bytes 688160 | tf_op jit(solution)/shard_map/ppermute | solution.py:69
  206.3 2.0 add_convert_fusion.4
  209.5 7.1 %fusion = bf16[1,3584,512]{2,1,0:T(8,128)(2,1)} fusion(bf16[768,3584]{1,0:T(8,128)(2,1)} %constant_dynamic-update-slice_fusion, bf16[768,512]{1,0:T(8,128)(2,1)S(1)} %copy-done.10), kind=kOutput, calls=%fused_computation.5 | convolution fusion | flops 2820407296 | bytes 9961472 | tf_op jit(solution)/shard_map/dot_general | solution.py:22
  216.6 7.1 %fusion.1 = bf16[1,3584,512]{2,1,0:T(8,128)(2,1)} fusion(bf16[768,3584]{1,0:T(8,128)(2,1)} %constant_dynamic-update-slice_fusion, bf16[768,512]{1,0:T(8,128)(2,1)S(1)} %copy-done.12), kind=kOutput, calls=%fused_computation.6 | convolution fusion | flops 2820407296 | bytes 9961472 | tf_op jit(solution)/shard_map/dot_general | solution.py:22
  223.7 11.2 %collective-permute-done.19 = bf16[192,3584]{1,0:T(8,128)(2,1)S(1)} collective-permute-done((bf16[192,3584]{1,0:T(8,128)(2,1)S(1)}, bf16[192,3584]{1,0:T(8,128)(2,1)S(1)}, u32[]{:S(2)}, u32[]{:S(2)}) %collective-permute-start.19) | collective-permute-done | bytes 1376288 | tf_op jit(solution)/shard_map/ppermute | solution.py:90
  235.4 2.9 %add_convert_fusion.1 = bf16[192,3584]{1,0:T(8,128)(2,1)} fusion(bf16[192,3584]{1,0:T(8,128)(2,1)S(1)} %collective-permute-done.19, bf16[192,3584]{1,0:T(8,128)(2,1)S(1)} %collective-permute-done.17, bf16[768,3584]{1,0:T(8,128)(2,1)} %copy-done.3), kind=kLoop, calls=%fused_computation.28 | loop fusion | flops 4128768 | bytes 5505024 | tf_op jit(solution)/shard_map/convert_element_type | solution.py:99
  238.3 4.7 %all-to-all-start.3 = ((bf16[8,24,3584]{2,1,0:T(8,128)(2,1)}), bf16[8,24,3584]{2,1,0:T(8,128)(2,1)}, u32[]{:S(2)}, u32[]{:S(2)}) async-start(bf16[8,24,3584]{2,1,0:T(8,128)(2,1)} %bitcast.83), calls=%async_computation.3 | async-start | bytes 2752512 | tf_op jit(solution)/shard_map/all_to_all | solution.py:28
  243.0 2.2 multiply_reduce_fusion
  246.2 1.9 convolution_convert_fusion.7
  248.1 28.6 %all-to-all-done.3 = bf16[8,24,3584]{2,1,0:T(8,128)(2,1)} async-done(((bf16[8,24,3584]{2,1,0:T(8,128)(2,1)}), bf16[8,24,3584]{2,1,0:T(8,128)(2,1)}, u32[]{:S(2)}, u32[]{:S(2)}) %all-to-all-start.3) | async-done | bytes 1376288 | tf_op jit(solution)/shard_map/all_to_all | solution.py:28
  276.7 2.7 convolution_convert_fusion.6
  (105 shorter events, 42.2 us)
Async XLA Ops:
  0.6 51.8 %copy-start = (bf16[128,3584]{1,0:T(8,128)(2,1)S(1)}, bf16[128,3584]{1,0:T(8,128)(2,1)}, u32[]{:S(2)}) copy-start(bf16[128,3584]{1,0:T(8,128)(2,1)} %param.10) | copy-start | bytes 2752516
  1.7 12.9 %copy-start.5 = (f32[128,8]{0,1:T(8,128)S(1)}, f32[128,8]{0,1:T(8,128)}, u32[]{:S(2)}) copy-start(f32[128,8]{0,1:T(8,128)} %param.8) | copy-start | bytes 12292
  8.3 39.9 %all-to-all-start = ((bf16[8,24,3584]{2,1,0:T(8,128)(2,1)}), bf16[8,24,3584]{2,1,0:T(8,128)(2,1)S(1)}, u32[]{:S(2)}, u32[]{:S(2)}) async-start(bf16[8,24,3584]{2,1,0:T(8,128)(2,1)} %bitcast.84), calls=%async_computation | async-start | bytes 2752512 | tf_op jit(solution)/shard_map/all_to_all | solution.py:28
  49.4 18.7 %collective-permute-start = (bf16[96,3584]{1,0:T(8,128)(2,1)}, bf16[96,3584]{1,0:T(8,128)(2,1)}, u32[]{:S(2)}, u32[]{:S(2)}) collective-permute-start(bf16[96,3584]{1,0:T(8,128)(2,1)} %bitcast.3), channel_id=1, source_target_pairs={{0,8},{8,0},{16,24},{24,16},{1,9},{9,1},{17,25},{25,17},{2,10},{10... | collective-permute-start | bytes 2064392 | tf_op jit(solution)/shard_map/ppermute | solution.py:40
  50.9 18.7 %collective-permute-start.3 = (bf16[96,3584]{1,0:T(8,128)(2,1)}, bf16[96,3584]{1,0:T(8,128)(2,1)S(1)}, u32[]{:S(2)}, u32[]{:S(2)}) collective-permute-start(bf16[96,3584]{1,0:T(8,128)(2,1)} %bitcast.4), channel_id=1, source_target_pairs={{0,16},{8,24},{16,0},{24,8},{1,17},{9,25},{17,1},{25,9},{2,18},{10... | collective-permute-start | bytes 2064392 | tf_op jit(solution)/shard_map/ppermute | solution.py:40
  54.9 44.2 %all-to-all-start.1 = ((bf16[8,24,3584]{2,1,0:T(8,128)(2,1)}), bf16[8,24,3584]{2,1,0:T(8,128)(2,1)S(1)}, u32[]{:S(2)}, u32[]{:S(2)}) async-start(bf16[8,24,3584]{2,1,0:T(8,128)(2,1)} %bitcast.81), calls=%async_computation.1 | async-start | bytes 2752512 | tf_op jit(solution)/shard_map/all_to_all | solution.py:28
  58.7 25.6 %collective-permute-start.2 = (bf16[96,3584]{1,0:T(8,128)(2,1)}, bf16[96,3584]{1,0:T(8,128)(2,1)S(1)}, u32[]{:S(2)}, u32[]{:S(2)}) collective-permute-start(bf16[96,3584]{1,0:T(8,128)(2,1)} %bitcast.3), channel_id=1, source_target_pairs={{0,16},{8,24},{16,0},{24,8},{1,17},{9,25},{17,1},{25,9},{2,18},{10... | collective-permute-start | bytes 2064392 | tf_op jit(solution)/shard_map/ppermute | solution.py:40
  59.2 23.5 %collective-permute-start.1 = (bf16[96,3584]{1,0:T(8,128)(2,1)}, bf16[96,3584]{1,0:T(8,128)(2,1)S(1)}, u32[]{:S(2)}, u32[]{:S(2)}) collective-permute-start(bf16[96,3584]{1,0:T(8,128)(2,1)} %bitcast.4), channel_id=1, source_target_pairs={{0,8},{8,0},{16,24},{24,16},{1,9},{9,1},{17,25},{25,17},{2,10},{10... | collective-permute-start | bytes 2064392 | tf_op jit(solution)/shard_map/ppermute | solution.py:40
  68.1 29.2 %collective-permute-start.4 = (bf16[96,3584]{1,0:T(8,128)(2,1)}, bf16[96,3584]{1,0:T(8,128)(2,1)S(1)}, u32[]{:S(2)}, u32[]{:S(2)}) collective-permute-start(bf16[96,3584]{1,0:T(8,128)(2,1)} %collective-permute-done), channel_id=1, source_target_pairs={{0,16},{8,24},{16,0},{24,8},{1,17},{9,25},{17,1},{25,9},{2,18},{10... | collective-permute-start | bytes 2064392 | tf_op jit(solution)/shard_map/ppermute | solution.py:50
  69.6 28.6 %collective-permute-start.5 = (bf16[96,3584]{1,0:T(8,128)(2,1)S(1)}, bf16[96,3584]{1,0:T(8,128)(2,1)S(1)}, u32[]{:S(2)}, u32[]{:S(2)}) collective-permute-start(bf16[96,3584]{1,0:T(8,128)(2,1)S(1)} %collective-permute-done.3), channel_id=1, source_target_pairs={{0,8},{8,0},{16,24},{24,16},{1,9},{9,1},{17,25},{25,17},{2,10},{10... | collective-permute-start | bytes 2064392 | tf_op jit(solution)/shard_map/ppermute | solution.py:51
  99.2 18.5 %collective-permute-start.9 = (bf16[96,3584]{1,0:T(8,128)(2,1)S(1)}, bf16[96,3584]{1,0:T(8,128)(2,1)S(1)}, u32[]{:S(2)}, u32[]{:S(2)}) collective-permute-start(bf16[96,3584]{1,0:T(8,128)(2,1)S(1)} %get-tuple-element.86), channel_id=1, source_target_pairs={{0,16},{8,24},{16,0},{24,8},{1,17},{9,25},{17,1},{25,9},{2,18},{10... | collective-permute-start | bytes 2064392 | tf_op jit(solution)/shard_map/ppermute | solution.py:40
  100.8 18.4 %collective-permute-start.7 = (bf16[96,3584]{1,0:T(8,128)(2,1)S(1)}, bf16[96,3584]{1,0:T(8,128)(2,1)S(1)}, u32[]{:S(2)}, u32[]{:S(2)}) collective-permute-start(bf16[96,3584]{1,0:T(8,128)(2,1)S(1)} %get-tuple-element.86), channel_id=1, source_target_pairs={{0,8},{8,0},{16,24},{24,16},{1,9},{9,1},{17,25},{25,17},{2,10},{10... | collective-permute-start | bytes 2064392 | tf_op jit(solution)/shard_map/ppermute | solution.py:40
  101.3 28.5 %collective-permute-start.8 = (bf16[96,3584]{1,0:T(8,128)(2,1)S(1)}, bf16[96,3584]{1,0:T(8,128)(2,1)S(1)}, u32[]{:S(2)}, u32[]{:S(2)}) collective-permute-start(bf16[96,3584]{1,0:T(8,128)(2,1)S(1)} %get-tuple-element.87), channel_id=1, source_target_pairs={{0,16},{8,24},{16,0},{24,8},{1,17},{9,25},{17,1},{25,9},{2,18},{10... | collective-permute-start | bytes 2064392 | tf_op jit(solution)/shard_map/ppermute | solution.py:40
  101.8 29.3 %collective-permute-start.6 = (bf16[96,3584]{1,0:T(8,128)(2,1)S(1)}, bf16[96,3584]{1,0:T(8,128)(2,1)S(1)}, u32[]{:S(2)}, u32[]{:S(2)}) collective-permute-start(bf16[96,3584]{1,0:T(8,128)(2,1)S(1)} %get-tuple-element.87), channel_id=1, source_target_pairs={{0,8},{8,0},{16,24},{24,16},{1,9},{9,1},{17,25},{25,17},{2,10},{10... | collective-permute-start | bytes 2064392 | tf_op jit(solution)/shard_map/ppermute | solution.py:40
  117.7 43.3 %copy-start.4 = (bf16[576,3584]{1,0:T(8,128)(2,1)}, bf16[576,3584]{1,0:T(8,128)(2,1)S(1)}, u32[]{:S(2)}) copy-start(bf16[576,3584]{1,0:T(8,128)(2,1)S(1)} %convolution_convert_fusion) | copy-start | bytes 12386308
  131.1 29.8 %collective-permute-start.12 = (bf16[96,3584]{1,0:T(8,128)(2,1)S(1)}, bf16[96,3584]{1,0:T(8,128)(2,1)S(1)}, u32[]{:S(2)}, u32[]{:S(2)}) collective-permute-start(bf16[96,3584]{1,0:T(8,128)(2,1)S(1)} %convolution_convert_fusion.9), channel_id=1, source_target_pairs={{0,8},{8,0},{16,24},{24,16},{1,9},{9,1},{17,25},{25,17},{2,10},{10... | collective-permute-start | bytes 2064392 | tf_op jit(solution)/shard_map/ppermute | solution.py:69
  131.7 29.3 %collective-permute-start.13 = (bf16[96,3584]{1,0:T(8,128)(2,1)S(1)}, bf16[96,3584]{1,0:T(8,128)(2,1)S(1)}, u32[]{:S(2)}, u32[]{:S(2)}) collective-permute-start(bf16[96,3584]{1,0:T(8,128)(2,1)S(1)} %convolution_convert_fusion.8), channel_id=1, source_target_pairs={{0,16},{8,24},{16,0},{24,8},{1,17},{9,25},{17,1},{25,9},{2,18},{10... | collective-permute-start | bytes 2064392 | tf_op jit(solution)/shard_map/ppermute | solution.py:70
  132.1 28.5 %collective-permute-start.10 = (bf16[96,3584]{1,0:T(8,128)(2,1)S(1)}, bf16[96,3584]{1,0:T(8,128)(2,1)S(1)}, u32[]{:S(2)}, u32[]{:S(2)}) collective-permute-start(bf16[96,3584]{1,0:T(8,128)(2,1)S(1)} %collective-permute-done.6), channel_id=1, source_target_pairs={{0,16},{8,24},{16,0},{24,8},{1,17},{9,25},{17,1},{25,9},{2,18},{10... | collective-permute-start | bytes 2064392 | tf_op jit(solution)/shard_map/ppermute | solution.py:50
  133.7 27.2 %collective-permute-start.11 = (bf16[96,3584]{1,0:T(8,128)(2,1)S(1)}, bf16[96,3584]{1,0:T(8,128)(2,1)S(1)}, u32[]{:S(2)}, u32[]{:S(2)}) collective-permute-start(bf16[96,3584]{1,0:T(8,128)(2,1)S(1)} %collective-permute-done.9), channel_id=1, source_target_pairs={{0,8},{8,0},{16,24},{24,16},{1,9},{9,1},{17,25},{25,17},{2,10},{10... | collective-permute-start | bytes 2064392 | tf_op jit(solution)/shard_map/ppermute | solution.py:51
  161.4 28.9 %collective-permute-start.14 = (bf16[192,3584]{1,0:T(8,128)(2,1)S(1)}, bf16[192,3584]{1,0:T(8,128)(2,1)S(1)}, u32[]{:S(2)}, u32[]{:S(2)}) collective-permute-start(bf16[192,3584]{1,0:T(8,128)(2,1)S(1)} %pad_maximum_fusion), channel_id=1, source_target_pairs={{0,8},{8,0},{16,24},{24,16},{1,9},{9,1},{17,25},{25,17},{2,10},{10... | collective-permute-start | bytes 4128776 | tf_op jit(solution)/shard_map/ppermute | solution.py:89
  162.9 28.0 %collective-permute-start.15 = (bf16[192,3584]{1,0:T(8,128)(2,1)S(1)}, bf16[192,3584]{1,0:T(8,128)(2,1)S(1)}, u32[]{:S(2)}, u32[]{:S(2)}) collective-permute-start(bf16[192,3584]{1,0:T(8,128)(2,1)S(1)} %pad_maximum_fusion.1), channel_id=1, source_target_pairs={{0,16},{8,24},{16,0},{24,8},{1,17},{9,25},{17,1},{25,9},{2,18},{10... | collective-permute-start | bytes 4128776 | tf_op jit(solution)/shard_map/ppermute | solution.py:90
  171.6 5.8 %copy-start.9 = (bf16[768,512]{1,0:T(8,128)(2,1)}, bf16[768,512]{1,0:T(8,128)(2,1)S(1)}, u32[]{:S(2)}) copy-start(bf16[768,512]{1,0:T(8,128)(2,1)S(1)} %get-tuple-element.49) | copy-start | bytes 2359300
  183.6 7.3 %copy-start.3 = (bf16[768,3584]{1,0:T(8,128)(2,1)}, bf16[768,3584]{1,0:T(8,128)(2,1)S(1)}, u32[]{:S(2)}) copy-start(bf16[768,3584]{1,0:T(8,128)(2,1)S(1)} %add_convert_fusion) | copy-start | bytes 16515076
  183.6 10.0 %slice-start = ((bf16[576,3584]{1,0:T(8,128)(2,1)}), bf16[192,3584]{1,0:T(8,128)(2,1)S(1)}, s32[]{:S(2)}) async-start(bf16[576,3584]{1,0:T(8,128)(2,1)} %copy-done.4), calls=%async_computation.4 | async-start | bytes 2752512 | tf_op jit(solution)/shard_map/split | solution.py:78
  192.1 12.7 %collective-permute-start.18 = (bf16[96,3584]{1,0:T(8,128)(2,1)}, bf16[96,3584]{1,0:T(8,128)(2,1)}, u32[]{:S(2)}, u32[]{:S(2)}) collective-permute-start(bf16[96,3584]{1,0:T(8,128)(2,1)} %get-tuple-element.76), channel_id=1, source_target_pairs={{0,8},{8,0},{16,24},{24,16},{1,9},{9,1},{17,25},{25,17},{2,10},{10... | collective-permute-start | bytes 2064392 | tf_op jit(solution)/shard_map/ppermute | solution.py:69
  193.0 13.3 %collective-permute-start.16 = (bf16[96,3584]{1,0:T(8,128)(2,1)}, bf16[96,3584]{1,0:T(8,128)(2,1)}, u32[]{:S(2)}, u32[]{:S(2)}) collective-permute-start(bf16[96,3584]{1,0:T(8,128)(2,1)} %get-tuple-element.77), channel_id=1, source_target_pairs={{0,16},{8,24},{16,0},{24,8},{1,17},{9,25},{17,1},{25,9},{2,18},{10... | collective-permute-start | bytes 2064392 | tf_op jit(solution)/shard_map/ppermute | solution.py:70
  195.2 43.1 %all-to-all-start.2 = ((bf16[8,24,3584]{2,1,0:T(8,128)(2,1)}), bf16[8,24,3584]{2,1,0:T(8,128)(2,1)S(1)}, u32[]{:S(2)}, u32[]{:S(2)}) async-start(bf16[8,24,3584]{2,1,0:T(8,128)(2,1)} %bitcast.82), calls=%async_computation.2 | async-start | bytes 2752512 | tf_op jit(solution)/shard_map/all_to_all | solution.py:28
  208.5 26.4 %collective-permute-start.19 = (bf16[192,3584]{1,0:T(8,128)(2,1)S(1)}, bf16[192,3584]{1,0:T(8,128)(2,1)S(1)}, u32[]{:S(2)}, u32[]{:S(2)}) collective-permute-start(bf16[192,3584]{1,0:T(8,128)(2,1)S(1)} %pad_maximum_fusion.3), channel_id=1, source_target_pairs={{0,16},{8,24},{16,0},{24,8},{1,17},{9,25},{17,1},{25,9},{2,18},{10... | collective-permute-start | bytes 4128776 | tf_op jit(solution)/shard_map/ppermute | solution.py:90
  208.7 7.9 %copy-start.12 = (bf16[768,512]{1,0:T(8,128)(2,1)S(1)}, bf16[768,512]{1,0:T(8,128)(2,1)}, u32[]{:S(2)}) copy-start(bf16[768,512]{1,0:T(8,128)(2,1)} %copy-done.11) | copy-start | bytes 2359300
  208.7 26.7 %collective-permute-start.17 = (bf16[192,3584]{1,0:T(8,128)(2,1)S(1)}, bf16[192,3584]{1,0:T(8,128)(2,1)S(1)}, u32[]{:S(2)}, u32[]{:S(2)}) collective-permute-start(bf16[192,3584]{1,0:T(8,128)(2,1)S(1)} %pad_maximum_fusion.2), channel_id=1, source_target_pairs={{0,8},{8,0},{16,24},{24,16},{1,9},{9,1},{17,25},{25,17},{2,10},{10... | collective-permute-start | bytes 4128776 | tf_op jit(solution)/shard_map/ppermute | solution.py:89
  238.3 38.5 %all-to-all-start.3 = ((bf16[8,24,3584]{2,1,0:T(8,128)(2,1)}), bf16[8,24,3584]{2,1,0:T(8,128)(2,1)}, u32[]{:S(2)}, u32[]{:S(2)}) async-start(bf16[8,24,3584]{2,1,0:T(8,128)(2,1)} %bitcast.83), calls=%async_computation.3 | async-start | bytes 2752512 | tf_op jit(solution)/shard_map/all_to_all | solution.py:28
  243.0 36.4 %copy-start.1 = (bf16[128,3584]{1,0:T(8,128)(2,1)S(1)}, bf16[128,3584]{1,0:T(8,128)(2,1)}, u32[]{:S(2)}) copy-start(bf16[128,3584]{1,0:T(8,128)(2,1)} %param.10) | copy-start | bytes 2752516
  (6 other events, 27.4 us)
